TPU v7x, 32 devices: a whole 2x2x4 slice. The times are simulated.
32 devices in a mesh: ctx: 8 (over z, y), dp: 2 (over x), section: 2 (over core).
Axes of the slice: x: 2, y: 2, z: 4, core: 2. Of those that a mesh axis runs over, the one named last changes fastest.
Arguments:
- normed: bfloat16 [2, 3072, 1024], P('dp', 'ctx'), may hold values from -40 to 40
- w_query: bfloat16 [1024, 1024], P('dp', 'section'), may hold values from -0.1875 to 0.1875
- w_key: bfloat16 [1024, 1024], P('dp', 'section'), may hold values from -0.28125 to 0.28125
- w_value: bfloat16 [1024, 1024], P('dp', 'section'), may hold values from -0.1875 to 0.1875
- block_mask: int32 [24, 7], replicated, may hold values from 0 to 1, as said below
- cotangent: bfloat16 [2, 3072, 1024], P('dp', 'ctx', 'section'), may hold values from -8 to 8
Outputs:
- attended: bfloat16 [2, 3072, 1024], P('dp', 'ctx', 'section')
- grad_input: bfloat16 [2, 3072, 1024], P('dp', 'ctx')
- grad_weights: float32 [1024, 3, 1024], P(('ctx', 'dp'), None, 'section')
Inputs may be any that keep to these rules, and one draw needn't show every extreme that they name: `block_mask`: every row has a 1 in column 3; no row names a key block outside 0 to 23; a row holds at most 5 ones, and some row holds exactly 5.
All inputs are finite; a program needn't handle non-finite values.
Results may differ from a plain program's by a relative error of at most 0.014.
The roundings to bfloat16 on the way count: a program that leaves them out, or rounds other values in their place, can miss the bound.
Values may be sent and summed in bfloat16 or wider, within the bound.
No kernel may reach another device: no remote copies, remote signals or barrier semaphores. Data moves between devices by JAX's collectives and lax.ppermute only.
A program may use at most 64 MiB of HBM per device.

v0:
```python
import jax
import jax.numpy as jnp
from jax import lax
from jax.sharding import PartitionSpec as P

HD = 64
BLOCK = 128
REACH = 3


def extended(cells, sides, width):
    for axis, dim in sides:
        count = lax.axis_size(axis)
        ends = count - 1
        head = lax.slice_in_dim(cells, 0, width, axis=dim)
        tail = lax.slice_in_dim(cells, cells.shape[dim] - width, cells.shape[dim], axis=dim)
        cells = jnp.concatenate(
            [
                lax.ppermute(tail, axis, [(i, (i + 1) % count) for i in range(ends)]),
                cells,
                lax.ppermute(head, axis, [((i + 1) % count, i) for i in range(ends)]),
            ],
            axis=dim,
        )
    return cells


def shifted(value, axis, steps):
    count = lax.axis_size(axis)
    leading, last = (max(0, -steps), min(count, count - steps))
    return lax.ppermute(value, axis, [(source, source + steps) for source in range(leading, last)])


def attend(query_block, key_window, seen_slots, score_scale):
    scores = (
        jnp.einsum("qhd,skhd->hqsk", query_block, key_window, preferred_element_type=jnp.float32)
        * score_scale
    )
    is_seen = seen_slots[None, None, :, None] > 0
    row_top = jnp.max(jnp.where(is_seen, scores, -jnp.inf), axis=(2, 3), keepdims=True)
    raised = jnp.where(is_seen, jnp.exp(scores - row_top), 0.0)
    row_total = jnp.sum(raised, axis=(2, 3), keepdims=True)
    return (raised / row_total, row_top, row_total)


def per_device(normed, w_query, w_key, w_value, block_mask, cotangent):
    tokens = normed[0]
    upstream = cotangent[0]
    length = tokens.shape[0]
    features = upstream.shape[1]
    head_count = features // HD
    blocks = length // BLOCK
    frame_len = blocks + 2 * REACH
    span_len = 2 * REACH + 1
    score_scale = HD ** (-0.5)
    query_full, key_full, value_full = (
        lax.all_gather(w_query, "dp", axis=0, tiled=True),
        lax.all_gather(w_key, "dp", axis=0, tiled=True),
        lax.all_gather(w_value, "dp", axis=0, tiled=True),
    )
    queries = jnp.dot(tokens, query_full, preferred_element_type=jnp.float32).astype(jnp.bfloat16)
    key_rows = jnp.dot(tokens, key_full, preferred_element_type=jnp.float32).astype(jnp.bfloat16)
    value_rows = jnp.dot(tokens, value_full, preferred_element_type=jnp.float32).astype(
        jnp.bfloat16
    )
    framed = extended(jnp.stack([key_rows, value_rows]), (("ctx", 1),), REACH * BLOCK)
    framed = framed.reshape(2, frame_len, BLOCK, head_count, HD)
    query_blocks = queries.reshape(blocks, BLOCK, head_count, HD)
    upstream_blocks = upstream.reshape(blocks, BLOCK, head_count, HD)
    first_block = lax.axis_index("ctx") * blocks
    padded_mask = jnp.pad(block_mask, ((REACH, REACH), (0, 0)))
    frame_mask = lax.dynamic_slice(padded_mask, (first_block, 0), (frame_len, span_len))
    own_mask = frame_mask[REACH : REACH + blocks]
    positions = jnp.arange(span_len, dtype=jnp.int32)
    slot_order = jnp.broadcast_to(positions[None, :], (blocks, span_len))
    slot_index = slot_order + jnp.arange(blocks, dtype=jnp.int32)[:, None]

    def windows(block_at):
        picked = lax.dynamic_slice_in_dim(framed, block_at, span_len, 1)
        return (picked[0], picked[1])

    def forward(running, block_at):
        query_block = lax.dynamic_index_in_dim(query_blocks, block_at, 0, False)
        key_window, value_window = windows(block_at)
        seen_slots = lax.dynamic_index_in_dim(own_mask, block_at, 0, False)
        probability, row_top, row_total = attend(query_block, key_window, seen_slots, score_scale)
        mixed_out = jnp.einsum(
            "hqsk,skhd->qhd",
            probability.astype(jnp.bfloat16),
            value_window,
            preferred_element_type=jnp.float32,
        ).astype(jnp.bfloat16)
        return (running, (mixed_out, row_top[:, :, 0, 0], row_total[:, :, 0, 0]))

    block_ids = jnp.arange(blocks, dtype=jnp.int32)
    _, (mixed_outs, row_tops, row_totals) = lax.scan(forward, jnp.zeros((), jnp.float32), block_ids)
    attended = mixed_outs.reshape(1, length, features)

    def backward(running, block_at):
        query_block = lax.dynamic_index_in_dim(query_blocks, block_at, 0, False)
        upstream_block = lax.dynamic_index_in_dim(upstream_blocks, block_at, 0, False)
        key_window, value_window = windows(block_at)
        seen_slots = lax.dynamic_index_in_dim(own_mask, block_at, 0, False)
        probability, _, _ = attend(query_block, key_window, seen_slots, score_scale)
        weights = probability.astype(jnp.bfloat16)
        prob_grad = jnp.einsum(
            "qhd,skhd->hqsk", upstream_block, value_window, preferred_element_type=jnp.float32
        )
        row_delta = jnp.sum(probability * prob_grad, axis=(2, 3), keepdims=True)
        score_grad = (probability * (prob_grad - row_delta)).astype(jnp.bfloat16)
        query_grad = (
            score_scale
            * jnp.einsum(
                "hqsk,skhd->qhd", score_grad, key_window, preferred_element_type=jnp.float32
            )
        ).astype(jnp.bfloat16)
        key_part = score_scale * jnp.einsum(
            "hqsk,qhd->skhd", score_grad, query_block, preferred_element_type=jnp.float32
        )
        value_part = jnp.einsum(
            "hqsk,qhd->skhd", weights, upstream_block, preferred_element_type=jnp.float32
        )
        slot_rows = lax.dynamic_index_in_dim(slot_index, block_at, 0, False)
        running = running.at[0, slot_rows].add(key_part).at[1, slot_rows].add(value_part)
        return (running, (query_grad, row_delta[:, :, 0, 0]))

    start_state = jnp.zeros((2, frame_len, BLOCK, head_count, HD), jnp.float32)
    frame_grads, (query_grads, row_deltas) = lax.scan(backward, start_state, block_ids)
    query_grad = query_grads.reshape(length, features)
    frame_grads = frame_grads.reshape(2, frame_len, BLOCK, features)
    left_side = frame_grads[:, :REACH]
    right_side = frame_grads[:, blocks + REACH :]
    middle = frame_grads[:, REACH : REACH + blocks]
    for offset in (1, -1):
        outgoing = right_side if offset == 1 else left_side
        arrived = shifted(outgoing.astype(jnp.bfloat16), "ctx", offset).astype(outgoing.dtype)
        if offset == 1:
            middle = middle.at[:, :REACH].add(arrived)
        else:
            middle = middle.at[:, blocks - REACH :].add(arrived)
    key_grad = middle[0].reshape(length, features).astype(jnp.bfloat16)
    value_grad = middle[1].reshape(length, features).astype(jnp.bfloat16)
    contract = (((1,), (1,)), ((), ()))
    partial_input = (
        lax.dot_general(query_grad, query_full, contract, preferred_element_type=jnp.float32)
        + lax.dot_general(key_grad, key_full, contract, preferred_element_type=jnp.float32)
        + lax.dot_general(value_grad, value_full, contract, preferred_element_type=jnp.float32)
    )
    grad_input = lax.psum(partial_input.astype(jnp.bfloat16), "section")[None]
    grads_all = jnp.stack([query_grad, key_grad, value_grad], axis=1)
    group_part = lax.psum_scatter(
        jnp.einsum("tr,tcf->rcf", tokens, grads_all, preferred_element_type=jnp.float32).astype(
            jnp.bfloat16
        ),
        "ctx",
        scatter_dimension=0,
        tiled=True,
    )
    summed = lax.psum_scatter(group_part, "dp", scatter_dimension=0, tiled=True).astype(jnp.float32)
    grad_weights = summed / lax.axis_size("dp")
    return (attended, grad_input, grad_weights)


def solution(mesh):
    in_specs = (
        P("dp", "ctx", None),
        P("dp", "section"),
        P("dp", "section"),
        P("dp", "section"),
        P(),
        P("dp", "ctx", "section"),
    )
    out_specs = (P("dp", "ctx", "section"), P("dp", "ctx", None), P(("ctx", "dp"), None, "section"))
    return jax.shard_map(
        per_device, mesh=mesh, in_specs=in_specs, out_specs=out_specs, check_vma=False
    )
```

profile of v0, /device:TPU:12, one launch (start us, length us, event | category | flops | bytes accessed | tf_op | source)
XLA Modules:
  0.0 377.8 jit_solution(11920346828465409349)
XLA Ops:
  9.5 22.5 %all-gather.6.cloned.1.call-done = bf16[1024,512]{1,0:T(8,128)(2,1)} async-done(((bf16[512,512]{1,0:T(8,128)(2,1)}), bf16[1024,512]{1,0:T(8,128)(2,1)}) %all-gather.6.cloned.1.call-update) | async-done | bytes 1048592 | tf_op jit(solution)/shard_map/all_gather | solution.py:59
  33.8 21.1 %all-gather.4.cloned.1.call-done = bf16[1024,512]{1,0:T(8,128)(2,1)} async-done(((bf16[512,512]{1,0:T(8,128)(2,1)}), bf16[1024,512]{1,0:T(8,128)(2,1)}) %all-gather.4.cloned.1.call-update) | async-done | bytes 1048592 | tf_op jit(solution)/shard_map/all_gather | solution.py:58
  57.5 2.5 collective-permute-start.1
  60.0 4.3 %collective-permute-start = (bf16[2,384,512]{2,1,0:T(8,128)(2,1)S(1)}, bf16[2,384,512]{2,1,0:T(8,128)(2,1)}, u32[]{:S(2)}, u32[]{:S(2)}) collective-permute-start(bf16[2,384,512]{2,1,0:T(8,128)(2,1)S(1)} %pad_maximum_fusion.1), channel_id=1, source_target_pairs={{0,4},{4,8},{8,12},{12,16},{16,20},{20,24},{24,28},{1,5},{5,9},{9,... | collective-permute-start | bytes 2359304 | tf_op jit(solution)/shard_map/ppermute | solution.py:19
  66.6 11.2 %all-gather.8.cloned.1.call-done = bf16[1024,512]{1,0:T(8,128)(2,1)} async-done(((bf16[512,512]{1,0:T(8,128)(2,1)}), bf16[1024,512]{1,0:T(8,128)(2,1)}) %all-gather.8.cloned.1.call-update) | async-done | bytes 1048592 | tf_op jit(solution)/shard_map/all_gather | solution.py:57
  80.5 13.2 %collective-permute-done.1 = bf16[2,384,512]{2,1,0:T(8,128)(2,1)S(1)} collective-permute-done((bf16[2,384,512]{2,1,0:T(8,128)(2,1)S(1)}, bf16[2,384,512]{2,1,0:T(8,128)(2,1)S(1)}, u32[]{:S(2)}, u32[]{:S(2)}) %collective-permute-start.1) | collective-permute-done | bytes 786464 | tf_op jit(solution)/shard_map/ppermute | solution.py:21
  98.3 4.6 %reshape.200 = bf16[2,9,128,8,64]{4,3,2,1,0:T(8,128)(2,1)} reshape(bf16[2,1152,512]{2,1,0:T(8,128)(2,1)S(1)} %pad_maximum_fusion) | data formatting | bytes 4718592 | tf_op jit(solution)/shard_map/reshape | solution.py:67
  102.9 6.1 %copy.83 = bf16[2,9,128,8,64]{2,4,1,3,0:T(8,128)(2,1)} copy(bf16[2,9,128,8,64]{4,3,2,1,0:T(8,128)(2,1)} %reshape.200) | data formatting | bytes 4718592 | tf_op jit(solution)/shard_map/while | solution.py:96
  109.1 2.8 broadcast_in_dim.61
  111.9 76.9 %while.27 = (s32[]{:T(128)}, f32[2,9,128,8,64]{2,4,3,1,0:T(8,128)}, bf16[3,128,8,64]{1,3,2,0:T(8,128)(2,1)S(1)}, s32[3]{0:T(128)S(1)}, s32[3,7]{1,0:T(4,128)S(1)...) while((s32[]{:T(128)}, f32[2,9,128,8,64]{2,4,3,1,0:T(8,128)}, ...), condition=%wide.region_10.11_spmd, body=%wide.region_4.10_spmd.sunk | while | flops 611644544 | bytes 56669256 | solution.py:128
  120.7 2.6 multiply_reduce_fusion.2
  128.4 4.8 %scatter_fusion = f32[2,9,128,8,64]{2,4,3,1,0:T(8,128)} fusion(f32[2,9,128,8,64]{2,4,3,1,0:T(8,128)} %get-tuple-element.398, s32[7]{0:T(128)S(1)} %select_bitcast_fusion.5, f32[7,128,8,64]{1,3,2,0:T(8,128)} %copy.129), kind=kCustom, calls=%fused_computation.clone.1 | custom fusion | flops 458752 | bytes 5505080 | tf_op jit(solution)/shard_map/while/body/eval_jaxpr/scatter-add | solution.py:124
  133.3 4.3 %scatter_fusion.1 = f32[2,9,128,8,64]{2,4,3,1,0:T(8,128)} fusion(f32[2,9,128,8,64]{2,4,3,1,0:T(8,128)} %scatter_fusion, s32[7]{0:T(128)S(1)} %get-tuple-element.349, f32[7,128,8,64]{1,3,2,0:T(8,128)S(1)} %copy.130), kind=kCustom, calls=%fused_computation.1.clone.1 | custom fusion | flops 458752 | bytes 5505080 | tf_op jit(solution)/shard_map/while/body/eval_jaxpr/scatter-add | solution.py:124
  146.3 2.6 multiply_reduce_fusion.2
  154.1 4.8 %scatter_fusion = f32[2,9,128,8,64]{2,4,3,1,0:T(8,128)} fusion(f32[2,9,128,8,64]{2,4,3,1,0:T(8,128)} %get-tuple-element.398, s32[7]{0:T(128)S(1)} %select_bitcast_fusion.5, f32[7,128,8,64]{1,3,2,0:T(8,128)} %copy.129), kind=kCustom, calls=%fused_computation.clone.1 | custom fusion | flops 458752 | bytes 5505080 | tf_op jit(solution)/shard_map/while/body/eval_jaxpr/scatter-add | solution.py:124
  158.9 4.2 %scatter_fusion.1 = f32[2,9,128,8,64]{2,4,3,1,0:T(8,128)} fusion(f32[2,9,128,8,64]{2,4,3,1,0:T(8,128)} %scatter_fusion, s32[7]{0:T(128)S(1)} %get-tuple-element.349, f32[7,128,8,64]{1,3,2,0:T(8,128)S(1)} %copy.130), kind=kCustom, calls=%fused_computation.1.clone.1 | custom fusion | flops 458752 | bytes 5505080 | tf_op jit(solution)/shard_map/while/body/eval_jaxpr/scatter-add | solution.py:124
  172.0 2.6 multiply_reduce_fusion.2
  179.8 4.8 %scatter_fusion = f32[2,9,128,8,64]{2,4,3,1,0:T(8,128)} fusion(f32[2,9,128,8,64]{2,4,3,1,0:T(8,128)} %get-tuple-element.398, s32[7]{0:T(128)S(1)} %select_bitcast_fusion.5, f32[7,128,8,64]{1,3,2,0:T(8,128)} %copy.129), kind=kCustom, calls=%fused_computation.clone.1 | custom fusion | flops 458752 | bytes 5505080 | tf_op jit(solution)/shard_map/while/body/eval_jaxpr/scatter-add | solution.py:124
  184.6 4.2 %scatter_fusion.1 = f32[2,9,128,8,64]{2,4,3,1,0:T(8,128)} fusion(f32[2,9,128,8,64]{2,4,3,1,0:T(8,128)} %scatter_fusion, s32[7]{0:T(128)S(1)} %get-tuple-element.349, f32[7,128,8,64]{1,3,2,0:T(8,128)S(1)} %copy.130), kind=kCustom, calls=%fused_computation.1.clone.1 | custom fusion | flops 458752 | bytes 5505080 | tf_op jit(solution)/shard_map/while/body/eval_jaxpr/scatter-add | solution.py:124
  188.8 2.9 bitcast_convert_fusion
  191.9 3.3 collective-permute-start.2
  195.1 2.8 collective-permute-start.3
  200.4 29.8 %collective-permute-done.2 = bf16[2,3,128,512]{2,3,1,0:T(8,128)(2,1)} collective-permute-done((bf16[2,3,128,512]{2,3,1,0:T(8,128)(2,1)S(1)}, bf16[2,3,128,512]{2,3,1,0:T(8,128)(2,1)}, u32[]{:S(2)}, u32[]{:S(2)}) %collective-permute-start.2) | collective-permute-done | bytes 786464 | tf_op jit(solution)/shard_map/ppermute | solution.py:31
  230.2 2.1 fusion.41
  233.2 4.5 %convolution_convert_fusion = bf16[3,512,1024]{2,1,0:T(8,128)(2,1)} fusion(bf16[384,1,512]{0,2,1:T(8,128)(2,1)S(1)} %copy.97, bf16[384,1,512]{0,2,1:T(8,128)(2,1)S(1)} %copy.96, bf16[384,1,512]{0,2,1:T(8,128)(2,1)} %stack_reshape.3, bf16[1,384,1024]{2,1,0:T(8,128)(2,1)S(1)} %copy-done), kind=kOutput, calls=%fused_computation.64 | convolution fusion | flops 1210712064 | bytes 5111808 | tf_op jit(solution)/shard_map/tr,tcf->rcf/dot_general | solution.py:152
  237.7 4.7 %copy.120 = bf16[1024,1536]{1,0:T(8,128)(2,1)} copy(bf16[1024,1536]{0,1:T(8,128)(2,1)} %bitcast.204) | data formatting | bytes 6291456
  245.6 70.1 %reduce-scatter.4.cloned.1.call-done = bf16[128,1536]{1,0:T(8,128)(2,1)} async-done(((bf16[1024,1536]{1,0:T(8,128)(2,1)}), bf16[128,1536]{1,0:T(8,128)(2,1)}) %reduce-scatter.4.cloned.1.call-update) | async-done | bytes 393232
  322.0 27.1 %while.26 = (s32[]{:T(128)}, bf16[3,128,8,64]{1,3,2,0:T(8,128)(2,1)S(1)}, s32[3]{0:T(128)S(1)}, bf16[2,9,128,8,64]{2,4,1,3,0:T(8,128)(2,1)}, s32[3,7]{1,0:T(4,12...) while((s32[]{:T(128)}, ...), condition=%wide.region_3.4_spmd, body=%wide.region_0.3_spmd.sunk | while | flops 245954576 | bytes 13128970 | solution.py:96
  328.6 2.4 fusion.82
  337.7 2.4 fusion.82
  346.7 2.4 fusion.82
  352.7 16.2 %all-reduce.7.cloned.1.call-done = bf16[1,384,1024]{2,1,0:T(8,128)(2,1)} async-done(((bf16[1,384,1024]{2,1,0:T(8,128)(2,1)}), bf16[1,384,1024]{2,1,0:T(8,128)(2,1)}) %all-reduce.7.cloned.1.call-update) | async-done | bytes 786448 | tf_op jit(solution)/shard_map/psum | solution.py:149
  (123 shorter events, 76.3 us)
Async XLA Ops:
  7.2 24.8 %copy-start = (bf16[1,384,1024]{2,1,0:T(8,128)(2,1)S(1)}, bf16[1,384,1024]{2,1,0:T(8,128)(2,1)}, u32[]{:S(2)}) copy-start(bf16[1,384,1024]{2,1,0:T(8,128)(2,1)} %param.18) | copy-start | bytes 2359300
  7.2 24.8 %all-gather.6.cloned.1.call-start = ((), (), s32[]{:S(2)}) async-start(), calls=%async_computation.2 | async-start | bytes 1572864 | tf_op jit(solution)/shard_map/all_gather | solution.py:59
  7.9 47.0 %all-gather.4.cloned.1.call-start = ((), (), s32[]{:S(2)}) async-start(), calls=%async_computation.1 | async-start | bytes 1572864 | tf_op jit(solution)/shard_map/all_gather | solution.py:58
  8.7 55.6 %copy-start.10 = (s32[24,7]{0,1:T(8,128)S(1)}, s32[24,7]{0,1:T(8,128)}, u32[]{:S(2)}) copy-start(s32[24,7]{0,1:T(8,128)} %param.22) | copy-start | bytes 2020
  8.7 55.7 %copy-start.9 = (bf16[1,384,512]{2,1,0:T(8,128)(2,1)S(1)}, bf16[1,384,512]{2,1,0:T(8,128)(2,1)}, u32[]{:S(2)}) copy-start(bf16[1,384,512]{2,1,0:T(8,128)(2,1)} %param.23) | copy-start | bytes 1179652
  8.7 69.1 %all-gather.8.cloned.1.call-start = ((), (), s32[]{:S(2)}) async-start(), calls=%async_computation.3 | async-start | bytes 1572864 | tf_op jit(solution)/shard_map/all_gather | solution.py:57
  9.4 306.3 %reduce-scatter.4.cloned.1.call-start = ((), (), s32[]{:S(2)}) async-start(), calls=%async_computation.5 | async-start | bytes 3538944
  33.8 30.5 %copy-start.4 = (bf16[1,384,512]{2,1,0:T(8,128)(2,1)}, bf16[1,384,512]{2,1,0:T(8,128)(2,1)S(1)}, u32[]{:S(2)}) copy-start(bf16[1,384,512]{2,1,0:T(8,128)(2,1)S(1)} %fusion.44) | copy-start | bytes 1179652
  56.7 0.7 copy-start.5
  57.5 36.1 %collective-permute-start.1 = (bf16[2,384,512]{2,1,0:T(8,128)(2,1)S(1)}, bf16[2,384,512]{2,1,0:T(8,128)(2,1)S(1)}, u32[]{:S(2)}, u32[]{:S(2)}) collective-permute-start(bf16[2,384,512]{2,1,0:T(8,128)(2,1)S(1)} %pad_maximum_fusion.1), channel_id=1, source_target_pairs={{4,0},{8,4},{12,8},{16,12},{20,16},{24,20},{28,24},{5,1},{9,5},{13... | collective-permute-start | bytes 2359304 | tf_op jit(solution)/shard_map/ppermute | solution.py:21
  60.0 36.6 %collective-permute-start = (bf16[2,384,512]{2,1,0:T(8,128)(2,1)S(1)}, bf16[2,384,512]{2,1,0:T(8,128)(2,1)}, u32[]{:S(2)}, u32[]{:S(2)}) collective-permute-start(bf16[2,384,512]{2,1,0:T(8,128)(2,1)S(1)} %pad_maximum_fusion.1), channel_id=1, source_target_pairs={{0,4},{4,8},{8,12},{12,16},{16,20},{20,24},{24,28},{1,5},{5,9},{9,... | collective-permute-start | bytes 2359304 | tf_op jit(solution)/shard_map/ppermute | solution.py:19
  93.6 0.9 copy-start.8
  109.0 2.9 copy-start.11
  188.8 3.1 copy-start.6
  191.9 38.3 %collective-permute-start.2 = (bf16[2,3,128,512]{2,3,1,0:T(8,128)(2,1)S(1)}, bf16[2,3,128,512]{2,3,1,0:T(8,128)(2,1)}, u32[]{:S(2)}, u32[]{:S(2)}) collective-permute-start(bf16[2,3,128,512]{2,3,1,0:T(8,128)(2,1)S(1)} %get-tuple-element.236), channel_id=1, source_target_pairs={{0,4},{4,8},{8,12},{12,16},{16,20},{20,24},{24,28},{1,5},{5,9},{9,... | collective-permute-start | bytes 2359304 | tf_op jit(solution)/shard_map/ppermute | solution.py:31
  195.1 35.0 %collective-permute-start.3 = (bf16[2,3,128,512]{2,3,1,0:T(8,128)(2,1)S(1)}, bf16[2,3,128,512]{2,3,1,0:T(8,128)(2,1)}, u32[]{:S(2)}, u32[]{:S(2)}) collective-permute-start(bf16[2,3,128,512]{2,3,1,0:T(8,128)(2,1)S(1)} %get-tuple-element.237), channel_id=1, source_target_pairs={{4,0},{8,4},{12,8},{16,12},{20,16},{24,20},{28,24},{5,1},{9,5},{13... | collective-permute-start | bytes 2359304 | tf_op jit(solution)/shard_map/ppermute | solution.py:31
  232.5 5.1 %copy-start.1 = (bf16[1,3,128,512]{3,2,1,0:T(8,128)(2,1)}, bf16[1,3,128,512]{3,2,1,0:T(8,128)(2,1)S(1)}, u32[]{:S(2)}) copy-start(bf16[1,3,128,512]{3,2,1,0:T(8,128)(2,1)S(1)} %copy.91) | copy-start | bytes 1179652
  232.7 4.9 %copy-start.2 = (bf16[1,3,128,512]{3,2,1,0:T(8,128)(2,1)}, bf16[1,3,128,512]{3,2,1,0:T(8,128)(2,1)S(1)}, u32[]{:S(2)}) copy-start(bf16[1,3,128,512]{3,2,1,0:T(8,128)(2,1)S(1)} %copy.92) | copy-start | bytes 1179652
  237.7 4.8 %copy-start.12 = (u32[32]{0:T(128)S(1)}, u32[32]{0:T(128)}, u32[]{:S(2)}) copy-start(u32[32]{0:T(128)} %constant.190) | copy-start | bytes 388
  242.4 108.3 %all-reduce.9.cloned.1.call-start = ((), (), s32[]{:S(2)}) async-start(), calls=%async_computation.6 | async-start | bytes 1048576
  245.6 74.7 %copy-start.3 = (bf16[1,3,128,512]{3,2,1,0:T(8,128)(2,1)S(1)}, bf16[1,3,128,512]{3,2,1,0:T(8,128)(2,1)}, u32[]{:S(2)}) copy-start(bf16[1,3,128,512]{3,2,1,0:T(8,128)(2,1)} %copy-done.2) | copy-start | bytes 1179652
  318.2 50.7 %all-reduce.7.cloned.1.call-start = ((), (), s32[]{:S(2)}) async-start(), calls=%async_computation.4 | async-start | bytes 1572864 | tf_op jit(solution)/shard_map/psum | solution.py:149
  318.2 2.1 copy-start.7
Sparse Core Ops, SparseCore 0:
  9.6 22.4 all-gather.5
  33.6 21.2 all-gather.3
  56.4 21.2 all-gather.7
  242.5 73.1 reduce-scatter.3
  318.3 28.0 all-reduce.8
  349.3 19.5 all-reduce.6
where the time goes:
time: 381 us; the launch traced here: 378 us
  waiting for transfers between devices  188 us (49%)
  matrix products  56 us (15%)
  other arithmetic  43.8 us (11%)
  local copies, waits for them, and re-layouts  41.8 us (11%)
  loops' own time  19.7 us (5%)
  between operations  15.1 us (4%)
  starting transfers between devices  13 us (3%)
    unnamed x8, waiting for transfers between devices  72.2 us
    ppermute x2, waiting for transfers between devices, shifted(): lax.ppermute(value, axis, [(source, source + steps) for source in range(l...  29.8 us
    scatter-add x6, other arithmetic, backward(): running.at[0, slot_rows].add(key_part).at[1, slot_rows].add(value_part)  27.2 us
    all_gather x1, waiting for transfers between devices, per_device(): lax.all_gather(w_value, 'dp', axis=0, tiled=True)  22.5 us
    all_gather x1, waiting for transfers between devices, per_device(): lax.all_gather(w_key, 'dp', axis=0, tiled=True)  21.1 us
    psum x1, waiting for transfers between devices, per_device(): grad_input = lax.psum(partial_input.astype(jnp.bfloat16), 'section')[None]  16.2 us
    ppermute x1, waiting for transfers between devices, extended(): lax.ppermute(head, axis, [((i + 1) % count, i) for i in range(ends)])  13.2 us
    unnamed x34, local copies, waits for them, and re-layouts  12.8 us
  transfers between devices with their start and end apart: 10, of which 8 were waited for; matrix products, arithmetic and copies ran while one was open for 10% of the time, Pallas kernels for 0%

commit v1 on v0

v1 whole, which is shorter than its diff:
```python
import jax
import jax.numpy as jnp
from jax import lax
from jax.sharding import PartitionSpec as P

HD = 64
BLOCK = 128
REACH = 3


def shifted(value, axis, steps):
    count = lax.axis_size(axis)
    leading, last = (max(0, -steps), min(count, count - steps))
    return lax.ppermute(value, axis, [(source, source + steps) for source in range(leading, last)])


def head_major(rows, heads):
    return rows.reshape(rows.shape[0], heads, HD).transpose(1, 0, 2)


def token_major(cells):
    return cells.transpose(1, 0, 2).reshape(cells.shape[1], cells.shape[0] * cells.shape[2])


def section_sum(partial):
    count = lax.axis_size("section")
    if count != 2:
        return lax.psum(partial.astype(jnp.bfloat16), "section")
    mine = partial.astype(jnp.bfloat16)
    other = lax.ppermute(mine, "section", [(0, 1), (1, 0)])
    return (mine.astype(jnp.float32) + other.astype(jnp.float32)).astype(jnp.bfloat16)


def per_device(normed, w_query, w_key, w_value, block_mask, cotangent):
    tokens = normed[0]
    upstream = cotangent[0]
    length = tokens.shape[0]
    features = upstream.shape[1]
    heads = features // HD
    blocks = length // BLOCK
    span_len = 2 * REACH + 1
    halo = REACH * BLOCK
    score_scale = HD ** (-0.5)

    left_tokens = shifted(tokens[length - halo :], "ctx", 1)
    right_tokens = shifted(tokens[:halo], "ctx", -1)
    gathered = lax.all_gather(jnp.stack([w_query, w_key, w_value]), "dp", axis=1, tiled=True)
    query_full, key_full, value_full = gathered[0], gathered[1], gathered[2]

    queries = jnp.dot(tokens, query_full, preferred_element_type=jnp.float32).astype(jnp.bfloat16)
    frame_tokens = jnp.concatenate([left_tokens, tokens, right_tokens], axis=0)
    kv_weights = jnp.concatenate([key_full, value_full], axis=1)
    frame_kv = jnp.dot(frame_tokens, kv_weights, preferred_element_type=jnp.float32).astype(
        jnp.bfloat16
    )
    key_h = head_major(frame_kv[:, :features], heads)
    value_h = head_major(frame_kv[:, features:], heads)
    query_h = head_major(queries, heads)
    upstream_h = head_major(upstream, heads)

    first_block = lax.axis_index("ctx") * blocks
    own_mask = lax.dynamic_slice(block_mask, (first_block, 0), (blocks, span_len))

    outs, query_grads = [], []
    key_frame = None
    value_frame = None
    for i in range(blocks):
        query_block = query_h[:, i * BLOCK : (i + 1) * BLOCK]
        upstream_block = upstream_h[:, i * BLOCK : (i + 1) * BLOCK]
        key_window = key_h[:, i * BLOCK : (i + span_len) * BLOCK]
        value_window = value_h[:, i * BLOCK : (i + span_len) * BLOCK]
        seen = jnp.repeat(own_mask[i] > 0, BLOCK)[None, None, :]
        scores = (
            jnp.einsum("hqd,hkd->hqk", query_block, key_window, preferred_element_type=jnp.float32)
            * score_scale
        )
        row_top = jnp.max(jnp.where(seen, scores, -jnp.inf), axis=2, keepdims=True)
        raised = jnp.where(seen, jnp.exp(scores - row_top), 0.0)
        probability = raised / jnp.sum(raised, axis=2, keepdims=True)
        weights = probability.astype(jnp.bfloat16)
        outs.append(
            jnp.einsum("hqk,hkd->hqd", weights, value_window, preferred_element_type=jnp.float32)
        )
        prob_grad = jnp.einsum(
            "hqd,hkd->hqk", upstream_block, value_window, preferred_element_type=jnp.float32
        )
        row_delta = jnp.sum(probability * prob_grad, axis=2, keepdims=True)
        score_grad = (probability * (prob_grad - row_delta)).astype(jnp.bfloat16)
        query_grads.append(
            score_scale
            * jnp.einsum("hqk,hkd->hqd", score_grad, key_window, preferred_element_type=jnp.float32)
        )
        key_part = score_scale * jnp.einsum(
            "hqk,hqd->hkd", score_grad, query_block, preferred_element_type=jnp.float32
        )
        value_part = jnp.einsum(
            "hqk,hqd->hkd", weights, upstream_block, preferred_element_type=jnp.float32
        )
        spread = ((0, 0), (i * BLOCK, (blocks - 1 - i) * BLOCK), (0, 0))
        key_part = jnp.pad(key_part, spread)
        value_part = jnp.pad(value_part, spread)
        key_frame = key_part if key_frame is None else key_frame + key_part
        value_frame = value_part if value_frame is None else value_frame + value_part

    attended = token_major(jnp.concatenate(outs, axis=1).astype(jnp.bfloat16))[None]
    query_grad = token_major(jnp.concatenate(query_grads, axis=1).astype(jnp.bfloat16))

    frame_grads = jnp.stack([token_major(key_frame), token_major(value_frame)])
    to_left = frame_grads[:, :halo].astype(jnp.bfloat16)
    to_right = frame_grads[:, halo + length :].astype(jnp.bfloat16)
    middle = frame_grads[:, halo : halo + length]
    from_left = shifted(to_right, "ctx", 1).astype(jnp.float32)
    from_right = shifted(to_left, "ctx", -1).astype(jnp.float32)
    middle = middle.at[:, :halo].add(from_left)
    middle = middle.at[:, length - halo :].add(from_right)
    key_grad = middle[0].astype(jnp.bfloat16)
    value_grad = middle[1].astype(jnp.bfloat16)

    term_query = jnp.einsum(
        "tr,tf->rf", tokens, query_grad, preferred_element_type=jnp.float32
    ).astype(jnp.bfloat16)
    reduced_query = lax.psum_scatter(term_query, ("ctx", "dp"), scatter_dimension=0, tiled=True)

    contract = (((1,), (1,)), ((), ()))
    partial_input = (
        lax.dot_general(query_grad, query_full, contract, preferred_element_type=jnp.float32)
        + lax.dot_general(key_grad, key_full, contract, preferred_element_type=jnp.float32)
        + lax.dot_general(value_grad, value_full, contract, preferred_element_type=jnp.float32)
    )
    grad_input = section_sum(partial_input)[None]

    term_kv = jnp.einsum(
        "tr,tcf->rcf",
        tokens,
        jnp.stack([key_grad, value_grad], axis=1),
        preferred_element_type=jnp.float32,
    ).astype(jnp.bfloat16)
    reduced_kv = lax.psum_scatter(
        term_kv.reshape(term_kv.shape[0], 2 * features), ("ctx", "dp"), scatter_dimension=0, tiled=True
    ).reshape(-1, 2, features)
    summed = jnp.concatenate([reduced_query[:, None], reduced_kv], axis=1).astype(jnp.float32)
    grad_weights = summed / lax.axis_size("dp")
    return (attended, grad_input, grad_weights)


def solution(mesh):
    in_specs = (
        P("dp", "ctx", None),
        P("dp", "section"),
        P("dp", "section"),
        P("dp", "section"),
        P(),
        P("dp", "ctx", "section"),
    )
    out_specs = (P("dp", "ctx", "section"), P("dp", "ctx", None), P(("ctx", "dp"), None, "section"))
    return jax.shard_map(
        per_device, mesh=mesh, in_specs=in_specs, out_specs=out_specs, check_vma=False
    )
```

time: 381 us -> 261 us (0.69)
  the two profiles are of different devices: /device:TPU:12 before, /device:TPU:0 now
where the time goes in v1:
time: 261 us; the launch traced here: 260 us
  waiting for transfers between devices  166 us (64%)
  matrix products  35.2 us (13%)
  local copies, waits for them, and re-layouts  17.7 us (7%)
  other arithmetic  15.2 us (6%)
  between operations  14.2 us (5%)
  starting transfers between devices  12.1 us (5%)
    reduce_scatter x1, waiting for transfers between devices, per_device(): lax.psum_scatter(term_kv.reshape(term_kv.shape[0], 2 * features), ('ctx',...  77.9 us
    all_gather x1, waiting for transfers between devices, per_device(): lax.all_gather(jnp.stack([w_query, w_key, w_value]), 'dp', axis=1, tiled=...  40.2 us
    ppermute x4, waiting for transfers between devices, shifted(): lax.ppermute(value, axis, [(source, source + steps) for source in range(l...  39 us
    ppermute x4, starting transfers between devices, shifted(): lax.ppermute(value, axis, [(source, source + steps) for source in range(l...  12 us
    unnamed x43, local copies, waits for them, and re-layouts  10.2 us
    unnamed x4, waiting for transfers between devices  8.86 us
    dot_general x3, matrix products, per_device(): jnp.einsum('hqk,hqd->hkd', weights, upstream_block, preferred_element_typ...  6.52 us
  transfers between devices with their start and end apart: 8, of which 4 were waited for; matrix products, arithmetic and copies ran while one was open for 10% of the time, Pallas kernels for 0%

profile of v1, /device:TPU:0, one launch (start us, length us, event | category | flops | bytes accessed | tf_op | source)
XLA Modules:
  0.0 260.4 jit_solution(1352695634074788476)
XLA Ops:
  7.3 2.8 %pad_maximum_fusion.1 = bf16[3,512,512]{2,1,0:T(8,128)(2,1)} fusion(bf16[1,512,512]{2,1,0:T(8,128)(2,1)} %bitcast.137, bf16[1,512,512]{2,1,0:T(8,128)(2,1)} %bitcast.138, bf16[1,512,512]{2,1,0:T(8,128)(2,1)} %bitcast.139), kind=kLoop, calls=%fused_computation.61 | loop fusion | flops 1572864 | bytes 3145728 | tf_op jit(solution)/shard_map/stack | solution.py:47
  10.1 1.3 collective-permute-start.1
  11.4 5.5 %collective-permute-start = (bf16[384,1024]{1,0:T(8,128)(2,1)S(1)}, bf16[384,1024]{1,0:T(8,128)(2,1)S(1)}, u32[]{:S(2)}, u32[]{:S(2)}) collective-permute-start(bf16[384,1024]{1,0:T(8,128)(2,1)S(1)} %bitcast.134), channel_id=1, source_target_pairs={{0,4},{4,8},{8,12},{12,16},{16,20},{20,24},{24,28},{1,5},{5,9},{9,... | collective-permute-start | bytes 2359304 | tf_op jit(solution)/shard_map/ppermute | solution.py:14
  17.6 40.2 %all-gather.2.cloned.1.call-done = bf16[3,1024,512]{2,1,0:T(8,128)(2,1)} async-done(((bf16[3,512,512]{2,1,0:T(8,128)(2,1)}), bf16[3,1024,512]{2,1,0:T(8,128)(2,1)}) %all-gather.2.cloned.1.call-update) | async-done | bytes 3145744 | tf_op jit(solution)/shard_map/all_gather | solution.py:47
  57.9 1.7 slice_bitcast_fusion.1
  59.6 3.1 %convolution_convert_fusion = bf16[1152,1024]{0,1:T(8,128)(2,1)S(1)} fusion(bf16[384,1024]{1,0:T(8,128)(2,1)S(1)} %collective-permute-done.1, bf16[384,1024]{1,0:T(8,128)(2,1)S(1)} %bitcast.135, bf16[384,1024]{1,0:T(8,128)(2,1)S(1)} %collective-permute-done, bf16[1024,512]{1,0:T(8,128)(2,1)S(1)} %get-tuple-element.59, ...), kind=kOutput, calls=%fused_computation.7 | convolution fusion | flops 2428370944 | bytes 6815744 | tf_op jit(solution)/shard_map/dot_general | solution.py:53
  62.8 1.7 copy-done.2
  67.5 1.2 fusion.116
  68.8 2.1 fusion.56
  70.9 1.1 fusion.10
  73.4 1.7 convolution_multiply_fusion.2
  75.1 1.2 fusion.115
  76.4 2.1 fusion.53
  78.4 1.1 fusion.7
  81.0 1.7 convolution_multiply_fusion.1
  82.7 1.2 fusion.114
  83.9 2.3 fusion.50
  86.2 1.1 fusion.4
  88.8 1.7 convolution_multiply_fusion
  90.5 1.7 fusion.45
  92.3 2.3 copy.45
  94.7 3.1 %pad_add_fusion = f32[8,1152,64]{1,2,0:T(8,128)S(1)} fusion(f32[8,896,64]{1,2,0:T(8,128)} %fusion.50, f32[8,896,64]{1,2,0:T(8,128)} %fusion.53, f32[8,896,64]{1,2,0:T(8,128)} %fusion.56), kind=kLoop, calls=%fused_computation.40 | loop fusion | flops 1179648 | bytes 7864320 | tf_op jit(solution)/shard_map/add | solution.py:103
  99.7 3.5 %collective-permute-start.2 = (bf16[2,384,512]{1,2,0:T(8,128)(2,1)S(1)}, bf16[2,384,512]{1,2,0:T(8,128)(2,1)S(1)}, u32[]{:S(2)}, u32[]{:S(2)}) collective-permute-start(bf16[2,384,512]{1,2,0:T(8,128)(2,1)S(1)} %get-tuple-element.60), channel_id=1, source_target_pairs={{0,4},{4,8},{8,12},{12,16},{16,20},{20,24},{24,28},{1,5},{5,9},{9,... | collective-permute-start | bytes 2359304 | tf_op jit(solution)/shard_map/ppermute | solution.py:14
  103.2 1.6 collective-permute-start.3
  104.8 39.0 %collective-permute-done.2 = bf16[2,384,512]{1,2,0:T(8,128)(2,1)S(1)} collective-permute-done((bf16[2,384,512]{1,2,0:T(8,128)(2,1)S(1)}, bf16[2,384,512]{1,2,0:T(8,128)(2,1)S(1)}, u32[]{:S(2)}, u32[]{:S(2)}) %collective-permute-start.2) | collective-permute-done | bytes 786464 | tf_op jit(solution)/shard_map/ppermute | solution.py:14
  144.2 2.6 convolution_convert_fusion.1
  146.8 4.0 %copy.36 = bf16[1024,1024]{1,0:T(8,128)(2,1)} copy(bf16[1024,1024]{0,1:T(8,128)(2,1)} %bitcast.119) | data formatting | bytes 4194304 | tf_op jit(solution)/shard_map/reshape | solution.py:139
  152.1 3.1 %convolution_convert_fusion.4 = bf16[8,128,64]{1,2,0:T(8,128)(2,1)S(1)} fusion(bf16[8,1152,64]{1,2,0:T(8,128)(2,1)S(1)} %bitcast.130, f32[8,128,896]{2,1,0:T(8,128)} %copy-done.12, f32[8,128]{1,0:T(8,128)S(1)} %get-tuple-element.66), kind=kOutput, calls=%fused_computation.76 | convolution fusion | flops 119341056 | bytes 4722688 | tf_op jit(solution)/shard_map/hqk,hkd->hqd/dot_general | solution.py:82
  155.8 1.6 add_convert_fusion.1
  161.6 2.3 fusion.77
  163.9 8.8 %reduce-scatter.7.cloned.1.call-done = bf16[64,512]{1,0:T(8,128)(2,1)} async-done(((bf16[1024,512]{1,0:T(8,128)(2,1)}), bf16[64,512]{1,0:T(8,128)(2,1)}) %reduce-scatter.7.cloned.1.call-update) | async-done | bytes 65552
  173.8 77.9 %reduce-scatter.5.cloned.1.call-done = bf16[64,1024]{1,0:T(8,128)(2,1)} async-done(((bf16[1024,1024]{1,0:T(8,128)(2,1)}), bf16[64,1024]{1,0:T(8,128)(2,1)}) %reduce-scatter.5.cloned.1.call-update) | async-done | bytes 131088 | tf_op jit(solution)/shard_map/reduce_scatter | solution.py:138
  (81 shorter events, 19.9 us)
Async XLA Ops:
  7.2 9.8 %copy-start = (s32[24,7]{0,1:T(8,128)S(1)}, s32[24,7]{0,1:T(8,128)}, u32[]{:S(2)}) copy-start(s32[24,7]{0,1:T(8,128)} %param.18) | copy-start | bytes 2020
  7.2 50.7 %all-gather.2.cloned.1.call-start = ((), (), s32[]{:S(2)}) async-start(), calls=%async_computation.2 | async-start | bytes 4718592 | tf_op jit(solution)/shard_map/all_gather | solution.py:47
  7.2 2.9 %copy-start.15 = (bf16[1,384,1024]{2,1,0:T(8,128)(2,1)S(1)}, bf16[1,384,1024]{2,1,0:T(8,128)(2,1)}, u32[]{:S(2)}) copy-start(bf16[1,384,1024]{2,1,0:T(8,128)(2,1)} %param.14) | copy-start | bytes 2359300
  7.2 10.0 %copy-start.18 = (bf16[1,384,512]{2,1,0:T(8,128)(2,1)S(1)}, bf16[1,384,512]{2,1,0:T(8,128)(2,1)}, u32[]{:S(2)}) copy-start(bf16[1,384,512]{2,1,0:T(8,128)(2,1)} %param.19) | copy-start | bytes 1179652
  10.0 162.6 %reduce-scatter.7.cloned.1.call-start = ((), (), s32[]{:S(2)}) async-start(), calls=%async_computation.4 | async-start | bytes 1114112
  10.1 49.4 %collective-permute-start.1 = (bf16[384,1024]{1,0:T(8,128)(2,1)S(1)}, bf16[384,1024]{1,0:T(8,128)(2,1)S(1)}, u32[]{:S(2)}, u32[]{:S(2)}) collective-permute-start(bf16[384,1024]{1,0:T(8,128)(2,1)S(1)} %bitcast.133), channel_id=1, source_target_pairs={{4,0},{8,4},{12,8},{16,12},{20,16},{24,20},{28,24},{5,1},{9,5},{13... | collective-permute-start | bytes 2359304 | tf_op jit(solution)/shard_map/ppermute | solution.py:14
  11.4 48.1 %collective-permute-start = (bf16[384,1024]{1,0:T(8,128)(2,1)S(1)}, bf16[384,1024]{1,0:T(8,128)(2,1)S(1)}, u32[]{:S(2)}, u32[]{:S(2)}) collective-permute-start(bf16[384,1024]{1,0:T(8,128)(2,1)S(1)} %bitcast.134), channel_id=1, source_target_pairs={{0,4},{4,8},{8,12},{12,16},{16,20},{20,24},{24,28},{1,5},{5,9},{9,... | collective-permute-start | bytes 2359304 | tf_op jit(solution)/shard_map/ppermute | solution.py:14
  62.6 1.9 copy-start.2
  62.6 2.1 copy-start.16
  64.7 21.5 %copy-start.13 = (bf16[1152,512]{0,1:T(8,128)(2,1)}, bf16[1152,512]{0,1:T(8,128)(2,1)S(1)}, u32[]{:S(2)}) copy-start(bf16[1152,512]{0,1:T(8,128)(2,1)S(1)} %get-tuple-element.63) | copy-start | bytes 3538948
  68.8 3.2 %copy-start.8 = (f32[8,128,896]{2,1,0:T(8,128)}, f32[8,128,896]{2,1,0:T(8,128)S(1)}, u32[]{:S(2)}) copy-start(f32[8,128,896]{2,1,0:T(8,128)S(1)} %get-tuple-element.71) | copy-start | bytes 11010052
  76.3 3.2 %copy-start.10 = (f32[8,128,896]{2,1,0:T(8,128)}, f32[8,128,896]{2,1,0:T(8,128)S(1)}, u32[]{:S(2)}) copy-start(f32[8,128,896]{2,1,0:T(8,128)S(1)} %get-tuple-element.69) | copy-start | bytes 11010052
  83.9 3.5 %copy-start.12 = (f32[8,128,896]{2,1,0:T(8,128)}, f32[8,128,896]{2,1,0:T(8,128)S(1)}, u32[]{:S(2)}) copy-start(f32[8,128,896]{2,1,0:T(8,128)S(1)} %get-tuple-element.67) | copy-start | bytes 11010052
  94.6 157.1 %reduce-scatter.5.cloned.1.call-start = ((), (), s32[]{:S(2)}) async-start(), calls=%async_computation.3 | async-start | bytes 2228224 | tf_op jit(solution)/shard_map/reduce_scatter | solution.py:138
  94.6 3.1 %copy-start.3 = (f32[8,896,64]{1,2,0:T(8,128)S(1)}, f32[8,896,64]{1,2,0:T(8,128)}, u32[]{:S(2)}) copy-start(f32[8,896,64]{1,2,0:T(8,128)} %convolution_multiply_fusion.2) | copy-start | bytes 5505028
  94.6 3.7 %copy-start.4 = (f32[8,896,64]{1,2,0:T(8,128)S(1)}, f32[8,896,64]{1,2,0:T(8,128)}, u32[]{:S(2)}) copy-start(f32[8,896,64]{1,2,0:T(8,128)} %convolution_multiply_fusion.1) | copy-start | bytes 5505028
  94.6 4.2 %copy-start.5 = (f32[8,896,64]{1,2,0:T(8,128)S(1)}, f32[8,896,64]{1,2,0:T(8,128)}, u32[]{:S(2)}) copy-start(f32[8,896,64]{1,2,0:T(8,128)} %convolution_multiply_fusion) | copy-start | bytes 5505028
  99.7 44.1 %collective-permute-start.2 = (bf16[2,384,512]{1,2,0:T(8,128)(2,1)S(1)}, bf16[2,384,512]{1,2,0:T(8,128)(2,1)S(1)}, u32[]{:S(2)}, u32[]{:S(2)}) collective-permute-start(bf16[2,384,512]{1,2,0:T(8,128)(2,1)S(1)} %get-tuple-element.60), channel_id=1, source_target_pairs={{0,4},{4,8},{8,12},{12,16},{16,20},{20,24},{24,28},{1,5},{5,9},{9,... | collective-permute-start | bytes 2359304 | tf_op jit(solution)/shard_map/ppermute | solution.py:14
  103.2 41.1 %copy-start.17 = (bf16[1,384,1024]{2,1,0:T(8,128)(2,1)S(1)}, bf16[1,384,1024]{2,1,0:T(8,128)(2,1)}, u32[]{:S(2)}) copy-start(bf16[1,384,1024]{2,1,0:T(8,128)(2,1)} %param.14) | copy-start | bytes 2359300
  103.2 40.6 %collective-permute-start.3 = (bf16[2,384,512]{1,2,0:T(8,128)(2,1)S(1)}, bf16[2,384,512]{1,2,0:T(8,128)(2,1)S(1)}, u32[]{:S(2)}, u32[]{:S(2)}) collective-permute-start(bf16[2,384,512]{1,2,0:T(8,128)(2,1)S(1)} %get-tuple-element.61), channel_id=1, source_target_pairs={{4,0},{8,4},{12,8},{16,12},{20,16},{24,20},{28,24},{5,1},{9,5},{13... | collective-permute-start | bytes 2359304 | tf_op jit(solution)/shard_map/ppermute | solution.py:14
  144.1 2.7 %copy-start.6 = (bf16[2,384,512]{1,2,0:T(8,128)(2,1)}, bf16[2,384,512]{1,2,0:T(8,128)(2,1)S(1)}, u32[]{:S(2)}) copy-start(bf16[2,384,512]{1,2,0:T(8,128)(2,1)S(1)} %fusion.44) | copy-start | bytes 2359300
  150.8 1.3 copy-start.14
  152.1 3.1 %copy-start.7 = (bf16[2,384,512]{1,2,0:T(8,128)(2,1)S(1)}, bf16[2,384,512]{1,2,0:T(8,128)(2,1)}, u32[]{:S(2)}) copy-start(bf16[2,384,512]{1,2,0:T(8,128)(2,1)} %copy-done.6) | copy-start | bytes 2359300
  155.8 2.3 copy-start.11
  157.4 2.2 copy-start.9
  157.4 4.2 %collective-permute-start.4 = (bf16[384,1024]{1,0:T(8,128)(2,1)}, bf16[384,1024]{1,0:T(8,128)(2,1)S(1)}, u32[]{:S(2)}, u32[]{:S(2)}) collective-permute-start(bf16[384,1024]{1,0:T(8,128)(2,1)} %add_convert_fusion.1), channel_id=1, source_target_pairs={{0,1},{1,0},{2,3},{3,2},{4,5},{5,4},{6,7},{7,6},{8,9},{9,8},{10,11... | collective-permute-start | bytes 2359304 | tf_op jit(solution)/shard_map/ppermute | solution.py:30
  160.6 93.3 %copy-start.1 = (s32[24,7]{0,1:T(8,128)S(1)}, s32[24,7]{0,1:T(8,128)}, u32[]{:S(2)}) copy-start(s32[24,7]{0,1:T(8,128)} %param.18) | copy-start | bytes 2020
Sparse Core Ops, SparseCore 0:
  10.2 47.6 all-gather.1
  94.7 77.9 reduce-scatter.6
  175.1 76.6 reduce-scatter.4

commit v2 on v1

--- a/solution.py
+++ b/solution.py
@@ -22,6 +22,43 @@
     return cells.transpose(1, 0, 2).reshape(cells.shape[1], cells.shape[0] * cells.shape[2])
 
 
+def ordered_pair(mine, other, axis, dim):
+    first = lax.axis_index(axis) == 0
+    return jnp.where(
+        first,
+        jnp.concatenate([mine, other], axis=dim),
+        jnp.concatenate([other, mine], axis=dim),
+    )
+
+
+def neighbour_tokens(tokens, halo):
+    count = lax.axis_size("section")
+    if count != 2:
+        return (shifted(tokens[-halo:], "ctx", 1), shifted(tokens[:halo], "ctx", -1))
+    half = tokens.shape[1] // 2
+    start = lax.axis_index("section") * half
+    share = lax.dynamic_slice_in_dim(tokens, start, half, 1)
+    fetched = jnp.stack([shifted(share[-halo:], "ctx", 1), shifted(share[:halo], "ctx", -1)])
+    partner = lax.ppermute(fetched, "section", [(0, 1), (1, 0)])
+    both = ordered_pair(fetched, partner, "section", 2)
+    return (both[0], both[1])
+
+
+def full_rows(weight):
+    if lax.axis_size("dp") != 2:
+        return lax.all_gather(weight, "dp", axis=0, tiled=True)
+    other = lax.ppermute(weight, "dp", [(0, 1), (1, 0)])
+    return ordered_pair(weight, other, "dp", 0)
+
+
+def summed_rows(term):
+    group = ("ctx", "dp")
+    count = lax.axis_size(group)
+    parts = lax.all_to_all(term, group, 0, 0, tiled=True)
+    parts = parts.reshape(count, term.shape[0] // count, *term.shape[1:])
+    return jnp.sum(parts.astype(jnp.float32), axis=0)
+
+
 def section_sum(partial):
     count = lax.axis_size("section")
     if count != 2:
@@ -42,10 +79,10 @@
     halo = REACH * BLOCK
     score_scale = HD ** (-0.5)
 
-    left_tokens = shifted(tokens[length - halo :], "ctx", 1)
-    right_tokens = shifted(tokens[:halo], "ctx", -1)
-    gathered = lax.all_gather(jnp.stack([w_query, w_key, w_value]), "dp", axis=1, tiled=True)
-    query_full, key_full, value_full = gathered[0], gathered[1], gathered[2]
+    left_tokens, right_tokens = neighbour_tokens(tokens, halo)
+    query_full = full_rows(w_query)
+    gathered = lax.all_gather(jnp.stack([w_key, w_value]), "dp", axis=1, tiled=True)
+    key_full, value_full = gathered[0], gathered[1]
 
     queries = jnp.dot(tokens, query_full, preferred_element_type=jnp.float32).astype(jnp.bfloat16)
     frame_tokens = jnp.concatenate([left_tokens, tokens, right_tokens], axis=0)
@@ -135,10 +172,8 @@
         jnp.stack([key_grad, value_grad], axis=1),
         preferred_element_type=jnp.float32,
     ).astype(jnp.bfloat16)
-    reduced_kv = lax.psum_scatter(
-        term_kv.reshape(term_kv.shape[0], 2 * features), ("ctx", "dp"), scatter_dimension=0, tiled=True
-    ).reshape(-1, 2, features)
-    summed = jnp.concatenate([reduced_query[:, None], reduced_kv], axis=1).astype(jnp.float32)
+    reduced_kv = summed_rows(term_kv)
+    summed = jnp.concatenate([reduced_query[:, None].astype(jnp.float32), reduced_kv], axis=1)
     grad_weights = summed / lax.axis_size("dp")
     return (attended, grad_input, grad_weights)
 

time: 261 us -> 228 us (0.87)
  waiting for transfers between devices: 166 us -> 134 us
  starting transfers between devices: 12.1 us -> 22.1 us
  matrix products: 35.2 us -> 26.4 us
    reduce_scatter x1 -> x0, waiting for transfers between devices: 77.9 us -> none  [per_device(): lax.psum_scatter(term_kv.reshape(term_kv.shape[0], 2 * features), ('ctx',...]
    unnamed x4 -> x3, waiting for transfers between devices: 8.86 us -> 74.1 us
    all_gather x1, waiting for transfers between devices: 40.2 us -> 9.97 us  [per_device(): lax.all_gather(jnp.stack([w_key, w_value]), 'dp', axis=1, tiled=True)]
    all_to_all x0 -> x1, starting transfers between devices: none -> 6.88 us  [summed_rows(): parts = lax.all_to_all(term, group, 0, 0, tiled=True)]
    ppermute x0 -> x2, waiting for transfers between devices: none -> 5.76 us  [the longest x1 5.76 us: full_rows(): other = lax.ppermute(weight, 'dp', [(0, 1), (1, 0)])]
    ppermute x4, waiting for transfers between devices: 39 us -> 44.4 us  [shifted(): lax.ppermute(value, axis, [(source, source + steps) for source in range(l...]
    reshape x2 -> x0, local copies, waits for them, and re-layouts: 4.94 us -> none  [the longest x1 3.96 us: per_device(): term_kv.reshape(term_kv.shape[0], 2 * features)]
    dot_general x3, matrix products: 6.52 us -> 1.6 us  [per_device(): jnp.einsum('hqk,hqd->hkd', weights, upstream_block, preferred_element_typ...]
  transfers between devices with their start and end apart: 8 -> 10, of which waited for: 4 -> 6; matrix products, arithmetic and copies ran while one was open for 10% -> 10% of each run, Pallas kernels for 0% -> 0%
where the time goes in v2:
time: 228 us
  waiting for transfers between devices  134 us (59%)
  matrix products  26.4 us (12%)
  starting transfers between devices  22.1 us (10%)
  local copies, waits for them, and re-layouts  17.1 us (8%)
  between operations  14.7 us (6%)
  other arithmetic  13.3 us (6%)
    unnamed x3, waiting for transfers between devices  74.1 us
    ppermute x4, waiting for transfers between devices, shifted(): lax.ppermute(value, axis, [(source, source + steps) for source in range(l...  44.4 us
    ppermute x4, starting transfers between devices, shifted(): lax.ppermute(value, axis, [(source, source + steps) for source in range(l...  12.7 us
    all_gather x1, waiting for transfers between devices, per_device(): lax.all_gather(jnp.stack([w_key, w_value]), 'dp', axis=1, tiled=True)  9.97 us
    unnamed x46, local copies, waits for them, and re-layouts  9.56 us
    all_to_all x1, starting transfers between devices, summed_rows(): parts = lax.all_to_all(term, group, 0, 0, tiled=True)  6.88 us
    ppermute x1, waiting for transfers between devices, full_rows(): other = lax.ppermute(weight, 'dp', [(0, 1), (1, 0)])  5.76 us
  transfers between devices with their start and end apart: 10, of which 6 were waited for; matrix products, arithmetic and copies ran while one was open for 10% of the time, Pallas kernels for 0%

profile of v2, /device:TPU:0, one launch (start us, length us, event | category | flops | bytes accessed | tf_op | source)
XLA Modules:
  0.0 227.8 jit_solution(8293904949246058886)
XLA Ops:
  7.2 2.3 %pad_maximum_fusion.1 = bf16[2,512,512]{2,1,0:T(8,128)(2,1)} fusion(bf16[1,512,512]{2,1,0:T(8,128)(2,1)} %bitcast.146, bf16[1,512,512]{2,1,0:T(8,128)(2,1)} %bitcast.147), kind=kLoop, calls=%fused_computation.83 | loop fusion | flops 524288 | bytes 2097152 | tf_op jit(solution)/shard_map/stack | solution.py:84
  9.7 1.3 collective-permute-start.2
  11.0 5.5 %collective-permute-start.1 = (bf16[384,512]{1,0:T(8,128)(2,1)S(1)}, bf16[384,512]{1,0:T(8,128)(2,1)S(1)}, u32[]{:S(2)}, u32[]{:S(2)}) collective-permute-start(bf16[384,512]{1,0:T(8,128)(2,1)S(1)} %dynamic-slice_bitcast_fusion), channel_id=1, source_target_pairs={{0,4},{4,8},{8,12},{12,16},{16,20},{20,24},{24,28},{1,5},{5,9},{9,... | collective-permute-start | bytes 1179656 | tf_op jit(solution)/shard_map/ppermute | solution.py:14
  16.5 2.1 collective-permute-start
  18.6 5.0 %collective-permute-done.2 = bf16[384,512]{1,0:T(8,128)(2,1)S(1)} collective-permute-done((bf16[384,512]{1,0:T(8,128)(2,1)S(1)}, bf16[384,512]{1,0:T(8,128)(2,1)S(1)}, u32[]{:S(2)}, u32[]{:S(2)}) %collective-permute-start.2) | collective-permute-done | bytes 393248 | tf_op jit(solution)/shard_map/ppermute | solution.py:14
  23.7 8.6 %collective-permute-done.1 = bf16[384,512]{1,0:T(8,128)(2,1)S(1)} collective-permute-done((bf16[384,512]{1,0:T(8,128)(2,1)S(1)}, bf16[384,512]{1,0:T(8,128)(2,1)S(1)}, u32[]{:S(2)}, u32[]{:S(2)}) %collective-permute-start.1) | collective-permute-done | bytes 393248 | tf_op jit(solution)/shard_map/ppermute | solution.py:14
  34.2 5.8 %collective-permute-done = bf16[512,512]{1,0:T(8,128)(2,1)} collective-permute-done((bf16[512,512]{1,0:T(8,128)(2,1)}, bf16[512,512]{1,0:T(8,128)(2,1)}, u32[]{:S(2)}, u32[]{:S(2)}) %collective-permute-start) | collective-permute-done | bytes 524320 | tf_op jit(solution)/shard_map/ppermute | solution.py:50
  40.0 2.3 %convolution_convert_fusion.2 = bf16[512,384]{1,0:T(8,128)(2,1)S(1)} fusion(bf16[512,512]{1,0:T(8,128)(2,1)} %collective-permute-done, bf16[512,512]{1,0:T(8,128)(2,1)} %param.15, pred[]{:T(512)S(6)} %eq.6, bf16[1,384,1024]{2,1,0:T(8,128)(2,1)S(1)} %copy-done.12), kind=kOutput, calls=%fused_computation.70 | convolution fusion | flops 407568384 | bytes 2228225 | tf_op jit(solution)/shard_map/dot_general | solution.py:87
  42.9 10.0 %all-gather.2.cloned.1.call-done = bf16[2,1024,512]{2,1,0:T(8,128)(2,1)} async-done(((bf16[2,512,512]{2,1,0:T(8,128)(2,1)}), bf16[2,1024,512]{2,1,0:T(8,128)(2,1)}) %all-gather.2.cloned.1.call-update) | async-done | bytes 2097168 | tf_op jit(solution)/shard_map/all_gather | solution.py:84
  52.9 1.7 slice_bitcast_fusion.1
  54.6 3.1 %convolution_convert_fusion = bf16[1152,1024]{0,1:T(8,128)(2,1)S(1)} fusion(bf16[384,1024]{1,0:T(8,128)(2,1)S(1)} %get-tuple-element.62, bf16[384,1024]{1,0:T(8,128)(2,1)S(1)} %bitcast.126, bf16[384,1024]{1,0:T(8,128)(2,1)S(1)} %get-tuple-element.61, bf16[1024,512]{1,0:T(8,128)(2,1)S(1)} %get-tuple-element.60, bf16[1024,512]{1,0:T(8,128)(2,1)S(1)} %get-tuple-element.59), kind=kOutput, calls=%fused_computation.8 | convolution fusion | flops 2428370944 | bytes 6815744 | tf_op jit(solution)/shard_map/dot_general | solution.py:90
  59.9 1.2 fusion.121
  61.7 1.3 fusion.10
  63.0 1.2 fusion.120
  64.8 1.1 fusion.7
  65.9 1.2 fusion.119
  67.7 1.1 fusion.4
  73.7 4.6 %collective-permute-start.4 = (bf16[2,384,512]{1,2,0:T(8,128)(2,1)S(1)}, bf16[2,384,512]{1,2,0:T(8,128)(2,1)S(1)}, u32[]{:S(2)}, u32[]{:S(2)}) collective-permute-start(bf16[2,384,512]{1,2,0:T(8,128)(2,1)S(1)} %get-tuple-element.55), channel_id=1, source_target_pairs={{0,4},{4,8},{8,12},{12,16},{16,20},{20,24},{24,28},{1,5},{5,9},{9,... | collective-permute-start | bytes 2359304 | tf_op jit(solution)/shard_map/ppermute | solution.py:14
  78.3 1.3 collective-permute-start.5
  81.3 30.8 %collective-permute-done.4 = bf16[2,384,512]{1,2,0:T(8,128)(2,1)S(1)} collective-permute-done((bf16[2,384,512]{1,2,0:T(8,128)(2,1)S(1)}, bf16[2,384,512]{1,2,0:T(8,128)(2,1)S(1)}, u32[]{:S(2)}, u32[]{:S(2)}) %collective-permute-start.4) | collective-permute-done | bytes 786464 | tf_op jit(solution)/shard_map/ppermute | solution.py:14
  113.4 1.3 convert_bitcast_fusion
  114.7 4.0 %copy.26 = bf16[1024,2,512]{2,1,0:T(2,128)(2,1)} copy(bf16[1024,2,512]{0,2,1:T(8,128)(2,1)S(1)} %convert_bitcast_fusion) | data formatting | bytes 4194304 | tf_op jit(solution)/shard_map/convert_element_type | solution.py:174
  118.7 6.9 %all-to-all-start = ((bf16[1024,2,512]{2,1,0:T(2,128)(2,1)}), bf16[1024,2,512]{2,1,0:T(2,128)(2,1)S(1)}, u32[]{:S(2)}, u32[]{:S(2)}) async-start(bf16[1024,2,512]{2,1,0:T(2,128)(2,1)} %copy.26), calls=%async_computation | async-start | bytes 4194304 | tf_op jit(solution)/shard_map/all_to_all | solution.py:57
  125.9 2.4 %fusion.48 = bf16[8,128,64]{1,2,0:T(8,128)(2,1)S(1)} fusion(bf16[8,128,896]{2,1,0:T(8,128)(2,1)} %copy-done.3, bf16[8,1152,64]{1,2,0:T(8,128)(2,1)S(1)} %bitcast.124), kind=kOutput, calls=%fused_computation.76 | convolution fusion | flops 117571584 | bytes 2883584 | tf_op jit(solution)/shard_map/hqk,hkd->hqd/dot_general | solution.py:128
  129.8 1.3 copy.33
  131.2 2.4 %fusion.87 = f32[384,1024]{1,0:T(8,128)S(1)} fusion(bf16[384,512]{0,1:T(8,128)(2,1)} %bitcast.129, bf16[512,512]{1,0:T(8,128)(2,1)} %collective-permute-done, bf16[512,512]{1,0:T(8,128)(2,1)} %param.15, pred[]{:T(512)S(6)} %eq.6), kind=kOutput, calls=%fused_computation.129 | convolution fusion | flops 407371776 | bytes 3014657 | tf_op jit(solution)/shard_map/dot_general | solution.py:163
  137.4 1.3 copy-done.9
  138.8 0.9 convolution_convert_fusion.4
  140.1 0.9 convolution_convert_fusion.5
  142.0 2.3 %fusion.76 = bf16[1,384,1024]{2,1,0:T(8,128)(2,1)} fusion(bf16[384,1024]{1,0:T(8,128)(2,1)} %collective-permute-done.6, bf16[384,1024]{1,0:T(8,128)(2,1)S(1)} %add_convert_fusion.1), kind=kLoop, calls=%fused_computation.111 | loop fusion | flops 1572864 | bytes 2359296 | tf_op jit(solution)/shard_map/broadcast_in_dim | solution.py:167
  144.3 74.0 %reduce-scatter.4.cloned.1.call-done = bf16[64,512]{1,0:T(8,128)(2,1)} async-done(((bf16[1024,512]{1,0:T(8,128)(2,1)}), bf16[64,512]{1,0:T(8,128)(2,1)}) %reduce-scatter.4.cloned.1.call-update) | async-done | bytes 65552
  218.4 1.0 copy.34
  (93 shorter events, 22.8 us)
Async XLA Ops:
  7.2 11.4 %copy-start = (s32[24,7]{0,1:T(8,128)S(1)}, s32[24,7]{0,1:T(8,128)}, u32[]{:S(2)}) copy-start(s32[24,7]{0,1:T(8,128)} %param.18) | copy-start | bytes 2020
  7.2 2.4 %copy-start.12 = (bf16[1,384,1024]{2,1,0:T(8,128)(2,1)S(1)}, bf16[1,384,1024]{2,1,0:T(8,128)(2,1)}, u32[]{:S(2)}) copy-start(bf16[1,384,1024]{2,1,0:T(8,128)(2,1)} %param.14) | copy-start | bytes 2359300
  7.2 45.7 %all-gather.2.cloned.1.call-start = ((), (), s32[]{:S(2)}) async-start(), calls=%async_computation.2 | async-start | bytes 3145728 | tf_op jit(solution)/shard_map/all_gather | solution.py:84
  7.2 25.4 %copy-start.18 = (bf16[1,384,512]{2,1,0:T(8,128)(2,1)S(1)}, bf16[1,384,512]{2,1,0:T(8,128)(2,1)}, u32[]{:S(2)}) copy-start(bf16[1,384,512]{2,1,0:T(8,128)(2,1)} %param.19) | copy-start | bytes 1179652
  9.7 14.0 %collective-permute-start.2 = (bf16[384,512]{1,0:T(8,128)(2,1)S(1)}, bf16[384,512]{1,0:T(8,128)(2,1)S(1)}, u32[]{:S(2)}, u32[]{:S(2)}) collective-permute-start(bf16[384,512]{1,0:T(8,128)(2,1)S(1)} %dynamic-slice_bitcast_fusion), channel_id=1, source_target_pairs={{4,0},{8,4},{12,8},{16,12},{20,16},{24,20},{28,24},{5,1},{9,5},{13... | collective-permute-start | bytes 1179656 | tf_op jit(solution)/shard_map/ppermute | solution.py:14
  11.0 21.3 %collective-permute-start.1 = (bf16[384,512]{1,0:T(8,128)(2,1)S(1)}, bf16[384,512]{1,0:T(8,128)(2,1)S(1)}, u32[]{:S(2)}, u32[]{:S(2)}) collective-permute-start(bf16[384,512]{1,0:T(8,128)(2,1)S(1)} %dynamic-slice_bitcast_fusion), channel_id=1, source_target_pairs={{0,4},{4,8},{8,12},{12,16},{16,20},{20,24},{24,28},{1,5},{5,9},{9,... | collective-permute-start | bytes 1179656 | tf_op jit(solution)/shard_map/ppermute | solution.py:14
  16.5 23.5 %collective-permute-start = (bf16[512,512]{1,0:T(8,128)(2,1)}, bf16[512,512]{1,0:T(8,128)(2,1)}, u32[]{:S(2)}, u32[]{:S(2)}) collective-permute-start(bf16[512,512]{1,0:T(8,128)(2,1)} %param.15), channel_id=1, source_target_pairs={{0,2},{2,0},{1,3},{3,1},{4,6},{6,4},{5,7},{7,5},{8,10},{10,8},{9,1... | collective-permute-start | bytes 1572872 | tf_op jit(solution)/shard_map/ppermute | solution.py:50
  32.3 10.0 %collective-permute-start.3 = (bf16[2,384,512]{2,1,0:T(8,128)(2,1)S(1)}, bf16[2,384,512]{2,1,0:T(8,128)(2,1)S(1)}, u32[]{:S(2)}, u32[]{:S(2)}) collective-permute-start(bf16[2,384,512]{2,1,0:T(8,128)(2,1)S(1)} %pad_maximum_fusion.2), channel_id=1, source_target_pairs={{0,1},{1,0},{2,3},{3,2},{4,5},{5,4},{6,7},{7,6},{8,9},{9,8},{10,11... | collective-permute-start | bytes 2359304 | tf_op jit(solution)/shard_map/ppermute | solution.py:42
  57.8 9.9 %copy-start.16 = (bf16[1152,512]{0,1:T(8,128)(2,1)}, bf16[1152,512]{0,1:T(8,128)(2,1)S(1)}, u32[]{:S(2)}) copy-start(bf16[1152,512]{0,1:T(8,128)(2,1)S(1)} %get-tuple-element.58) | copy-start | bytes 3538948
  59.2 0.7 copy-start.20
  59.9 1.3 copy-start.19
  61.2 7.7 %copy-start.6 = (f32[8,128,896]{2,1,0:T(8,128)}, f32[8,128,896]{2,1,0:T(8,128)S(1)}, u32[]{:S(2)}) copy-start(f32[8,128,896]{2,1,0:T(8,128)S(1)} %get-tuple-element.70) | copy-start | bytes 11010052
  64.3 5.7 %copy-start.8 = (f32[8,128,896]{2,1,0:T(8,128)}, f32[8,128,896]{2,1,0:T(8,128)S(1)}, u32[]{:S(2)}) copy-start(f32[8,128,896]{2,1,0:T(8,128)S(1)} %get-tuple-element.68) | copy-start | bytes 11010052
  67.2 3.9 %copy-start.10 = (f32[8,128,896]{2,1,0:T(8,128)}, f32[8,128,896]{2,1,0:T(8,128)S(1)}, u32[]{:S(2)}) copy-start(f32[8,128,896]{2,1,0:T(8,128)S(1)} %get-tuple-element.66) | copy-start | bytes 11010052
  71.7 1.2 copy-start.3
  73.7 38.4 %collective-permute-start.4 = (bf16[2,384,512]{1,2,0:T(8,128)(2,1)S(1)}, bf16[2,384,512]{1,2,0:T(8,128)(2,1)S(1)}, u32[]{:S(2)}, u32[]{:S(2)}) collective-permute-start(bf16[2,384,512]{1,2,0:T(8,128)(2,1)S(1)} %get-tuple-element.55), channel_id=1, source_target_pairs={{0,4},{4,8},{8,12},{12,16},{16,20},{20,24},{24,28},{1,5},{5,9},{9,... | collective-permute-start | bytes 2359304 | tf_op jit(solution)/shard_map/ppermute | solution.py:14
  78.3 33.8 %collective-permute-start.5 = (bf16[2,384,512]{1,2,0:T(8,128)(2,1)S(1)}, bf16[2,384,512]{1,2,0:T(8,128)(2,1)S(1)}, u32[]{:S(2)}, u32[]{:S(2)}) collective-permute-start(bf16[2,384,512]{1,2,0:T(8,128)(2,1)S(1)} %get-tuple-element.56), channel_id=1, source_target_pairs={{4,0},{8,4},{12,8},{16,12},{20,16},{24,20},{28,24},{5,1},{9,5},{13... | collective-permute-start | bytes 2359304 | tf_op jit(solution)/shard_map/ppermute | solution.py:14
  81.3 32.1 %copy-start.13 = (bf16[1,384,1024]{2,1,0:T(8,128)(2,1)S(1)}, bf16[1,384,1024]{2,1,0:T(8,128)(2,1)}, u32[]{:S(2)}) copy-start(bf16[1,384,1024]{2,1,0:T(8,128)(2,1)} %param.14) | copy-start | bytes 2359300
  112.4 0.9 copy-start.4
  118.7 100.8 %all-to-all-start = ((bf16[1024,2,512]{2,1,0:T(2,128)(2,1)}), bf16[1024,2,512]{2,1,0:T(2,128)(2,1)S(1)}, u32[]{:S(2)}, u32[]{:S(2)}) async-start(bf16[1024,2,512]{2,1,0:T(2,128)(2,1)} %copy.26), calls=%async_computation | async-start | bytes 4194304 | tf_op jit(solution)/shard_map/all_to_all | solution.py:57
  125.6 92.8 %reduce-scatter.4.cloned.1.call-start = ((), (), s32[]{:S(2)}) async-start(), calls=%async_computation.3 | async-start | bytes 1114112
  125.9 3.2 %copy-start.14 = (bf16[1,384,1024]{2,1,0:T(8,128)(2,1)S(1)}, bf16[1,384,1024]{2,1,0:T(8,128)(2,1)}, u32[]{:S(2)}) copy-start(bf16[1,384,1024]{2,1,0:T(8,128)(2,1)} %param.14) | copy-start | bytes 2359300
  128.3 0.7 copy-start.15
  131.2 2.8 %copy-start.11 = (f32[8,128,896]{2,1,0:T(8,128)S(1)}, f32[8,128,896]{2,1,0:T(8,128)}, u32[]{:S(2)}) copy-start(f32[8,128,896]{2,1,0:T(8,128)} %copy-done.10) | copy-start | bytes 11010052
  131.2 3.1 %copy-start.17 = (bf16[1152,512]{0,1:T(8,128)(2,1)S(1)}, bf16[1152,512]{0,1:T(8,128)(2,1)}, u32[]{:S(2)}) copy-start(bf16[1152,512]{0,1:T(8,128)(2,1)} %copy-done.16) | copy-start | bytes 3538948
  134.3 1.6 copy-start.2
  134.3 1.8 copy-start.5
  136.7 2.1 copy-start.9
  137.4 2.7 %copy-start.7 = (f32[8,128,896]{2,1,0:T(8,128)S(1)}, f32[8,128,896]{2,1,0:T(8,128)}, u32[]{:S(2)}) copy-start(f32[8,128,896]{2,1,0:T(8,128)} %copy-done.6) | copy-start | bytes 11010052
  137.4 4.7 %collective-permute-start.6 = (bf16[384,1024]{1,0:T(8,128)(2,1)S(1)}, bf16[384,1024]{1,0:T(8,128)(2,1)}, u32[]{:S(2)}, u32[]{:S(2)}) collective-permute-start(bf16[384,1024]{1,0:T(8,128)(2,1)S(1)} %add_convert_fusion.1), channel_id=1, source_target_pairs={{0,1},{1,0},{2,3},{3,2},{4,5},{5,4},{6,7},{7,6},{8,9},{9,8},{10,11... | collective-permute-start | bytes 2359304 | tf_op jit(solution)/shard_map/ppermute | solution.py:67
  219.5 1.4 copy-start.1
Sparse Core Ops, SparseCore 0:
  9.7 43.0 all-gather.1
  131.3 87.0 reduce-scatter.3

commit v3 on v2

--- a/solution.py
+++ b/solution.py
@@ -156,7 +156,7 @@
     term_query = jnp.einsum(
         "tr,tf->rf", tokens, query_grad, preferred_element_type=jnp.float32
     ).astype(jnp.bfloat16)
-    reduced_query = lax.psum_scatter(term_query, ("ctx", "dp"), scatter_dimension=0, tiled=True)
+    reduced_query = summed_rows(term_query)
 
     contract = (((1,), (1,)), ((), ()))
     partial_input = (
@@ -173,7 +173,7 @@
         preferred_element_type=jnp.float32,
     ).astype(jnp.bfloat16)
     reduced_kv = summed_rows(term_kv)
-    summed = jnp.concatenate([reduced_query[:, None].astype(jnp.float32), reduced_kv], axis=1)
+    summed = jnp.concatenate([reduced_query[:, None], reduced_kv], axis=1)
     grad_weights = summed / lax.axis_size("dp")
     return (attended, grad_input, grad_weights)
 

time: 228 us -> 207 us (0.908)
  the two profiles are of different devices: /device:TPU:0 before, /device:TPU:12 now
where the time goes in v3:
time: 207 us
  waiting for transfers between devices  99.3 us (48%)
  matrix products  32.8 us (16%)
  starting transfers between devices  27.6 us (13%)
  other arithmetic  18.9 us (9%)
  between operations  14.5 us (7%)
  local copies, waits for them, and re-layouts  13.6 us (7%)
    ppermute x4, waiting for transfers between devices, shifted(): lax.ppermute(value, axis, [(source, source + steps) for source in range(l...  51.8 us
    all_to_all x2, waiting for transfers between devices, summed_rows(): parts = lax.all_to_all(term, group, 0, 0, tiled=True)  32.9 us
    ppermute x4, starting transfers between devices, shifted(): lax.ppermute(value, axis, [(source, source + steps) for source in range(l...  12.9 us
    all_to_all x2, starting transfers between devices, summed_rows(): parts = lax.all_to_all(term, group, 0, 0, tiled=True)  12.8 us
    ppermute x1, waiting for transfers between devices, full_rows(): other = lax.ppermute(weight, 'dp', [(0, 1), (1, 0)])  7.63 us
    all_gather x1, waiting for transfers between devices, per_device(): lax.all_gather(jnp.stack([w_key, w_value]), 'dp', axis=1, tiled=True)  7.02 us
    dot_general x3, matrix products, per_device(): jnp.einsum('hqk,hqd->hkd', weights, upstream_block, preferred_element_typ...  6.55 us
    unnamed x38, local copies, waits for them, and re-layouts  4.4 us
  transfers between devices with their start and end apart: 10, of which 7 were waited for; matrix products, arithmetic and copies ran while one was open for 13% of the time, Pallas kernels for 0%

profile of v3, /device:TPU:12, one launch (start us, length us, event | category | flops | bytes accessed | tf_op | source)
XLA Modules:
  0.0 206.8 jit_solution(5009121823529442694)
XLA Ops:
  7.2 2.3 %pad_maximum_fusion.1 = bf16[2,512,512]{2,1,0:T(8,128)(2,1)} fusion(bf16[1,512,512]{2,1,0:T(8,128)(2,1)} %bitcast.145, bf16[1,512,512]{2,1,0:T(8,128)(2,1)} %bitcast.146), kind=kLoop, calls=%fused_computation.84 | loop fusion | flops 524288 | bytes 2097152 | tf_op jit(solution)/shard_map/stack | solution.py:84
  9.7 2.4 %collective-permute-start.2 = (bf16[384,512]{1,0:T(8,128)(2,1)S(1)}, bf16[384,512]{1,0:T(8,128)(2,1)S(1)}, u32[]{:S(2)}, u32[]{:S(2)}) collective-permute-start(bf16[384,512]{1,0:T(8,128)(2,1)S(1)} %dynamic-slice_bitcast_fusion), channel_id=1, source_target_pairs={{4,0},{8,4},{12,8},{16,12},{20,16},{24,20},{28,24},{5,1},{9,5},{13... | collective-permute-start | bytes 1179656 | tf_op jit(solution)/shard_map/ppermute | solution.py:14
  12.1 4.3 %collective-permute-start.1 = (bf16[384,512]{1,0:T(8,128)(2,1)S(1)}, bf16[384,512]{1,0:T(8,128)(2,1)S(1)}, u32[]{:S(2)}, u32[]{:S(2)}) collective-permute-start(bf16[384,512]{1,0:T(8,128)(2,1)S(1)} %dynamic-slice_bitcast_fusion), channel_id=1, source_target_pairs={{0,4},{4,8},{8,12},{12,16},{16,20},{20,24},{24,28},{1,5},{5,9},{9,... | collective-permute-start | bytes 1179656 | tf_op jit(solution)/shard_map/ppermute | solution.py:14
  16.4 1.6 collective-permute-start
  18.1 10.8 %collective-permute-done.2 = bf16[384,512]{1,0:T(8,128)(2,1)S(1)} collective-permute-done((bf16[384,512]{1,0:T(8,128)(2,1)S(1)}, bf16[384,512]{1,0:T(8,128)(2,1)S(1)}, u32[]{:S(2)}, u32[]{:S(2)}) %collective-permute-start.2) | collective-permute-done | bytes 393248 | tf_op jit(solution)/shard_map/ppermute | solution.py:14
  28.9 2.9 %collective-permute-done.1 = bf16[384,512]{1,0:T(8,128)(2,1)S(1)} collective-permute-done((bf16[384,512]{1,0:T(8,128)(2,1)S(1)}, bf16[384,512]{1,0:T(8,128)(2,1)S(1)}, u32[]{:S(2)}, u32[]{:S(2)}) %collective-permute-start.1) | collective-permute-done | bytes 393248 | tf_op jit(solution)/shard_map/ppermute | solution.py:14
  32.6 7.6 %collective-permute-done = bf16[512,512]{1,0:T(8,128)(2,1)} collective-permute-done((bf16[512,512]{1,0:T(8,128)(2,1)}, bf16[512,512]{1,0:T(8,128)(2,1)}, u32[]{:S(2)}, u32[]{:S(2)}) %collective-permute-start) | collective-permute-done | bytes 524320 | tf_op jit(solution)/shard_map/ppermute | solution.py:50
  40.2 2.4 %convolution_convert_fusion.2 = bf16[512,384]{1,0:T(8,128)(2,1)S(1)} fusion(bf16[512,512]{1,0:T(8,128)(2,1)} %collective-permute-done, bf16[512,512]{1,0:T(8,128)(2,1)} %param.15, pred[]{:T(512)S(6)} %eq.6, bf16[1,384,1024]{2,1,0:T(8,128)(2,1)S(1)} %copy-done.11), kind=kOutput, calls=%fused_computation.71 | convolution fusion | flops 407568384 | bytes 2228225 | tf_op jit(solution)/shard_map/dot_general | solution.py:87
  42.6 1.9 maximum_select_fusion
  45.5 7.0 %all-gather.2.cloned.1.call-done = bf16[2,1024,512]{2,1,0:T(8,128)(2,1)} async-done(((bf16[2,512,512]{2,1,0:T(8,128)(2,1)}), bf16[2,1024,512]{2,1,0:T(8,128)(2,1)}) %all-gather.2.cloned.1.call-update) | async-done | bytes 2097168 | tf_op jit(solution)/shard_map/all_gather | solution.py:84
  52.5 1.7 slice_bitcast_fusion.1
  54.3 3.1 %convolution_convert_fusion = bf16[1152,1024]{0,1:T(8,128)(2,1)S(1)} fusion(bf16[384,1024]{1,0:T(8,128)(2,1)S(1)} %copy-done.16, bf16[384,1024]{1,0:T(8,128)(2,1)S(1)} %bitcast.124, bf16[384,1024]{1,0:T(8,128)(2,1)S(1)} %get-tuple-element.61, bf16[1024,512]{1,0:T(8,128)(2,1)S(1)} %get-tuple-element.60, bf16[1024,512]{1,0:T(8,128)(2,1)S(1)} %get-tuple-element.59), kind=kOutput, calls=%fused_computation.8 | convolution fusion | flops 2428370944 | bytes 6815744 | tf_op jit(solution)/shard_map/dot_general | solution.py:90
  59.6 1.2 fusion.121
  60.9 2.1 %fusion.55 = f32[8,896,64]{1,2,0:T(8,128)} fusion(bf16[8,384,64]{1,2,0:T(8,128)(2,1)S(1)} %bitcast.147, f32[8,128,896]{2,1,0:T(8,128)S(1)} %get-tuple-element.70, f32[8,128]{1,0:T(8,128)S(1)} %get-tuple-element.69), kind=kOutput, calls=%fused_computation.91 | convolution fusion | flops 119275520 | bytes 5640192 | tf_op jit(solution)/shard_map/hqk,hqd->hkd/dot_general | solution.py:133
  67.3 2.1 %fusion.52 = f32[8,896,64]{1,2,0:T(8,128)} fusion(bf16[8,384,64]{1,2,0:T(8,128)(2,1)S(1)} %bitcast.149, f32[8,128,896]{2,1,0:T(8,128)S(1)} %get-tuple-element.68, f32[8,128]{1,0:T(8,128)S(1)} %get-tuple-element.67), kind=kOutput, calls=%fused_computation.88 | convolution fusion | flops 119275520 | bytes 5640192 | tf_op jit(solution)/shard_map/hqk,hqd->hkd/dot_general | solution.py:133
  72.0 1.7 convolution_multiply_fusion.1
  74.8 2.3 %fusion.49 = f32[8,896,64]{1,2,0:T(8,128)} fusion(bf16[8,384,64]{1,2,0:T(8,128)(2,1)S(1)} %bitcast.151, f32[8,128,896]{2,1,0:T(8,128)S(1)} %get-tuple-element.66, f32[8,128]{1,0:T(8,128)S(1)} %get-tuple-element.65), kind=kOutput, calls=%fused_computation.85 | convolution fusion | flops 119275520 | bytes 5640192 | tf_op jit(solution)/shard_map/hqk,hqd->hkd/dot_general | solution.py:133
  79.7 1.7 convolution_multiply_fusion
  82.2 1.4 copy.25
  83.6 6.2 %all-to-all-start = ((bf16[16,64,512]{2,1,0:T(8,128)(2,1)}), bf16[16,64,512]{2,1,0:T(8,128)(2,1)}, u32[]{:S(2)}, u32[]{:S(2)}) async-start(bf16[16,64,512]{2,1,0:T(8,128)(2,1)} %bitcast.43), calls=%async_computation | async-start | bytes 2097152 | tf_op jit(solution)/shard_map/all_to_all | solution.py:57
  89.7 3.1 %pad_add_fusion = f32[8,1152,64]{1,2,0:T(8,128)S(1)} fusion(f32[8,896,64]{1,2,0:T(8,128)} %fusion.49, f32[8,896,64]{1,2,0:T(8,128)} %fusion.52, f32[8,896,64]{1,2,0:T(8,128)} %fusion.55), kind=kLoop, calls=%fused_computation.41 | loop fusion | flops 1179648 | bytes 7864320 | tf_op jit(solution)/shard_map/add | solution.py:140
  94.2 3.4 %collective-permute-start.4 = (bf16[2,384,512]{1,2,0:T(8,128)(2,1)S(1)}, bf16[2,384,512]{1,2,0:T(8,128)(2,1)S(1)}, u32[]{:S(2)}, u32[]{:S(2)}) collective-permute-start(bf16[2,384,512]{1,2,0:T(8,128)(2,1)S(1)} %get-tuple-element.55), channel_id=1, source_target_pairs={{0,4},{4,8},{8,12},{12,16},{16,20},{20,24},{24,28},{1,5},{5,9},{9,... | collective-permute-start | bytes 2359304 | tf_op jit(solution)/shard_map/ppermute | solution.py:14
  97.6 2.8 %collective-permute-start.5 = (bf16[2,384,512]{1,2,0:T(8,128)(2,1)S(1)}, bf16[2,384,512]{1,2,0:T(8,128)(2,1)S(1)}, u32[]{:S(2)}, u32[]{:S(2)}) collective-permute-start(bf16[2,384,512]{1,2,0:T(8,128)(2,1)S(1)} %get-tuple-element.56), channel_id=1, source_target_pairs={{4,0},{8,4},{12,8},{16,12},{20,16},{24,20},{28,24},{5,1},{9,5},{13... | collective-permute-start | bytes 2359304 | tf_op jit(solution)/shard_map/ppermute | solution.py:14
  100.4 37.7 %collective-permute-done.4 = bf16[2,384,512]{1,2,0:T(8,128)(2,1)S(1)} collective-permute-done((bf16[2,384,512]{1,2,0:T(8,128)(2,1)S(1)}, bf16[2,384,512]{1,2,0:T(8,128)(2,1)S(1)}, u32[]{:S(2)}, u32[]{:S(2)}) %collective-permute-start.4) | collective-permute-done | bytes 786464 | tf_op jit(solution)/shard_map/ppermute | solution.py:14
  139.0 1.3 convert_bitcast_fusion
  140.2 4.1 %copy.26 = bf16[1024,2,512]{2,1,0:T(2,128)(2,1)} copy(bf16[1024,2,512]{0,2,1:T(8,128)(2,1)S(1)} %convert_bitcast_fusion) | data formatting | bytes 4194304 | tf_op jit(solution)/shard_map/convert_element_type | solution.py:174
  144.3 6.7 %all-to-all-start.1 = ((bf16[1024,2,512]{2,1,0:T(2,128)(2,1)}), bf16[1024,2,512]{2,1,0:T(2,128)(2,1)S(1)}, u32[]{:S(2)}, u32[]{:S(2)}) async-start(bf16[1024,2,512]{2,1,0:T(2,128)(2,1)} %copy.26), calls=%async_computation.1 | async-start | bytes 4194304 | tf_op jit(solution)/shard_map/all_to_all | solution.py:57
  151.0 2.3 %fusion.87 = f32[384,1024]{1,0:T(8,128)S(1)} fusion(bf16[384,512]{0,1:T(8,128)(2,1)S(1)} %bitcast.127, bf16[512,512]{1,0:T(8,128)(2,1)} %collective-permute-done, bf16[512,512]{1,0:T(8,128)(2,1)} %param.15, pred[]{:T(512)S(6)} %eq.6), kind=kOutput, calls=%fused_computation.130 | convolution fusion | flops 407371776 | bytes 3014657 | tf_op jit(solution)/shard_map/dot_general | solution.py:163
  156.2 1.5 add_convert_fusion.1
  162.0 2.3 %fusion.76 = bf16[1,384,1024]{2,1,0:T(8,128)(2,1)} fusion(bf16[384,1024]{1,0:T(8,128)(2,1)S(1)} %collective-permute-done.6, bf16[384,1024]{1,0:T(8,128)(2,1)} %add_convert_fusion.1), kind=kLoop, calls=%fused_computation.112 | loop fusion | flops 1572864 | bytes 2359296 | tf_op jit(solution)/shard_map/broadcast_in_dim | solution.py:167
  164.3 1.4 convert_reduce_fusion.1
  165.7 32.9 %all-to-all-done.1 = bf16[1024,2,512]{2,1,0:T(2,128)(2,1)S(1)} async-done(((bf16[1024,2,512]{2,1,0:T(2,128)(2,1)}), bf16[1024,2,512]{2,1,0:T(2,128)(2,1)S(1)}, u32[]{:S(2)}, u32[]{:S(2)}) %all-to-all-start.1) | async-done | bytes 2097184 | tf_op jit(solution)/shard_map/all_to_all | solution.py:57
  (84 shorter events, 26.1 us)
Async XLA Ops:
  7.2 10.8 %copy-start = (s32[24,7]{0,1:T(8,128)S(1)}, s32[24,7]{0,1:T(8,128)}, u32[]{:S(2)}) copy-start(s32[24,7]{0,1:T(8,128)} %param.18) | copy-start | bytes 2020
  7.2 2.4 %copy-start.11 = (bf16[1,384,1024]{2,1,0:T(8,128)(2,1)S(1)}, bf16[1,384,1024]{2,1,0:T(8,128)(2,1)}, u32[]{:S(2)}) copy-start(bf16[1,384,1024]{2,1,0:T(8,128)(2,1)} %param.14) | copy-start | bytes 2359300
  7.2 45.3 %all-gather.2.cloned.1.call-start = ((), (), s32[]{:S(2)}) async-start(), calls=%async_computation.2 | async-start | bytes 3145728 | tf_op jit(solution)/shard_map/all_gather | solution.py:84
  7.2 25.0 %copy-start.17 = (bf16[1,384,512]{2,1,0:T(8,128)(2,1)S(1)}, bf16[1,384,512]{2,1,0:T(8,128)(2,1)}, u32[]{:S(2)}) copy-start(bf16[1,384,512]{2,1,0:T(8,128)(2,1)} %param.19) | copy-start | bytes 1179652
  9.7 19.2 %collective-permute-start.2 = (bf16[384,512]{1,0:T(8,128)(2,1)S(1)}, bf16[384,512]{1,0:T(8,128)(2,1)S(1)}, u32[]{:S(2)}, u32[]{:S(2)}) collective-permute-start(bf16[384,512]{1,0:T(8,128)(2,1)S(1)} %dynamic-slice_bitcast_fusion), channel_id=1, source_target_pairs={{4,0},{8,4},{12,8},{16,12},{20,16},{24,20},{28,24},{5,1},{9,5},{13... | collective-permute-start | bytes 1179656 | tf_op jit(solution)/shard_map/ppermute | solution.py:14
  12.1 19.7 %collective-permute-start.1 = (bf16[384,512]{1,0:T(8,128)(2,1)S(1)}, bf16[384,512]{1,0:T(8,128)(2,1)S(1)}, u32[]{:S(2)}, u32[]{:S(2)}) collective-permute-start(bf16[384,512]{1,0:T(8,128)(2,1)S(1)} %dynamic-slice_bitcast_fusion), channel_id=1, source_target_pairs={{0,4},{4,8},{8,12},{12,16},{16,20},{20,24},{24,28},{1,5},{5,9},{9,... | collective-permute-start | bytes 1179656 | tf_op jit(solution)/shard_map/ppermute | solution.py:14
  16.4 23.8 %collective-permute-start = (bf16[512,512]{1,0:T(8,128)(2,1)}, bf16[512,512]{1,0:T(8,128)(2,1)}, u32[]{:S(2)}, u32[]{:S(2)}) collective-permute-start(bf16[512,512]{1,0:T(8,128)(2,1)} %param.15), channel_id=1, source_target_pairs={{0,2},{2,0},{1,3},{3,1},{4,6},{6,4},{5,7},{7,5},{8,10},{10,8},{9,1... | collective-permute-start | bytes 1572872 | tf_op jit(solution)/shard_map/ppermute | solution.py:50
  31.8 10.8 %collective-permute-start.3 = (bf16[2,384,512]{2,1,0:T(8,128)(2,1)S(1)}, bf16[2,384,512]{2,1,0:T(8,128)(2,1)}, u32[]{:S(2)}, u32[]{:S(2)}) collective-permute-start(bf16[2,384,512]{2,1,0:T(8,128)(2,1)S(1)} %pad_maximum_fusion.2), channel_id=1, source_target_pairs={{0,1},{1,0},{2,3},{3,2},{4,5},{5,4},{6,7},{7,6},{8,9},{9,8},{10,11... | collective-permute-start | bytes 2359304 | tf_op jit(solution)/shard_map/ppermute | solution.py:42
  52.5 1.8 copy-start.16
  57.6 19.6 %copy-start.14 = (bf16[1152,512]{0,1:T(8,128)(2,1)}, bf16[1152,512]{0,1:T(8,128)(2,1)S(1)}, u32[]{:S(2)}) copy-start(bf16[1152,512]{0,1:T(8,128)(2,1)S(1)} %get-tuple-element.58) | copy-start | bytes 3538948
  60.9 3.3 %copy-start.5 = (f32[8,128,896]{2,1,0:T(8,128)}, f32[8,128,896]{2,1,0:T(8,128)S(1)}, u32[]{:S(2)}) copy-start(f32[8,128,896]{2,1,0:T(8,128)S(1)} %get-tuple-element.70) | copy-start | bytes 11010052
  67.2 3.3 %copy-start.7 = (f32[8,128,896]{2,1,0:T(8,128)}, f32[8,128,896]{2,1,0:T(8,128)S(1)}, u32[]{:S(2)}) copy-start(f32[8,128,896]{2,1,0:T(8,128)S(1)} %get-tuple-element.68) | copy-start | bytes 11010052
  74.8 3.4 %copy-start.9 = (f32[8,128,896]{2,1,0:T(8,128)}, f32[8,128,896]{2,1,0:T(8,128)S(1)}, u32[]{:S(2)}) copy-start(f32[8,128,896]{2,1,0:T(8,128)S(1)} %get-tuple-element.66) | copy-start | bytes 11010052
  79.7 1.7 copy-start.12
  83.6 60.7 %all-to-all-start = ((bf16[16,64,512]{2,1,0:T(8,128)(2,1)}), bf16[16,64,512]{2,1,0:T(8,128)(2,1)}, u32[]{:S(2)}, u32[]{:S(2)}) async-start(bf16[16,64,512]{2,1,0:T(8,128)(2,1)} %bitcast.43), calls=%async_computation | async-start | bytes 2097152 | tf_op jit(solution)/shard_map/all_to_all | solution.py:57
  89.7 3.1 %copy-start.3 = (f32[8,896,64]{1,2,0:T(8,128)S(1)}, f32[8,896,64]{1,2,0:T(8,128)}, u32[]{:S(2)}) copy-start(f32[8,896,64]{1,2,0:T(8,128)} %convolution_multiply_fusion.1) | copy-start | bytes 5505028
  89.7 3.7 %copy-start.4 = (f32[8,896,64]{1,2,0:T(8,128)S(1)}, f32[8,896,64]{1,2,0:T(8,128)}, u32[]{:S(2)}) copy-start(f32[8,896,64]{1,2,0:T(8,128)} %convolution_multiply_fusion) | copy-start | bytes 5505028
  94.2 43.9 %collective-permute-start.4 = (bf16[2,384,512]{1,2,0:T(8,128)(2,1)S(1)}, bf16[2,384,512]{1,2,0:T(8,128)(2,1)S(1)}, u32[]{:S(2)}, u32[]{:S(2)}) collective-permute-start(bf16[2,384,512]{1,2,0:T(8,128)(2,1)S(1)} %get-tuple-element.55), channel_id=1, source_target_pairs={{0,4},{4,8},{8,12},{12,16},{16,20},{20,24},{24,28},{1,5},{5,9},{9,... | collective-permute-start | bytes 2359304 | tf_op jit(solution)/shard_map/ppermute | solution.py:14
  97.6 41.4 %copy-start.13 = (bf16[1,384,1024]{2,1,0:T(8,128)(2,1)S(1)}, bf16[1,384,1024]{2,1,0:T(8,128)(2,1)}, u32[]{:S(2)}) copy-start(bf16[1,384,1024]{2,1,0:T(8,128)(2,1)} %param.14) | copy-start | bytes 2359300
  97.6 41.0 %collective-permute-start.5 = (bf16[2,384,512]{1,2,0:T(8,128)(2,1)S(1)}, bf16[2,384,512]{1,2,0:T(8,128)(2,1)S(1)}, u32[]{:S(2)}, u32[]{:S(2)}) collective-permute-start(bf16[2,384,512]{1,2,0:T(8,128)(2,1)S(1)} %get-tuple-element.56), channel_id=1, source_target_pairs={{4,0},{8,4},{12,8},{16,12},{20,16},{24,20},{28,24},{5,1},{9,5},{13... | collective-permute-start | bytes 2359304 | tf_op jit(solution)/shard_map/ppermute | solution.py:14
  144.3 54.2 %all-to-all-start.1 = ((bf16[1024,2,512]{2,1,0:T(2,128)(2,1)}), bf16[1024,2,512]{2,1,0:T(2,128)(2,1)S(1)}, u32[]{:S(2)}, u32[]{:S(2)}) async-start(bf16[1024,2,512]{2,1,0:T(2,128)(2,1)} %copy.26), calls=%async_computation.1 | async-start | bytes 4194304 | tf_op jit(solution)/shard_map/all_to_all | solution.py:57
  151.0 2.7 %copy-start.10 = (f32[8,128,896]{2,1,0:T(8,128)S(1)}, f32[8,128,896]{2,1,0:T(8,128)}, u32[]{:S(2)}) copy-start(f32[8,128,896]{2,1,0:T(8,128)} %copy-done.9) | copy-start | bytes 11010052
  151.0 3.0 %copy-start.15 = (bf16[1152,512]{0,1:T(8,128)(2,1)S(1)}, bf16[1152,512]{0,1:T(8,128)(2,1)}, u32[]{:S(2)}) copy-start(bf16[1152,512]{0,1:T(8,128)(2,1)} %copy-done.14) | copy-start | bytes 3538948
  154.0 1.6 copy-start.2
  156.2 2.3 %copy-start.8 = (f32[8,128,896]{2,1,0:T(8,128)S(1)}, f32[8,128,896]{2,1,0:T(8,128)}, u32[]{:S(2)}) copy-start(f32[8,128,896]{2,1,0:T(8,128)} %copy-done.7) | copy-start | bytes 11010052
  157.8 2.2 %copy-start.6 = (f32[8,128,896]{2,1,0:T(8,128)S(1)}, f32[8,128,896]{2,1,0:T(8,128)}, u32[]{:S(2)}) copy-start(f32[8,128,896]{2,1,0:T(8,128)} %copy-done.5) | copy-start | bytes 11010052
  157.8 4.2 %collective-permute-start.6 = (bf16[384,1024]{1,0:T(8,128)(2,1)}, bf16[384,1024]{1,0:T(8,128)(2,1)S(1)}, u32[]{:S(2)}, u32[]{:S(2)}) collective-permute-start(bf16[384,1024]{1,0:T(8,128)(2,1)} %add_convert_fusion.1), channel_id=1, source_target_pairs={{0,1},{1,0},{2,3},{3,2},{4,5},{5,4},{6,7},{7,6},{8,9},{9,8},{10,11... | collective-permute-start | bytes 2359304 | tf_op jit(solution)/shard_map/ppermute | solution.py:67
  198.5 1.4 copy-start.1
Sparse Core Ops, SparseCore 0:
  9.7 42.7 all-gather.1

commit v4 on v3

--- a/solution.py
+++ b/solution.py
@@ -68,6 +68,13 @@
     return (mine.astype(jnp.float32) + other.astype(jnp.float32)).astype(jnp.bfloat16)
 
 
+def softmax_stats(scores, seen):
+    row_top = jnp.max(jnp.where(seen, scores, -jnp.inf), axis=2, keepdims=True)
+    raised = jnp.where(seen, jnp.exp(scores - row_top), 0.0)
+    row_total = jnp.sum(raised, axis=2, keepdims=True)
+    return raised / row_total, row_top, row_total
+
+
 def per_device(normed, w_query, w_key, w_value, block_mask, cotangent):
     tokens = normed[0]
     upstream = cotangent[0]
@@ -77,43 +84,56 @@
     blocks = length // BLOCK
     span_len = 2 * REACH + 1
     halo = REACH * BLOCK
+    frame_blocks = blocks + 2 * REACH
     score_scale = HD ** (-0.5)
 
     left_tokens, right_tokens = neighbour_tokens(tokens, halo)
-    query_full = full_rows(w_query)
-    gathered = lax.all_gather(jnp.stack([w_key, w_value]), "dp", axis=1, tiled=True)
-    key_full, value_full = gathered[0], gathered[1]
-
-    queries = jnp.dot(tokens, query_full, preferred_element_type=jnp.float32).astype(jnp.bfloat16)
+    left_up = shifted(upstream[length - halo :], "ctx", 1)
+    right_up = shifted(upstream[:halo], "ctx", -1)
+    gathered = lax.all_gather(jnp.stack([w_query, w_key, w_value]), "dp", axis=1, tiled=True)
+    query_full, key_full, value_full = gathered[0], gathered[1], gathered[2]
+
     frame_tokens = jnp.concatenate([left_tokens, tokens, right_tokens], axis=0)
-    kv_weights = jnp.concatenate([key_full, value_full], axis=1)
-    frame_kv = jnp.dot(frame_tokens, kv_weights, preferred_element_type=jnp.float32).astype(
+    all_weights = jnp.concatenate([query_full, key_full, value_full], axis=1)
+    frame_proj = jnp.dot(frame_tokens, all_weights, preferred_element_type=jnp.float32).astype(
         jnp.bfloat16
     )
-    key_h = head_major(frame_kv[:, :features], heads)
-    value_h = head_major(frame_kv[:, features:], heads)
-    query_h = head_major(queries, heads)
-    upstream_h = head_major(upstream, heads)
+    query_h = head_major(frame_proj[:, :features], heads)
+    key_h = head_major(frame_proj[:, features : 2 * features], heads)
+    value_h = head_major(frame_proj[:, 2 * features :], heads)
+    upstream_h = head_major(jnp.concatenate([left_up, upstream, right_up], axis=0), heads)
 
     first_block = lax.axis_index("ctx") * blocks
-    own_mask = lax.dynamic_slice(block_mask, (first_block, 0), (blocks, span_len))
-
-    outs, query_grads = [], []
-    key_frame = None
-    value_frame = None
+    padded_mask = jnp.pad(block_mask, ((REACH, REACH), (0, 0)))
+    frame_mask = lax.dynamic_slice(padded_mask, (first_block, 0), (frame_blocks, span_len))
+
+    def rows(cells, at, count=1):
+        return cells[:, at * BLOCK : (at + count) * BLOCK]
+
+    def seen_keys(at, low, high):
+        picked = frame_mask[at, low - at + REACH : high - at + REACH + 1] > 0
+        return jnp.repeat(picked, BLOCK)[None, None, :]
+
+    own_low, own_high = REACH, REACH + blocks - 1
+    key_own = jnp.zeros((heads, length, HD), jnp.float32)
+    value_own = jnp.zeros((heads, length, HD), jnp.float32)
+
+    def add_own(acc, part, low, high):
+        spread = ((0, 0), ((low - own_low) * BLOCK, (own_high - high) * BLOCK), (0, 0))
+        return acc + jnp.pad(part, spread)
+
+    outs, query_grads, tops, totals, deltas = [], [], [], [], []
     for i in range(blocks):
-        query_block = query_h[:, i * BLOCK : (i + 1) * BLOCK]
-        upstream_block = upstream_h[:, i * BLOCK : (i + 1) * BLOCK]
-        key_window = key_h[:, i * BLOCK : (i + span_len) * BLOCK]
-        value_window = value_h[:, i * BLOCK : (i + span_len) * BLOCK]
-        seen = jnp.repeat(own_mask[i] > 0, BLOCK)[None, None, :]
+        at = REACH + i
+        query_block = rows(query_h, at)
+        upstream_block = rows(upstream_h, at)
+        key_window = rows(key_h, i, span_len)
+        value_window = rows(value_h, i, span_len)
         scores = (
             jnp.einsum("hqd,hkd->hqk", query_block, key_window, preferred_element_type=jnp.float32)
             * score_scale
         )
-        row_top = jnp.max(jnp.where(seen, scores, -jnp.inf), axis=2, keepdims=True)
-        raised = jnp.where(seen, jnp.exp(scores - row_top), 0.0)
-        probability = raised / jnp.sum(raised, axis=2, keepdims=True)
+        probability, row_top, row_total = softmax_stats(scores, seen_keys(at, i, i + 2 * REACH))
         weights = probability.astype(jnp.bfloat16)
         outs.append(
             jnp.einsum("hqk,hkd->hqd", weights, value_window, preferred_element_type=jnp.float32)
@@ -127,36 +147,83 @@
             score_scale
             * jnp.einsum("hqk,hkd->hqd", score_grad, key_window, preferred_element_type=jnp.float32)
         )
-        key_part = score_scale * jnp.einsum(
-            "hqk,hqd->hkd", score_grad, query_block, preferred_element_type=jnp.float32
-        )
-        value_part = jnp.einsum(
-            "hqk,hqd->hkd", weights, upstream_block, preferred_element_type=jnp.float32
-        )
-        spread = ((0, 0), (i * BLOCK, (blocks - 1 - i) * BLOCK), (0, 0))
-        key_part = jnp.pad(key_part, spread)
-        value_part = jnp.pad(value_part, spread)
-        key_frame = key_part if key_frame is None else key_frame + key_part
-        value_frame = value_part if value_frame is None else value_frame + value_part
+        tops.append(row_top)
+        totals.append(row_total)
+        deltas.append(row_delta)
+        low, high = max(own_low, i), min(own_high, i + 2 * REACH)
+        cut = slice((low - i) * BLOCK, (high - i + 1) * BLOCK)
+        key_own = add_own(
+            key_own,
+            score_scale
+            * jnp.einsum(
+                "hqk,hqd->hkd", score_grad[:, :, cut], query_block, preferred_element_type=jnp.float32
+            ),
+            low,
+            high,
+        )
+        value_own = add_own(
+            value_own,
+            jnp.einsum(
+                "hqk,hqd->hkd", weights[:, :, cut], upstream_block, preferred_element_type=jnp.float32
+            ),
+            low,
+            high,
+        )
 
     attended = token_major(jnp.concatenate(outs, axis=1).astype(jnp.bfloat16))[None]
     query_grad = token_major(jnp.concatenate(query_grads, axis=1).astype(jnp.bfloat16))
-
-    frame_grads = jnp.stack([token_major(key_frame), token_major(value_frame)])
-    to_left = frame_grads[:, :halo].astype(jnp.bfloat16)
-    to_right = frame_grads[:, halo + length :].astype(jnp.bfloat16)
-    middle = frame_grads[:, halo : halo + length]
-    from_left = shifted(to_right, "ctx", 1).astype(jnp.float32)
-    from_right = shifted(to_left, "ctx", -1).astype(jnp.float32)
-    middle = middle.at[:, :halo].add(from_left)
-    middle = middle.at[:, length - halo :].add(from_right)
-    key_grad = middle[0].astype(jnp.bfloat16)
-    value_grad = middle[1].astype(jnp.bfloat16)
 
     term_query = jnp.einsum(
         "tr,tf->rf", tokens, query_grad, preferred_element_type=jnp.float32
     ).astype(jnp.bfloat16)
     reduced_query = summed_rows(term_query)
+
+    stats = jnp.stack(
+        [jnp.concatenate(tops, axis=1), jnp.concatenate(totals, axis=1), jnp.concatenate(deltas, axis=1)]
+    )
+    stats_left = shifted(stats[:, :, length - halo :], "ctx", 1)
+    stats_right = shifted(stats[:, :, :halo], "ctx", -1)
+
+    for at in list(range(REACH)) + list(range(REACH + blocks, frame_blocks)):
+        low, high = max(own_low, at - REACH), min(own_high, at + REACH)
+        if low > high:
+            continue
+        if at < REACH:
+            top, total, delta = (part[:, at * BLOCK : (at + 1) * BLOCK] for part in stats_left)
+        else:
+            place = at - REACH - blocks
+            top, total, delta = (part[:, place * BLOCK : (place + 1) * BLOCK] for part in stats_right)
+        query_block = rows(query_h, at)
+        upstream_block = rows(upstream_h, at)
+        key_part = rows(key_h, low, high - low + 1)
+        value_part = rows(value_h, low, high - low + 1)
+        seen = seen_keys(at, low, high)
+        scores = (
+            jnp.einsum("hqd,hkd->hqk", query_block, key_part, preferred_element_type=jnp.float32)
+            * score_scale
+        )
+        probability = jnp.where(seen, jnp.exp(scores - top) / total, 0.0)
+        weights = probability.astype(jnp.bfloat16)
+        prob_grad = jnp.einsum(
+            "hqd,hkd->hqk", upstream_block, value_part, preferred_element_type=jnp.float32
+        )
+        score_grad = (probability * (prob_grad - delta)).astype(jnp.bfloat16)
+        key_own = add_own(
+            key_own,
+            score_scale
+            * jnp.einsum("hqk,hqd->hkd", score_grad, query_block, preferred_element_type=jnp.float32),
+            low,
+            high,
+        )
+        value_own = add_own(
+            value_own,
+            jnp.einsum("hqk,hqd->hkd", weights, upstream_block, preferred_element_type=jnp.float32),
+            low,
+            high,
+        )
+
+    key_grad = token_major(key_own).astype(jnp.bfloat16)
+    value_grad = token_major(value_own).astype(jnp.bfloat16)
 
     contract = (((1,), (1,)), ((), ()))
     partial_input = (

time: 207 us -> 221 us (1.068)
  waiting for transfers between devices: 99.3 us -> 59.2 us
  matrix products: 32.8 us -> 58.2 us
  local copies, waits for them, and re-layouts: 13.6 us -> 33.3 us
  starting transfers between devices: 27.6 us -> 32.7 us
    ppermute x4 -> x6, waiting for transfers between devices: 51.8 us -> 19.8 us  [shifted(): lax.ppermute(value, axis, [(source, source + steps) for source in range(l...]
    dot_general x2 -> x13, matrix products: 5.46 us -> 20.6 us  [the longest x6 6.88 us: per_device(): jnp.einsum('hqd,hkd->hqk', query_block, key_part, preferred_element_type=...]
    dot_general x3 -> x6, matrix products: 3.76 us -> 15.5 us  [per_device(): jnp.einsum('hqk,hqd->hkd', score_grad, query_block, preferred_element_typ...]
    ppermute x1 -> x0, waiting for transfers between devices: 7.63 us -> none  [full_rows(): other = lax.ppermute(weight, 'dp', [(0, 1), (1, 0)])]
    ppermute x4 -> x6, starting transfers between devices: 12.9 us -> 20.3 us  [shifted(): lax.ppermute(value, axis, [(source, source + steps) for source in range(l...]
    unnamed x38 -> x74, local copies, waits for them, and re-layouts: 4.4 us -> 10.6 us
    slice x2 -> x5, local copies, waits for them, and re-layouts: 0.34 us -> 5.68 us  [the longest x2 2.72 us: per_device(): value_h = head_major(frame_proj[:, 2 * features:], heads)]
    convert_element_type x3, other arithmetic: 1.9 us -> 6.06 us  [per_device(): score_grad = (probability * (prob_grad - row_delta)).astype(jnp.bfloat16)]
  transfers between devices with their start and end apart: 10 -> 11, of which waited for: 7 -> 6; matrix products, arithmetic and copies ran while one was open for 13% -> 34% of each run, Pallas kernels for 0% -> 0%
where the time goes in v4:
time: 221 us; the launch traced here: 220 us
  waiting for transfers between devices  59.2 us (27%)
  matrix products  58.2 us (26%)
  local copies, waits for them, and re-layouts  33.3 us (15%)
  starting transfers between devices  32.7 us (15%)
  other arithmetic  20.7 us (9%)
  between operations  15.9 us (7%)
    all_to_all x2, waiting for transfers between devices, summed_rows(): parts = lax.all_to_all(term, group, 0, 0, tiled=True)  35.5 us
    ppermute x6, starting transfers between devices, shifted(): lax.ppermute(value, axis, [(source, source + steps) for source in range(l...  20.3 us
    ppermute x6, waiting for transfers between devices, shifted(): lax.ppermute(value, axis, [(source, source + steps) for source in range(l...  19.8 us
    dot_general x6, matrix products, per_device(): jnp.einsum('hqk,hqd->hkd', score_grad, query_block, preferred_element_typ...  15.5 us
    all_to_all x2, starting transfers between devices, summed_rows(): parts = lax.all_to_all(term, group, 0, 0, tiled=True)  12.3 us
    unnamed x74, local copies, waits for them, and re-layouts  10.6 us
    dot_general x6, matrix products, per_device(): jnp.einsum('hqd,hkd->hqk', query_block, key_part, preferred_element_type=...  6.88 us
    convert_element_type x3, other arithmetic, per_device(): score_grad = (probability * (prob_grad - row_delta)).astype(jnp.bfloat16)  6.06 us
  transfers between devices with their start and end apart: 11, of which 6 were waited for; matrix products, arithmetic and copies ran while one was open for 34% of the time, Pallas kernels for 0%

profile of v4, /device:TPU:12, one launch (start us, length us, event | category | flops | bytes accessed | tf_op | source)
XLA Modules:
  0.0 220.0 jit_solution(17130411712364401270)
XLA Ops:
  7.2 2.8 %pad_maximum_fusion = bf16[3,512,512]{2,1,0:T(8,128)(2,1)} fusion(bf16[1,512,512]{2,1,0:T(8,128)(2,1)} %bitcast.216, bf16[1,512,512]{2,1,0:T(8,128)(2,1)} %bitcast.217, bf16[1,512,512]{2,1,0:T(8,128)(2,1)} %bitcast.218), kind=kLoop, calls=%fused_computation.33 | loop fusion | flops 1572864 | bytes 3145728 | tf_op jit(solution)/shard_map/stack | solution.py:93
  10.1 2.5 %collective-permute-start.1 = (bf16[384,512]{1,0:T(8,128)(2,1)S(1)}, bf16[384,512]{1,0:T(8,128)(2,1)S(1)}, u32[]{:S(2)}, u32[]{:S(2)}) collective-permute-start(bf16[384,512]{1,0:T(8,128)(2,1)S(1)} %dynamic-slice_bitcast_fusion), channel_id=1, source_target_pairs={{4,0},{8,4},{12,8},{16,12},{20,16},{24,20},{28,24},{5,1},{9,5},{13... | collective-permute-start | bytes 1179656 | tf_op jit(solution)/shard_map/ppermute | solution.py:14
  12.6 4.3 %collective-permute-start = (bf16[384,512]{1,0:T(8,128)(2,1)S(1)}, bf16[384,512]{1,0:T(8,128)(2,1)S(1)}, u32[]{:S(2)}, u32[]{:S(2)}) collective-permute-start(bf16[384,512]{1,0:T(8,128)(2,1)S(1)} %dynamic-slice_bitcast_fusion), channel_id=1, source_target_pairs={{0,4},{4,8},{8,12},{12,16},{16,20},{20,24},{24,28},{1,5},{5,9},{9,... | collective-permute-start | bytes 1179656 | tf_op jit(solution)/shard_map/ppermute | solution.py:14
  17.0 1.9 collective-permute-start.4
  18.9 4.8 %collective-permute-start.3 = (bf16[384,512]{1,0:T(8,128)(2,1)S(1)}, bf16[384,512]{1,0:T(8,128)(2,1)S(1)}, u32[]{:S(2)}, u32[]{:S(2)}) collective-permute-start(bf16[384,512]{1,0:T(8,128)(2,1)S(1)} %bitcast.220), channel_id=1, source_target_pairs={{0,4},{4,8},{8,12},{12,16},{16,20},{20,24},{24,28},{1,5},{5,9},{9,... | collective-permute-start | bytes 1179656 | tf_op jit(solution)/shard_map/ppermute | solution.py:14
  27.7 11.3 %collective-permute-done.1 = bf16[384,512]{1,0:T(8,128)(2,1)S(1)} collective-permute-done((bf16[384,512]{1,0:T(8,128)(2,1)S(1)}, bf16[384,512]{1,0:T(8,128)(2,1)S(1)}, u32[]{:S(2)}, u32[]{:S(2)}) %collective-permute-start.1) | collective-permute-done | bytes 393248 | tf_op jit(solution)/shard_map/ppermute | solution.py:14
  42.2 4.1 %collective-permute-done.4 = bf16[384,512]{1,0:T(8,128)(2,1)S(1)} collective-permute-done((bf16[384,512]{1,0:T(8,128)(2,1)S(1)}, bf16[384,512]{1,0:T(8,128)(2,1)S(1)}, u32[]{:S(2)}, u32[]{:S(2)}) %collective-permute-start.4) | collective-permute-done | bytes 393248 | tf_op jit(solution)/shard_map/ppermute | solution.py:14
  46.5 2.7 %collective-permute-done.3 = bf16[384,512]{1,0:T(8,128)(2,1)S(1)} collective-permute-done((bf16[384,512]{1,0:T(8,128)(2,1)S(1)}, bf16[384,512]{1,0:T(8,128)(2,1)S(1)}, u32[]{:S(2)}, u32[]{:S(2)}) %collective-permute-start.3) | collective-permute-done | bytes 393248 | tf_op jit(solution)/shard_map/ppermute | solution.py:14
  52.4 3.9 %all-gather.2.cloned.1.call-done = bf16[3,1024,512]{2,1,0:T(8,128)(2,1)} async-done(((bf16[3,512,512]{2,1,0:T(8,128)(2,1)}), bf16[3,1024,512]{2,1,0:T(8,128)(2,1)}) %all-gather.2.cloned.1.call-update) | async-done | bytes 3145744 | tf_op jit(solution)/shard_map/all_gather | solution.py:93
  56.2 2.1 slice_bitcast_fusion.2
  58.3 3.8 %convolution_convert_fusion = bf16[1152,1536]{1,0:T(8,128)(2,1)S(1)} fusion(bf16[1024,512]{1,0:T(8,128)(2,1)S(1)} %get-tuple-element.29, bf16[1024,512]{1,0:T(8,128)(2,1)S(1)} %get-tuple-element.30, bf16[1024,512]{1,0:T(8,128)(2,1)S(1)} %get-tuple-element.28, bf16[384,1024]{1,0:T(8,128)(2,1)S(1)} %get-tuple-element.32, bf16[384,1024]{1,0:T(8,128)(2,1)S(1)} %bitcast.202, ...), kind=kOutput, calls=%fused_computation | convolution fusion | flops 3642163200 | bytes 9043968 | tf_op jit(solution)/shard_map/dot_general | solution.py:98
  78.0 2.4 %collective-permute-start.6 = (f32[3,8,384,1]{2,1,3,0:T(8,128)}, f32[3,8,384,1]{2,1,3,0:T(8,128)}, u32[]{:S(2)}, u32[]{:S(2)}) collective-permute-start(f32[3,8,384,1]{2,1,3,0:T(8,128)} %pad_maximum_fusion.4), channel_id=1, source_target_pairs={{4,0},{8,4},{12,8},{16,12},{20,16},{24,20},{28,24},{5,1},{9,5},{13... | collective-permute-start | bytes 110600 | tf_op jit(solution)/shard_map/ppermute | solution.py:14
  80.4 4.3 %collective-permute-start.5 = (f32[3,8,384,1]{2,1,3,0:T(8,128)}, f32[3,8,384,1]{2,1,3,0:T(8,128)}, u32[]{:S(2)}, u32[]{:S(2)}) collective-permute-start(f32[3,8,384,1]{2,1,3,0:T(8,128)} %pad_maximum_fusion.4), channel_id=1, source_target_pairs={{0,4},{4,8},{8,12},{12,16},{16,20},{20,24},{24,28},{1,5},{5,9},{9,... | collective-permute-start | bytes 110600 | tf_op jit(solution)/shard_map/ppermute | solution.py:14
  87.4 2.2 %multiply_convert_fusion = (bf16[8,128,896]{2,1,0:T(8,128)(2,1)S(1)}, bf16[8,128,896]{2,1,0:T(8,128)(2,1)}) fusion(f32[8,128,896]{2,1,0:T(8,128)S(1)} %get-tuple-element.62, f32[8,128]{1,0:T(8,128)S(1)} %get-tuple-element.61, f32[8,128]{1,0:T(8,128)S(1)} %fusion.10, f32[8,128]{1,0:T(8,128)S(1)} %get-tuple-element.59, ...), kind=kLoop, calls=%fused_computation.2 | loop fusion | flops 7340032 | bytes 11023232 | tf_op jit(solution)/shard_map/convert_element_type | solution.py:145
  90.5 2.3 %multiply_convert_fusion.1 = (bf16[8,128,896]{2,1,0:T(8,128)(2,1)S(1)}, bf16[8,128,896]{2,1,0:T(8,128)(2,1)}) fusion(f32[8,128,896]{2,1,0:T(8,128)S(1)} %get-tuple-element.66, f32[8,128]{1,0:T(8,128)S(1)} %get-tuple-element.65, f32[8,128]{1,0:T(8,128)S(1)} %fusion.8, f32[8,128]{1,0:T(8,128)S(1)} %get-tuple-element.63, ...), kind=kLoop, calls=%fused_computation.4 | loop fusion | flops 7340032 | bytes 11023232 | tf_op jit(solution)/shard_map/convert_element_type | solution.py:145
  98.5 2.3 %copy.31 = bf16[1024,512]{1,0:T(8,128)(2,1)} copy(bf16[1024,512]{0,1:T(8,128)(2,1)} %fusion.16) | data formatting | bytes 2097152 | tf_op jit(solution)/shard_map/convert_element_type | solution.py:178
  100.7 5.1 %all-to-all-start = ((bf16[16,64,512]{2,1,0:T(8,128)(2,1)}), bf16[16,64,512]{2,1,0:T(8,128)(2,1)}, u32[]{:S(2)}, u32[]{:S(2)}) async-start(bf16[16,64,512]{2,1,0:T(8,128)(2,1)} %bitcast.199), calls=%async_computation | async-start | bytes 2097152 | tf_op jit(solution)/shard_map/all_to_all | solution.py:57
  105.9 2.5 %convolution_add_fusion.3 = f32[8,384,64]{1,2,0:T(8,128)} fusion(f32[8,384,64]{1,2,0:T(8,128)} %fusion.58, bf16[8,128,896]{2,1,0:T(8,128)(2,1)} %get-tuple-element.22, bf16[8,1152,64]{1,2,0:T(8,128)(2,1)S(1)} %maximum_bitcast_fusion), kind=kOutput, calls=%fused_computation.47 | convolution fusion | flops 50528256 | bytes 2490368 | tf_op jit(solution)/shard_map/hqk,hqd->hkd/dot_general | solution.py:166
  115.3 2.2 %convolution_multiply_fusion.9 = f32[8,128,64]{1,2,0:T(8,128)} fusion(f32[8,128,128]{2,1,0:T(8,128)} %copy-done.19, f32[8,128]{1,0:T(8,128)} %get-tuple-element.39, bf16[8,1152,64]{1,2,0:T(8,128)(2,1)} %bitcast.187, bf16[8,1152,64]{1,2,0:T(8,128)(2,1)S(1)} %maximum_bitcast_fusion, bf16[8,1152,64]{1,2,0:T(8,128)(2,1)S(1)} %bitcast.175), kind=kOutput, calls=%fused_computation.71 | convolution fusion | flops 34013184 | bytes 1183744 | tf_op jit(solution)/shard_map/hqk,hqd->hkd/dot_general | solution.py:214
  120.7 2.6 %convolution_multiply_fusion.7 = f32[8,256,64]{1,2,0:T(8,128)} fusion(f32[8,128,256]{2,1,0:T(8,128)} %copy-done.6, f32[8,128]{1,0:T(8,128)} %get-tuple-element.41, bf16[8,1152,64]{1,2,0:T(8,128)(2,1)} %bitcast.188, bf16[8,1152,64]{1,2,0:T(8,128)(2,1)S(1)} %maximum_bitcast_fusion, bf16[8,1152,64]{1,2,0:T(8,128)(2,1)S(1)} %bitcast.177), kind=kOutput, calls=%fused_computation.68 | convolution fusion | flops 68026368 | bytes 2101248 | tf_op jit(solution)/shard_map/hqk,hqd->hkd/dot_general | solution.py:214
  126.5 2.6 %convolution_multiply_fusion.6 = f32[8,256,64]{1,2,0:T(8,128)} fusion(f32[8,128,256]{2,1,0:T(8,128)} %copy-done.7, f32[8,128]{1,0:T(8,128)S(1)} %get-tuple-element.48, bf16[8,1152,64]{1,2,0:T(8,128)(2,1)} %bitcast.189, bf16[8,1152,64]{1,2,0:T(8,128)(2,1)S(1)} %maximum_bitcast_fusion, bf16[8,1152,64]{1,2,0:T(8,128)(2,1)S(1)} %bitcast.179), kind=kOutput, calls=%fused_computation.67 | convolution fusion | flops 68026368 | bytes 2101248 | tf_op jit(solution)/shard_map/hqk,hqd->hkd/dot_general | solution.py:214
  129.2 2.0 divide_select_fusion.4
  131.1 2.3 %convolution_multiply_fusion.8 = f32[8,128,64]{1,2,0:T(8,128)} fusion(f32[8,128,128]{2,1,0:T(8,128)} %divide_select_fusion.4, f32[8,128]{1,0:T(8,128)S(1)} %get-tuple-element.49, bf16[8,1152,64]{1,2,0:T(8,128)(2,1)} %bitcast.190, bf16[8,1152,64]{1,2,0:T(8,128)(2,1)S(1)} %maximum_bitcast_fusion, bf16[8,1152,64]{1,2,0:T(8,128)(2,1)S(1)} %bitcast.181), kind=kOutput, calls=%fused_computation.70 | convolution fusion | flops 34013184 | bytes 1183744 | tf_op jit(solution)/shard_map/hqk,hqd->hkd/dot_general | solution.py:214
  134.8 2.0 fusion.25
  141.1 2.8 %convolution_multiply_fusion.2 = f32[8,384,64]{1,2,0:T(8,128)} fusion(f32[8,128,384]{2,1,0:T(8,128)} %copy-done.5, f32[8,128]{1,0:T(8,128)S(1)} %get-tuple-element.50, bf16[8,1152,64]{1,2,0:T(8,128)(2,1)S(1)} %bitcast.194, bf16[8,1152,64]{1,2,0:T(8,128)(2,1)S(1)} %maximum_bitcast_fusion, bf16[8,1152,64]{1,2,0:T(8,128)(2,1)S(1)} %bitcast.184), kind=kOutput, calls=%fused_computation.48 | convolution fusion | flops 102039552 | bytes 3018752 | tf_op jit(solution)/shard_map/hqk,hqd->hkd/dot_general | solution.py:214
  143.9 2.9 %convolution_multiply_fusion.3 = f32[8,384,64]{1,2,0:T(8,128)} fusion(f32[8,128,384]{2,1,0:T(8,128)} %copy-done.4, f32[8,128]{1,0:T(8,128)S(1)} %get-tuple-element.40, bf16[8,1152,64]{1,2,0:T(8,128)(2,1)S(1)} %bitcast.195, bf16[8,1152,64]{1,2,0:T(8,128)(2,1)S(1)} %maximum_bitcast_fusion, bf16[8,1152,64]{1,2,0:T(8,128)(2,1)S(1)} %bitcast.185), kind=kOutput, calls=%fused_computation.49 | convolution fusion | flops 102039552 | bytes 3018752 | tf_op jit(solution)/shard_map/hqk,hqd->hkd/dot_general | solution.py:214
  146.8 2.7 %fusion.29 = bf16[8,384,64]{1,2,0:T(8,128)(2,1)S(1)} fusion(f32[8,384,64]{1,2,0:T(8,128)} %convolution_multiply_fusion.2, f32[8,384,64]{1,2,0:T(8,128)} %convolution_multiply_fusion.3, f32[8,384,64]{1,2,0:T(8,128)} %convolution_add_fusion.5, bf16[8,128,896]{2,1,0:T(8,128)(2,1)} %copy-done.9, f32[8,128,64]{1,2,0:T(8,128)} %convolution_multiply_fusion.8, ...), kind=kOutput, calls=%fused_computation.64 | convolution fusion | flops 52101120 | bytes 5242880 | tf_op jit(solution)/shard_map/hqk,hqd->hkd/dot_general | solution.py:158
  151.5 4.1 %copy.32 = bf16[1024,2,512]{2,1,0:T(2,128)(2,1)} copy(bf16[1024,2,512]{0,2,1:T(8,128)(2,1)S(1)} %convert_bitcast_fusion) | data formatting | bytes 4194304 | tf_op jit(solution)/shard_map/convert_element_type | solution.py:241
  155.6 7.2 %all-to-all-start.1 = ((bf16[1024,2,512]{2,1,0:T(2,128)(2,1)}), bf16[1024,2,512]{2,1,0:T(2,128)(2,1)}, u32[]{:S(2)}, u32[]{:S(2)}) async-start(bf16[1024,2,512]{2,1,0:T(2,128)(2,1)} %copy.32), calls=%async_computation.1 | async-start | bytes 4194304 | tf_op jit(solution)/shard_map/all_to_all | solution.py:57
  171.0 2.3 %fusion.55 = bf16[1,384,1024]{2,1,0:T(8,128)(2,1)} fusion(bf16[384,1024]{1,0:T(8,128)(2,1)S(1)} %collective-permute-done.7, bf16[384,1024]{1,0:T(8,128)(2,1)} %add_convert_fusion.1), kind=kLoop, calls=%fused_computation.108 | loop fusion | flops 1572864 | bytes 2359296 | tf_op jit(solution)/shard_map/broadcast_in_dim | solution.py:234
  174.7 35.5 %all-to-all-done.1 = bf16[1024,2,512]{2,1,0:T(2,128)(2,1)} async-done(((bf16[1024,2,512]{2,1,0:T(2,128)(2,1)}), bf16[1024,2,512]{2,1,0:T(2,128)(2,1)}, u32[]{:S(2)}, u32[]{:S(2)}) %all-to-all-start.1) | async-done | bytes 2097184 | tf_op jit(solution)/shard_map/all_to_all | solution.py:57
  210.2 1.9 copy.33
  (156 shorter events, 65.6 us)
Async XLA Ops:
  7.2 49.0 %all-gather.2.cloned.1.call-start = ((), (), s32[]{:S(2)}) async-start(), calls=%async_computation.2 | async-start | bytes 4718592 | tf_op jit(solution)/shard_map/all_gather | solution.py:93
  7.2 2.8 %copy-start.20 = (bf16[1,384,1024]{2,1,0:T(8,128)(2,1)S(1)}, bf16[1,384,1024]{2,1,0:T(8,128)(2,1)}, u32[]{:S(2)}) copy-start(bf16[1,384,1024]{2,1,0:T(8,128)(2,1)} %param.6) | copy-start | bytes 2359300
  10.0 7.0 %copy-start.30 = (bf16[1,384,512]{2,1,0:T(8,128)(2,1)S(1)}, bf16[1,384,512]{2,1,0:T(8,128)(2,1)}, u32[]{:S(2)}) copy-start(bf16[1,384,512]{2,1,0:T(8,128)(2,1)} %param.11) | copy-start | bytes 1179652
  10.0 14.0 %copy-start.31 = (s32[24,7]{0,1:T(8,128)S(1)}, s32[24,7]{0,1:T(8,128)}, u32[]{:S(2)}) copy-start(s32[24,7]{0,1:T(8,128)} %param.10) | copy-start | bytes 2020
  10.1 28.9 %collective-permute-start.1 = (bf16[384,512]{1,0:T(8,128)(2,1)S(1)}, bf16[384,512]{1,0:T(8,128)(2,1)S(1)}, u32[]{:S(2)}, u32[]{:S(2)}) collective-permute-start(bf16[384,512]{1,0:T(8,128)(2,1)S(1)} %dynamic-slice_bitcast_fusion), channel_id=1, source_target_pairs={{4,0},{8,4},{12,8},{16,12},{20,16},{24,20},{28,24},{5,1},{9,5},{13... | collective-permute-start | bytes 1179656 | tf_op jit(solution)/shard_map/ppermute | solution.py:14
  12.6 28.2 %collective-permute-start = (bf16[384,512]{1,0:T(8,128)(2,1)S(1)}, bf16[384,512]{1,0:T(8,128)(2,1)S(1)}, u32[]{:S(2)}, u32[]{:S(2)}) collective-permute-start(bf16[384,512]{1,0:T(8,128)(2,1)S(1)} %dynamic-slice_bitcast_fusion), channel_id=1, source_target_pairs={{0,4},{4,8},{8,12},{12,16},{16,20},{20,24},{24,28},{1,5},{5,9},{9,... | collective-permute-start | bytes 1179656 | tf_op jit(solution)/shard_map/ppermute | solution.py:14
  17.0 29.3 %collective-permute-start.4 = (bf16[384,512]{1,0:T(8,128)(2,1)S(1)}, bf16[384,512]{1,0:T(8,128)(2,1)S(1)}, u32[]{:S(2)}, u32[]{:S(2)}) collective-permute-start(bf16[384,512]{1,0:T(8,128)(2,1)S(1)} %bitcast.219), channel_id=1, source_target_pairs={{4,0},{8,4},{12,8},{16,12},{20,16},{24,20},{28,24},{5,1},{9,5},{13... | collective-permute-start | bytes 1179656 | tf_op jit(solution)/shard_map/ppermute | solution.py:14
  18.9 30.2 %collective-permute-start.3 = (bf16[384,512]{1,0:T(8,128)(2,1)S(1)}, bf16[384,512]{1,0:T(8,128)(2,1)S(1)}, u32[]{:S(2)}, u32[]{:S(2)}) collective-permute-start(bf16[384,512]{1,0:T(8,128)(2,1)S(1)} %bitcast.220), channel_id=1, source_target_pairs={{0,4},{4,8},{8,12},{12,16},{16,20},{20,24},{24,28},{1,5},{5,9},{9,... | collective-permute-start | bytes 1179656 | tf_op jit(solution)/shard_map/ppermute | solution.py:14
  40.8 1.4 copy-start.25
  41.8 7.7 %collective-permute-start.2 = (bf16[2,384,512]{2,1,0:T(8,128)(2,1)}, bf16[2,384,512]{2,1,0:T(8,128)(2,1)}, u32[]{:S(2)}, u32[]{:S(2)}) collective-permute-start(bf16[2,384,512]{2,1,0:T(8,128)(2,1)} %pad_maximum_fusion.1), channel_id=1, source_target_pairs={{0,1},{1,0},{2,3},{3,2},{4,5},{5,4},{6,7},{7,6},{8,9},{9,8},{10,11... | collective-permute-start | bytes 2359304 | tf_op jit(solution)/shard_map/ppermute | solution.py:42
  78.0 30.4 %collective-permute-start.6 = (f32[3,8,384,1]{2,1,3,0:T(8,128)}, f32[3,8,384,1]{2,1,3,0:T(8,128)}, u32[]{:S(2)}, u32[]{:S(2)}) collective-permute-start(f32[3,8,384,1]{2,1,3,0:T(8,128)} %pad_maximum_fusion.4), channel_id=1, source_target_pairs={{4,0},{8,4},{12,8},{16,12},{20,16},{24,20},{28,24},{5,1},{9,5},{13... | collective-permute-start | bytes 110600 | tf_op jit(solution)/shard_map/ppermute | solution.py:14
  80.4 29.9 %collective-permute-start.5 = (f32[3,8,384,1]{2,1,3,0:T(8,128)}, f32[3,8,384,1]{2,1,3,0:T(8,128)}, u32[]{:S(2)}, u32[]{:S(2)}) collective-permute-start(f32[3,8,384,1]{2,1,3,0:T(8,128)} %pad_maximum_fusion.4), channel_id=1, source_target_pairs={{0,4},{4,8},{8,12},{12,16},{16,20},{20,24},{24,28},{1,5},{5,9},{9,... | collective-permute-start | bytes 110600 | tf_op jit(solution)/shard_map/ppermute | solution.py:14
  86.3 8.5 %copy-start.10 = (bf16[8,128,896]{2,1,0:T(8,128)(2,1)}, bf16[8,128,896]{2,1,0:T(8,128)(2,1)S(1)}, u32[]{:S(2)}) copy-start(bf16[8,128,896]{2,1,0:T(8,128)(2,1)S(1)} %get-tuple-element.20) | copy-start | bytes 5505028
  89.7 3.1 %copy-start.9 = (bf16[8,128,896]{2,1,0:T(8,128)(2,1)}, bf16[8,128,896]{2,1,0:T(8,128)(2,1)S(1)}, u32[]{:S(2)}) copy-start(bf16[8,128,896]{2,1,0:T(8,128)(2,1)S(1)} %get-tuple-element.23) | copy-start | bytes 5505028
  94.8 2.0 copy-start.21
  100.7 54.9 %all-to-all-start = ((bf16[16,64,512]{2,1,0:T(8,128)(2,1)}), bf16[16,64,512]{2,1,0:T(8,128)(2,1)}, u32[]{:S(2)}, u32[]{:S(2)}) async-start(bf16[16,64,512]{2,1,0:T(8,128)(2,1)} %bitcast.199), calls=%async_computation | async-start | bytes 2097152 | tf_op jit(solution)/shard_map/all_to_all | solution.py:57
  129.2 4.2 %copy-start.34 = (f32[8,128]{1,0:T(8,128)S(1)}, f32[8,128]{1,0:T(8,128)}, u32[]{:S(2)}) copy-start(f32[8,128]{1,0:T(8,128)} %get-tuple-element.46) | copy-start | bytes 12292
  133.4 1.4 copy-start.15
  133.4 1.4 copy-start.17
  133.4 1.4 copy-start.29
  134.8 2.3 %copy-start.4 = (f32[8,128,384]{2,1,0:T(8,128)}, f32[8,128,384]{2,1,0:T(8,128)S(1)}, u32[]{:S(2)}) copy-start(f32[8,128,384]{2,1,0:T(8,128)S(1)} %divide_select_fusion.1) | copy-start | bytes 4718596
  139.1 2.0 copy-start.2
  146.8 3.5 %copy-start.22 = (bf16[1,384,1024]{2,1,0:T(8,128)(2,1)S(1)}, bf16[1,384,1024]{2,1,0:T(8,128)(2,1)}, u32[]{:S(2)}) copy-start(bf16[1,384,1024]{2,1,0:T(8,128)(2,1)} %param.6) | copy-start | bytes 2359300
  146.8 3.5 %copy-start.27 = (bf16[8,384,64]{1,2,0:T(8,128)(2,1)S(1)}, bf16[8,384,64]{1,2,0:T(8,128)(2,1)}, u32[]{:S(2)}) copy-start(bf16[8,384,64]{1,2,0:T(8,128)(2,1)} %fusion.28) | copy-start | bytes 1179652
  155.6 7.2 %copy-start = (bf16[3,1024,512]{2,1,0:T(8,128)(2,1)S(1)}, bf16[3,1024,512]{2,1,0:T(8,128)(2,1)}, u32[]{:S(2)}) copy-start(bf16[3,1024,512]{2,1,0:T(8,128)(2,1)} %all-gather.2.cloned.1.call-done) | copy-start | bytes 9437188
  155.6 7.2 %copy-start.14 = (bf16[8,384,64]{1,2,0:T(8,128)(2,1)S(1)}, bf16[8,384,64]{1,2,0:T(8,128)(2,1)}, u32[]{:S(2)}) copy-start(bf16[8,384,64]{1,2,0:T(8,128)(2,1)} %copy-done.13) | copy-start | bytes 1179652
  155.6 54.6 %all-to-all-start.1 = ((bf16[1024,2,512]{2,1,0:T(2,128)(2,1)}), bf16[1024,2,512]{2,1,0:T(2,128)(2,1)}, u32[]{:S(2)}, u32[]{:S(2)}) async-start(bf16[1024,2,512]{2,1,0:T(2,128)(2,1)} %copy.32), calls=%async_computation.1 | async-start | bytes 4194304 | tf_op jit(solution)/shard_map/all_to_all | solution.py:57
  164.5 1.6 copy-start.3
  164.5 2.1 copy-start.12
  166.1 1.6 copy-start.8
  166.1 4.9 %collective-permute-start.7 = (bf16[384,1024]{1,0:T(8,128)(2,1)}, bf16[384,1024]{1,0:T(8,128)(2,1)S(1)}, u32[]{:S(2)}, u32[]{:S(2)}) collective-permute-start(bf16[384,1024]{1,0:T(8,128)(2,1)} %add_convert_fusion.1), channel_id=1, source_target_pairs={{0,1},{1,0},{2,3},{3,2},{4,5},{5,4},{6,7},{7,6},{8,9},{9,8},{10,11... | collective-permute-start | bytes 2359304 | tf_op jit(solution)/shard_map/ppermute | solution.py:67
  167.7 1.5 copy-start.11
  (15 other events, 15.6 us)
Sparse Core Ops, SparseCore 0:
  10.1 46.0 all-gather.1

commit v5 on v4

--- a/solution.py
+++ b/solution.py
@@ -115,14 +115,8 @@
         return jnp.repeat(picked, BLOCK)[None, None, :]
 
     own_low, own_high = REACH, REACH + blocks - 1
-    key_own = jnp.zeros((heads, length, HD), jnp.float32)
-    value_own = jnp.zeros((heads, length, HD), jnp.float32)
-
-    def add_own(acc, part, low, high):
-        spread = ((0, 0), ((low - own_low) * BLOCK, (own_high - high) * BLOCK), (0, 0))
-        return acc + jnp.pad(part, spread)
-
     outs, query_grads, tops, totals, deltas = [], [], [], [], []
+    own_score_grads, own_weights = [], []
     for i in range(blocks):
         at = REACH + i
         query_block = rows(query_h, at)
@@ -150,25 +144,9 @@
         tops.append(row_top)
         totals.append(row_total)
         deltas.append(row_delta)
-        low, high = max(own_low, i), min(own_high, i + 2 * REACH)
-        cut = slice((low - i) * BLOCK, (high - i + 1) * BLOCK)
-        key_own = add_own(
-            key_own,
-            score_scale
-            * jnp.einsum(
-                "hqk,hqd->hkd", score_grad[:, :, cut], query_block, preferred_element_type=jnp.float32
-            ),
-            low,
-            high,
-        )
-        value_own = add_own(
-            value_own,
-            jnp.einsum(
-                "hqk,hqd->hkd", weights[:, :, cut], upstream_block, preferred_element_type=jnp.float32
-            ),
-            low,
-            high,
-        )
+        cut = slice((own_low - i) * BLOCK, (own_high - i + 1) * BLOCK)
+        own_score_grads.append(score_grad[:, :, cut])
+        own_weights.append(weights[:, :, cut])
 
     attended = token_major(jnp.concatenate(outs, axis=1).astype(jnp.bfloat16))[None]
     query_grad = token_major(jnp.concatenate(query_grads, axis=1).astype(jnp.bfloat16))
@@ -184,43 +162,43 @@
     stats_left = shifted(stats[:, :, length - halo :], "ctx", 1)
     stats_right = shifted(stats[:, :, :halo], "ctx", -1)
 
-    for at in list(range(REACH)) + list(range(REACH + blocks, frame_blocks)):
-        low, high = max(own_low, at - REACH), min(own_high, at + REACH)
-        if low > high:
-            continue
-        if at < REACH:
-            top, total, delta = (part[:, at * BLOCK : (at + 1) * BLOCK] for part in stats_left)
-        else:
-            place = at - REACH - blocks
-            top, total, delta = (part[:, place * BLOCK : (place + 1) * BLOCK] for part in stats_right)
-        query_block = rows(query_h, at)
-        upstream_block = rows(upstream_h, at)
-        key_part = rows(key_h, low, high - low + 1)
-        value_part = rows(value_h, low, high - low + 1)
-        seen = seen_keys(at, low, high)
-        scores = (
-            jnp.einsum("hqd,hkd->hqk", query_block, key_part, preferred_element_type=jnp.float32)
-            * score_scale
-        )
-        probability = jnp.where(seen, jnp.exp(scores - top) / total, 0.0)
-        weights = probability.astype(jnp.bfloat16)
-        prob_grad = jnp.einsum(
-            "hqd,hkd->hqk", upstream_block, value_part, preferred_element_type=jnp.float32
-        )
-        score_grad = (probability * (prob_grad - delta)).astype(jnp.bfloat16)
-        key_own = add_own(
-            key_own,
-            score_scale
-            * jnp.einsum("hqk,hqd->hkd", score_grad, query_block, preferred_element_type=jnp.float32),
-            low,
-            high,
-        )
-        value_own = add_own(
-            value_own,
-            jnp.einsum("hqk,hqd->hkd", weights, upstream_block, preferred_element_type=jnp.float32),
-            low,
-            high,
-        )
+    near = list(range(REACH)) + list(range(REACH + blocks, frame_blocks))
+    allowed = []
+    for at in near:
+        row = []
+        for block in range(own_low, own_high + 1):
+            slot = block - at + REACH
+            row.append(frame_mask[at, slot] > 0 if 0 <= slot < span_len else jnp.zeros((), bool))
+        allowed.append(jnp.stack(row))
+    allowed = jnp.repeat(jnp.repeat(jnp.stack(allowed), BLOCK, axis=0), BLOCK, axis=1)[None]
+    near_stats = jnp.concatenate([stats_left, stats_right], axis=2)
+    top, total, delta = near_stats[0], near_stats[1], near_stats[2]
+    near_query = jnp.concatenate([rows(query_h, 0, REACH), rows(query_h, REACH + blocks, REACH)], axis=1)
+    near_upstream = jnp.concatenate(
+        [rows(upstream_h, 0, REACH), rows(upstream_h, REACH + blocks, REACH)], axis=1
+    )
+    key_part = rows(key_h, own_low, blocks)
+    value_part = rows(value_h, own_low, blocks)
+    scores = (
+        jnp.einsum("hqd,hkd->hqk", near_query, key_part, preferred_element_type=jnp.float32)
+        * score_scale
+    )
+    probability = jnp.where(allowed, jnp.exp(scores - top) / total, 0.0)
+    weights = probability.astype(jnp.bfloat16)
+    prob_grad = jnp.einsum(
+        "hqd,hkd->hqk", near_upstream, value_part, preferred_element_type=jnp.float32
+    )
+    score_grad = (probability * (prob_grad - delta)).astype(jnp.bfloat16)
+    all_score_grads = jnp.concatenate(own_score_grads + [score_grad], axis=1)
+    all_weights = jnp.concatenate(own_weights + [weights], axis=1)
+    all_queries = jnp.concatenate([rows(query_h, REACH, blocks), near_query], axis=1)
+    all_upstream = jnp.concatenate([rows(upstream_h, REACH, blocks), near_upstream], axis=1)
+    key_own = score_scale * jnp.einsum(
+        "hqk,hqd->hkd", all_score_grads, all_queries, preferred_element_type=jnp.float32
+    )
+    value_own = jnp.einsum(
+        "hqk,hqd->hkd", all_weights, all_upstream, preferred_element_type=jnp.float32
+    )
 
     key_grad = token_major(key_own).astype(jnp.bfloat16)
     value_grad = token_major(value_own).astype(jnp.bfloat16)

time: 221 us -> 194 us (0.88)
  matrix products: 58.2 us -> 37 us
  between operations: 15.9 us -> 22.5 us
  waiting for transfers between devices: 59.2 us -> 55.3 us
  other arithmetic: 20.7 us -> 16.9 us
  local copies, waits for them, and re-layouts: 33.3 us -> 30.1 us
    dot_general x24 -> x4, matrix products: 36.7 us -> 11.1 us  [the longest x1 4.68 us: per_device(): jnp.einsum('hqd,hkd->hqk', near_query, key_part, preferred_element_type=j...]
    unnamed x74 -> x67, local copies, waits for them, and re-layouts: 10.6 us -> 2.99 us
    slice x1 -> x9, local copies, waits for them, and re-layouts: 0.58 us -> 7.98 us  [the longest x3 2.97 us: per_device(): own_weights.append(weights[:, :, cut])]
    ppermute x6, waiting for transfers between devices: 19.8 us -> 13.5 us  [shifted(): lax.ppermute(value, axis, [(source, source + steps) for source in range(l...]
    all_to_all x2, waiting for transfers between devices: 35.5 us -> 39.5 us  [summed_rows(): parts = lax.all_to_all(term, group, 0, 0, tiled=True)]
    dot_general x3, matrix products: 4.62 us -> 7.58 us  [per_device(): jnp.einsum('hqd,hkd->hqk', upstream_block, value_window, preferred_elemen...]
    convert_element_type x1, local copies, waits for them, and re-layouts: 4.09 us -> 6.32 us  [per_device(): term_kv = jnp.einsum('tr,tcf->rcf', tokens, jnp.stack([key_grad, value_gr...]
  transfers between devices with their start and end apart: 11 -> 11, of which waited for: 6 -> 7; matrix products, arithmetic and copies ran while one was open for 34% -> 25% of each run, Pallas kernels for 0% -> 0%
where the time goes in v5:
time: 194 us; the launch traced here: 193 us
  waiting for transfers between devices  55.3 us (29%)
  matrix products  37 us (19%)
  starting transfers between devices  30.8 us (16%)
  local copies, waits for them, and re-layouts  30.1 us (16%)
  between operations  22.5 us (12%)
  other arithmetic  16.9 us (9%)
    all_to_all x2, waiting for transfers between devices, summed_rows(): parts = lax.all_to_all(term, group, 0, 0, tiled=True)  39.5 us
    ppermute x6, starting transfers between devices, shifted(): lax.ppermute(value, axis, [(source, source + steps) for source in range(l...  19.7 us
    ppermute x6, waiting for transfers between devices, shifted(): lax.ppermute(value, axis, [(source, source + steps) for source in range(l...  13.5 us
    all_to_all x2, starting transfers between devices, summed_rows(): parts = lax.all_to_all(term, group, 0, 0, tiled=True)  11 us
    dot_general x3, matrix products, per_device(): jnp.einsum('hqd,hkd->hqk', upstream_block, value_window, preferred_elemen...  7.58 us
    convert_element_type x1, local copies, waits for them, and re-layouts, per_device(): term_kv = jnp.einsum('tr,tcf->rcf', tokens, jnp.stack([key_grad, value_gr...  6.32 us
    dot_general x1, matrix products, per_device(): jnp.einsum('hqd,hkd->hqk', near_query, key_part, preferred_element_type=j...  4.68 us
    convert_element_type x3, other arithmetic, per_device(): score_grad = (probability * (prob_grad - row_delta)).astype(jnp.bfloat16)  3.96 us
  transfers between devices with their start and end apart: 11, of which 7 were waited for; matrix products, arithmetic and copies ran while one was open for 25% of the time, Pallas kernels for 0%

profile of v5, /device:TPU:12, one launch (start us, length us, event | category | flops | bytes accessed | tf_op | source)
XLA Modules:
  0.0 192.6 jit_solution(8300541867180203147)
XLA Ops:
  7.2 2.8 %pad_maximum_fusion = bf16[3,512,512]{2,1,0:T(8,128)(2,1)} fusion(bf16[1,512,512]{2,1,0:T(8,128)(2,1)} %bitcast.168, bf16[1,512,512]{2,1,0:T(8,128)(2,1)} %bitcast.169, bf16[1,512,512]{2,1,0:T(8,128)(2,1)} %bitcast.170), kind=kLoop, calls=%fused_computation.51 | loop fusion | flops 1572864 | bytes 3145728 | tf_op jit(solution)/shard_map/stack | solution.py:93
  10.1 2.4 %collective-permute-start.1 = (bf16[384,512]{1,0:T(8,128)(2,1)S(1)}, bf16[384,512]{1,0:T(8,128)(2,1)S(1)}, u32[]{:S(2)}, u32[]{:S(2)}) collective-permute-start(bf16[384,512]{1,0:T(8,128)(2,1)S(1)} %dynamic-slice_bitcast_fusion), channel_id=1, source_target_pairs={{4,0},{8,4},{12,8},{16,12},{20,16},{24,20},{28,24},{5,1},{9,5},{13... | collective-permute-start | bytes 1179656 | tf_op jit(solution)/shard_map/ppermute | solution.py:14
  12.5 4.3 %collective-permute-start = (bf16[384,512]{1,0:T(8,128)(2,1)S(1)}, bf16[384,512]{1,0:T(8,128)(2,1)S(1)}, u32[]{:S(2)}, u32[]{:S(2)}) collective-permute-start(bf16[384,512]{1,0:T(8,128)(2,1)S(1)} %dynamic-slice_bitcast_fusion), channel_id=1, source_target_pairs={{0,4},{4,8},{8,12},{12,16},{16,20},{20,24},{24,28},{1,5},{5,9},{9,... | collective-permute-start | bytes 1179656 | tf_op jit(solution)/shard_map/ppermute | solution.py:14
  16.9 1.9 collective-permute-start.4
  18.8 4.8 %collective-permute-start.3 = (bf16[384,512]{1,0:T(8,128)(2,1)S(1)}, bf16[384,512]{1,0:T(8,128)(2,1)}, u32[]{:S(2)}, u32[]{:S(2)}) collective-permute-start(bf16[384,512]{1,0:T(8,128)(2,1)S(1)} %bitcast.172), channel_id=1, source_target_pairs={{0,4},{4,8},{8,12},{12,16},{16,20},{20,24},{24,28},{1,5},{5,9},{9,... | collective-permute-start | bytes 1179656 | tf_op jit(solution)/shard_map/ppermute | solution.py:14
  32.7 6.1 %collective-permute-done.1 = bf16[384,512]{1,0:T(8,128)(2,1)S(1)} collective-permute-done((bf16[384,512]{1,0:T(8,128)(2,1)S(1)}, bf16[384,512]{1,0:T(8,128)(2,1)S(1)}, u32[]{:S(2)}, u32[]{:S(2)}) %collective-permute-start.1) | collective-permute-done | bytes 393248 | tf_op jit(solution)/shard_map/ppermute | solution.py:14
  38.9 1.8 collective-permute-done
  42.5 3.7 %collective-permute-done.4 = bf16[384,512]{1,0:T(8,128)(2,1)} collective-permute-done((bf16[384,512]{1,0:T(8,128)(2,1)S(1)}, bf16[384,512]{1,0:T(8,128)(2,1)}, u32[]{:S(2)}, u32[]{:S(2)}) %collective-permute-start.4) | collective-permute-done | bytes 393248 | tf_op jit(solution)/shard_map/ppermute | solution.py:14
  47.4 1.8 collective-permute-done.3
  51.9 1.9 maximum_select_fusion
  53.9 2.3 %all-gather.2.cloned.1.call-done = bf16[3,1024,512]{2,1,0:T(8,128)(2,1)} async-done(((bf16[3,512,512]{2,1,0:T(8,128)(2,1)}), bf16[3,1024,512]{2,1,0:T(8,128)(2,1)}) %all-gather.2.cloned.1.call-update) | async-done | bytes 3145744 | tf_op jit(solution)/shard_map/all_gather | solution.py:93
  56.3 2.1 %slice_bitcast_fusion.2 = (bf16[1024,512]{1,0:T(8,128)(2,1)S(1)}, bf16[1024,512]{1,0:T(8,128)(2,1)S(1)}, bf16[1024,512]{1,0:T(8,128)(2,1)S(1)}) fusion(bf16[3,1024,512]{2,1,0:T(8,128)(2,1)} %all-gather.2.cloned.1.call-done), kind=kLoop, calls=%fused_computation.81 | loop fusion | bytes 6291456 | tf_op jit(solution)/shard_map/squeeze | solution.py:94
  58.3 3.8 %convolution_convert_fusion = bf16[1152,1536]{1,0:T(8,128)(2,1)S(1)} fusion(bf16[1024,512]{1,0:T(8,128)(2,1)S(1)} %get-tuple-element.25, bf16[1024,512]{1,0:T(8,128)(2,1)S(1)} %get-tuple-element.26, bf16[1024,512]{1,0:T(8,128)(2,1)S(1)} %get-tuple-element.24, bf16[384,1024]{1,0:T(8,128)(2,1)S(1)} %get-tuple-element.28, bf16[384,1024]{1,0:T(8,128)(2,1)S(1)} %bitcast.157, ...), kind=kOutput, calls=%fused_computation.2 | convolution fusion | flops 3642163200 | bytes 9043968 | tf_op jit(solution)/shard_map/dot_general | solution.py:98
  62.5 1.6 copy.29
  67.2 2.5 %multiply_reduce_fusion = (f32[8,128]{1,0:T(8,128)S(1)}, f32[8,128,896]{2,1,0:T(8,128)S(1)}) fusion(f32[8,128]{1,0:T(8,128)S(1)} %fusion.26, f32[8,128]{1,0:T(8,128)S(1)} %get-tuple-element.50, f32[8,128,896]{2,1,0:T(8,128)S(1)} %get-tuple-element.51, pred[896]{0:T(1024)(128)(4,1)S(1)} %get-tuple-element.64, bf16[8,1152,64]{1,2,0:T(8,128)(2,1)S(1)} %bitcast.151, ...), kind=kOutput, calls=%fused_computation.21 | convolution fusion | flops 122944512 | bytes 8401920 | tf_op jit(solution)/shard_map/hqd,hkd->hqk/dot_general | solution.py:135
  74.4 2.5 %multiply_reduce_fusion.2 = (f32[8,128]{1,0:T(8,128)S(1)}, f32[8,128,896]{2,1,0:T(8,128)S(1)}) fusion(f32[8,128]{1,0:T(8,128)S(1)} %fusion.22, f32[8,128]{1,0:T(8,128)S(1)} %get-tuple-element.58, f32[8,128,896]{2,1,0:T(8,128)S(1)} %get-tuple-element.59, pred[896]{0:T(1024)(128)(4,1)S(1)} %broadcast_bitcast_fusion.3, bf16[8,1152,64]{1,2,0:T(8,128)(2,1)S(1)} %bitcast.152, ...), kind=kOutput, calls=%fused_computation.25 | convolution fusion | flops 122944512 | bytes 8401920 | tf_op jit(solution)/shard_map/hqd,hkd->hqk/dot_general | solution.py:135
  80.0 2.5 %multiply_reduce_fusion.1 = (f32[8,128]{1,0:T(8,128)S(1)}, f32[8,128,896]{2,1,0:T(8,128)S(1)}) fusion(f32[8,128]{1,0:T(8,128)S(1)} %fusion.24, f32[8,128]{1,0:T(8,128)S(1)} %get-tuple-element.54, f32[8,128,896]{2,1,0:T(8,128)S(1)} %get-tuple-element.55, pred[896]{0:T(1024)(128)(4,1)S(1)} %get-tuple-element.65, bf16[8,1152,64]{1,2,0:T(8,128)(2,1)S(1)} %bitcast.153, ...), kind=kOutput, calls=%fused_computation.23 | convolution fusion | flops 122944512 | bytes 8401920 | tf_op jit(solution)/shard_map/hqd,hkd->hqk/dot_general | solution.py:135
  84.0 3.5 %collective-permute-start.5 = (f32[3,8,384,1]{2,1,3,0:T(8,128)S(1)}, f32[3,8,384,1]{2,1,3,0:T(8,128)S(1)}, u32[]{:S(2)}, u32[]{:S(2)}) collective-permute-start(f32[3,8,384,1]{2,1,3,0:T(8,128)S(1)} %pad_maximum_fusion.4), channel_id=1, source_target_pairs={{0,4},{4,8},{8,12},{12,16},{16,20},{20,24},{24,28},{1,5},{5,9},{9,... | collective-permute-start | bytes 110600 | tf_op jit(solution)/shard_map/ppermute | solution.py:14
  92.0 2.6 %collective-permute-start.6 = (f32[3,8,384,1]{2,1,3,0:T(8,128)S(1)}, f32[3,8,384,1]{2,1,3,0:T(8,128)S(1)}, u32[]{:S(2)}, u32[]{:S(2)}) collective-permute-start(f32[3,8,384,1]{2,1,3,0:T(8,128)S(1)} %pad_maximum_fusion.4), channel_id=1, source_target_pairs={{4,0},{8,4},{12,8},{16,12},{20,16},{24,20},{28,24},{5,1},{9,5},{13... | collective-permute-start | bytes 110600 | tf_op jit(solution)/shard_map/ppermute | solution.py:14
  99.9 6.1 %all-to-all-start = ((bf16[16,64,512]{2,1,0:T(8,128)(2,1)}), bf16[16,64,512]{2,1,0:T(8,128)(2,1)}, u32[]{:S(2)}, u32[]{:S(2)}) async-start(bf16[16,64,512]{2,1,0:T(8,128)(2,1)} %bitcast.74), calls=%async_computation | async-start | bytes 2097152 | tf_op jit(solution)/shard_map/all_to_all | solution.py:57
  106.1 4.7 %fusion.114 = (bf16[8,768,384]{2,1,0:T(8,128)(2,1)S(1)}, f32[8,768,384]{2,1,0:T(8,128)S(1)}) fusion(f32[8,768]{1,0:T(8,128)S(1)} %get-tuple-element.36, f32[8,768]{1,0:T(8,128)S(1)} %get-tuple-element.37, bf16[8,1152,64]{1,2,0:T(8,128)(2,1)S(1)} %bitcast.142, bf16[8,384,64]{1,2,0:T(8,128)(2,1)S(1)} %copy-done.24, ...), kind=kOutput, calls=%fused_computation.170 | convolution fusion | flops 315359232 | bytes 15679488 | tf_op jit(solution)/shard_map/hqd,hkd->hqk/dot_general | solution.py:183
  110.9 3.2 %multiply_convert_fusion = bf16[8,768,384]{2,1,0:T(8,128)(2,1)S(1)} fusion(f32[8,768,384]{2,1,0:T(8,128)S(1)} %get-tuple-element.63, f32[8,768]{1,0:T(8,128)S(1)} %get-tuple-element.35, bf16[8,384,64]{1,2,0:T(8,128)(2,1)S(1)} %copy-done.15, bf16[8,384,64]{1,2,0:T(8,128)(2,1)S(1)} %copy-done.16, bf16[8,1152,64]{1,2,0:T(8,128)(2,1)} %bitcast.150), kind=kOutput, calls=%fused_computation | convolution fusion | flops 310640640 | bytes 15360000 | tf_op jit(solution)/shard_map/hqd,hkd->hqk/dot_general | solution.py:188
  114.1 1.6 fusion.39
  115.8 1.6 fusion.36
  118.2 2.6 %convert_bitcast_fusion = bf16[1024,2,512]{0,2,1:T(8,128)(2,1)} fusion(bf16[384,1,512]{0,2,1:T(8,128)(2,1)S(1)} %bitcast.175, bf16[384,1,512]{0,2,1:T(8,128)(2,1)S(1)} %bitcast.173, bf16[1,384,1024]{2,1,0:T(8,128)(2,1)S(1)} %copy-done.14), kind=kOutput, calls=%fused_computation.48 | convolution fusion | flops 806748160 | bytes 3670016 | tf_op jit(solution)/shard_map/tr,tcf->rcf/dot_general | solution.py:214
  120.8 6.3 %copy.36 = bf16[1024,2,512]{2,1,0:T(2,128)(2,1)} copy(bf16[1024,2,512]{0,2,1:T(8,128)(2,1)} %convert_bitcast_fusion) | data formatting | bytes 4194304 | tf_op jit(solution)/shard_map/convert_element_type | solution.py:219
  127.1 3.8 %all-to-all-done = bf16[16,64,512]{2,1,0:T(8,128)(2,1)} async-done(((bf16[16,64,512]{2,1,0:T(8,128)(2,1)}), bf16[16,64,512]{2,1,0:T(8,128)(2,1)}, u32[]{:S(2)}, u32[]{:S(2)}) %all-to-all-start) | async-done | bytes 1048608 | tf_op jit(solution)/shard_map/all_to_all | solution.py:57
  130.9 5.0 %all-to-all-start.1 = ((bf16[1024,2,512]{2,1,0:T(2,128)(2,1)}), bf16[1024,2,512]{2,1,0:T(2,128)(2,1)}, u32[]{:S(2)}, u32[]{:S(2)}) async-start(bf16[1024,2,512]{2,1,0:T(2,128)(2,1)} %copy.36), calls=%async_computation.1 | async-start | bytes 4194304 | tf_op jit(solution)/shard_map/all_to_all | solution.py:57
  136.5 1.8 fusion.106
  143.3 2.3 %fusion.73 = bf16[1,384,1024]{2,1,0:T(8,128)(2,1)} fusion(bf16[384,1024]{1,0:T(8,128)(2,1)S(1)} %collective-permute-done.7, bf16[384,1024]{1,0:T(8,128)(2,1)} %add_convert_fusion.1), kind=kLoop, calls=%fused_computation.100 | loop fusion | flops 1572864 | bytes 2359296 | tf_op jit(solution)/shard_map/broadcast_in_dim | solution.py:212
  147.0 35.8 %all-to-all-done.1 = bf16[1024,2,512]{2,1,0:T(2,128)(2,1)} async-done(((bf16[1024,2,512]{2,1,0:T(2,128)(2,1)}), bf16[1024,2,512]{2,1,0:T(2,128)(2,1)}, u32[]{:S(2)}, u32[]{:S(2)}) %all-to-all-start.1) | async-done | bytes 2097184 | tf_op jit(solution)/shard_map/all_to_all | solution.py:57
  182.8 1.9 copy.37
  (134 shorter events, 38.4 us)
Async XLA Ops:
  7.2 2.9 %copy-start.12 = (bf16[1,384,1024]{2,1,0:T(8,128)(2,1)S(1)}, bf16[1,384,1024]{2,1,0:T(8,128)(2,1)}, u32[]{:S(2)}) copy-start(bf16[1,384,1024]{2,1,0:T(8,128)(2,1)} %param.6) | copy-start | bytes 2359300
  7.2 9.7 %copy-start.26 = (bf16[1,384,512]{2,1,0:T(8,128)(2,1)S(1)}, bf16[1,384,512]{2,1,0:T(8,128)(2,1)}, u32[]{:S(2)}) copy-start(bf16[1,384,512]{2,1,0:T(8,128)(2,1)} %param.11) | copy-start | bytes 1179652
  7.2 16.5 %copy-start.30 = (s32[24,7]{0,1:T(8,128)S(1)}, s32[24,7]{0,1:T(8,128)}, u32[]{:S(2)}) copy-start(s32[24,7]{0,1:T(8,128)} %param.10) | copy-start | bytes 2020
  7.2 49.1 %all-gather.2.cloned.1.call-start = ((), (), s32[]{:S(2)}) async-start(), calls=%async_computation.2 | async-start | bytes 4718592 | tf_op jit(solution)/shard_map/all_gather | solution.py:93
  10.1 28.8 %collective-permute-start.1 = (bf16[384,512]{1,0:T(8,128)(2,1)S(1)}, bf16[384,512]{1,0:T(8,128)(2,1)S(1)}, u32[]{:S(2)}, u32[]{:S(2)}) collective-permute-start(bf16[384,512]{1,0:T(8,128)(2,1)S(1)} %dynamic-slice_bitcast_fusion), channel_id=1, source_target_pairs={{4,0},{8,4},{12,8},{16,12},{20,16},{24,20},{28,24},{5,1},{9,5},{13... | collective-permute-start | bytes 1179656 | tf_op jit(solution)/shard_map/ppermute | solution.py:14
  12.5 28.2 %collective-permute-start = (bf16[384,512]{1,0:T(8,128)(2,1)S(1)}, bf16[384,512]{1,0:T(8,128)(2,1)S(1)}, u32[]{:S(2)}, u32[]{:S(2)}) collective-permute-start(bf16[384,512]{1,0:T(8,128)(2,1)S(1)} %dynamic-slice_bitcast_fusion), channel_id=1, source_target_pairs={{0,4},{4,8},{8,12},{12,16},{16,20},{20,24},{24,28},{1,5},{5,9},{9,... | collective-permute-start | bytes 1179656 | tf_op jit(solution)/shard_map/ppermute | solution.py:14
  16.9 29.3 %collective-permute-start.4 = (bf16[384,512]{1,0:T(8,128)(2,1)S(1)}, bf16[384,512]{1,0:T(8,128)(2,1)}, u32[]{:S(2)}, u32[]{:S(2)}) collective-permute-start(bf16[384,512]{1,0:T(8,128)(2,1)S(1)} %bitcast.171), channel_id=1, source_target_pairs={{4,0},{8,4},{12,8},{16,12},{20,16},{24,20},{28,24},{5,1},{9,5},{13... | collective-permute-start | bytes 1179656 | tf_op jit(solution)/shard_map/ppermute | solution.py:14
  18.8 30.3 %collective-permute-start.3 = (bf16[384,512]{1,0:T(8,128)(2,1)S(1)}, bf16[384,512]{1,0:T(8,128)(2,1)}, u32[]{:S(2)}, u32[]{:S(2)}) collective-permute-start(bf16[384,512]{1,0:T(8,128)(2,1)S(1)} %bitcast.172), channel_id=1, source_target_pairs={{0,4},{4,8},{8,12},{12,16},{16,20},{20,24},{24,28},{1,5},{5,9},{9,... | collective-permute-start | bytes 1179656 | tf_op jit(solution)/shard_map/ppermute | solution.py:14
  40.8 11.1 %collective-permute-start.2 = (bf16[2,384,512]{2,1,0:T(8,128)(2,1)S(1)}, bf16[2,384,512]{2,1,0:T(8,128)(2,1)}, u32[]{:S(2)}, u32[]{:S(2)}) collective-permute-start(bf16[2,384,512]{2,1,0:T(8,128)(2,1)S(1)} %pad_maximum_fusion.1), channel_id=1, source_target_pairs={{0,1},{1,0},{2,3},{3,2},{4,5},{5,4},{6,7},{7,6},{8,9},{9,8},{10,11... | collective-permute-start | bytes 2359304 | tf_op jit(solution)/shard_map/ppermute | solution.py:42
  71.1 24.5 %copy-start.2 = (bf16[8,128,896]{2,1,0:T(8,128)(2,1)}, bf16[8,128,896]{2,1,0:T(8,128)(2,1)S(1)}, u32[]{:S(2)}) copy-start(bf16[8,128,896]{2,1,0:T(8,128)(2,1)S(1)} %get-tuple-element.20) | copy-start | bytes 5505028
  78.3 18.3 %copy-start.4 = (bf16[8,128,896]{2,1,0:T(8,128)(2,1)}, bf16[8,128,896]{2,1,0:T(8,128)(2,1)S(1)}, u32[]{:S(2)}) copy-start(bf16[8,128,896]{2,1,0:T(8,128)(2,1)S(1)} %get-tuple-element.16) | copy-start | bytes 5505028
  83.9 13.7 %copy-start.6 = (bf16[8,128,896]{2,1,0:T(8,128)(2,1)}, bf16[8,128,896]{2,1,0:T(8,128)(2,1)S(1)}, u32[]{:S(2)}) copy-start(bf16[8,128,896]{2,1,0:T(8,128)(2,1)S(1)} %get-tuple-element.18) | copy-start | bytes 5505028
  83.9 5.3 %copy-start.13 = (bf16[1,384,1024]{2,1,0:T(8,128)(2,1)S(1)}, bf16[1,384,1024]{2,1,0:T(8,128)(2,1)}, u32[]{:S(2)}) copy-start(bf16[1,384,1024]{2,1,0:T(8,128)(2,1)} %param.6) | copy-start | bytes 2359300
  84.0 22.1 %collective-permute-start.5 = (f32[3,8,384,1]{2,1,3,0:T(8,128)S(1)}, f32[3,8,384,1]{2,1,3,0:T(8,128)S(1)}, u32[]{:S(2)}, u32[]{:S(2)}) collective-permute-start(f32[3,8,384,1]{2,1,3,0:T(8,128)S(1)} %pad_maximum_fusion.4), channel_id=1, source_target_pairs={{0,4},{4,8},{8,12},{12,16},{16,20},{20,24},{24,28},{1,5},{5,9},{9,... | collective-permute-start | bytes 110600 | tf_op jit(solution)/shard_map/ppermute | solution.py:14
  92.0 14.1 %collective-permute-start.6 = (f32[3,8,384,1]{2,1,3,0:T(8,128)S(1)}, f32[3,8,384,1]{2,1,3,0:T(8,128)S(1)}, u32[]{:S(2)}, u32[]{:S(2)}) collective-permute-start(f32[3,8,384,1]{2,1,3,0:T(8,128)S(1)} %pad_maximum_fusion.4), channel_id=1, source_target_pairs={{4,0},{8,4},{12,8},{16,12},{20,16},{24,20},{28,24},{5,1},{9,5},{13... | collective-permute-start | bytes 110600 | tf_op jit(solution)/shard_map/ppermute | solution.py:14
  96.6 9.5 %copy-start.24 = (bf16[8,384,64]{1,2,0:T(8,128)(2,1)S(1)}, bf16[8,384,64]{1,2,0:T(8,128)(2,1)}, u32[]{:S(2)}) copy-start(bf16[8,384,64]{1,2,0:T(8,128)(2,1)} %get-tuple-element.33) | copy-start | bytes 1179652
  99.9 30.9 %all-to-all-start = ((bf16[16,64,512]{2,1,0:T(8,128)(2,1)}), bf16[16,64,512]{2,1,0:T(8,128)(2,1)}, u32[]{:S(2)}, u32[]{:S(2)}) async-start(bf16[16,64,512]{2,1,0:T(8,128)(2,1)} %bitcast.74), calls=%async_computation | async-start | bytes 2097152 | tf_op jit(solution)/shard_map/all_to_all | solution.py:57
  106.1 4.7 %copy-start.15 = (bf16[8,384,64]{1,2,0:T(8,128)(2,1)S(1)}, bf16[8,384,64]{1,2,0:T(8,128)(2,1)}, u32[]{:S(2)}) copy-start(bf16[8,384,64]{1,2,0:T(8,128)(2,1)} %get-tuple-element.30) | copy-start | bytes 1179652
  106.1 4.7 %copy-start.16 = (bf16[8,384,64]{1,2,0:T(8,128)(2,1)S(1)}, bf16[8,384,64]{1,2,0:T(8,128)(2,1)}, u32[]{:S(2)}) copy-start(bf16[8,384,64]{1,2,0:T(8,128)(2,1)} %get-tuple-element.31) | copy-start | bytes 1179652
  110.8 3.2 %copy-start.19 = (bf16[8,128,384]{2,1,0:T(8,128)(2,1)S(1)}, bf16[8,128,384]{2,1,0:T(8,128)(2,1)}, u32[]{:S(2)}) copy-start(bf16[8,128,384]{2,1,0:T(8,128)(2,1)} %slice.244) | copy-start | bytes 2359300
  110.8 3.2 %copy-start.20 = (bf16[8,128,384]{2,1,0:T(8,128)(2,1)S(1)}, bf16[8,128,384]{2,1,0:T(8,128)(2,1)}, u32[]{:S(2)}) copy-start(bf16[8,128,384]{2,1,0:T(8,128)(2,1)} %slice.242) | copy-start | bytes 2359300
  110.8 3.2 %copy-start.21 = (bf16[8,128,384]{2,1,0:T(8,128)(2,1)S(1)}, bf16[8,128,384]{2,1,0:T(8,128)(2,1)}, u32[]{:S(2)}) copy-start(bf16[8,128,384]{2,1,0:T(8,128)(2,1)} %slice.243) | copy-start | bytes 2359300
  110.8 3.2 %copy-start.22 = (bf16[8,384,64]{1,2,0:T(8,128)(2,1)S(1)}, bf16[8,384,64]{1,2,0:T(8,128)(2,1)}, u32[]{:S(2)}) copy-start(bf16[8,384,64]{1,2,0:T(8,128)(2,1)} %get-tuple-element.29) | copy-start | bytes 1179652
  115.8 2.4 %copy-start.14 = (bf16[1,384,1024]{2,1,0:T(8,128)(2,1)S(1)}, bf16[1,384,1024]{2,1,0:T(8,128)(2,1)}, u32[]{:S(2)}) copy-start(bf16[1,384,1024]{2,1,0:T(8,128)(2,1)} %param.6) | copy-start | bytes 2359300
  120.8 15.1 %copy-start = (bf16[3,1024,512]{2,1,0:T(8,128)(2,1)S(1)}, bf16[3,1024,512]{2,1,0:T(8,128)(2,1)}, u32[]{:S(2)}) copy-start(bf16[3,1024,512]{2,1,0:T(8,128)(2,1)} %all-gather.2.cloned.1.call-done) | copy-start | bytes 9437188
  120.8 15.1 %copy-start.9 = (bf16[8,384,64]{1,2,0:T(8,128)(2,1)S(1)}, bf16[8,384,64]{1,2,0:T(8,128)(2,1)}, u32[]{:S(2)}) copy-start(bf16[8,384,64]{1,2,0:T(8,128)(2,1)} %copy-done.8) | copy-start | bytes 1179652
  130.9 51.9 %all-to-all-start.1 = ((bf16[1024,2,512]{2,1,0:T(2,128)(2,1)}), bf16[1024,2,512]{2,1,0:T(2,128)(2,1)}, u32[]{:S(2)}, u32[]{:S(2)}) async-start(bf16[1024,2,512]{2,1,0:T(2,128)(2,1)} %copy.36), calls=%async_computation.1 | async-start | bytes 4194304 | tf_op jit(solution)/shard_map/all_to_all | solution.py:57
  135.9 2.4 %copy-start.29 = (bf16[8,384,64]{1,2,0:T(8,128)(2,1)S(1)}, bf16[8,384,64]{1,2,0:T(8,128)(2,1)}, u32[]{:S(2)}) copy-start(bf16[8,384,64]{1,2,0:T(8,128)(2,1)} %copy-done.28) | copy-start | bytes 1179652
  136.5 3.4 %copy-start.3 = (bf16[8,128,896]{2,1,0:T(8,128)(2,1)S(1)}, bf16[8,128,896]{2,1,0:T(8,128)(2,1)}, u32[]{:S(2)}) copy-start(bf16[8,128,896]{2,1,0:T(8,128)(2,1)} %copy-done.2) | copy-start | bytes 5505028
  136.5 3.4 %copy-start.11 = (bf16[1152,512]{0,1:T(8,128)(2,1)S(1)}, bf16[1152,512]{0,1:T(8,128)(2,1)}, u32[]{:S(2)}) copy-start(bf16[1152,512]{0,1:T(8,128)(2,1)} %copy.29) | copy-start | bytes 3538948
  138.3 2.4 %copy-start.5 = (bf16[8,128,896]{2,1,0:T(8,128)(2,1)S(1)}, bf16[8,128,896]{2,1,0:T(8,128)(2,1)}, u32[]{:S(2)}) copy-start(bf16[8,128,896]{2,1,0:T(8,128)(2,1)} %copy-done.4) | copy-start | bytes 5505028
  139.9 3.5 %collective-permute-start.7 = (bf16[384,1024]{1,0:T(8,128)(2,1)}, bf16[384,1024]{1,0:T(8,128)(2,1)S(1)}, u32[]{:S(2)}, u32[]{:S(2)}) collective-permute-start(bf16[384,1024]{1,0:T(8,128)(2,1)} %add_convert_fusion.1), channel_id=1, source_target_pairs={{0,1},{1,0},{2,3},{3,2},{4,5},{5,4},{6,7},{7,6},{8,9},{9,8},{10,11... | collective-permute-start | bytes 2359304 | tf_op jit(solution)/shard_map/ppermute | solution.py:67
  (10 other events, 14.6 us)
Sparse Core Ops, SparseCore 0:
  10.2 46.0 all-gather.1

commit v6 on v5

--- a/solution.py
+++ b/solution.py
@@ -88,16 +88,20 @@
     score_scale = HD ** (-0.5)
 
     left_tokens, right_tokens = neighbour_tokens(tokens, halo)
-    left_up = shifted(upstream[length - halo :], "ctx", 1)
-    right_up = shifted(upstream[:halo], "ctx", -1)
-    gathered = lax.all_gather(jnp.stack([w_query, w_key, w_value]), "dp", axis=1, tiled=True)
-    query_full, key_full, value_full = gathered[0], gathered[1], gathered[2]
+    query_full = full_rows(w_query)
+    gathered = lax.all_gather(jnp.stack([w_key, w_value]), "dp", axis=1, tiled=True)
+    key_full, value_full = gathered[0], gathered[1]
 
     frame_tokens = jnp.concatenate([left_tokens, tokens, right_tokens], axis=0)
     all_weights = jnp.concatenate([query_full, key_full, value_full], axis=1)
     frame_proj = jnp.dot(frame_tokens, all_weights, preferred_element_type=jnp.float32).astype(
         jnp.bfloat16
     )
+    frame_proj, up_head, up_tail = lax.optimization_barrier(
+        (frame_proj, upstream[:halo], upstream[length - halo :])
+    )
+    left_up = shifted(up_tail, "ctx", 1)
+    right_up = shifted(up_head, "ctx", -1)
     query_h = head_major(frame_proj[:, :features], heads)
     key_h = head_major(frame_proj[:, features : 2 * features], heads)
     value_h = head_major(frame_proj[:, 2 * features :], heads)
@@ -212,12 +216,12 @@
     grad_input = section_sum(partial_input)[None]
 
     term_kv = jnp.einsum(
-        "tr,tcf->rcf",
+        "tr,tf->rf",
         tokens,
-        jnp.stack([key_grad, value_grad], axis=1),
+        jnp.concatenate([key_grad, value_grad], axis=1),
         preferred_element_type=jnp.float32,
     ).astype(jnp.bfloat16)
-    reduced_kv = summed_rows(term_kv)
+    reduced_kv = summed_rows(term_kv).reshape(-1, 2, features)
     summed = jnp.concatenate([reduced_query[:, None], reduced_kv], axis=1)
     grad_weights = summed / lax.axis_size("dp")
     return (attended, grad_input, grad_weights)

time: 194 us -> 207 us (1.067)
  waiting for transfers between devices: 55.3 us -> 65.3 us
    all_gather x1, waiting for transfers between devices: 2.34 us -> 14.1 us  [per_device(): lax.all_gather(jnp.stack([w_key, w_value]), 'dp', axis=1, tiled=True)]
    ppermute x6, waiting for transfers between devices: 13.5 us -> 5.63 us  [shifted(): lax.ppermute(value, axis, [(source, source + steps) for source in range(l...]
    convert_element_type x1 -> x0, local copies, waits for them, and re-layouts: 6.32 us -> none  [per_device(): term_kv = jnp.einsum('tr,tcf->rcf', tokens, jnp.stack([key_grad, value_gr...]
    all_to_all x2, waiting for transfers between devices: 39.5 us -> 45.5 us  [summed_rows(): parts = lax.all_to_all(term, group, 0, 0, tiled=True)]
    unnamed x67 -> x102, local copies, waits for them, and re-layouts: 2.99 us -> 8.01 us
  transfers between devices with their start and end apart: 11 -> 12, of which waited for: 7 -> 5; matrix products, arithmetic and copies ran while one was open for 25% -> 28% of each run, Pallas kernels for 0% -> 0%
where the time goes in v6:
time: 207 us; the launch traced here: 206 us
  waiting for transfers between devices  65.3 us (32%)
  matrix products  36.3 us (18%)
  local copies, waits for them, and re-layouts  31.7 us (15%)
  starting transfers between devices  31.7 us (15%)
  between operations  22.5 us (11%)
  other arithmetic  18.6 us (9%)
    all_to_all x2, waiting for transfers between devices, summed_rows(): parts = lax.all_to_all(term, group, 0, 0, tiled=True)  45.5 us
    ppermute x6, starting transfers between devices, shifted(): lax.ppermute(value, axis, [(source, source + steps) for source in range(l...  18.7 us
    all_gather x1, waiting for transfers between devices, per_device(): lax.all_gather(jnp.stack([w_key, w_value]), 'dp', axis=1, tiled=True)  14.1 us
    all_to_all x2, starting transfers between devices, summed_rows(): parts = lax.all_to_all(term, group, 0, 0, tiled=True)  11.1 us
    unnamed x102, local copies, waits for them, and re-layouts  8.01 us
    dot_general x3, matrix products, per_device(): jnp.einsum('hqd,hkd->hqk', upstream_block, value_window, preferred_elemen...  6.39 us
    ppermute x6, waiting for transfers between devices, shifted(): lax.ppermute(value, axis, [(source, source + steps) for source in range(l...  5.63 us
    dot_general x1, matrix products, per_device(): jnp.einsum('hqd,hkd->hqk', near_query, key_part, preferred_element_type=j...  4.94 us
  transfers between devices with their start and end apart: 12, of which 5 were waited for; matrix products, arithmetic and copies ran while one was open for 28% of the time, Pallas kernels for 0%

profile of v6, /device:TPU:12, one launch (start us, length us, event | category | flops | bytes accessed | tf_op | source)
XLA Modules:
  0.0 206.0 jit_solution(18156405367710046032)
XLA Ops:
  8.3 2.4 %collective-permute-start.1 = (bf16[384,512]{1,0:T(8,128)(2,1)S(1)}, bf16[384,512]{1,0:T(8,128)(2,1)S(1)}, u32[]{:S(2)}, u32[]{:S(2)}) collective-permute-start(bf16[384,512]{1,0:T(8,128)(2,1)S(1)} %dynamic-slice_bitcast_fusion), channel_id=1, source_target_pairs={{4,0},{8,4},{12,8},{16,12},{20,16},{24,20},{28,24},{5,1},{9,5},{13... | collective-permute-start | bytes 1179656 | tf_op jit(solution)/shard_map/ppermute | solution.py:14
  10.7 4.3 %collective-permute-start = (bf16[384,512]{1,0:T(8,128)(2,1)S(1)}, bf16[384,512]{1,0:T(8,128)(2,1)S(1)}, u32[]{:S(2)}, u32[]{:S(2)}) collective-permute-start(bf16[384,512]{1,0:T(8,128)(2,1)S(1)} %dynamic-slice_bitcast_fusion), channel_id=1, source_target_pairs={{0,4},{4,8},{8,12},{12,16},{16,20},{20,24},{24,28},{1,5},{5,9},{9,... | collective-permute-start | bytes 1179656 | tf_op jit(solution)/shard_map/ppermute | solution.py:14
  15.0 1.6 collective-permute-start.3
  16.6 2.3 %pad_maximum_fusion = bf16[2,512,512]{2,1,0:T(8,128)(2,1)} fusion(bf16[1,512,512]{2,1,0:T(8,128)(2,1)} %bitcast.158, bf16[1,512,512]{2,1,0:T(8,128)(2,1)} %bitcast.159), kind=kLoop, calls=%fused_computation.81 | loop fusion | flops 524288 | bytes 2097152 | tf_op jit(solution)/shard_map/stack | solution.py:92
  27.6 2.7 %collective-permute-done = bf16[384,512]{1,0:T(8,128)(2,1)S(1)} collective-permute-done((bf16[384,512]{1,0:T(8,128)(2,1)S(1)}, bf16[384,512]{1,0:T(8,128)(2,1)S(1)}, u32[]{:S(2)}, u32[]{:S(2)}) %collective-permute-start) | collective-permute-done | bytes 393248 | tf_op jit(solution)/shard_map/ppermute | solution.py:14
  31.9 1.9 copy.20
  34.7 1.8 maximum_select_fusion.1
  37.2 14.1 %all-gather.2.cloned.1.call-done = bf16[2,1024,512]{2,1,0:T(8,128)(2,1)} async-done(((bf16[2,512,512]{2,1,0:T(8,128)(2,1)}), bf16[2,1024,512]{2,1,0:T(8,128)(2,1)}) %all-gather.2.cloned.1.call-update) | async-done | bytes 2097168 | tf_op jit(solution)/shard_map/all_gather | solution.py:92
  51.3 1.7 slice_bitcast_fusion.1
  53.0 3.8 %convolution_convert_fusion = bf16[1152,1536]{1,0:T(8,128)(2,1)S(1)} fusion(bf16[1024,512]{1,0:T(8,128)(2,1)S(1)} %get-tuple-element.28, bf16[1024,512]{1,0:T(8,128)(2,1)S(1)} %get-tuple-element.27, bf16[1024,512]{1,0:T(8,128)(2,1)S(1)} %maximum_select_fusion.1, bf16[384,1024]{1,0:T(8,128)(2,1)S(1)} %get-tuple-element.30, ...), kind=kOutput, calls=%fused_computation.2 | convolution fusion | flops 3642163200 | bytes 9043968 | tf_op jit(solution)/shard_map/dot_general | solution.py:97
  58.2 3.4 %collective-permute-start.4 = (bf16[384,512]{1,0:T(8,128)(2,1)}, bf16[384,512]{1,0:T(8,128)(2,1)}, u32[]{:S(2)}, u32[]{:S(2)}) collective-permute-start(bf16[384,512]{1,0:T(8,128)(2,1)} %bitcast.11), channel_id=1, source_target_pairs={{0,4},{4,8},{8,12},{12,16},{16,20},{20,24},{24,28},{1,5},{5,9},{9,... | collective-permute-start | bytes 1179656 | tf_op jit(solution)/shard_map/ppermute | solution.py:14
  61.6 2.6 %collective-permute-start.5 = (bf16[384,512]{1,0:T(8,128)(2,1)}, bf16[384,512]{1,0:T(8,128)(2,1)}, u32[]{:S(2)}, u32[]{:S(2)}) collective-permute-start(bf16[384,512]{1,0:T(8,128)(2,1)} %bitcast.11), channel_id=1, source_target_pairs={{4,0},{8,4},{12,8},{16,12},{20,16},{24,20},{28,24},{5,1},{9,5},{13... | collective-permute-start | bytes 1179656 | tf_op jit(solution)/shard_map/ppermute | solution.py:14
  64.9 1.7 copy.16
  76.8 2.9 %collective-permute-done.4 = bf16[384,512]{1,0:T(8,128)(2,1)} collective-permute-done((bf16[384,512]{1,0:T(8,128)(2,1)}, bf16[384,512]{1,0:T(8,128)(2,1)}, u32[]{:S(2)}, u32[]{:S(2)}) %collective-permute-start.4) | collective-permute-done | bytes 393248 | tf_op jit(solution)/shard_map/ppermute | solution.py:14
  83.3 3.3 %multiply_reduce_fusion = (f32[8,128]{1,0:T(8,128)S(1)}, f32[8,128,896]{2,1,0:T(8,128)S(1)}) fusion(f32[8,128]{1,0:T(8,128)S(1)} %copy-done.39, f32[8,128]{1,0:T(8,128)S(1)} %get-tuple-element.52, f32[8,128,896]{2,1,0:T(8,128)} %copy-done.4, pred[896]{0:T(1024)(128)(4,1)S(1)} %copy-done.44, bf16[8,1152,64]{1,2,0:T(8,128)(2,1)S(1)} %bitcast.142, ...), kind=kOutput, calls=%fused_computation.21 | convolution fusion | flops 122944512 | bytes 8401920 | tf_op jit(solution)/shard_map/hqd,hkd->hqk/dot_general | solution.py:139
  86.7 1.5 multiply_reduce_fusion.2
  88.7 1.5 multiply_reduce_fusion.1
  95.1 1.5 multiply_convert_fusion.2
  97.3 3.2 %collective-permute-start.6 = (f32[3,8,384,1]{2,1,3,0:T(8,128)}, f32[3,8,384,1]{2,1,3,0:T(8,128)}, u32[]{:S(2)}, u32[]{:S(2)}) collective-permute-start(f32[3,8,384,1]{2,1,3,0:T(8,128)} %pad_maximum_fusion.4), channel_id=1, source_target_pairs={{0,4},{4,8},{8,12},{12,16},{16,20},{20,24},{24,28},{1,5},{5,9},{9,... | collective-permute-start | bytes 110600 | tf_op jit(solution)/shard_map/ppermute | solution.py:14
  105.2 2.8 %collective-permute-start.7 = (f32[3,8,384,1]{2,1,3,0:T(8,128)}, f32[3,8,384,1]{2,1,3,0:T(8,128)}, u32[]{:S(2)}, u32[]{:S(2)}) collective-permute-start(f32[3,8,384,1]{2,1,3,0:T(8,128)} %pad_maximum_fusion.4), channel_id=1, source_target_pairs={{4,0},{8,4},{12,8},{16,12},{20,16},{24,20},{28,24},{5,1},{9,5},{13... | collective-permute-start | bytes 110600 | tf_op jit(solution)/shard_map/ppermute | solution.py:14
  113.2 6.2 %all-to-all-start = ((bf16[16,64,512]{2,1,0:T(8,128)(2,1)}), bf16[16,64,512]{2,1,0:T(8,128)(2,1)S(1)}, u32[]{:S(2)}, u32[]{:S(2)}) async-start(bf16[16,64,512]{2,1,0:T(8,128)(2,1)} %bitcast.137), calls=%async_computation | async-start | bytes 2097152 | tf_op jit(solution)/shard_map/all_to_all | solution.py:57
  121.0 4.9 %fusion.114 = (bf16[8,768,384]{2,1,0:T(8,128)(2,1)S(1)}, f32[8,768,384]{2,1,0:T(8,128)S(1)}) fusion(f32[8,768]{1,0:T(8,128)S(1)} %get-tuple-element.38, f32[8,768]{1,0:T(8,128)S(1)} %get-tuple-element.39, bf16[8,1152,64]{1,2,0:T(8,128)(2,1)S(1)} %bitcast.132, bf16[8,384,64]{1,2,0:T(8,128)(2,1)} %get-tuple-element.32, ...), kind=kOutput, calls=%fused_computation.170 | convolution fusion | flops 315359232 | bytes 15679488 | tf_op jit(solution)/shard_map/hqd,hkd->hqk/dot_general | solution.py:187
  126.0 3.2 %multiply_convert_fusion = bf16[8,768,384]{2,1,0:T(8,128)(2,1)S(1)} fusion(f32[8,768,384]{2,1,0:T(8,128)S(1)} %get-tuple-element.65, f32[8,768]{1,0:T(8,128)S(1)} %get-tuple-element.37, bf16[8,384,64]{1,2,0:T(8,128)(2,1)S(1)} %copy-done.20, bf16[8,384,64]{1,2,0:T(8,128)(2,1)S(1)} %copy-done.21, bf16[8,1152,64]{1,2,0:T(8,128)(2,1)} %bitcast.141), kind=kOutput, calls=%fused_computation | convolution fusion | flops 310640640 | bytes 15360000 | tf_op jit(solution)/shard_map/hqd,hkd->hqk/dot_general | solution.py:192
  129.3 1.6 fusion.39
  131.1 1.6 fusion.36
  133.5 2.7 %convolution_convert_fusion.1 = bf16[1024,1024]{0,1:T(8,128)(2,1)} fusion(bf16[384,512]{0,1:T(8,128)(2,1)S(1)} %bitcast.160, bf16[384,512]{0,1:T(8,128)(2,1)S(1)} %bitcast.162, bf16[1,384,1024]{2,1,0:T(8,128)(2,1)S(1)} %copy-done.19), kind=kOutput, calls=%fused_computation.49 | convolution fusion | flops 807927808 | bytes 3670016 | tf_op jit(solution)/shard_map/tr,tf->rf/dot_general | solution.py:218
  136.2 7.7 %all-to-all-done = bf16[16,64,512]{2,1,0:T(8,128)(2,1)S(1)} async-done(((bf16[16,64,512]{2,1,0:T(8,128)(2,1)}), bf16[16,64,512]{2,1,0:T(8,128)(2,1)S(1)}, u32[]{:S(2)}, u32[]{:S(2)}) %all-to-all-start) | async-done | bytes 1048608 | tf_op jit(solution)/shard_map/all_to_all | solution.py:57
  143.9 4.9 %all-to-all-start.1 = ((bf16[16,64,1024]{2,1,0:T(8,128)(2,1)}), bf16[16,64,1024]{2,1,0:T(8,128)(2,1)}, u32[]{:S(2)}, u32[]{:S(2)}) async-start(bf16[16,64,1024]{2,1,0:T(8,128)(2,1)} %bitcast.140), calls=%async_computation.1 | async-start | bytes 4194304 | tf_op jit(solution)/shard_map/all_to_all | solution.py:57
  148.8 1.7 fusion.106
  150.5 1.8 fusion.105
  158.0 37.7 %all-to-all-done.1 = bf16[16,64,1024]{2,1,0:T(8,128)(2,1)} async-done(((bf16[16,64,1024]{2,1,0:T(8,128)(2,1)}), bf16[16,64,1024]{2,1,0:T(8,128)(2,1)}, u32[]{:S(2)}, u32[]{:S(2)}) %all-to-all-start.1) | async-done | bytes 2097184 | tf_op jit(solution)/shard_map/all_to_all | solution.py:57
  195.8 2.0 convert_reduce_fusion
  (172 shorter events, 46.3 us)
Async XLA Ops:
  7.2 11.7 %copy-start.47 = (s32[24,7]{0,1:T(8,128)S(1)}, s32[24,7]{0,1:T(8,128)}, u32[]{:S(2)}) copy-start(s32[24,7]{0,1:T(8,128)} %param.10) | copy-start | bytes 2020
  7.2 44.1 %all-gather.2.cloned.1.call-start = ((), (), s32[]{:S(2)}) async-start(), calls=%async_computation.2 | async-start | bytes 3145728 | tf_op jit(solution)/shard_map/all_gather | solution.py:92
  8.3 19.3 %collective-permute-start.1 = (bf16[384,512]{1,0:T(8,128)(2,1)S(1)}, bf16[384,512]{1,0:T(8,128)(2,1)S(1)}, u32[]{:S(2)}, u32[]{:S(2)}) collective-permute-start(bf16[384,512]{1,0:T(8,128)(2,1)S(1)} %dynamic-slice_bitcast_fusion), channel_id=1, source_target_pairs={{4,0},{8,4},{12,8},{16,12},{20,16},{24,20},{28,24},{5,1},{9,5},{13... | collective-permute-start | bytes 1179656 | tf_op jit(solution)/shard_map/ppermute | solution.py:14
  10.7 19.7 %collective-permute-start = (bf16[384,512]{1,0:T(8,128)(2,1)S(1)}, bf16[384,512]{1,0:T(8,128)(2,1)S(1)}, u32[]{:S(2)}, u32[]{:S(2)}) collective-permute-start(bf16[384,512]{1,0:T(8,128)(2,1)S(1)} %dynamic-slice_bitcast_fusion), channel_id=1, source_target_pairs={{0,4},{4,8},{8,12},{12,16},{16,20},{20,24},{24,28},{1,5},{5,9},{9,... | collective-permute-start | bytes 1179656 | tf_op jit(solution)/shard_map/ppermute | solution.py:14
  15.0 19.7 %collective-permute-start.3 = (bf16[512,512]{1,0:T(8,128)(2,1)}, bf16[512,512]{1,0:T(8,128)(2,1)}, u32[]{:S(2)}, u32[]{:S(2)}) collective-permute-start(bf16[512,512]{1,0:T(8,128)(2,1)} %param.7), channel_id=1, source_target_pairs={{0,2},{2,0},{1,3},{3,1},{4,6},{6,4},{5,7},{7,5},{8,10},{10,8},{9,1... | collective-permute-start | bytes 1572872 | tf_op jit(solution)/shard_map/ppermute | solution.py:50
  30.4 6.2 %collective-permute-start.2 = (bf16[2,384,512]{2,1,0:T(8,128)(2,1)S(1)}, bf16[2,384,512]{2,1,0:T(8,128)(2,1)S(1)}, u32[]{:S(2)}, u32[]{:S(2)}) collective-permute-start(bf16[2,384,512]{2,1,0:T(8,128)(2,1)S(1)} %pad_maximum_fusion.1), channel_id=1, source_target_pairs={{0,1},{1,0},{2,3},{3,2},{4,5},{5,4},{6,7},{7,6},{8,9},{9,8},{10,11... | collective-permute-start | bytes 2359304 | tf_op jit(solution)/shard_map/ppermute | solution.py:42
  34.7 32.7 %copy-start.40 = (pred[896]{0:T(1024)(128)(4,1)}, pred[896]{0:T(1024)(128)(4,1)S(1)}, u32[]{:S(2)}) copy-start(pred[896]{0:T(1024)(128)(4,1)S(1)} %get-tuple-element.67) | copy-start | bytes 2692
  34.7 34.3 %copy-start.43 = (pred[896]{0:T(1024)(128)(4,1)}, pred[896]{0:T(1024)(128)(4,1)S(1)}, u32[]{:S(2)}) copy-start(pred[896]{0:T(1024)(128)(4,1)S(1)} %get-tuple-element.66) | copy-start | bytes 2692
  36.6 16.4 %copy-start.7 = (bf16[1024,512]{1,0:T(8,128)(2,1)}, bf16[1024,512]{1,0:T(8,128)(2,1)S(1)}, u32[]{:S(2)}) copy-start(bf16[1024,512]{1,0:T(8,128)(2,1)S(1)} %maximum_select_fusion.1) | copy-start | bytes 3145732
  37.0 16.0 %copy-start.17 = (bf16[1,384,1024]{2,1,0:T(8,128)(2,1)S(1)}, bf16[1,384,1024]{2,1,0:T(8,128)(2,1)}, u32[]{:S(2)}) copy-start(bf16[1,384,1024]{2,1,0:T(8,128)(2,1)} %param.6) | copy-start | bytes 2359300
  58.2 21.5 %collective-permute-start.4 = (bf16[384,512]{1,0:T(8,128)(2,1)}, bf16[384,512]{1,0:T(8,128)(2,1)}, u32[]{:S(2)}, u32[]{:S(2)}) collective-permute-start(bf16[384,512]{1,0:T(8,128)(2,1)} %bitcast.11), channel_id=1, source_target_pairs={{0,4},{4,8},{8,12},{12,16},{16,20},{20,24},{24,28},{1,5},{5,9},{9,... | collective-permute-start | bytes 1179656 | tf_op jit(solution)/shard_map/ppermute | solution.py:14
  61.6 19.3 %collective-permute-start.5 = (bf16[384,512]{1,0:T(8,128)(2,1)}, bf16[384,512]{1,0:T(8,128)(2,1)}, u32[]{:S(2)}, u32[]{:S(2)}) collective-permute-start(bf16[384,512]{1,0:T(8,128)(2,1)} %bitcast.11), channel_id=1, source_target_pairs={{4,0},{8,4},{12,8},{16,12},{20,16},{24,20},{28,24},{5,1},{9,5},{13... | collective-permute-start | bytes 1179656 | tf_op jit(solution)/shard_map/ppermute | solution.py:14
  75.1 8.1 %copy-start.15 = (bf16[1152,512]{0,1:T(8,128)(2,1)S(1)}, bf16[1152,512]{0,1:T(8,128)(2,1)}, u32[]{:S(2)}) copy-start(bf16[1152,512]{0,1:T(8,128)(2,1)} %copy.18) | copy-start | bytes 3538948
  76.8 6.5 %copy-start.39 = (f32[8,128]{1,0:T(8,128)S(1)}, f32[8,128]{1,0:T(8,128)}, u32[]{:S(2)}) copy-start(f32[8,128]{1,0:T(8,128)} %copy-done.38) | copy-start | bytes 12292
  76.8 6.5 %copy-start.44 = (pred[896]{0:T(1024)(128)(4,1)S(1)}, pred[896]{0:T(1024)(128)(4,1)}, u32[]{:S(2)}) copy-start(pred[896]{0:T(1024)(128)(4,1)} %copy-done.43) | copy-start | bytes 2692
  83.3 3.4 %copy-start.3 = (f32[8,128,896]{2,1,0:T(8,128)S(1)}, f32[8,128,896]{2,1,0:T(8,128)}, u32[]{:S(2)}) copy-start(f32[8,128,896]{2,1,0:T(8,128)} %copy-done.2) | copy-start | bytes 11010052
  83.3 3.4 %copy-start.37 = (f32[8,128]{1,0:T(8,128)S(1)}, f32[8,128]{1,0:T(8,128)}, u32[]{:S(2)}) copy-start(f32[8,128]{1,0:T(8,128)} %copy-done.36) | copy-start | bytes 12292
  83.3 3.4 %copy-start.46 = (pred[896]{0:T(1024)(128)(4,1)S(1)}, pred[896]{0:T(1024)(128)(4,1)}, u32[]{:S(2)}) copy-start(pred[896]{0:T(1024)(128)(4,1)} %broadcast_bitcast_fusion.3) | copy-start | bytes 2692
  92.1 16.9 %copy-start.9 = (bf16[8,128,896]{2,1,0:T(8,128)(2,1)}, bf16[8,128,896]{2,1,0:T(8,128)(2,1)S(1)}, u32[]{:S(2)}) copy-start(bf16[8,128,896]{2,1,0:T(8,128)(2,1)S(1)} %get-tuple-element.23) | copy-start | bytes 5505028
  94.2 15.7 %copy-start.11 = (bf16[8,128,896]{2,1,0:T(8,128)(2,1)}, bf16[8,128,896]{2,1,0:T(8,128)(2,1)S(1)}, u32[]{:S(2)}) copy-start(bf16[8,128,896]{2,1,0:T(8,128)(2,1)S(1)} %get-tuple-element.19) | copy-start | bytes 5505028
  96.7 14.2 %copy-start.13 = (bf16[8,128,896]{2,1,0:T(8,128)(2,1)}, bf16[8,128,896]{2,1,0:T(8,128)(2,1)S(1)}, u32[]{:S(2)}) copy-start(bf16[8,128,896]{2,1,0:T(8,128)(2,1)S(1)} %get-tuple-element.21) | copy-start | bytes 5505028
  96.7 4.8 %copy-start.18 = (bf16[1,384,1024]{2,1,0:T(8,128)(2,1)S(1)}, bf16[1,384,1024]{2,1,0:T(8,128)(2,1)}, u32[]{:S(2)}) copy-start(bf16[1,384,1024]{2,1,0:T(8,128)(2,1)} %param.6) | copy-start | bytes 2359300
  97.3 22.1 %collective-permute-start.6 = (f32[3,8,384,1]{2,1,3,0:T(8,128)}, f32[3,8,384,1]{2,1,3,0:T(8,128)}, u32[]{:S(2)}, u32[]{:S(2)}) collective-permute-start(f32[3,8,384,1]{2,1,3,0:T(8,128)} %pad_maximum_fusion.4), channel_id=1, source_target_pairs={{0,4},{4,8},{8,12},{12,16},{16,20},{20,24},{24,28},{1,5},{5,9},{9,... | collective-permute-start | bytes 110600 | tf_op jit(solution)/shard_map/ppermute | solution.py:14
  105.2 15.0 %collective-permute-start.7 = (f32[3,8,384,1]{2,1,3,0:T(8,128)}, f32[3,8,384,1]{2,1,3,0:T(8,128)}, u32[]{:S(2)}, u32[]{:S(2)}) collective-permute-start(f32[3,8,384,1]{2,1,3,0:T(8,128)} %pad_maximum_fusion.4), channel_id=1, source_target_pairs={{4,0},{8,4},{12,8},{16,12},{20,16},{24,20},{28,24},{5,1},{9,5},{13... | collective-permute-start | bytes 110600 | tf_op jit(solution)/shard_map/ppermute | solution.py:14
  113.2 30.7 %all-to-all-start = ((bf16[16,64,512]{2,1,0:T(8,128)(2,1)}), bf16[16,64,512]{2,1,0:T(8,128)(2,1)S(1)}, u32[]{:S(2)}, u32[]{:S(2)}) async-start(bf16[16,64,512]{2,1,0:T(8,128)(2,1)} %bitcast.137), calls=%async_computation | async-start | bytes 2097152 | tf_op jit(solution)/shard_map/all_to_all | solution.py:57
  120.9 5.0 %copy-start.20 = (bf16[8,384,64]{1,2,0:T(8,128)(2,1)S(1)}, bf16[8,384,64]{1,2,0:T(8,128)(2,1)}, u32[]{:S(2)}) copy-start(bf16[8,384,64]{1,2,0:T(8,128)(2,1)} %get-tuple-element.35) | copy-start | bytes 1179652
  121.0 5.0 %copy-start.21 = (bf16[8,384,64]{1,2,0:T(8,128)(2,1)S(1)}, bf16[8,384,64]{1,2,0:T(8,128)(2,1)}, u32[]{:S(2)}) copy-start(bf16[8,384,64]{1,2,0:T(8,128)(2,1)} %get-tuple-element.36) | copy-start | bytes 1179652
  125.9 3.2 %copy-start.25 = (bf16[8,128,384]{2,1,0:T(8,128)(2,1)S(1)}, bf16[8,128,384]{2,1,0:T(8,128)(2,1)}, u32[]{:S(2)}) copy-start(bf16[8,128,384]{2,1,0:T(8,128)(2,1)} %slice.236) | copy-start | bytes 2359300
  133.5 15.3 %copy-start.6 = (bf16[2,1024,512]{2,1,0:T(8,128)(2,1)S(1)}, bf16[2,1024,512]{2,1,0:T(8,128)(2,1)}, u32[]{:S(2)}) copy-start(bf16[2,1024,512]{2,1,0:T(8,128)(2,1)} %all-gather.2.cloned.1.call-done) | copy-start | bytes 6291460
  143.9 51.9 %all-to-all-start.1 = ((bf16[16,64,1024]{2,1,0:T(8,128)(2,1)}), bf16[16,64,1024]{2,1,0:T(8,128)(2,1)}, u32[]{:S(2)}, u32[]{:S(2)}) async-start(bf16[16,64,1024]{2,1,0:T(8,128)(2,1)} %bitcast.140), calls=%async_computation.1 | async-start | bytes 4194304 | tf_op jit(solution)/shard_map/all_to_all | solution.py:57
  148.8 3.5 %copy-start.8 = (bf16[1024,512]{1,0:T(8,128)(2,1)S(1)}, bf16[1024,512]{1,0:T(8,128)(2,1)}, u32[]{:S(2)}) copy-start(bf16[1024,512]{1,0:T(8,128)(2,1)} %copy-done.7) | copy-start | bytes 3145732
  153.0 3.6 %collective-permute-start.8 = (bf16[384,1024]{1,0:T(8,128)(2,1)S(1)}, bf16[384,1024]{1,0:T(8,128)(2,1)S(1)}, u32[]{:S(2)}, u32[]{:S(2)}) collective-permute-start(bf16[384,1024]{1,0:T(8,128)(2,1)S(1)} %add_convert_fusion.1), channel_id=1, source_target_pairs={{0,1},{1,0},{2,3},{3,2},{4,5},{5,4},{6,7},{7,6},{8,9},{9,8},{10,11... | collective-permute-start | bytes 2359304 | tf_op jit(solution)/shard_map/ppermute | solution.py:67
  (28 other events, 56.0 us)
Sparse Core Ops, SparseCore 0:
  19.0 32.2 all-gather.1

commit v7 on v6

--- a/solution.py
+++ b/solution.py
@@ -105,7 +105,8 @@
     query_h = head_major(frame_proj[:, :features], heads)
     key_h = head_major(frame_proj[:, features : 2 * features], heads)
     value_h = head_major(frame_proj[:, 2 * features :], heads)
-    upstream_h = head_major(jnp.concatenate([left_up, upstream, right_up], axis=0), heads)
+    own_upstream = head_major(upstream, heads)
+    near_upstream = head_major(jnp.concatenate([left_up, right_up], axis=0), heads)
 
     first_block = lax.axis_index("ctx") * blocks
     padded_mask = jnp.pad(block_mask, ((REACH, REACH), (0, 0)))
@@ -124,7 +125,7 @@
     for i in range(blocks):
         at = REACH + i
         query_block = rows(query_h, at)
-        upstream_block = rows(upstream_h, at)
+        upstream_block = rows(own_upstream, i)
         key_window = rows(key_h, i, span_len)
         value_window = rows(value_h, i, span_len)
         scores = (
@@ -178,9 +179,6 @@
     near_stats = jnp.concatenate([stats_left, stats_right], axis=2)
     top, total, delta = near_stats[0], near_stats[1], near_stats[2]
     near_query = jnp.concatenate([rows(query_h, 0, REACH), rows(query_h, REACH + blocks, REACH)], axis=1)
-    near_upstream = jnp.concatenate(
-        [rows(upstream_h, 0, REACH), rows(upstream_h, REACH + blocks, REACH)], axis=1
-    )
     key_part = rows(key_h, own_low, blocks)
     value_part = rows(value_h, own_low, blocks)
     scores = (
@@ -196,7 +194,7 @@
     all_score_grads = jnp.concatenate(own_score_grads + [score_grad], axis=1)
     all_weights = jnp.concatenate(own_weights + [weights], axis=1)
     all_queries = jnp.concatenate([rows(query_h, REACH, blocks), near_query], axis=1)
-    all_upstream = jnp.concatenate([rows(upstream_h, REACH, blocks), near_upstream], axis=1)
+    all_upstream = jnp.concatenate([own_upstream, near_upstream], axis=1)
     key_own = score_scale * jnp.einsum(
         "hqk,hqd->hkd", all_score_grads, all_queries, preferred_element_type=jnp.float32
     )

time: 207 us -> 198 us (0.957)
  local copies, waits for them, and re-layouts: 31.7 us -> 23.9 us
  waiting for transfers between devices: 65.3 us -> 57.6 us
  starting transfers between devices: 31.7 us -> 36.6 us
  matrix products: 36.3 us -> 39 us
    all_to_all x2, waiting for transfers between devices: 45.5 us -> 39.9 us  [summed_rows(): parts = lax.all_to_all(term, group, 0, 0, tiled=True)]
    all_to_all x2, starting transfers between devices: 11.1 us -> 15.8 us  [summed_rows(): parts = lax.all_to_all(term, group, 0, 0, tiled=True)]
    dot_general x1, matrix products: 4.94 us -> 8.22 us  [per_device(): jnp.einsum('hqd,hkd->hqk', near_query, key_part, preferred_element_type=j...]
    ppermute x6, waiting for transfers between devices: 5.63 us -> 2.9 us  [shifted(): lax.ppermute(value, axis, [(source, source + steps) for source in range(l...]
    ppermute x2 -> x0, local copies, waits for them, and re-layouts: 2.41 us -> none  [shifted(): lax.ppermute(value, axis, [(source, source + steps) for source in range(l...]
    unnamed x102 -> x74, local copies, waits for them, and re-layouts: 8.01 us -> 6.62 us
  transfers between devices with their start and end apart: 12 -> 12, of which waited for: 5 -> 4; matrix products, arithmetic and copies ran while one was open for 28% -> 25% of each run, Pallas kernels for 0% -> 0%
where the time goes in v7:
time: 198 us; the launch traced here: 197 us
  waiting for transfers between devices  57.6 us (29%)
  matrix products  39 us (20%)
  starting transfers between devices  36.6 us (18%)
  local copies, waits for them, and re-layouts  23.9 us (12%)
  between operations  22.3 us (11%)
  other arithmetic  18.1 us (9%)
    all_to_all x2, waiting for transfers between devices, summed_rows(): parts = lax.all_to_all(term, group, 0, 0, tiled=True)  39.9 us
    ppermute x6, starting transfers between devices, shifted(): lax.ppermute(value, axis, [(source, source + steps) for source in range(l...  18.9 us
    all_to_all x2, starting transfers between devices, summed_rows(): parts = lax.all_to_all(term, group, 0, 0, tiled=True)  15.8 us
    all_gather x1, waiting for transfers between devices, per_device(): lax.all_gather(jnp.stack([w_key, w_value]), 'dp', axis=1, tiled=True)  14.7 us
    dot_general x1, matrix products, per_device(): jnp.einsum('hqd,hkd->hqk', near_query, key_part, preferred_element_type=j...  8.22 us
    unnamed x74, local copies, waits for them, and re-layouts  6.62 us
    dot_general x1, matrix products, per_device(): jnp.einsum('hqd,hkd->hqk', near_upstream, value_part, preferred_element_t...  4.98 us
    dot_general x3, matrix products, per_device(): jnp.einsum('hqd,hkd->hqk', upstream_block, value_window, preferred_elemen...  4.57 us
  transfers between devices with their start and end apart: 12, of which 4 were waited for; matrix products, arithmetic and copies ran while one was open for 25% of the time, Pallas kernels for 0%

profile of v7, /device:TPU:12, one launch (start us, length us, event | category | flops | bytes accessed | tf_op | source)
XLA Modules:
  0.0 197.4 jit_solution(225298450829000411)
XLA Ops:
  8.3 2.4 %collective-permute-start.1 = (bf16[384,512]{1,0:T(8,128)(2,1)S(1)}, bf16[384,512]{1,0:T(8,128)(2,1)S(1)}, u32[]{:S(2)}, u32[]{:S(2)}) collective-permute-start(bf16[384,512]{1,0:T(8,128)(2,1)S(1)} %dynamic-slice_bitcast_fusion), channel_id=1, source_target_pairs={{4,0},{8,4},{12,8},{16,12},{20,16},{24,20},{28,24},{5,1},{9,5},{13... | collective-permute-start | bytes 1179656 | tf_op jit(solution)/shard_map/ppermute | solution.py:14
  10.7 4.3 %collective-permute-start = (bf16[384,512]{1,0:T(8,128)(2,1)S(1)}, bf16[384,512]{1,0:T(8,128)(2,1)S(1)}, u32[]{:S(2)}, u32[]{:S(2)}) collective-permute-start(bf16[384,512]{1,0:T(8,128)(2,1)S(1)} %dynamic-slice_bitcast_fusion), channel_id=1, source_target_pairs={{0,4},{4,8},{8,12},{12,16},{16,20},{20,24},{24,28},{1,5},{5,9},{9,... | collective-permute-start | bytes 1179656 | tf_op jit(solution)/shard_map/ppermute | solution.py:14
  15.0 1.6 collective-permute-start.3
  16.6 2.3 %pad_maximum_fusion = bf16[2,512,512]{2,1,0:T(8,128)(2,1)} fusion(bf16[1,512,512]{2,1,0:T(8,128)(2,1)} %bitcast.185, bf16[1,512,512]{2,1,0:T(8,128)(2,1)} %bitcast.186), kind=kLoop, calls=%fused_computation.87 | loop fusion | flops 524288 | bytes 2097152 | tf_op jit(solution)/shard_map/stack | solution.py:92
  27.5 2.9 %collective-permute-done = bf16[384,512]{1,0:T(8,128)(2,1)S(1)} collective-permute-done((bf16[384,512]{1,0:T(8,128)(2,1)S(1)}, bf16[384,512]{1,0:T(8,128)(2,1)S(1)}, u32[]{:S(2)}, u32[]{:S(2)}) %collective-permute-start) | collective-permute-done | bytes 393248 | tf_op jit(solution)/shard_map/ppermute | solution.py:14
  31.9 1.9 copy.21
  34.2 1.8 maximum_select_fusion.1
  36.6 14.7 %all-gather.2.cloned.1.call-done = bf16[2,1024,512]{2,1,0:T(8,128)(2,1)} async-done(((bf16[2,512,512]{2,1,0:T(8,128)(2,1)}), bf16[2,1024,512]{2,1,0:T(8,128)(2,1)}) %all-gather.2.cloned.1.call-update) | async-done | bytes 2097168 | tf_op jit(solution)/shard_map/all_gather | solution.py:92
  51.3 1.7 slice_bitcast_fusion.1
  53.0 3.8 %convolution_convert_fusion = bf16[1152,1536]{1,0:T(8,128)(2,1)S(1)} fusion(bf16[1024,512]{1,0:T(8,128)(2,1)S(1)} %get-tuple-element.28, bf16[1024,512]{1,0:T(8,128)(2,1)S(1)} %get-tuple-element.27, bf16[1024,512]{1,0:T(8,128)(2,1)S(1)} %maximum_select_fusion.1, bf16[384,1024]{1,0:T(8,128)(2,1)S(1)} %get-tuple-element.30, ...), kind=kOutput, calls=%fused_computation.2 | convolution fusion | flops 3642163200 | bytes 9043968 | tf_op jit(solution)/shard_map/dot_general | solution.py:97
  57.2 1.6 copy.20
  61.9 1.5 fusion.16
  63.4 1.3 fusion.18
  68.1 1.5 fusion.22
  69.6 1.3 fusion.24
  72.7 1.5 fusion.19
  74.2 1.5 fusion.21
  75.8 3.5 %collective-permute-start.4 = (f32[3,8,384,1]{2,1,3,0:T(8,128)S(1)}, f32[3,8,384,1]{2,1,3,0:T(8,128)S(1)}, u32[]{:S(2)}, u32[]{:S(2)}) collective-permute-start(f32[3,8,384,1]{2,1,3,0:T(8,128)S(1)} %pad_maximum_fusion.5), channel_id=1, source_target_pairs={{0,4},{4,8},{8,12},{12,16},{16,20},{20,24},{24,28},{1,5},{5,9},{9,... | collective-permute-start | bytes 110600 | tf_op jit(solution)/shard_map/ppermute | solution.py:14
  84.7 2.4 %collective-permute-start.5 = (f32[3,8,384,1]{2,1,3,0:T(8,128)S(1)}, f32[3,8,384,1]{2,1,3,0:T(8,128)S(1)}, u32[]{:S(2)}, u32[]{:S(2)}) collective-permute-start(f32[3,8,384,1]{2,1,3,0:T(8,128)S(1)} %pad_maximum_fusion.5), channel_id=1, source_target_pairs={{4,0},{8,4},{12,8},{16,12},{20,16},{24,20},{28,24},{5,1},{9,5},{13... | collective-permute-start | bytes 110600 | tf_op jit(solution)/shard_map/ppermute | solution.py:14
  88.1 4.3 %collective-permute-start.6 = (bf16[384,512]{1,0:T(8,128)(2,1)}, bf16[384,512]{1,0:T(8,128)(2,1)S(1)}, u32[]{:S(2)}, u32[]{:S(2)}) collective-permute-start(bf16[384,512]{1,0:T(8,128)(2,1)} %bitcast.11), channel_id=1, source_target_pairs={{0,4},{4,8},{8,12},{12,16},{16,20},{20,24},{24,28},{1,5},{5,9},{9,... | collective-permute-start | bytes 1179656 | tf_op jit(solution)/shard_map/ppermute | solution.py:14
  92.4 1.9 collective-permute-start.7
  97.3 1.4 copy.28
  98.7 6.6 %all-to-all-start = ((bf16[16,64,512]{2,1,0:T(8,128)(2,1)}), bf16[16,64,512]{2,1,0:T(8,128)(2,1)}, u32[]{:S(2)}, u32[]{:S(2)}) async-start(bf16[16,64,512]{2,1,0:T(8,128)(2,1)} %bitcast.77), calls=%async_computation | async-start | bytes 2097152 | tf_op jit(solution)/shard_map/all_to_all | solution.py:57
  105.4 8.2 %fusion.113 = (bf16[8,768,384]{2,1,0:T(8,128)(2,1)}, f32[8,768,384]{2,1,0:T(8,128)}) fusion(f32[8,768]{1,0:T(8,128)S(1)} %get-tuple-element.35, f32[8,768]{1,0:T(8,128)S(1)} %get-tuple-element.36, bf16[8,1152,64]{1,2,0:T(8,128)(2,1)S(1)} %bitcast.161, bf16[8,384,64]{1,2,0:T(8,128)(2,1)S(1)} %copy-done.23, bf16[8,384,64]{1,2,0:T(8,128)(2,1)S(1)} %copy-done.24, ...), kind=kOutput, calls=%fused_computation.171 | convolution fusion | flops 315359232 | bytes 15679488 | tf_op jit(solution)/shard_map/hqd,hkd->hqk/dot_general | solution.py:185
  115.8 5.0 %multiply_convert_fusion = bf16[8,768,384]{2,1,0:T(8,128)(2,1)S(1)} fusion(f32[8,768,384]{2,1,0:T(8,128)} %get-tuple-element.62, f32[8,768]{1,0:T(8,128)S(1)} %get-tuple-element.34, bf16[8,768,64]{1,2,0:T(8,128)(2,1)S(1)} %bitcast.168, bf16[8,1152,64]{1,2,0:T(8,128)(2,1)} %bitcast.171), kind=kOutput, calls=%fused_computation | convolution fusion | flops 309067776 | bytes 15360000 | tf_op jit(solution)/shard_map/hqd,hkd->hqk/dot_general | solution.py:190
  120.9 3.2 %fusion.48 = bf16[8,384,64]{1,2,0:T(8,128)(2,1)S(1)} fusion(bf16[8,768,384]{2,1,0:T(8,128)(2,1)} %get-tuple-element.61, bf16[8,128,384]{2,1,0:T(8,128)(2,1)S(1)} %copy-done.19, bf16[8,128,384]{2,1,0:T(8,128)(2,1)S(1)} %copy-done.21, bf16[8,128,384]{2,1,0:T(8,128)(2,1)S(1)} %copy-done.20, bf16[8,768,64]{1,2,0:T(8,128)(2,1)S(1)} %bitcast.169, ...), kind=kOutput, calls=%fused_computation.66 | convolution fusion | flops 483852288 | bytes 8650752 | tf_op jit(solution)/shard_map/hqk,hqd->hkd/dot_general | solution.py:201
  124.2 1.6 fusion.45
  126.6 2.7 %convolution_convert_fusion.1 = bf16[1024,1024]{0,1:T(8,128)(2,1)} fusion(bf16[384,512]{0,1:T(8,128)(2,1)S(1)} %bitcast.191, bf16[384,512]{0,1:T(8,128)(2,1)S(1)} %bitcast.193, bf16[1,384,1024]{2,1,0:T(8,128)(2,1)S(1)} %copy-done.15), kind=kOutput, calls=%fused_computation.58 | convolution fusion | flops 807927808 | bytes 3670016 | tf_op jit(solution)/shard_map/tr,tf->rf/dot_general | solution.py:216
  129.6 9.2 %all-to-all-start.1 = ((bf16[16,64,1024]{2,1,0:T(8,128)(2,1)}), bf16[16,64,1024]{2,1,0:T(8,128)(2,1)}, u32[]{:S(2)}, u32[]{:S(2)}) async-start(bf16[16,64,1024]{2,1,0:T(8,128)(2,1)} %bitcast.170), calls=%async_computation.1 | async-start | bytes 4194304 | tf_op jit(solution)/shard_map/all_to_all | solution.py:57
  146.1 1.4 convert_reduce_fusion.1
  147.6 39.6 %all-to-all-done.1 = bf16[16,64,1024]{2,1,0:T(8,128)(2,1)} async-done(((bf16[16,64,1024]{2,1,0:T(8,128)(2,1)}), bf16[16,64,1024]{2,1,0:T(8,128)(2,1)}, u32[]{:S(2)}, u32[]{:S(2)}) %all-to-all-start.1) | async-done | bytes 2097184 | tf_op jit(solution)/shard_map/all_to_all | solution.py:57
  187.2 2.0 %convert_reduce_fusion = f32[64,1024]{1,0:T(8,128)S(1)} fusion(bf16[16,64,1024]{2,1,0:T(8,128)(2,1)} %all-to-all-done.1), kind=kLoop, calls=%fused_computation.19 | loop fusion | flops 2031616 | bytes 2359296 | tf_op jit(solution)/shard_map/reduce_sum | solution.py:59
  (142 shorter events, 34.3 us)
Async XLA Ops:
  7.2 11.7 %copy-start.33 = (s32[24,7]{0,1:T(8,128)S(1)}, s32[24,7]{0,1:T(8,128)}, u32[]{:S(2)}) copy-start(s32[24,7]{0,1:T(8,128)} %param.10) | copy-start | bytes 2020
  7.2 44.1 %all-gather.2.cloned.1.call-start = ((), (), s32[]{:S(2)}) async-start(), calls=%async_computation.2 | async-start | bytes 3145728 | tf_op jit(solution)/shard_map/all_gather | solution.py:92
  8.3 19.2 %collective-permute-start.1 = (bf16[384,512]{1,0:T(8,128)(2,1)S(1)}, bf16[384,512]{1,0:T(8,128)(2,1)S(1)}, u32[]{:S(2)}, u32[]{:S(2)}) collective-permute-start(bf16[384,512]{1,0:T(8,128)(2,1)S(1)} %dynamic-slice_bitcast_fusion), channel_id=1, source_target_pairs={{4,0},{8,4},{12,8},{16,12},{20,16},{24,20},{28,24},{5,1},{9,5},{13... | collective-permute-start | bytes 1179656 | tf_op jit(solution)/shard_map/ppermute | solution.py:14
  10.7 19.7 %collective-permute-start = (bf16[384,512]{1,0:T(8,128)(2,1)S(1)}, bf16[384,512]{1,0:T(8,128)(2,1)S(1)}, u32[]{:S(2)}, u32[]{:S(2)}) collective-permute-start(bf16[384,512]{1,0:T(8,128)(2,1)S(1)} %dynamic-slice_bitcast_fusion), channel_id=1, source_target_pairs={{0,4},{4,8},{8,12},{12,16},{16,20},{20,24},{24,28},{1,5},{5,9},{9,... | collective-permute-start | bytes 1179656 | tf_op jit(solution)/shard_map/ppermute | solution.py:14
  15.0 19.1 %collective-permute-start.3 = (bf16[512,512]{1,0:T(8,128)(2,1)}, bf16[512,512]{1,0:T(8,128)(2,1)}, u32[]{:S(2)}, u32[]{:S(2)}) collective-permute-start(bf16[512,512]{1,0:T(8,128)(2,1)} %param.7), channel_id=1, source_target_pairs={{0,2},{2,0},{1,3},{3,1},{4,6},{6,4},{5,7},{7,5},{8,10},{10,8},{9,1... | collective-permute-start | bytes 1572872 | tf_op jit(solution)/shard_map/ppermute | solution.py:50
  30.4 5.6 %collective-permute-start.2 = (bf16[2,384,512]{2,1,0:T(8,128)(2,1)S(1)}, bf16[2,384,512]{2,1,0:T(8,128)(2,1)S(1)}, u32[]{:S(2)}, u32[]{:S(2)}) collective-permute-start(bf16[2,384,512]{2,1,0:T(8,128)(2,1)S(1)} %pad_maximum_fusion.1), channel_id=1, source_target_pairs={{0,1},{1,0},{2,3},{3,2},{4,5},{5,4},{6,7},{7,6},{8,9},{9,8},{10,11... | collective-permute-start | bytes 2359304 | tf_op jit(solution)/shard_map/ppermute | solution.py:42
  36.0 17.0 %copy-start.1 = (bf16[1024,512]{1,0:T(8,128)(2,1)}, bf16[1024,512]{1,0:T(8,128)(2,1)S(1)}, u32[]{:S(2)}) copy-start(bf16[1024,512]{1,0:T(8,128)(2,1)S(1)} %maximum_select_fusion.1) | copy-start | bytes 3145732
  36.4 16.6 %copy-start.13 = (bf16[1,384,1024]{2,1,0:T(8,128)(2,1)S(1)}, bf16[1,384,1024]{2,1,0:T(8,128)(2,1)}, u32[]{:S(2)}) copy-start(bf16[1,384,1024]{2,1,0:T(8,128)(2,1)} %param.6) | copy-start | bytes 2359300
  64.8 29.6 %copy-start.3 = (bf16[8,128,896]{2,1,0:T(8,128)(2,1)}, bf16[8,128,896]{2,1,0:T(8,128)(2,1)S(1)}, u32[]{:S(2)}) copy-start(bf16[8,128,896]{2,1,0:T(8,128)(2,1)S(1)} %get-tuple-element.23) | copy-start | bytes 5505028
  70.9 24.4 %copy-start.5 = (bf16[8,128,896]{2,1,0:T(8,128)(2,1)}, bf16[8,128,896]{2,1,0:T(8,128)(2,1)S(1)}, u32[]{:S(2)}) copy-start(bf16[8,128,896]{2,1,0:T(8,128)(2,1)S(1)} %get-tuple-element.19) | copy-start | bytes 5505028
  75.8 20.6 %copy-start.7 = (bf16[8,128,896]{2,1,0:T(8,128)(2,1)}, bf16[8,128,896]{2,1,0:T(8,128)(2,1)S(1)}, u32[]{:S(2)}) copy-start(bf16[8,128,896]{2,1,0:T(8,128)(2,1)S(1)} %get-tuple-element.21) | copy-start | bytes 5505028
  75.8 5.2 %copy-start.14 = (bf16[1,384,1024]{2,1,0:T(8,128)(2,1)S(1)}, bf16[1,384,1024]{2,1,0:T(8,128)(2,1)}, u32[]{:S(2)}) copy-start(bf16[1,384,1024]{2,1,0:T(8,128)(2,1)} %param.6) | copy-start | bytes 2359300
  75.8 29.5 %collective-permute-start.4 = (f32[3,8,384,1]{2,1,3,0:T(8,128)S(1)}, f32[3,8,384,1]{2,1,3,0:T(8,128)S(1)}, u32[]{:S(2)}, u32[]{:S(2)}) collective-permute-start(f32[3,8,384,1]{2,1,3,0:T(8,128)S(1)} %pad_maximum_fusion.5), channel_id=1, source_target_pairs={{0,4},{4,8},{8,12},{12,16},{16,20},{20,24},{24,28},{1,5},{5,9},{9,... | collective-permute-start | bytes 110600 | tf_op jit(solution)/shard_map/ppermute | solution.py:14
  84.7 20.6 %collective-permute-start.5 = (f32[3,8,384,1]{2,1,3,0:T(8,128)S(1)}, f32[3,8,384,1]{2,1,3,0:T(8,128)S(1)}, u32[]{:S(2)}, u32[]{:S(2)}) collective-permute-start(f32[3,8,384,1]{2,1,3,0:T(8,128)S(1)} %pad_maximum_fusion.5), channel_id=1, source_target_pairs={{4,0},{8,4},{12,8},{16,12},{20,16},{24,20},{28,24},{5,1},{9,5},{13... | collective-permute-start | bytes 110600 | tf_op jit(solution)/shard_map/ppermute | solution.py:14
  88.1 25.5 %collective-permute-start.6 = (bf16[384,512]{1,0:T(8,128)(2,1)}, bf16[384,512]{1,0:T(8,128)(2,1)S(1)}, u32[]{:S(2)}, u32[]{:S(2)}) collective-permute-start(bf16[384,512]{1,0:T(8,128)(2,1)} %bitcast.11), channel_id=1, source_target_pairs={{0,4},{4,8},{8,12},{12,16},{16,20},{20,24},{24,28},{1,5},{5,9},{9,... | collective-permute-start | bytes 1179656 | tf_op jit(solution)/shard_map/ppermute | solution.py:14
  92.4 21.9 %collective-permute-start.7 = (bf16[384,512]{1,0:T(8,128)(2,1)}, bf16[384,512]{1,0:T(8,128)(2,1)}, u32[]{:S(2)}, u32[]{:S(2)}) collective-permute-start(bf16[384,512]{1,0:T(8,128)(2,1)} %bitcast.11), channel_id=1, source_target_pairs={{4,0},{8,4},{12,8},{16,12},{20,16},{24,20},{28,24},{5,1},{9,5},{13... | collective-permute-start | bytes 1179656 | tf_op jit(solution)/shard_map/ppermute | solution.py:14
  95.3 10.0 %copy-start.23 = (bf16[8,384,64]{1,2,0:T(8,128)(2,1)S(1)}, bf16[8,384,64]{1,2,0:T(8,128)(2,1)}, u32[]{:S(2)}) copy-start(bf16[8,384,64]{1,2,0:T(8,128)(2,1)} %get-tuple-element.32) | copy-start | bytes 1179652
  95.3 10.0 %copy-start.24 = (bf16[8,384,64]{1,2,0:T(8,128)(2,1)S(1)}, bf16[8,384,64]{1,2,0:T(8,128)(2,1)}, u32[]{:S(2)}) copy-start(bf16[8,384,64]{1,2,0:T(8,128)(2,1)} %get-tuple-element.33) | copy-start | bytes 1179652
  98.7 30.9 %all-to-all-start = ((bf16[16,64,512]{2,1,0:T(8,128)(2,1)}), bf16[16,64,512]{2,1,0:T(8,128)(2,1)}, u32[]{:S(2)}, u32[]{:S(2)}) async-start(bf16[16,64,512]{2,1,0:T(8,128)(2,1)} %bitcast.77), calls=%async_computation | async-start | bytes 2097152 | tf_op jit(solution)/shard_map/all_to_all | solution.py:57
  115.8 5.0 %copy-start.19 = (bf16[8,128,384]{2,1,0:T(8,128)(2,1)S(1)}, bf16[8,128,384]{2,1,0:T(8,128)(2,1)}, u32[]{:S(2)}) copy-start(bf16[8,128,384]{2,1,0:T(8,128)(2,1)} %slice.221) | copy-start | bytes 2359300
  115.8 5.0 %copy-start.20 = (bf16[8,128,384]{2,1,0:T(8,128)(2,1)S(1)}, bf16[8,128,384]{2,1,0:T(8,128)(2,1)}, u32[]{:S(2)}) copy-start(bf16[8,128,384]{2,1,0:T(8,128)(2,1)} %slice.219) | copy-start | bytes 2359300
  115.8 5.0 %copy-start.21 = (bf16[8,128,384]{2,1,0:T(8,128)(2,1)S(1)}, bf16[8,128,384]{2,1,0:T(8,128)(2,1)}, u32[]{:S(2)}) copy-start(bf16[8,128,384]{2,1,0:T(8,128)(2,1)} %slice.220) | copy-start | bytes 2359300
  115.8 5.0 %copy-start.27 = (bf16[1,384,512]{1,2,0:T(8,128)(2,1)S(1)}, bf16[1,384,512]{1,2,0:T(8,128)(2,1)}, u32[]{:S(2)}) copy-start(bf16[1,384,512]{1,2,0:T(8,128)(2,1)} %copy.21) | copy-start | bytes 1179652
  120.9 3.3 %copy-start.16 = (bf16[8,128,384]{2,1,0:T(8,128)(2,1)S(1)}, bf16[8,128,384]{2,1,0:T(8,128)(2,1)}, u32[]{:S(2)}) copy-start(bf16[8,128,384]{2,1,0:T(8,128)(2,1)} %slice.213) | copy-start | bytes 2359300
  120.9 3.3 %copy-start.17 = (bf16[8,128,384]{2,1,0:T(8,128)(2,1)S(1)}, bf16[8,128,384]{2,1,0:T(8,128)(2,1)}, u32[]{:S(2)}) copy-start(bf16[8,128,384]{2,1,0:T(8,128)(2,1)} %slice.211) | copy-start | bytes 2359300
  120.9 3.3 %copy-start.18 = (bf16[8,128,384]{2,1,0:T(8,128)(2,1)S(1)}, bf16[8,128,384]{2,1,0:T(8,128)(2,1)}, u32[]{:S(2)}) copy-start(bf16[8,128,384]{2,1,0:T(8,128)(2,1)} %slice.212) | copy-start | bytes 2359300
  120.9 3.3 %copy-start.22 = (bf16[8,384,64]{1,2,0:T(8,128)(2,1)S(1)}, bf16[8,384,64]{1,2,0:T(8,128)(2,1)}, u32[]{:S(2)}) copy-start(bf16[8,384,64]{1,2,0:T(8,128)(2,1)} %get-tuple-element.31) | copy-start | bytes 1179652
  126.6 12.3 %copy-start = (bf16[2,1024,512]{2,1,0:T(8,128)(2,1)S(1)}, bf16[2,1024,512]{2,1,0:T(8,128)(2,1)}, u32[]{:S(2)}) copy-start(bf16[2,1024,512]{2,1,0:T(8,128)(2,1)} %all-gather.2.cloned.1.call-done) | copy-start | bytes 6291460
  129.3 9.6 %copy-start.30 = (bf16[8,384,64]{1,2,0:T(8,128)(2,1)S(1)}, bf16[8,384,64]{1,2,0:T(8,128)(2,1)}, u32[]{:S(2)}) copy-start(bf16[8,384,64]{1,2,0:T(8,128)(2,1)} %copy-done.29) | copy-start | bytes 1179652
  129.3 10.3 %copy-start.32 = (bf16[8,384,64]{1,2,0:T(8,128)(2,1)S(1)}, bf16[8,384,64]{1,2,0:T(8,128)(2,1)}, u32[]{:S(2)}) copy-start(bf16[8,384,64]{1,2,0:T(8,128)(2,1)} %copy-done.31) | copy-start | bytes 1179652
  129.6 57.5 %all-to-all-start.1 = ((bf16[16,64,1024]{2,1,0:T(8,128)(2,1)}), bf16[16,64,1024]{2,1,0:T(8,128)(2,1)}, u32[]{:S(2)}, u32[]{:S(2)}) async-start(bf16[16,64,1024]{2,1,0:T(8,128)(2,1)} %bitcast.170), calls=%async_computation.1 | async-start | bytes 4194304 | tf_op jit(solution)/shard_map/all_to_all | solution.py:57
  140.9 4.0 %collective-permute-start.8 = (bf16[384,1024]{1,0:T(8,128)(2,1)S(1)}, bf16[384,1024]{1,0:T(8,128)(2,1)S(1)}, u32[]{:S(2)}, u32[]{:S(2)}) collective-permute-start(bf16[384,1024]{1,0:T(8,128)(2,1)S(1)} %add_convert_fusion.1), channel_id=1, source_target_pairs={{0,1},{1,0},{2,3},{3,2},{4,5},{5,4},{6,7},{7,6},{8,9},{9,8},{10,11... | collective-permute-start | bytes 2359304 | tf_op jit(solution)/shard_map/ppermute | solution.py:67
  (14 other events, 23.5 us)
Sparse Core Ops, SparseCore 0:
  19.0 32.2 all-gather.1

commit v8 on v7

--- a/solution.py
+++ b/solution.py
@@ -120,53 +120,6 @@
         return jnp.repeat(picked, BLOCK)[None, None, :]
 
     own_low, own_high = REACH, REACH + blocks - 1
-    outs, query_grads, tops, totals, deltas = [], [], [], [], []
-    own_score_grads, own_weights = [], []
-    for i in range(blocks):
-        at = REACH + i
-        query_block = rows(query_h, at)
-        upstream_block = rows(own_upstream, i)
-        key_window = rows(key_h, i, span_len)
-        value_window = rows(value_h, i, span_len)
-        scores = (
-            jnp.einsum("hqd,hkd->hqk", query_block, key_window, preferred_element_type=jnp.float32)
-            * score_scale
-        )
-        probability, row_top, row_total = softmax_stats(scores, seen_keys(at, i, i + 2 * REACH))
-        weights = probability.astype(jnp.bfloat16)
-        outs.append(
-            jnp.einsum("hqk,hkd->hqd", weights, value_window, preferred_element_type=jnp.float32)
-        )
-        prob_grad = jnp.einsum(
-            "hqd,hkd->hqk", upstream_block, value_window, preferred_element_type=jnp.float32
-        )
-        row_delta = jnp.sum(probability * prob_grad, axis=2, keepdims=True)
-        score_grad = (probability * (prob_grad - row_delta)).astype(jnp.bfloat16)
-        query_grads.append(
-            score_scale
-            * jnp.einsum("hqk,hkd->hqd", score_grad, key_window, preferred_element_type=jnp.float32)
-        )
-        tops.append(row_top)
-        totals.append(row_total)
-        deltas.append(row_delta)
-        cut = slice((own_low - i) * BLOCK, (own_high - i + 1) * BLOCK)
-        own_score_grads.append(score_grad[:, :, cut])
-        own_weights.append(weights[:, :, cut])
-
-    attended = token_major(jnp.concatenate(outs, axis=1).astype(jnp.bfloat16))[None]
-    query_grad = token_major(jnp.concatenate(query_grads, axis=1).astype(jnp.bfloat16))
-
-    term_query = jnp.einsum(
-        "tr,tf->rf", tokens, query_grad, preferred_element_type=jnp.float32
-    ).astype(jnp.bfloat16)
-    reduced_query = summed_rows(term_query)
-
-    stats = jnp.stack(
-        [jnp.concatenate(tops, axis=1), jnp.concatenate(totals, axis=1), jnp.concatenate(deltas, axis=1)]
-    )
-    stats_left = shifted(stats[:, :, length - halo :], "ctx", 1)
-    stats_right = shifted(stats[:, :, :halo], "ctx", -1)
-
     near = list(range(REACH)) + list(range(REACH + blocks, frame_blocks))
     allowed = []
     for at in near:
@@ -176,34 +129,118 @@
             row.append(frame_mask[at, slot] > 0 if 0 <= slot < span_len else jnp.zeros((), bool))
         allowed.append(jnp.stack(row))
     allowed = jnp.repeat(jnp.repeat(jnp.stack(allowed), BLOCK, axis=0), BLOCK, axis=1)[None]
-    near_stats = jnp.concatenate([stats_left, stats_right], axis=2)
-    top, total, delta = near_stats[0], near_stats[1], near_stats[2]
-    near_query = jnp.concatenate([rows(query_h, 0, REACH), rows(query_h, REACH + blocks, REACH)], axis=1)
-    key_part = rows(key_h, own_low, blocks)
-    value_part = rows(value_h, own_low, blocks)
-    scores = (
-        jnp.einsum("hqd,hkd->hqk", near_query, key_part, preferred_element_type=jnp.float32)
-        * score_scale
-    )
-    probability = jnp.where(allowed, jnp.exp(scores - top) / total, 0.0)
-    weights = probability.astype(jnp.bfloat16)
-    prob_grad = jnp.einsum(
-        "hqd,hkd->hqk", near_upstream, value_part, preferred_element_type=jnp.float32
-    )
-    score_grad = (probability * (prob_grad - delta)).astype(jnp.bfloat16)
-    all_score_grads = jnp.concatenate(own_score_grads + [score_grad], axis=1)
-    all_weights = jnp.concatenate(own_weights + [weights], axis=1)
-    all_queries = jnp.concatenate([rows(query_h, REACH, blocks), near_query], axis=1)
-    all_upstream = jnp.concatenate([own_upstream, near_upstream], axis=1)
-    key_own = score_scale * jnp.einsum(
-        "hqk,hqd->hkd", all_score_grads, all_queries, preferred_element_type=jnp.float32
-    )
-    value_own = jnp.einsum(
-        "hqk,hqd->hkd", all_weights, all_upstream, preferred_element_type=jnp.float32
-    )
-
-    key_grad = token_major(key_own).astype(jnp.bfloat16)
-    value_grad = token_major(value_own).astype(jnp.bfloat16)
+
+    def group_pass(query_g, key_g, value_g, own_up_g, near_up_g):
+        outs, query_grads, tops, totals, deltas = [], [], [], [], []
+        own_score_grads, own_weights = [], []
+        for i in range(blocks):
+            at = REACH + i
+            query_block = rows(query_g, at)
+            upstream_block = rows(own_up_g, i)
+            key_window = rows(key_g, i, span_len)
+            value_window = rows(value_g, i, span_len)
+            scores = (
+                jnp.einsum(
+                    "hqd,hkd->hqk", query_block, key_window, preferred_element_type=jnp.float32
+                )
+                * score_scale
+            )
+            probability, row_top, row_total = softmax_stats(scores, seen_keys(at, i, i + 2 * REACH))
+            weights = probability.astype(jnp.bfloat16)
+            outs.append(
+                jnp.einsum("hqk,hkd->hqd", weights, value_window, preferred_element_type=jnp.float32)
+            )
+            prob_grad = jnp.einsum(
+                "hqd,hkd->hqk", upstream_block, value_window, preferred_element_type=jnp.float32
+            )
+            row_delta = jnp.sum(probability * prob_grad, axis=2, keepdims=True)
+            score_grad = (probability * (prob_grad - row_delta)).astype(jnp.bfloat16)
+            query_grads.append(
+                score_scale
+                * jnp.einsum(
+                    "hqk,hkd->hqd", score_grad, key_window, preferred_element_type=jnp.float32
+                )
+            )
+            tops.append(row_top)
+            totals.append(row_total)
+            deltas.append(row_delta)
+            cut = slice((own_low - i) * BLOCK, (own_high - i + 1) * BLOCK)
+            own_score_grads.append(score_grad[:, :, cut])
+            own_weights.append(weights[:, :, cut])
+
+        out_g = jnp.concatenate(outs, axis=1).astype(jnp.bfloat16)
+        query_grad_g = jnp.concatenate(query_grads, axis=1).astype(jnp.bfloat16)
+        term_query_g = summed_rows(
+            jnp.einsum(
+                "tr,tf->rf", tokens, token_major(query_grad_g), preferred_element_type=jnp.float32
+            ).astype(jnp.bfloat16)
+        )
+
+        stats = jnp.stack(
+            [
+                jnp.concatenate(tops, axis=1),
+                jnp.concatenate(totals, axis=1),
+                jnp.concatenate(deltas, axis=1),
+            ]
+        )
+        stats_left = shifted(stats[:, :, length - halo :], "ctx", 1)
+        stats_right = shifted(stats[:, :, :halo], "ctx", -1)
+        near_stats = jnp.concatenate([stats_left, stats_right], axis=2)
+        top, total, delta = near_stats[0], near_stats[1], near_stats[2]
+        near_query = jnp.concatenate(
+            [rows(query_g, 0, REACH), rows(query_g, REACH + blocks, REACH)], axis=1
+        )
+        key_part = rows(key_g, own_low, blocks)
+        value_part = rows(value_g, own_low, blocks)
+        scores = (
+            jnp.einsum("hqd,hkd->hqk", near_query, key_part, preferred_element_type=jnp.float32)
+            * score_scale
+        )
+        probability = jnp.where(allowed, jnp.exp(scores - top) / total, 0.0)
+        weights = probability.astype(jnp.bfloat16)
+        prob_grad = jnp.einsum(
+            "hqd,hkd->hqk", near_up_g, value_part, preferred_element_type=jnp.float32
+        )
+        score_grad = (probability * (prob_grad - delta)).astype(jnp.bfloat16)
+        all_score_grads = jnp.concatenate(own_score_grads + [score_grad], axis=1)
+        all_weights = jnp.concatenate(own_weights + [weights], axis=1)
+        all_queries = jnp.concatenate([rows(query_g, REACH, blocks), near_query], axis=1)
+        all_upstream = jnp.concatenate([own_up_g, near_up_g], axis=1)
+        key_own = score_scale * jnp.einsum(
+            "hqk,hqd->hkd", all_score_grads, all_queries, preferred_element_type=jnp.float32
+        )
+        value_own = jnp.einsum(
+            "hqk,hqd->hkd", all_weights, all_upstream, preferred_element_type=jnp.float32
+        )
+        key_grad_g = token_major(key_own).astype(jnp.bfloat16)
+        value_grad_g = token_major(value_own).astype(jnp.bfloat16)
+        term_kv_g = summed_rows(
+            jnp.einsum(
+                "tr,tf->rf",
+                tokens,
+                jnp.concatenate([key_grad_g, value_grad_g], axis=1),
+                preferred_element_type=jnp.float32,
+            ).astype(jnp.bfloat16)
+        )
+        return out_g, query_grad_g, key_grad_g, value_grad_g, term_query_g, term_kv_g
+
+    groups = 2 if heads % 2 == 0 else 1
+    size = heads // groups
+    results = []
+    for g in range(groups):
+        pick = slice(g * size, (g + 1) * size)
+        results.append(
+            group_pass(query_h[pick], key_h[pick], value_h[pick], own_upstream[pick], near_upstream[pick])
+        )
+    out_all = jnp.concatenate([r[0] for r in results], axis=0)
+    attended = token_major(out_all)[None]
+    query_grad = token_major(jnp.concatenate([r[1] for r in results], axis=0))
+    key_grad = jnp.concatenate([r[2] for r in results], axis=1)
+    value_grad = jnp.concatenate([r[3] for r in results], axis=1)
+    width = size * HD
+    reduced_query = jnp.concatenate([r[4] for r in results], axis=1)
+    reduced_key = jnp.concatenate([r[5][:, :width] for r in results], axis=1)
+    reduced_value = jnp.concatenate([r[5][:, width:] for r in results], axis=1)
 
     contract = (((1,), (1,)), ((), ()))
     partial_input = (
@@ -213,14 +250,7 @@
     )
     grad_input = section_sum(partial_input)[None]
 
-    term_kv = jnp.einsum(
-        "tr,tf->rf",
-        tokens,
-        jnp.concatenate([key_grad, value_grad], axis=1),
-        preferred_element_type=jnp.float32,
-    ).astype(jnp.bfloat16)
-    reduced_kv = summed_rows(term_kv).reshape(-1, 2, features)
-    summed = jnp.concatenate([reduced_query[:, None], reduced_kv], axis=1)
+    summed = jnp.stack([reduced_query, reduced_key, reduced_value], axis=1)
     grad_weights = summed / lax.axis_size("dp")
     return (attended, grad_input, grad_weights)
 

time: 198 us -> 247 us (1.25)
  matrix products: 39 us -> 65.2 us
  local copies, waits for them, and re-layouts: 23.9 us -> 42 us
  waiting for transfers between devices: 57.6 us -> 44.8 us
  starting transfers between devices: 36.6 us -> 48.5 us
  other arithmetic: 18.1 us -> 21.7 us
    dot_general x18 -> x36, matrix products: 33.2 us -> 54.2 us  [the longest x2 10.2 us: group_pass(): jnp.einsum('hqd,hkd->hqk', near_query, key_part, preferred_element_type=j...]
    all_to_all x2 -> x4, waiting for transfers between devices: 39.9 us -> 25.3 us  [summed_rows(): parts = lax.all_to_all(term, group, 0, 0, tiled=True)]
    all_to_all x2 -> x4, starting transfers between devices: 15.8 us -> 22 us  [summed_rows(): parts = lax.all_to_all(term, group, 0, 0, tiled=True)]
    ppermute x6 -> x8, starting transfers between devices: 18.9 us -> 24.6 us  [shifted(): lax.ppermute(value, axis, [(source, source + steps) for source in range(l...]
    slice x6 -> x16, local copies, waits for them, and re-layouts: 5.86 us -> 11.4 us  [the longest x6 4.89 us: group_pass(): own_score_grads.append(score_grad[:, :, cut])]
    convert_element_type x1 -> x4, local copies, waits for them, and re-layouts: 1.36 us -> 6.64 us  [the longest x2 4.63 us: group_pass(): term_kv_g = summed_rows(jnp.einsum('tr,tf->rf', tokens, jnp.concatenate([...]
    ppermute x6 -> x8, waiting for transfers between devices: 2.9 us -> 6.17 us  [shifted(): lax.ppermute(value, axis, [(source, source + steps) for source in range(l...]
    unnamed x74 -> x100, local copies, waits for them, and re-layouts: 6.62 us -> 7.32 us
  transfers between devices with their start and end apart: 12 -> 16, of which waited for: 4 -> 6; matrix products, arithmetic and copies ran while one was open for 25% -> 29% of each run, Pallas kernels for 0% -> 0%
where the time goes in v8:
time: 247 us; the launch traced here: 245 us
  matrix products  65.2 us (26%)
  starting transfers between devices  48.5 us (20%)
  waiting for transfers between devices  44.8 us (18%)
  local copies, waits for them, and re-layouts  42 us (17%)
  between operations  22.5 us (9%)
  other arithmetic  21.7 us (9%)
    all_to_all x4, waiting for transfers between devices, summed_rows(): parts = lax.all_to_all(term, group, 0, 0, tiled=True)  25.3 us
    ppermute x8, starting transfers between devices, shifted(): lax.ppermute(value, axis, [(source, source + steps) for source in range(l...  24.6 us
    all_to_all x4, starting transfers between devices, summed_rows(): parts = lax.all_to_all(term, group, 0, 0, tiled=True)  22 us
    all_gather x1, waiting for transfers between devices, per_device(): lax.all_gather(jnp.stack([w_key, w_value]), 'dp', axis=1, tiled=True)  13.3 us
    dot_general x2, matrix products, group_pass(): jnp.einsum('hqd,hkd->hqk', near_query, key_part, preferred_element_type=j...  10.2 us
    dot_general x6, matrix products, group_pass(): jnp.einsum('hqd,hkd->hqk', query_block, key_window, preferred_element_typ...  9.39 us
    dot_general x6, matrix products, group_pass(): jnp.einsum('hqd,hkd->hqk', upstream_block, value_window, preferred_elemen...  7.87 us
    unnamed x100, local copies, waits for them, and re-layouts  7.32 us
  transfers between devices with their start and end apart: 16, of which 6 were waited for; matrix products, arithmetic and copies ran while one was open for 29% of the time, Pallas kernels for 0%

profile of v8, /device:TPU:12, one launch (start us, length us, event | category | flops | bytes accessed | tf_op | source)
XLA Modules:
  0.0 244.6 jit_solution(4193012258092473903)
XLA Ops:
  8.3 2.4 collective-permute-start.1
  10.7 4.3 %collective-permute-start = (bf16[384,512]{1,0:T(8,128)(2,1)S(1)}, bf16[384,512]{1,0:T(8,128)(2,1)S(1)}, u32[]{:S(2)}, u32[]{:S(2)}) collective-permute-start(bf16[384,512]{1,0:T(8,128)(2,1)S(1)} %dynamic-slice_bitcast_fusion), channel_id=1, source_target_pairs={{0,4},{4,8},{8,12},{12,16},{16,20},{20,24},{24,28},{1,5},{5,9},{9,... | collective-permute-start | bytes 1179656 | tf_op jit(solution)/shard_map/ppermute | solution.py:14
  16.6 2.3 pad_maximum_fusion
  27.8 2.5 %collective-permute-done = bf16[384,512]{1,0:T(8,128)(2,1)S(1)} collective-permute-done((bf16[384,512]{1,0:T(8,128)(2,1)S(1)}, bf16[384,512]{1,0:T(8,128)(2,1)S(1)}, u32[]{:S(2)}, u32[]{:S(2)}) %collective-permute-start) | collective-permute-done | bytes 393248 | tf_op jit(solution)/shard_map/ppermute | solution.py:14
  38.0 13.3 %all-gather.2.cloned.1.call-done = bf16[2,1024,512]{2,1,0:T(8,128)(2,1)} async-done(((bf16[2,512,512]{2,1,0:T(8,128)(2,1)}), bf16[2,1024,512]{2,1,0:T(8,128)(2,1)}) %all-gather.2.cloned.1.call-update) | async-done | bytes 2097168 | tf_op jit(solution)/shard_map/all_gather | solution.py:92
  53.1 3.8 %convolution_convert_fusion = bf16[1152,1536]{1,0:T(8,128)(2,1)S(1)} fusion(bf16[1024,512]{1,0:T(8,128)(2,1)S(1)} %get-tuple-element.34, bf16[1024,512]{1,0:T(8,128)(2,1)S(1)} %get-tuple-element.33, bf16[1024,512]{1,0:T(8,128)(2,1)S(1)} %maximum_select_fusion.1, bf16[384,1024]{1,0:T(8,128)(2,1)S(1)} %copy-done.15, bf16[384,1024]{1,0:T(8,128)(2,1)S(1)} %bitcast.272, ...), kind=kOutput, calls=%fused_computation | convolution fusion | flops 3642163200 | bytes 9043968 | tf_op jit(solution)/shard_map/dot_general | solution.py:97
  63.3 2.4 copy.22
  65.7 2.4 copy.21
  68.0 2.5 %fusion.206 = (bf16[4,384,64]{1,2,0:T(8,128)(2,1)}, bf16[4,384,64]{1,2,0:T(8,128)(2,1)}, bf16[4,384,64]{1,2,0:T(8,128)(2,1)}, bf16[4,384,64]{1,2,0:T(8,128)(2,1)...) fusion(bf16[8,1152,64]{1,2,0:T(8,128)(2,1)} %bitcast.265), kind=kLoop, calls=%fused_computation.300 | loop fusion | bytes 2359296 | tf_op jit(solution)/shard_map/slice | solution.py:116
  103.2 2.5 %collective-permute-start.9 = (f32[3,4,384,1]{2,1,3,0:T(4,128)S(1)}, f32[3,4,384,1]{2,1,3,0:T(4,128)S(1)}, u32[]{:S(2)}, u32[]{:S(2)}) collective-permute-start(f32[3,4,384,1]{2,1,3,0:T(4,128)S(1)} %pad_maximum_fusion.14), channel_id=1, source_target_pairs={{4,0},{8,4},{12,8},{16,12},{20,16},{24,20},{28,24},{5,1},{9,5},{13... | collective-permute-start | bytes 55304 | tf_op jit(solution)/shard_map/ppermute | solution.py:14
  105.7 4.3 %collective-permute-start.8 = (f32[3,4,384,1]{2,1,3,0:T(4,128)S(1)}, f32[3,4,384,1]{2,1,3,0:T(4,128)}, u32[]{:S(2)}, u32[]{:S(2)}) collective-permute-start(f32[3,4,384,1]{2,1,3,0:T(4,128)S(1)} %pad_maximum_fusion.14), channel_id=1, source_target_pairs={{0,4},{4,8},{8,12},{12,16},{16,20},{20,24},{24,28},{1,5},{5,9},{9,... | collective-permute-start | bytes 55304 | tf_op jit(solution)/shard_map/ppermute | solution.py:14
  111.9 4.8 %collective-permute-start.4 = (f32[3,4,384,1]{2,1,3,0:T(4,128)S(1)}, f32[3,4,384,1]{2,1,3,0:T(4,128)}, u32[]{:S(2)}, u32[]{:S(2)}) collective-permute-start(f32[3,4,384,1]{2,1,3,0:T(4,128)S(1)} %pad_maximum_fusion.13), channel_id=1, source_target_pairs={{0,4},{4,8},{8,12},{12,16},{16,20},{20,24},{24,28},{1,5},{5,9},{9,... | collective-permute-start | bytes 55304 | tf_op jit(solution)/shard_map/ppermute | solution.py:14
  126.7 6.5 %all-to-all-start.1 = ((bf16[16,64,256]{2,1,0:T(8,128)(2,1)}), bf16[16,64,256]{2,1,0:T(8,128)(2,1)}, u32[]{:S(2)}, u32[]{:S(2)}) async-start(bf16[16,64,256]{2,1,0:T(8,128)(2,1)} %bitcast.104), calls=%async_computation.1 | async-start | bytes 1048576 | tf_op jit(solution)/shard_map/all_to_all | solution.py:57
  134.6 2.5 %collective-permute-start.7 = (bf16[384,512]{1,0:T(8,128)(2,1)S(1)}, bf16[384,512]{1,0:T(8,128)(2,1)S(1)}, u32[]{:S(2)}, u32[]{:S(2)}) collective-permute-start(bf16[384,512]{1,0:T(8,128)(2,1)S(1)} %bitcast.297), channel_id=1, source_target_pairs={{4,0},{8,4},{12,8},{16,12},{20,16},{24,20},{28,24},{5,1},{9,5},{13... | collective-permute-start | bytes 1179656 | tf_op jit(solution)/shard_map/ppermute | solution.py:14
  139.2 5.0 %fusion.212 = (bf16[4,768,384]{2,1,0:T(8,128)(2,1)}, f32[4,768,384]{2,1,0:T(8,128)}) fusion(f32[4,768]{1,0:T(4,128)S(1)} %get-tuple-element.64, f32[4,768]{1,0:T(4,128)S(1)} %get-tuple-element.65, bf16[8,1152,64]{1,2,0:T(8,128)(2,1)} %bitcast.251, bf16[4,384,64]{1,2,0:T(8,128)(2,1)} %get-tuple-element.50, bf16[4,384,64]{1,2,0:T(8,128)(2,1)} %get-tuple-element.51, ...), kind=kOutput, calls=%fused_computation.306 | convolution fusion | flops 157679616 | bytes 7987200 | tf_op jit(solution)/shard_map/hqd,hkd->hqk/dot_general | solution.py:196
  144.2 5.2 %fusion.213 = (bf16[4,768,384]{2,1,0:T(8,128)(2,1)}, f32[4,768,384]{2,1,0:T(8,128)}) fusion(f32[4,768]{1,0:T(4,128)S(1)} %get-tuple-element.67, f32[4,768]{1,0:T(4,128)S(1)} %get-tuple-element.68, bf16[8,1152,64]{1,2,0:T(8,128)(2,1)} %bitcast.252, bf16[4,384,64]{1,2,0:T(8,128)(2,1)S(1)} %copy-done.29, bf16[4,384,64]{1,2,0:T(8,128)(2,1)S(1)} %copy-done.31, ...), kind=kOutput, calls=%fused_computation.307 | convolution fusion | flops 157679616 | bytes 7987200 | tf_op jit(solution)/shard_map/hqd,hkd->hqk/dot_general | solution.py:196
  150.2 3.6 %collective-permute-done.7 = bf16[384,512]{1,0:T(8,128)(2,1)S(1)} collective-permute-done((bf16[384,512]{1,0:T(8,128)(2,1)S(1)}, bf16[384,512]{1,0:T(8,128)(2,1)S(1)}, u32[]{:S(2)}, u32[]{:S(2)}) %collective-permute-start.7) | collective-permute-done | bytes 393248 | tf_op jit(solution)/shard_map/ppermute | solution.py:14
  155.2 4.1 %multiply_convert_fusion = bf16[4,768,384]{2,1,0:T(8,128)(2,1)} fusion(f32[4,768,384]{2,1,0:T(8,128)} %get-tuple-element.100, f32[4,768]{1,0:T(4,128)} %get-tuple-element.63, bf16[8,768,64]{1,2,0:T(8,128)(2,1)S(1)} %bitcast.274, bf16[8,1152,64]{1,2,0:T(8,128)(2,1)S(1)} %bitcast.247), kind=kOutput, calls=%fused_computation.1 | convolution fusion | flops 154533888 | bytes 8073216 | tf_op jit(solution)/shard_map/hqd,hkd->hqk/dot_general | solution.py:201
  159.2 4.8 %all-to-all-start = ((bf16[16,64,256]{2,1,0:T(8,128)(2,1)}), bf16[16,64,256]{2,1,0:T(8,128)(2,1)S(1)}, u32[]{:S(2)}, u32[]{:S(2)}) async-start(bf16[16,64,256]{2,1,0:T(8,128)(2,1)} %bitcast.284), calls=%async_computation | async-start | bytes 1048576 | tf_op jit(solution)/shard_map/all_to_all | solution.py:57
  164.8 2.9 %fusion.88 = bf16[4,384,64]{1,2,0:T(8,128)(2,1)S(1)} fusion(bf16[4,768,384]{2,1,0:T(8,128)(2,1)} %get-tuple-element.99, bf16[4,128,384]{2,1,0:T(8,128)(2,1)} %slice.430, bf16[4,128,384]{2,1,0:T(8,128)(2,1)} %slice.429, bf16[4,128,384]{2,1,0:T(8,128)(2,1)} %slice.428, bf16[4,768,64]{1,2,0:T(8,128)(2,1)S(1)} %get-tuple-element.56, ...), kind=kOutput, calls=%fused_computation.118 | convolution fusion | flops 241926144 | bytes 4325376 | tf_op jit(solution)/shard_map/hqk,hqd->hkd/dot_general | solution.py:212
  171.4 2.4 copy.37
  173.7 3.2 %all-to-all-done = bf16[16,64,256]{2,1,0:T(8,128)(2,1)S(1)} async-done(((bf16[16,64,256]{2,1,0:T(8,128)(2,1)}), bf16[16,64,256]{2,1,0:T(8,128)(2,1)S(1)}, u32[]{:S(2)}, u32[]{:S(2)}) %all-to-all-start) | async-done | bytes 524320 | tf_op jit(solution)/shard_map/all_to_all | solution.py:57
  177.0 5.7 %all-to-all-start.3 = ((bf16[16,64,512]{2,1,0:T(8,128)(2,1)}), bf16[16,64,512]{2,1,0:T(8,128)(2,1)}, u32[]{:S(2)}, u32[]{:S(2)}) async-start(bf16[16,64,512]{2,1,0:T(8,128)(2,1)} %bitcast.113), calls=%async_computation.3 | async-start | bytes 2097152 | tf_op jit(solution)/shard_map/all_to_all | solution.py:57
  182.7 2.6 %fusion.91 = bf16[4,384,64]{1,2,0:T(8,128)(2,1)S(1)} fusion(bf16[4,768,384]{2,1,0:T(8,128)(2,1)} %get-tuple-element.101, bf16[4,128,384]{2,1,0:T(8,128)(2,1)S(1)} %copy-done.22, bf16[4,128,384]{2,1,0:T(8,128)(2,1)} %slice.424, bf16[4,128,384]{2,1,0:T(8,128)(2,1)S(1)} %copy-done.19, bf16[4,768,64]{1,2,0:T(8,128)(2,1)} %get-tuple-element.55, ...), kind=kOutput, calls=%fused_computation.119 | convolution fusion | flops 241926144 | bytes 4325376 | tf_op jit(solution)/shard_map/hqk,hqd->hkd/dot_general | solution.py:212
  185.4 3.1 %multiply_convert_fusion.1 = bf16[4,768,384]{2,1,0:T(8,128)(2,1)S(1)} fusion(f32[4,768,384]{2,1,0:T(8,128)} %get-tuple-element.102, f32[4,768]{1,0:T(4,128)S(1)} %get-tuple-element.66, bf16[8,768,64]{1,2,0:T(8,128)(2,1)S(1)} %bitcast.276, bf16[8,1152,64]{1,2,0:T(8,128)(2,1)S(1)} %bitcast.248), kind=kOutput, calls=%fused_computation.3 | convolution fusion | flops 154533888 | bytes 8073216 | tf_op jit(solution)/shard_map/hqd,hkd->hqk/dot_general | solution.py:201
  191.8 2.3 copy.36
  194.1 2.8 %fusion.153 = f32[384,1024]{1,0:T(8,128)} fusion(bf16[384,256]{0,1:T(8,128)(2,1)S(1)} %bitcast.299, bf16[384,256]{0,1:T(8,128)(2,1)} %bitcast.303, bf16[2,1024,512]{2,1,0:T(8,128)(2,1)S(1)} %copy-done), kind=kOutput, calls=%fused_computation.205 | convolution fusion | flops 403439616 | bytes 3014656 | tf_op jit(solution)/shard_map/dot_general | solution.py:249
  198.6 7.8 %all-to-all-done.3 = bf16[16,64,512]{2,1,0:T(8,128)(2,1)} async-done(((bf16[16,64,512]{2,1,0:T(8,128)(2,1)}), bf16[16,64,512]{2,1,0:T(8,128)(2,1)}, u32[]{:S(2)}, u32[]{:S(2)}) %all-to-all-start.3) | async-done | bytes 1048608 | tf_op jit(solution)/shard_map/all_to_all | solution.py:57
  206.4 5.1 %all-to-all-start.2 = ((bf16[16,64,512]{2,1,0:T(8,128)(2,1)}), bf16[16,64,512]{2,1,0:T(8,128)(2,1)}, u32[]{:S(2)}, u32[]{:S(2)}) async-start(bf16[16,64,512]{2,1,0:T(8,128)(2,1)} %bitcast.273), calls=%async_computation.2 | async-start | bytes 2097152 | tf_op jit(solution)/shard_map/all_to_all | solution.py:57
  211.6 2.6 %add_convert_fusion.1 = bf16[384,1024]{1,0:T(8,128)(2,1)S(1)} fusion(f32[384,1024]{1,0:T(8,128)S(1)} %copy-done.3, f32[384,1024]{1,0:T(8,128)} %fusion.154, bf16[384,512]{0,1:T(8,128)(2,1)} %bitcast.290, bf16[1024,512]{1,0:T(8,128)(2,1)} %copy-done.8), kind=kOutput, calls=%fused_computation.93 | convolution fusion | flops 403832832 | bytes 5373952 | tf_op jit(solution)/shard_map/dot_general | solution.py:247
  217.6 2.3 fusion.100
  221.3 14.2 %all-to-all-done.2 = bf16[16,64,512]{2,1,0:T(8,128)(2,1)} async-done(((bf16[16,64,512]{2,1,0:T(8,128)(2,1)}), bf16[16,64,512]{2,1,0:T(8,128)(2,1)}, u32[]{:S(2)}, u32[]{:S(2)}) %all-to-all-start.2) | async-done | bytes 1048608 | tf_op jit(solution)/shard_map/all_to_all | solution.py:57
  (218 shorter events, 86.1 us)
Async XLA Ops:
  7.2 44.2 %all-gather.2.cloned.1.call-start = ((), (), s32[]{:S(2)}) async-start(), calls=%async_computation.4 | async-start | bytes 3145728 | tf_op jit(solution)/shard_map/all_gather | solution.py:92
  7.2 11.7 %copy-start.45 = (s32[24,7]{0,1:T(8,128)S(1)}, s32[24,7]{0,1:T(8,128)}, u32[]{:S(2)}) copy-start(s32[24,7]{0,1:T(8,128)} %param.10) | copy-start | bytes 2020
  8.3 19.6 %collective-permute-start.1 = (bf16[384,512]{1,0:T(8,128)(2,1)S(1)}, bf16[384,512]{1,0:T(8,128)(2,1)S(1)}, u32[]{:S(2)}, u32[]{:S(2)}) collective-permute-start(bf16[384,512]{1,0:T(8,128)(2,1)S(1)} %dynamic-slice_bitcast_fusion), channel_id=1, source_target_pairs={{4,0},{8,4},{12,8},{16,12},{20,16},{24,20},{28,24},{5,1},{9,5},{13... | collective-permute-start | bytes 1179656 | tf_op jit(solution)/shard_map/ppermute | solution.py:14
  10.7 19.7 %collective-permute-start = (bf16[384,512]{1,0:T(8,128)(2,1)S(1)}, bf16[384,512]{1,0:T(8,128)(2,1)S(1)}, u32[]{:S(2)}, u32[]{:S(2)}) collective-permute-start(bf16[384,512]{1,0:T(8,128)(2,1)S(1)} %dynamic-slice_bitcast_fusion), channel_id=1, source_target_pairs={{0,4},{4,8},{8,12},{12,16},{16,20},{20,24},{24,28},{1,5},{5,9},{9,... | collective-permute-start | bytes 1179656 | tf_op jit(solution)/shard_map/ppermute | solution.py:14
  15.0 17.9 %collective-permute-start.3 = (bf16[512,512]{1,0:T(8,128)(2,1)}, bf16[512,512]{1,0:T(8,128)(2,1)}, u32[]{:S(2)}, u32[]{:S(2)}) collective-permute-start(bf16[512,512]{1,0:T(8,128)(2,1)} %param.7), channel_id=1, source_target_pairs={{0,2},{2,0},{1,3},{3,1},{4,6},{6,4},{5,7},{7,5},{8,10},{10,8},{9,1... | collective-permute-start | bytes 1572872 | tf_op jit(solution)/shard_map/ppermute | solution.py:50
  18.9 13.0 %copy-start.16 = (bf16[1,384,512]{2,1,0:T(8,128)(2,1)S(1)}, bf16[1,384,512]{2,1,0:T(8,128)(2,1)}, u32[]{:S(2)}) copy-start(bf16[1,384,512]{2,1,0:T(8,128)(2,1)} %param.11) | copy-start | bytes 1179652
  30.4 4.4 %collective-permute-start.2 = (bf16[2,384,512]{2,1,0:T(8,128)(2,1)S(1)}, bf16[2,384,512]{2,1,0:T(8,128)(2,1)}, u32[]{:S(2)}, u32[]{:S(2)}) collective-permute-start(bf16[2,384,512]{2,1,0:T(8,128)(2,1)S(1)} %pad_maximum_fusion.1), channel_id=1, source_target_pairs={{0,1},{1,0},{2,3},{3,2},{4,5},{5,4},{6,7},{7,6},{8,9},{9,8},{10,11... | collective-permute-start | bytes 2359304 | tf_op jit(solution)/shard_map/ppermute | solution.py:42
  34.8 18.3 %copy-start.8 = (bf16[1024,512]{1,0:T(8,128)(2,1)}, bf16[1024,512]{1,0:T(8,128)(2,1)S(1)}, u32[]{:S(2)}) copy-start(bf16[1024,512]{1,0:T(8,128)(2,1)S(1)} %maximum_select_fusion.1) | copy-start | bytes 3145732
  38.0 15.1 %copy-start.5 = (bf16[1,384,1024]{2,1,0:T(8,128)(2,1)S(1)}, bf16[1,384,1024]{2,1,0:T(8,128)(2,1)}, u32[]{:S(2)}) copy-start(bf16[1,384,1024]{2,1,0:T(8,128)(2,1)} %param.6) | copy-start | bytes 2359300
  103.2 34.6 %collective-permute-start.9 = (f32[3,4,384,1]{2,1,3,0:T(4,128)S(1)}, f32[3,4,384,1]{2,1,3,0:T(4,128)S(1)}, u32[]{:S(2)}, u32[]{:S(2)}) collective-permute-start(f32[3,4,384,1]{2,1,3,0:T(4,128)S(1)} %pad_maximum_fusion.14), channel_id=1, source_target_pairs={{4,0},{8,4},{12,8},{16,12},{20,16},{24,20},{28,24},{5,1},{9,5},{13... | collective-permute-start | bytes 55304 | tf_op jit(solution)/shard_map/ppermute | solution.py:14
  105.7 28.9 %collective-permute-start.8 = (f32[3,4,384,1]{2,1,3,0:T(4,128)S(1)}, f32[3,4,384,1]{2,1,3,0:T(4,128)}, u32[]{:S(2)}, u32[]{:S(2)}) collective-permute-start(f32[3,4,384,1]{2,1,3,0:T(4,128)S(1)} %pad_maximum_fusion.14), channel_id=1, source_target_pairs={{0,4},{4,8},{8,12},{12,16},{16,20},{20,24},{24,28},{1,5},{5,9},{9,... | collective-permute-start | bytes 55304 | tf_op jit(solution)/shard_map/ppermute | solution.py:14
  110.0 29.1 %collective-permute-start.5 = (f32[3,4,384,1]{2,1,3,0:T(4,128)S(1)}, f32[3,4,384,1]{2,1,3,0:T(4,128)S(1)}, u32[]{:S(2)}, u32[]{:S(2)}) collective-permute-start(f32[3,4,384,1]{2,1,3,0:T(4,128)S(1)} %pad_maximum_fusion.13), channel_id=1, source_target_pairs={{4,0},{8,4},{12,8},{16,12},{20,16},{24,20},{28,24},{5,1},{9,5},{13... | collective-permute-start | bytes 55304 | tf_op jit(solution)/shard_map/ppermute | solution.py:14
  111.9 26.5 %collective-permute-start.4 = (f32[3,4,384,1]{2,1,3,0:T(4,128)S(1)}, f32[3,4,384,1]{2,1,3,0:T(4,128)}, u32[]{:S(2)}, u32[]{:S(2)}) collective-permute-start(f32[3,4,384,1]{2,1,3,0:T(4,128)S(1)} %pad_maximum_fusion.13), channel_id=1, source_target_pairs={{0,4},{4,8},{8,12},{12,16},{16,20},{20,24},{24,28},{1,5},{5,9},{9,... | collective-permute-start | bytes 55304 | tf_op jit(solution)/shard_map/ppermute | solution.py:14
  118.1 5.5 %copy-start.13 = (bf16[4,128,896]{2,1,0:T(8,128)(2,1)}, bf16[4,128,896]{2,1,0:T(8,128)(2,1)S(1)}, u32[]{:S(2)}) copy-start(bf16[4,128,896]{2,1,0:T(8,128)(2,1)S(1)} %get-tuple-element.38) | copy-start | bytes 2752516
  118.1 6.3 %copy-start.11 = (bf16[4,128,896]{2,1,0:T(8,128)(2,1)}, bf16[4,128,896]{2,1,0:T(8,128)(2,1)S(1)}, u32[]{:S(2)}) copy-start(bf16[4,128,896]{2,1,0:T(8,128)(2,1)S(1)} %get-tuple-element.83) | copy-start | bytes 2752516
  120.0 5.3 %copy-start.6 = (bf16[1,384,1024]{2,1,0:T(8,128)(2,1)S(1)}, bf16[1,384,1024]{2,1,0:T(8,128)(2,1)}, u32[]{:S(2)}) copy-start(bf16[1,384,1024]{2,1,0:T(8,128)(2,1)} %param.6) | copy-start | bytes 2359300
  121.7 27.8 %collective-permute-start.6 = (bf16[384,512]{1,0:T(8,128)(2,1)S(1)}, bf16[384,512]{1,0:T(8,128)(2,1)S(1)}, u32[]{:S(2)}, u32[]{:S(2)}) collective-permute-start(bf16[384,512]{1,0:T(8,128)(2,1)S(1)} %bitcast.296), channel_id=1, source_target_pairs={{0,4},{4,8},{8,12},{12,16},{16,20},{20,24},{24,28},{1,5},{5,9},{9,... | collective-permute-start | bytes 1179656 | tf_op jit(solution)/shard_map/ppermute | solution.py:14
  126.7 32.5 %all-to-all-start.1 = ((bf16[16,64,256]{2,1,0:T(8,128)(2,1)}), bf16[16,64,256]{2,1,0:T(8,128)(2,1)}, u32[]{:S(2)}, u32[]{:S(2)}) async-start(bf16[16,64,256]{2,1,0:T(8,128)(2,1)} %bitcast.104), calls=%async_computation.1 | async-start | bytes 1048576 | tf_op jit(solution)/shard_map/all_to_all | solution.py:57
  134.6 19.2 %collective-permute-start.7 = (bf16[384,512]{1,0:T(8,128)(2,1)S(1)}, bf16[384,512]{1,0:T(8,128)(2,1)S(1)}, u32[]{:S(2)}, u32[]{:S(2)}) collective-permute-start(bf16[384,512]{1,0:T(8,128)(2,1)S(1)} %bitcast.297), channel_id=1, source_target_pairs={{4,0},{8,4},{12,8},{16,12},{20,16},{24,20},{28,24},{5,1},{9,5},{13... | collective-permute-start | bytes 1179656 | tf_op jit(solution)/shard_map/ppermute | solution.py:14
  139.2 5.0 %copy-start.27 = (pred[768,384]{1,0:T(8,128)(4,1)S(1)}, pred[768,384]{1,0:T(8,128)(4,1)}, u32[]{:S(2)}) copy-start(pred[768,384]{1,0:T(8,128)(4,1)} %copy.32) | copy-start | bytes 884740
  139.2 5.0 %copy-start.29 = (bf16[4,384,64]{1,2,0:T(8,128)(2,1)S(1)}, bf16[4,384,64]{1,2,0:T(8,128)(2,1)}, u32[]{:S(2)}) copy-start(bf16[4,384,64]{1,2,0:T(8,128)(2,1)} %get-tuple-element.53) | copy-start | bytes 589828
  139.2 5.0 %copy-start.31 = (bf16[4,384,64]{1,2,0:T(8,128)(2,1)S(1)}, bf16[4,384,64]{1,2,0:T(8,128)(2,1)}, u32[]{:S(2)}) copy-start(bf16[4,384,64]{1,2,0:T(8,128)(2,1)} %get-tuple-element.54) | copy-start | bytes 589828
  159.2 17.8 %all-to-all-start = ((bf16[16,64,256]{2,1,0:T(8,128)(2,1)}), bf16[16,64,256]{2,1,0:T(8,128)(2,1)S(1)}, u32[]{:S(2)}, u32[]{:S(2)}) async-start(bf16[16,64,256]{2,1,0:T(8,128)(2,1)} %bitcast.284), calls=%async_computation | async-start | bytes 1048576 | tf_op jit(solution)/shard_map/all_to_all | solution.py:57
  171.4 11.3 %copy-start.19 = (bf16[4,128,384]{2,1,0:T(8,128)(2,1)S(1)}, bf16[4,128,384]{2,1,0:T(8,128)(2,1)}, u32[]{:S(2)}) copy-start(bf16[4,128,384]{2,1,0:T(8,128)(2,1)} %slice.423) | copy-start | bytes 1179652
  171.4 11.3 %copy-start.22 = (bf16[4,128,384]{2,1,0:T(8,128)(2,1)S(1)}, bf16[4,128,384]{2,1,0:T(8,128)(2,1)}, u32[]{:S(2)}) copy-start(bf16[4,128,384]{2,1,0:T(8,128)(2,1)} %slice.425) | copy-start | bytes 1179652
  177.0 8.3 %copy-start.9 = (bf16[16,64,256]{2,1,0:T(8,128)(2,1)}, bf16[16,64,256]{2,1,0:T(8,128)(2,1)S(1)}, u32[]{:S(2)}) copy-start(bf16[16,64,256]{2,1,0:T(8,128)(2,1)S(1)} %all-to-all-done) | copy-start | bytes 1572868
  177.0 29.4 %all-to-all-start.3 = ((bf16[16,64,512]{2,1,0:T(8,128)(2,1)}), bf16[16,64,512]{2,1,0:T(8,128)(2,1)}, u32[]{:S(2)}, u32[]{:S(2)}) async-start(bf16[16,64,512]{2,1,0:T(8,128)(2,1)} %bitcast.113), calls=%async_computation.3 | async-start | bytes 2097152 | tf_op jit(solution)/shard_map/all_to_all | solution.py:57
  185.3 4.1 %copy-start.38 = (bf16[4,384,64]{1,2,0:T(8,128)(2,1)}, bf16[4,384,64]{1,2,0:T(8,128)(2,1)S(1)}, u32[]{:S(2)}) copy-start(bf16[4,384,64]{1,2,0:T(8,128)(2,1)S(1)} %fusion.91) | copy-start | bytes 589828
  190.1 4.0 %copy-start = (bf16[2,1024,512]{2,1,0:T(8,128)(2,1)S(1)}, bf16[2,1024,512]{2,1,0:T(8,128)(2,1)}, u32[]{:S(2)}) copy-start(bf16[2,1024,512]{2,1,0:T(8,128)(2,1)} %all-gather.2.cloned.1.call-done) | copy-start | bytes 6291460
  198.6 12.9 %copy-start.3 = (f32[384,1024]{1,0:T(8,128)S(1)}, f32[384,1024]{1,0:T(8,128)}, u32[]{:S(2)}) copy-start(f32[384,1024]{1,0:T(8,128)} %fusion.153) | copy-start | bytes 4718596
  206.4 29.1 %all-to-all-start.2 = ((bf16[16,64,512]{2,1,0:T(8,128)(2,1)}), bf16[16,64,512]{2,1,0:T(8,128)(2,1)}, u32[]{:S(2)}, u32[]{:S(2)}) async-start(bf16[16,64,512]{2,1,0:T(8,128)(2,1)} %bitcast.273), calls=%async_computation.2 | async-start | bytes 2097152 | tf_op jit(solution)/shard_map/all_to_all | solution.py:57
  214.2 3.3 %collective-permute-start.10 = (bf16[384,1024]{1,0:T(8,128)(2,1)S(1)}, bf16[384,1024]{1,0:T(8,128)(2,1)}, u32[]{:S(2)}, u32[]{:S(2)}) collective-permute-start(bf16[384,1024]{1,0:T(8,128)(2,1)S(1)} %add_convert_fusion.1), channel_id=1, source_target_pairs={{0,1},{1,0},{2,3},{3,2},{4,5},{5,4},{6,7},{7,6},{8,9},{9,8},{10,11... | collective-permute-start | bytes 2359304 | tf_op jit(solution)/shard_map/ppermute | solution.py:67
  (31 other events, 71.8 us)
Sparse Core Ops, SparseCore 0:
  19.0 32.2 all-gather.1

commit v9 on v7

--- a/solution.py
+++ b/solution.py
@@ -88,20 +88,16 @@
     score_scale = HD ** (-0.5)
 
     left_tokens, right_tokens = neighbour_tokens(tokens, halo)
-    query_full = full_rows(w_query)
-    gathered = lax.all_gather(jnp.stack([w_key, w_value]), "dp", axis=1, tiled=True)
-    key_full, value_full = gathered[0], gathered[1]
+    left_up = shifted(upstream[length - halo :], "ctx", 1)
+    right_up = shifted(upstream[:halo], "ctx", -1)
+    gathered = lax.all_gather(jnp.stack([w_query, w_key, w_value]), "dp", axis=1, tiled=True)
+    query_full, key_full, value_full = gathered[0], gathered[1], gathered[2]
 
     frame_tokens = jnp.concatenate([left_tokens, tokens, right_tokens], axis=0)
     all_weights = jnp.concatenate([query_full, key_full, value_full], axis=1)
     frame_proj = jnp.dot(frame_tokens, all_weights, preferred_element_type=jnp.float32).astype(
         jnp.bfloat16
     )
-    frame_proj, up_head, up_tail = lax.optimization_barrier(
-        (frame_proj, upstream[:halo], upstream[length - halo :])
-    )
-    left_up = shifted(up_tail, "ctx", 1)
-    right_up = shifted(up_head, "ctx", -1)
     query_h = head_major(frame_proj[:, :features], heads)
     key_h = head_major(frame_proj[:, features : 2 * features], heads)
     value_h = head_major(frame_proj[:, 2 * features :], heads)

time: 198 us -> 191 us (0.965)
  starting transfers between devices: 36.6 us -> 30.6 us
  waiting for transfers between devices: 57.6 us -> 61.3 us
  local copies, waits for them, and re-layouts: 23.9 us -> 20.4 us
  matrix products: 39 us -> 36 us
    all_gather x1, waiting for transfers between devices: 14.7 us -> 2.79 us  [per_device(): lax.all_gather(jnp.stack([w_query, w_key, w_value]), 'dp', axis=1, tiled=...]
    ppermute x6, waiting for transfers between devices: 2.9 us -> 14 us  [shifted(): lax.ppermute(value, axis, [(source, source + steps) for source in range(l...]
    all_to_all x2, starting transfers between devices: 15.8 us -> 11 us  [summed_rows(): parts = lax.all_to_all(term, group, 0, 0, tiled=True)]
    all_to_all x2, waiting for transfers between devices: 39.9 us -> 44.5 us  [summed_rows(): parts = lax.all_to_all(term, group, 0, 0, tiled=True)]
    dot_general x1, matrix products: 8.22 us -> 4.68 us  [per_device(): jnp.einsum('hqd,hkd->hqk', near_query, key_part, preferred_element_type=j...]
    unnamed x74 -> x64, local copies, waits for them, and re-layouts: 6.62 us -> 3.68 us
  transfers between devices with their start and end apart: 12 -> 11, of which waited for: 4 -> 7; matrix products, arithmetic and copies ran while one was open for 25% -> 23% of each run, Pallas kernels for 0% -> 0%
where the time goes in v9:
time: 191 us; the launch traced here: 190 us
  waiting for transfers between devices  61.3 us (32%)
  matrix products  36 us (19%)
  starting transfers between devices  30.6 us (16%)
  between operations  22.4 us (12%)
  local copies, waits for them, and re-layouts  20.4 us (11%)
  other arithmetic  19.3 us (10%)
    all_to_all x2, waiting for transfers between devices, summed_rows(): parts = lax.all_to_all(term, group, 0, 0, tiled=True)  44.5 us
    ppermute x6, starting transfers between devices, shifted(): lax.ppermute(value, axis, [(source, source + steps) for source in range(l...  19.4 us
    ppermute x6, waiting for transfers between devices, shifted(): lax.ppermute(value, axis, [(source, source + steps) for source in range(l...  14 us
    all_to_all x2, starting transfers between devices, summed_rows(): parts = lax.all_to_all(term, group, 0, 0, tiled=True)  11 us
    dot_general x1, matrix products, per_device(): jnp.einsum('hqd,hkd->hqk', near_query, key_part, preferred_element_type=j...  4.68 us
    dot_general x3, matrix products, per_device(): jnp.einsum('hqd,hkd->hqk', upstream_block, value_window, preferred_elemen...  4.56 us
    convert_element_type x3, other arithmetic, per_device(): score_grad = (probability * (prob_grad - row_delta)).astype(jnp.bfloat16)  4.18 us
    dot_general x1, matrix products, per_device(): jnp.dot(frame_tokens, all_weights, preferred_element_type=jnp.float32)  3.85 us
  transfers between devices with their start and end apart: 11, of which 7 were waited for; matrix products, arithmetic and copies ran while one was open for 23% of the time, Pallas kernels for 0%

profile of v9, /device:TPU:12, one launch (start us, length us, event | category | flops | bytes accessed | tf_op | source)
XLA Modules:
  0.0 190.0 jit_solution(12258948018400554267)
XLA Ops:
  7.2 2.8 %pad_maximum_fusion = bf16[3,512,512]{2,1,0:T(8,128)(2,1)} fusion(bf16[1,512,512]{2,1,0:T(8,128)(2,1)} %bitcast.188, bf16[1,512,512]{2,1,0:T(8,128)(2,1)} %bitcast.189, bf16[1,512,512]{2,1,0:T(8,128)(2,1)} %bitcast.190), kind=kLoop, calls=%fused_computation.60 | loop fusion | flops 1572864 | bytes 3145728 | tf_op jit(solution)/shard_map/stack | solution.py:93
  10.1 2.4 %collective-permute-start.1 = (bf16[384,512]{1,0:T(8,128)(2,1)S(1)}, bf16[384,512]{1,0:T(8,128)(2,1)S(1)}, u32[]{:S(2)}, u32[]{:S(2)}) collective-permute-start(bf16[384,512]{1,0:T(8,128)(2,1)S(1)} %dynamic-slice_bitcast_fusion), channel_id=1, source_target_pairs={{4,0},{8,4},{12,8},{16,12},{20,16},{24,20},{28,24},{5,1},{9,5},{13... | collective-permute-start | bytes 1179656 | tf_op jit(solution)/shard_map/ppermute | solution.py:14
  12.5 4.3 %collective-permute-start = (bf16[384,512]{1,0:T(8,128)(2,1)S(1)}, bf16[384,512]{1,0:T(8,128)(2,1)S(1)}, u32[]{:S(2)}, u32[]{:S(2)}) collective-permute-start(bf16[384,512]{1,0:T(8,128)(2,1)S(1)} %dynamic-slice_bitcast_fusion), channel_id=1, source_target_pairs={{0,4},{4,8},{8,12},{12,16},{16,20},{20,24},{24,28},{1,5},{5,9},{9,... | collective-permute-start | bytes 1179656 | tf_op jit(solution)/shard_map/ppermute | solution.py:14
  16.9 1.9 %collective-permute-start.6 = (bf16[384,512]{1,0:T(8,128)(2,1)S(1)}, bf16[384,512]{1,0:T(8,128)(2,1)S(1)}, u32[]{:S(2)}, u32[]{:S(2)}) collective-permute-start(bf16[384,512]{1,0:T(8,128)(2,1)S(1)} %bitcast.191), channel_id=1, source_target_pairs={{4,0},{8,4},{12,8},{16,12},{20,16},{24,20},{28,24},{5,1},{9,5},{13... | collective-permute-start | bytes 1179656 | tf_op jit(solution)/shard_map/ppermute | solution.py:14
  18.8 4.8 %collective-permute-start.5 = (bf16[384,512]{1,0:T(8,128)(2,1)S(1)}, bf16[384,512]{1,0:T(8,128)(2,1)}, u32[]{:S(2)}, u32[]{:S(2)}) collective-permute-start(bf16[384,512]{1,0:T(8,128)(2,1)S(1)} %bitcast.192), channel_id=1, source_target_pairs={{0,4},{4,8},{8,12},{12,16},{16,20},{20,24},{24,28},{1,5},{5,9},{9,... | collective-permute-start | bytes 1179656 | tf_op jit(solution)/shard_map/ppermute | solution.py:14
  32.4 6.4 %collective-permute-done.1 = bf16[384,512]{1,0:T(8,128)(2,1)S(1)} collective-permute-done((bf16[384,512]{1,0:T(8,128)(2,1)S(1)}, bf16[384,512]{1,0:T(8,128)(2,1)S(1)}, u32[]{:S(2)}, u32[]{:S(2)}) %collective-permute-start.1) | collective-permute-done | bytes 393248 | tf_op jit(solution)/shard_map/ppermute | solution.py:14
  38.9 1.8 collective-permute-done
  43.4 2.7 %collective-permute-done.6 = bf16[384,512]{1,0:T(8,128)(2,1)S(1)} collective-permute-done((bf16[384,512]{1,0:T(8,128)(2,1)S(1)}, bf16[384,512]{1,0:T(8,128)(2,1)S(1)}, u32[]{:S(2)}, u32[]{:S(2)}) %collective-permute-start.6) | collective-permute-done | bytes 393248 | tf_op jit(solution)/shard_map/ppermute | solution.py:14
  46.2 3.0 %collective-permute-done.5 = bf16[384,512]{1,0:T(8,128)(2,1)} collective-permute-done((bf16[384,512]{1,0:T(8,128)(2,1)S(1)}, bf16[384,512]{1,0:T(8,128)(2,1)}, u32[]{:S(2)}, u32[]{:S(2)}) %collective-permute-start.5) | collective-permute-done | bytes 393248 | tf_op jit(solution)/shard_map/ppermute | solution.py:14
  51.3 2.0 %maximum_select_fusion = bf16[2,384,1024]{2,1,0:T(8,128)(2,1)S(1)} fusion(bf16[2,384,512]{2,1,0:T(8,128)(2,1)} %collective-permute-done.2, bf16[1,384,512]{2,1,0:T(8,128)(2,1)S(1)} %bitcast.184, bf16[1,384,512]{2,1,0:T(8,128)(2,1)S(1)} %bitcast.186, pred[]{:T(512)S(6)} %eq.3), kind=kLoop, calls=%fused_computation.59 | loop fusion | flops 10223616 | bytes 3145729 | tf_op jit(solution)/shard_map/jit(_where)/select_n | solution.py:27
  53.5 2.8 %all-gather.2.cloned.1.call-done = bf16[3,1024,512]{2,1,0:T(8,128)(2,1)} async-done(((bf16[3,512,512]{2,1,0:T(8,128)(2,1)}), bf16[3,1024,512]{2,1,0:T(8,128)(2,1)}) %all-gather.2.cloned.1.call-update) | async-done | bytes 3145744 | tf_op jit(solution)/shard_map/all_gather | solution.py:93
  56.2 2.1 %slice_bitcast_fusion.2 = (bf16[1024,512]{1,0:T(8,128)(2,1)S(1)}, bf16[1024,512]{1,0:T(8,128)(2,1)S(1)}, bf16[1024,512]{1,0:T(8,128)(2,1)S(1)}) fusion(bf16[3,1024,512]{2,1,0:T(8,128)(2,1)} %all-gather.2.cloned.1.call-done), kind=kLoop, calls=%fused_computation.87 | loop fusion | bytes 6291456 | tf_op jit(solution)/shard_map/squeeze | solution.py:94
  58.3 3.8 %convolution_convert_fusion = bf16[1152,1536]{1,0:T(8,128)(2,1)S(1)} fusion(bf16[1024,512]{1,0:T(8,128)(2,1)S(1)} %get-tuple-element.22, bf16[1024,512]{1,0:T(8,128)(2,1)S(1)} %get-tuple-element.23, bf16[1024,512]{1,0:T(8,128)(2,1)S(1)} %get-tuple-element.21, bf16[384,1024]{1,0:T(8,128)(2,1)S(1)} %get-tuple-element.25, bf16[384,1024]{1,0:T(8,128)(2,1)S(1)} %bitcast.181, ...), kind=kOutput, calls=%fused_computation.2 | convolution fusion | flops 3642163200 | bytes 9043968 | tf_op jit(solution)/shard_map/dot_general | solution.py:98
  62.4 1.6 copy.20
  73.4 1.5 fusion.22
  78.0 1.5 fusion.19
  79.5 1.5 fusion.21
  81.1 3.5 %collective-permute-start.3 = (f32[3,8,384,1]{2,1,3,0:T(8,128)S(1)}, f32[3,8,384,1]{2,1,3,0:T(8,128)S(1)}, u32[]{:S(2)}, u32[]{:S(2)}) collective-permute-start(f32[3,8,384,1]{2,1,3,0:T(8,128)S(1)} %pad_maximum_fusion.5), channel_id=1, source_target_pairs={{0,4},{4,8},{8,12},{12,16},{16,20},{20,24},{24,28},{1,5},{5,9},{9,... | collective-permute-start | bytes 110600 | tf_op jit(solution)/shard_map/ppermute | solution.py:14
  89.1 2.4 %collective-permute-start.4 = (f32[3,8,384,1]{2,1,3,0:T(8,128)S(1)}, f32[3,8,384,1]{2,1,3,0:T(8,128)S(1)}, u32[]{:S(2)}, u32[]{:S(2)}) collective-permute-start(f32[3,8,384,1]{2,1,3,0:T(8,128)S(1)} %pad_maximum_fusion.5), channel_id=1, source_target_pairs={{4,0},{8,4},{12,8},{16,12},{20,16},{24,20},{28,24},{5,1},{9,5},{13... | collective-permute-start | bytes 110600 | tf_op jit(solution)/shard_map/ppermute | solution.py:14
  96.9 6.1 %all-to-all-start = ((bf16[16,64,512]{2,1,0:T(8,128)(2,1)}), bf16[16,64,512]{2,1,0:T(8,128)(2,1)}, u32[]{:S(2)}, u32[]{:S(2)}) async-start(bf16[16,64,512]{2,1,0:T(8,128)(2,1)} %bitcast.79), calls=%async_computation | async-start | bytes 2097152 | tf_op jit(solution)/shard_map/all_to_all | solution.py:57
  103.0 4.7 %fusion.113 = (bf16[8,768,384]{2,1,0:T(8,128)(2,1)S(1)}, f32[8,768,384]{2,1,0:T(8,128)S(1)}) fusion(f32[8,768]{1,0:T(8,128)S(1)} %get-tuple-element.30, f32[8,768]{1,0:T(8,128)S(1)} %get-tuple-element.31, bf16[8,1152,64]{1,2,0:T(8,128)(2,1)S(1)} %bitcast.164, bf16[8,384,64]{1,2,0:T(8,128)(2,1)S(1)} %copy-done.21, ...), kind=kOutput, calls=%fused_computation.171 | convolution fusion | flops 315359232 | bytes 15679488 | tf_op jit(solution)/shard_map/hqd,hkd->hqk/dot_general | solution.py:181
  107.8 3.2 %multiply_convert_fusion = bf16[8,768,384]{2,1,0:T(8,128)(2,1)S(1)} fusion(f32[8,768,384]{2,1,0:T(8,128)S(1)} %get-tuple-element.57, f32[8,768]{1,0:T(8,128)S(1)} %get-tuple-element.29, bf16[8,768,64]{1,2,0:T(8,128)(2,1)S(1)} %bitcast.171, bf16[8,1152,64]{1,2,0:T(8,128)(2,1)} %bitcast.174), kind=kOutput, calls=%fused_computation | convolution fusion | flops 309067776 | bytes 15360000 | tf_op jit(solution)/shard_map/hqd,hkd->hqk/dot_general | solution.py:186
  111.0 1.6 fusion.48
  112.7 2.5 %fusion.45 = bf16[8,384,64]{1,2,0:T(8,128)(2,1)} fusion(bf16[8,768,384]{2,1,0:T(8,128)(2,1)S(1)} %multiply_convert_fusion, bf16[8,128,384]{2,1,0:T(8,128)(2,1)S(1)} %slice.221, bf16[8,128,384]{2,1,0:T(8,128)(2,1)S(1)} %copy-done.16, bf16[8,128,384]{2,1,0:T(8,128)(2,1)S(1)} %copy-done.15, bf16[8,384,64]{1,2,0:T(8,128)(2,1)S(1)} %copy-done.21, ...), kind=kOutput, calls=%fused_computation.66 | convolution fusion | flops 485228544 | bytes 8650752 | tf_op jit(solution)/shard_map/hqk,hqd->hkd/dot_general | solution.py:194
  115.2 3.8 %convolution_convert_fusion.1 = bf16[1024,1024]{0,1:T(8,128)(2,1)} fusion(bf16[384,512]{0,1:T(8,128)(2,1)S(1)} %bitcast.197, bf16[384,512]{0,1:T(8,128)(2,1)} %bitcast.72, bf16[1,384,1024]{2,1,0:T(8,128)(2,1)S(1)} %copy-done.14), kind=kOutput, calls=%fused_computation.58 | convolution fusion | flops 807927808 | bytes 3670016 | tf_op jit(solution)/shard_map/tr,tf->rf/dot_general | solution.py:212
  119.0 8.8 %all-to-all-done = bf16[16,64,512]{2,1,0:T(8,128)(2,1)} async-done(((bf16[16,64,512]{2,1,0:T(8,128)(2,1)}), bf16[16,64,512]{2,1,0:T(8,128)(2,1)}, u32[]{:S(2)}, u32[]{:S(2)}) %all-to-all-start) | async-done | bytes 1048608 | tf_op jit(solution)/shard_map/all_to_all | solution.py:57
  127.8 5.0 %all-to-all-start.1 = ((bf16[16,64,1024]{2,1,0:T(8,128)(2,1)}), bf16[16,64,1024]{2,1,0:T(8,128)(2,1)}, u32[]{:S(2)}, u32[]{:S(2)}) async-start(bf16[16,64,1024]{2,1,0:T(8,128)(2,1)} %bitcast.173), calls=%async_computation.1 | async-start | bytes 4194304 | tf_op jit(solution)/shard_map/all_to_all | solution.py:57
  133.4 1.8 fusion.106
  135.2 1.6 add_convert_fusion.1
  140.3 2.3 %fusion.80 = bf16[1,384,1024]{2,1,0:T(8,128)(2,1)} fusion(bf16[384,1024]{1,0:T(8,128)(2,1)S(1)} %collective-permute-done.7, bf16[384,1024]{1,0:T(8,128)(2,1)} %add_convert_fusion.1), kind=kLoop, calls=%fused_computation.106 | loop fusion | flops 1572864 | bytes 2359296 | tf_op jit(solution)/shard_map/broadcast_in_dim | solution.py:210
  144.1 35.7 %all-to-all-done.1 = bf16[16,64,1024]{2,1,0:T(8,128)(2,1)} async-done(((bf16[16,64,1024]{2,1,0:T(8,128)(2,1)}), bf16[16,64,1024]{2,1,0:T(8,128)(2,1)}, u32[]{:S(2)}, u32[]{:S(2)}) %all-to-all-start.1) | async-done | bytes 2097184 | tf_op jit(solution)/shard_map/all_to_all | solution.py:57
  179.7 2.0 %convert_reduce_fusion = f32[64,1024]{1,0:T(8,128)S(1)} fusion(bf16[16,64,1024]{2,1,0:T(8,128)(2,1)} %all-to-all-done.1), kind=kLoop, calls=%fused_computation.19 | loop fusion | flops 2031616 | bytes 2359296 | tf_op jit(solution)/shard_map/reduce_sum | solution.py:59
  (129 shorter events, 35.6 us)
Async XLA Ops:
  7.2 2.9 %copy-start.12 = (bf16[1,384,1024]{2,1,0:T(8,128)(2,1)S(1)}, bf16[1,384,1024]{2,1,0:T(8,128)(2,1)}, u32[]{:S(2)}) copy-start(bf16[1,384,1024]{2,1,0:T(8,128)(2,1)} %param.6) | copy-start | bytes 2359300
  7.2 9.7 %copy-start.23 = (bf16[1,384,512]{2,1,0:T(8,128)(2,1)S(1)}, bf16[1,384,512]{2,1,0:T(8,128)(2,1)}, u32[]{:S(2)}) copy-start(bf16[1,384,512]{2,1,0:T(8,128)(2,1)} %param.11) | copy-start | bytes 1179652
  7.2 16.4 %copy-start.28 = (s32[24,7]{0,1:T(8,128)S(1)}, s32[24,7]{0,1:T(8,128)}, u32[]{:S(2)}) copy-start(s32[24,7]{0,1:T(8,128)} %param.10) | copy-start | bytes 2020
  7.2 49.0 %all-gather.2.cloned.1.call-start = ((), (), s32[]{:S(2)}) async-start(), calls=%async_computation.2 | async-start | bytes 4718592 | tf_op jit(solution)/shard_map/all_gather | solution.py:93
  10.1 28.8 %collective-permute-start.1 = (bf16[384,512]{1,0:T(8,128)(2,1)S(1)}, bf16[384,512]{1,0:T(8,128)(2,1)S(1)}, u32[]{:S(2)}, u32[]{:S(2)}) collective-permute-start(bf16[384,512]{1,0:T(8,128)(2,1)S(1)} %dynamic-slice_bitcast_fusion), channel_id=1, source_target_pairs={{4,0},{8,4},{12,8},{16,12},{20,16},{24,20},{28,24},{5,1},{9,5},{13... | collective-permute-start | bytes 1179656 | tf_op jit(solution)/shard_map/ppermute | solution.py:14
  12.5 28.2 %collective-permute-start = (bf16[384,512]{1,0:T(8,128)(2,1)S(1)}, bf16[384,512]{1,0:T(8,128)(2,1)S(1)}, u32[]{:S(2)}, u32[]{:S(2)}) collective-permute-start(bf16[384,512]{1,0:T(8,128)(2,1)S(1)} %dynamic-slice_bitcast_fusion), channel_id=1, source_target_pairs={{0,4},{4,8},{8,12},{12,16},{16,20},{20,24},{24,28},{1,5},{5,9},{9,... | collective-permute-start | bytes 1179656 | tf_op jit(solution)/shard_map/ppermute | solution.py:14
  16.9 29.3 %collective-permute-start.6 = (bf16[384,512]{1,0:T(8,128)(2,1)S(1)}, bf16[384,512]{1,0:T(8,128)(2,1)S(1)}, u32[]{:S(2)}, u32[]{:S(2)}) collective-permute-start(bf16[384,512]{1,0:T(8,128)(2,1)S(1)} %bitcast.191), channel_id=1, source_target_pairs={{4,0},{8,4},{12,8},{16,12},{20,16},{24,20},{28,24},{5,1},{9,5},{13... | collective-permute-start | bytes 1179656 | tf_op jit(solution)/shard_map/ppermute | solution.py:14
  18.8 30.3 %collective-permute-start.5 = (bf16[384,512]{1,0:T(8,128)(2,1)S(1)}, bf16[384,512]{1,0:T(8,128)(2,1)}, u32[]{:S(2)}, u32[]{:S(2)}) collective-permute-start(bf16[384,512]{1,0:T(8,128)(2,1)S(1)} %bitcast.192), channel_id=1, source_target_pairs={{0,4},{4,8},{8,12},{12,16},{16,20},{20,24},{24,28},{1,5},{5,9},{9,... | collective-permute-start | bytes 1179656 | tf_op jit(solution)/shard_map/ppermute | solution.py:14
  40.8 10.6 %collective-permute-start.2 = (bf16[2,384,512]{2,1,0:T(8,128)(2,1)S(1)}, bf16[2,384,512]{2,1,0:T(8,128)(2,1)}, u32[]{:S(2)}, u32[]{:S(2)}) collective-permute-start(bf16[2,384,512]{2,1,0:T(8,128)(2,1)S(1)} %pad_maximum_fusion.1), channel_id=1, source_target_pairs={{0,1},{1,0},{2,3},{3,2},{4,5},{5,4},{6,7},{7,6},{8,9},{9,8},{10,11... | collective-permute-start | bytes 2359304 | tf_op jit(solution)/shard_map/ppermute | solution.py:42
  70.0 22.5 %copy-start.1 = (bf16[8,128,896]{2,1,0:T(8,128)(2,1)}, bf16[8,128,896]{2,1,0:T(8,128)(2,1)S(1)}, u32[]{:S(2)}) copy-start(bf16[8,128,896]{2,1,0:T(8,128)(2,1)S(1)} %get-tuple-element.17) | copy-start | bytes 5505028
  76.2 17.4 %copy-start.3 = (bf16[8,128,896]{2,1,0:T(8,128)(2,1)}, bf16[8,128,896]{2,1,0:T(8,128)(2,1)S(1)}, u32[]{:S(2)}) copy-start(bf16[8,128,896]{2,1,0:T(8,128)(2,1)S(1)} %get-tuple-element.13) | copy-start | bytes 5505028
  81.0 13.5 %copy-start.5 = (bf16[8,128,896]{2,1,0:T(8,128)(2,1)}, bf16[8,128,896]{2,1,0:T(8,128)(2,1)S(1)}, u32[]{:S(2)}) copy-start(bf16[8,128,896]{2,1,0:T(8,128)(2,1)S(1)} %get-tuple-element.15) | copy-start | bytes 5505028
  81.1 5.3 %copy-start.13 = (bf16[1,384,1024]{2,1,0:T(8,128)(2,1)S(1)}, bf16[1,384,1024]{2,1,0:T(8,128)(2,1)}, u32[]{:S(2)}) copy-start(bf16[1,384,1024]{2,1,0:T(8,128)(2,1)} %param.6) | copy-start | bytes 2359300
  81.1 21.8 %collective-permute-start.3 = (f32[3,8,384,1]{2,1,3,0:T(8,128)S(1)}, f32[3,8,384,1]{2,1,3,0:T(8,128)S(1)}, u32[]{:S(2)}, u32[]{:S(2)}) collective-permute-start(f32[3,8,384,1]{2,1,3,0:T(8,128)S(1)} %pad_maximum_fusion.5), channel_id=1, source_target_pairs={{0,4},{4,8},{8,12},{12,16},{16,20},{20,24},{24,28},{1,5},{5,9},{9,... | collective-permute-start | bytes 110600 | tf_op jit(solution)/shard_map/ppermute | solution.py:14
  89.1 13.8 %collective-permute-start.4 = (f32[3,8,384,1]{2,1,3,0:T(8,128)S(1)}, f32[3,8,384,1]{2,1,3,0:T(8,128)S(1)}, u32[]{:S(2)}, u32[]{:S(2)}) collective-permute-start(f32[3,8,384,1]{2,1,3,0:T(8,128)S(1)} %pad_maximum_fusion.5), channel_id=1, source_target_pairs={{4,0},{8,4},{12,8},{16,12},{20,16},{24,20},{28,24},{5,1},{9,5},{13... | collective-permute-start | bytes 110600 | tf_op jit(solution)/shard_map/ppermute | solution.py:14
  93.6 9.4 %copy-start.21 = (bf16[8,384,64]{1,2,0:T(8,128)(2,1)S(1)}, bf16[8,384,64]{1,2,0:T(8,128)(2,1)}, u32[]{:S(2)}) copy-start(bf16[8,384,64]{1,2,0:T(8,128)(2,1)} %get-tuple-element.27) | copy-start | bytes 1179652
  96.9 30.9 %all-to-all-start = ((bf16[16,64,512]{2,1,0:T(8,128)(2,1)}), bf16[16,64,512]{2,1,0:T(8,128)(2,1)}, u32[]{:S(2)}, u32[]{:S(2)}) async-start(bf16[16,64,512]{2,1,0:T(8,128)(2,1)} %bitcast.79), calls=%async_computation | async-start | bytes 2097152 | tf_op jit(solution)/shard_map/all_to_all | solution.py:57
  103.0 4.7 %copy-start.9 = (bf16[768,512]{0,1:T(8,128)(2,1)S(1)}, bf16[768,512]{0,1:T(8,128)(2,1)}, u32[]{:S(2)}) copy-start(bf16[768,512]{0,1:T(8,128)(2,1)} %copy.27) | copy-start | bytes 2359300
  107.7 3.2 %copy-start.17 = (bf16[8,128,384]{2,1,0:T(8,128)(2,1)S(1)}, bf16[8,128,384]{2,1,0:T(8,128)(2,1)}, u32[]{:S(2)}) copy-start(bf16[8,128,384]{2,1,0:T(8,128)(2,1)} %slice.229) | copy-start | bytes 2359300
  107.7 3.2 %copy-start.18 = (bf16[8,128,384]{2,1,0:T(8,128)(2,1)S(1)}, bf16[8,128,384]{2,1,0:T(8,128)(2,1)}, u32[]{:S(2)}) copy-start(bf16[8,128,384]{2,1,0:T(8,128)(2,1)} %slice.227) | copy-start | bytes 2359300
  107.8 3.2 %copy-start.19 = (bf16[8,128,384]{2,1,0:T(8,128)(2,1)S(1)}, bf16[8,128,384]{2,1,0:T(8,128)(2,1)}, u32[]{:S(2)}) copy-start(bf16[8,128,384]{2,1,0:T(8,128)(2,1)} %slice.228) | copy-start | bytes 2359300
  107.8 3.2 %copy-start.25 = (bf16[1,384,512]{1,2,0:T(8,128)(2,1)S(1)}, bf16[1,384,512]{1,2,0:T(8,128)(2,1)}, u32[]{:S(2)}) copy-start(bf16[1,384,512]{1,2,0:T(8,128)(2,1)} %copy.21) | copy-start | bytes 1179652
  112.6 2.6 %copy-start.26 = (bf16[8,384,64]{1,2,0:T(8,128)(2,1)}, bf16[8,384,64]{1,2,0:T(8,128)(2,1)S(1)}, u32[]{:S(2)}) copy-start(bf16[8,384,64]{1,2,0:T(8,128)(2,1)S(1)} %fusion.48) | copy-start | bytes 1179652
  112.7 2.5 %copy-start.14 = (bf16[1,384,1024]{2,1,0:T(8,128)(2,1)S(1)}, bf16[1,384,1024]{2,1,0:T(8,128)(2,1)}, u32[]{:S(2)}) copy-start(bf16[1,384,1024]{2,1,0:T(8,128)(2,1)} %param.6) | copy-start | bytes 2359300
  115.2 17.6 %copy-start = (bf16[3,1024,512]{2,1,0:T(8,128)(2,1)S(1)}, bf16[3,1024,512]{2,1,0:T(8,128)(2,1)}, u32[]{:S(2)}) copy-start(bf16[3,1024,512]{2,1,0:T(8,128)(2,1)} %all-gather.2.cloned.1.call-done) | copy-start | bytes 9437188
  115.2 17.6 %copy-start.8 = (bf16[8,384,64]{1,2,0:T(8,128)(2,1)S(1)}, bf16[8,384,64]{1,2,0:T(8,128)(2,1)}, u32[]{:S(2)}) copy-start(bf16[8,384,64]{1,2,0:T(8,128)(2,1)} %copy-done.7) | copy-start | bytes 1179652
  127.8 51.9 %all-to-all-start.1 = ((bf16[16,64,1024]{2,1,0:T(8,128)(2,1)}), bf16[16,64,1024]{2,1,0:T(8,128)(2,1)}, u32[]{:S(2)}, u32[]{:S(2)}) async-start(bf16[16,64,1024]{2,1,0:T(8,128)(2,1)} %bitcast.173), calls=%async_computation.1 | async-start | bytes 4194304 | tf_op jit(solution)/shard_map/all_to_all | solution.py:57
  132.8 2.4 %copy-start.27 = (bf16[8,384,64]{1,2,0:T(8,128)(2,1)S(1)}, bf16[8,384,64]{1,2,0:T(8,128)(2,1)}, u32[]{:S(2)}) copy-start(bf16[8,384,64]{1,2,0:T(8,128)(2,1)} %copy-done.26) | copy-start | bytes 1179652
  133.4 3.4 %copy-start.2 = (bf16[8,128,896]{2,1,0:T(8,128)(2,1)S(1)}, bf16[8,128,896]{2,1,0:T(8,128)(2,1)}, u32[]{:S(2)}) copy-start(bf16[8,128,896]{2,1,0:T(8,128)(2,1)} %copy-done.1) | copy-start | bytes 5505028
  133.4 3.4 %copy-start.11 = (bf16[1152,512]{0,1:T(8,128)(2,1)S(1)}, bf16[1152,512]{0,1:T(8,128)(2,1)}, u32[]{:S(2)}) copy-start(bf16[1152,512]{0,1:T(8,128)(2,1)} %copy.20) | copy-start | bytes 3538948
  135.2 2.4 %copy-start.4 = (bf16[8,128,896]{2,1,0:T(8,128)(2,1)S(1)}, bf16[8,128,896]{2,1,0:T(8,128)(2,1)}, u32[]{:S(2)}) copy-start(bf16[8,128,896]{2,1,0:T(8,128)(2,1)} %copy-done.3) | copy-start | bytes 5505028
  136.8 3.5 %collective-permute-start.7 = (bf16[384,1024]{1,0:T(8,128)(2,1)}, bf16[384,1024]{1,0:T(8,128)(2,1)S(1)}, u32[]{:S(2)}, u32[]{:S(2)}) collective-permute-start(bf16[384,1024]{1,0:T(8,128)(2,1)} %add_convert_fusion.1), channel_id=1, source_target_pairs={{0,1},{1,0},{2,3},{3,2},{4,5},{5,4},{6,7},{7,6},{8,9},{9,8},{10,11... | collective-permute-start | bytes 2359304 | tf_op jit(solution)/shard_map/ppermute | solution.py:67
  (8 other events, 12.5 us)
Sparse Core Ops, SparseCore 0:
  10.2 46.0 all-gather.1

commit v10 on v9

--- a/solution.py
+++ b/solution.py
@@ -116,50 +116,55 @@
         return jnp.repeat(picked, BLOCK)[None, None, :]
 
     own_low, own_high = REACH, REACH + blocks - 1
-    outs, query_grads, tops, totals, deltas = [], [], [], [], []
-    own_score_grads, own_weights = [], []
-    for i in range(blocks):
-        at = REACH + i
-        query_block = rows(query_h, at)
-        upstream_block = rows(own_upstream, i)
-        key_window = rows(key_h, i, span_len)
-        value_window = rows(value_h, i, span_len)
+    own_mask = frame_mask[REACH : REACH + blocks]
+
+    def own_block(i):
+        query_block = lax.dynamic_slice_in_dim(query_h, (REACH + i) * BLOCK, BLOCK, 1)
+        upstream_block = lax.dynamic_slice_in_dim(own_upstream, i * BLOCK, BLOCK, 1)
+        key_window = lax.dynamic_slice_in_dim(key_h, i * BLOCK, span_len * BLOCK, 1)
+        value_window = lax.dynamic_slice_in_dim(value_h, i * BLOCK, span_len * BLOCK, 1)
+        seen = jnp.repeat(lax.dynamic_index_in_dim(own_mask, i, 0, False) > 0, BLOCK)[None, None, :]
         scores = (
             jnp.einsum("hqd,hkd->hqk", query_block, key_window, preferred_element_type=jnp.float32)
             * score_scale
         )
-        probability, row_top, row_total = softmax_stats(scores, seen_keys(at, i, i + 2 * REACH))
+        probability, row_top, row_total = softmax_stats(scores, seen)
         weights = probability.astype(jnp.bfloat16)
-        outs.append(
-            jnp.einsum("hqk,hkd->hqd", weights, value_window, preferred_element_type=jnp.float32)
-        )
+        out = jnp.einsum("hqk,hkd->hqd", weights, value_window, preferred_element_type=jnp.float32)
         prob_grad = jnp.einsum(
             "hqd,hkd->hqk", upstream_block, value_window, preferred_element_type=jnp.float32
         )
         row_delta = jnp.sum(probability * prob_grad, axis=2, keepdims=True)
         score_grad = (probability * (prob_grad - row_delta)).astype(jnp.bfloat16)
-        query_grads.append(
-            score_scale
-            * jnp.einsum("hqk,hkd->hqd", score_grad, key_window, preferred_element_type=jnp.float32)
-        )
-        tops.append(row_top)
-        totals.append(row_total)
-        deltas.append(row_delta)
-        cut = slice((own_low - i) * BLOCK, (own_high - i + 1) * BLOCK)
-        own_score_grads.append(score_grad[:, :, cut])
-        own_weights.append(weights[:, :, cut])
-
-    attended = token_major(jnp.concatenate(outs, axis=1).astype(jnp.bfloat16))[None]
-    query_grad = token_major(jnp.concatenate(query_grads, axis=1).astype(jnp.bfloat16))
+        query_grad = score_scale * jnp.einsum(
+            "hqk,hkd->hqd", score_grad, key_window, preferred_element_type=jnp.float32
+        )
+        first = (own_low - i) * BLOCK
+        own_grad = lax.dynamic_slice_in_dim(score_grad, first, blocks * BLOCK, 2)
+        own_weight = lax.dynamic_slice_in_dim(weights, first, blocks * BLOCK, 2)
+        return (
+            out.astype(jnp.bfloat16),
+            query_grad.astype(jnp.bfloat16),
+            jnp.stack([row_top, row_total, row_delta]),
+            own_grad,
+            own_weight,
+        )
+
+    outs, query_grads, block_stats, own_grads, own_weights_all = lax.map(
+        own_block, jnp.arange(blocks, dtype=jnp.int32)
+    )
+
+    attended = token_major(jnp.concatenate([outs[i] for i in range(blocks)], axis=1))[None]
+    query_grad = token_major(jnp.concatenate([query_grads[i] for i in range(blocks)], axis=1))
+    own_score_grads = [own_grads[i] for i in range(blocks)]
+    own_weights = [own_weights_all[i] for i in range(blocks)]
 
     term_query = jnp.einsum(
         "tr,tf->rf", tokens, query_grad, preferred_element_type=jnp.float32
     ).astype(jnp.bfloat16)
     reduced_query = summed_rows(term_query)
 
-    stats = jnp.stack(
-        [jnp.concatenate(tops, axis=1), jnp.concatenate(totals, axis=1), jnp.concatenate(deltas, axis=1)]
-    )
+    stats = jnp.concatenate([block_stats[i] for i in range(blocks)], axis=2)
     stats_left = shifted(stats[:, :, length - halo :], "ctx", 1)
     stats_right = shifted(stats[:, :, :halo], "ctx", -1)
 

time: 191 us -> 244 us (1.28)
  local copies, waits for them, and re-layouts: 20.4 us -> 41.4 us
  matrix products: 36 us -> 50.5 us
  loops' own time: 0 us -> 9.64 us
  other arithmetic: 19.3 us -> 24 us
  waiting for transfers between devices: 61.3 us -> 65.2 us
    dot_general x12, matrix products: 11.8 us -> 29.5 us  [the longest x3 12 us: own_block(): jnp.einsum('hqd,hkd->hqk', upstream_block, value_window, preferred_elemen...]
    another operation x0 -> x1, loops' own time: none -> 9.64 us  [per_device(): lax.map(own_block, jnp.arange(blocks, dtype=jnp.int32))]
    dynamic_update_slice x0 -> x3, local copies, waits for them, and re-layouts: none -> 7.96 us  [per_device(): lax.map(own_block, jnp.arange(blocks, dtype=jnp.int32))]
    squeeze x0 -> x4, local copies, waits for them, and re-layouts: none -> 6.36 us  [the longest x1 3.14 us: per_device(): own_weights = [own_weights_all[i] for i in range(blocks)]]
    while x0 -> x18, local copies, waits for them, and re-layouts: none -> 5.42 us
    slice x6 -> x1, local copies, waits for them, and re-layouts: 4.98 us -> 0.01 us  [per_device(): own_mask = frame_mask[REACH:REACH + blocks]]
    convert_element_type x3, other arithmetic: 4.18 us -> 6.71 us  [own_block(): score_grad = (probability * (prob_grad - row_delta)).astype(jnp.bfloat16)]
    unnamed x64 -> x61, local copies, waits for them, and re-layouts: 3.68 us -> 4.96 us
  transfers between devices with their start and end apart: 11 -> 11, of which waited for: 7 -> 6; matrix products, arithmetic and copies ran while one was open for 23% -> 17% of each run, Pallas kernels for 0% -> 0%
where the time goes in v10:
time: 244 us; the launch traced here: 243 us
  waiting for transfers between devices  65.2 us (27%)
  matrix products  50.5 us (21%)
  local copies, waits for them, and re-layouts  41.4 us (17%)
  starting transfers between devices  29.7 us (12%)
  other arithmetic  24 us (10%)
  between operations  22.3 us (9%)
  loops' own time  9.64 us (4%)
    all_to_all x2, waiting for transfers between devices, summed_rows(): parts = lax.all_to_all(term, group, 0, 0, tiled=True)  45.9 us
    ppermute x6, starting transfers between devices, shifted(): lax.ppermute(value, axis, [(source, source + steps) for source in range(l...  18.1 us
    ppermute x6, waiting for transfers between devices, shifted(): lax.ppermute(value, axis, [(source, source + steps) for source in range(l...  13.9 us
    dot_general x3, matrix products, own_block(): jnp.einsum('hqd,hkd->hqk', upstream_block, value_window, preferred_elemen...  12 us
    all_to_all x2, starting transfers between devices, summed_rows(): parts = lax.all_to_all(term, group, 0, 0, tiled=True)  11.4 us
    another operation x1, loops' own time, per_device(): lax.map(own_block, jnp.arange(blocks, dtype=jnp.int32))  9.64 us
    dynamic_update_slice x3, local copies, waits for them, and re-layouts, per_device(): lax.map(own_block, jnp.arange(blocks, dtype=jnp.int32))  7.96 us
    dot_general x3, matrix products, own_block(): jnp.einsum('hqk,hkd->hqd', weights, value_window, preferred_element_type=...  7.92 us
  transfers between devices with their start and end apart: 11, of which 6 were waited for; matrix products, arithmetic and copies ran while one was open for 17% of the time, Pallas kernels for 0%

profile of v10, /device:TPU:12, one launch (start us, length us, event | category | flops | bytes accessed | tf_op | source)
XLA Modules:
  0.0 242.7 jit_solution(4738223067111498098)
XLA Ops:
  7.2 2.8 %pad_maximum_fusion = bf16[3,512,512]{2,1,0:T(8,128)(2,1)} fusion(bf16[1,512,512]{2,1,0:T(8,128)(2,1)} %bitcast.199, bf16[1,512,512]{2,1,0:T(8,128)(2,1)} %bitcast.200, bf16[1,512,512]{2,1,0:T(8,128)(2,1)} %bitcast.201), kind=kLoop, calls=%fused_computation.66 | loop fusion | flops 1572864 | bytes 3145728 | tf_op jit(solution)/shard_map/stack | solution.py:93
  10.1 3.4 %collective-permute-start = (bf16[384,512]{1,0:T(8,128)(2,1)S(1)}, bf16[384,512]{1,0:T(8,128)(2,1)S(1)}, u32[]{:S(2)}, u32[]{:S(2)}) collective-permute-start(bf16[384,512]{1,0:T(8,128)(2,1)S(1)} %dynamic-slice_bitcast_fusion), channel_id=1, source_target_pairs={{0,4},{4,8},{8,12},{12,16},{16,20},{20,24},{24,28},{1,5},{5,9},{9,... | collective-permute-start | bytes 1179656 | tf_op jit(solution)/shard_map/ppermute | solution.py:14
  13.6 2.4 collective-permute-start.1
  16.0 4.3 %collective-permute-start.5 = (bf16[384,512]{1,0:T(8,128)(2,1)S(1)}, bf16[384,512]{1,0:T(8,128)(2,1)S(1)}, u32[]{:S(2)}, u32[]{:S(2)}) collective-permute-start(bf16[384,512]{1,0:T(8,128)(2,1)S(1)} %bitcast.203), channel_id=1, source_target_pairs={{0,4},{4,8},{8,12},{12,16},{16,20},{20,24},{24,28},{1,5},{5,9},{9,... | collective-permute-start | bytes 1179656 | tf_op jit(solution)/shard_map/ppermute | solution.py:14
  32.4 8.5 %collective-permute-done = bf16[384,512]{1,0:T(8,128)(2,1)S(1)} collective-permute-done((bf16[384,512]{1,0:T(8,128)(2,1)S(1)}, bf16[384,512]{1,0:T(8,128)(2,1)S(1)}, u32[]{:S(2)}, u32[]{:S(2)}) %collective-permute-start) | collective-permute-done | bytes 393248 | tf_op jit(solution)/shard_map/ppermute | solution.py:14
  42.7 5.4 %collective-permute-done.5 = bf16[384,512]{1,0:T(8,128)(2,1)S(1)} collective-permute-done((bf16[384,512]{1,0:T(8,128)(2,1)S(1)}, bf16[384,512]{1,0:T(8,128)(2,1)S(1)}, u32[]{:S(2)}, u32[]{:S(2)}) %collective-permute-start.5) | collective-permute-done | bytes 393248 | tf_op jit(solution)/shard_map/ppermute | solution.py:14
  52.4 3.8 %all-gather.2.cloned.1.call-done = bf16[3,1024,512]{2,1,0:T(8,128)(2,1)} async-done(((bf16[3,512,512]{2,1,0:T(8,128)(2,1)}), bf16[3,1024,512]{2,1,0:T(8,128)(2,1)}) %all-gather.2.cloned.1.call-update) | async-done | bytes 3145744 | tf_op jit(solution)/shard_map/all_gather | solution.py:93
  58.3 3.8 %convolution_convert_fusion.1 = bf16[1152,1536]{1,0:T(8,128)(2,1)S(1)} fusion(bf16[1024,512]{1,0:T(8,128)(2,1)S(1)} %get-tuple-element.113, bf16[1024,512]{1,0:T(8,128)(2,1)S(1)} %get-tuple-element.114, bf16[1024,512]{1,0:T(8,128)(2,1)S(1)} %get-tuple-element.112, bf16[384,1024]{1,0:T(8,128)(2,1)S(1)} %get-tuple-element.122, ...), kind=kOutput, calls=%fused_computation.35 | convolution fusion | flops 3642163200 | bytes 9043968 | tf_op jit(solution)/shard_map/dot_general | solution.py:98
  66.0 65.9 %while.18 = (s32[]{:T(128)}, bf16[3,8,128,64]{2,3,1,0:T(8,128)(2,1)}, bf16[3,8,128,64]{2,3,1,0:T(8,128)(2,1)}, f32[3,3,8,128,1]{3,2,1,4,0:T(8,128)}, bf16[3,8,12...) while((s32[]{:T(128)}, ...), condition=%wide.region_4.5_spmd, body=%wide.region_0.4_spmd.sunk | while | flops 489229312 | bytes 73468960 | solution.py:153
  73.7 4.0 %multiply_reduce_fusion.2 = (f32[8,128]{1,0:T(8,128)S(1)}, f32[8,128,896]{2,1,0:T(8,128)S(1)}) fusion(f32[8,128]{1,0:T(8,128)S(1)} %fusion.105, f32[8,128]{1,0:T(8,128)S(1)} %get-tuple-element.243, f32[8,128,896]{2,1,0:T(8,128)} %copy-done, pred[896]{0:T(1024)(128)(4,1)S(1)} %broadcast_bitcast_fusion.3, bf16[8,1152,64]{1,2,0:T(8,128)(2,1)} %get-tuple-element.298, ...), kind=kOutput, calls=%fused_computation.1.clone.1 | convolution fusion | flops 122944512 | bytes 8401800 | tf_op jit(solution)/shard_map/while/body/eval_jaxpr/hqd,hkd->hqk/dot_general | solution.py:134
  77.7 2.2 multiply_convert_fusion.3
  80.6 2.6 %bitcast_dynamic-update-slice_fusion.3 = (bf16[3,8,128,384]{3,2,1,0:T(8,128)(2,1)}, bf16[3,8,128,384]{3,2,1,0:T(8,128)(2,1)}) fusion(bf16[3,8,128,384]{3,2,1,0:T(8,128)(2,1)} %get-tuple-element.274, s32[]{:T(128)} %get-tuple-element.269, bf16[8,128,896]{2,1,0:T(8,128)(2,1)S(1)} %get-tuple-element.246, s32[]{:T(128)S(6)} %select_n.80, ...), kind=kLoop, calls=%fused_computation.19.clone.1 | loop fusion | bytes 3146244 | tf_op jit(solution)/shard_map/while/body/jit(dynamic_update_index_in_dim)/dynamic_update_slice | solution.py:153
  85.3 2.6 %fusion.106 = bf16[3,8,128,64]{2,3,1,0:T(8,128)(2,1)} fusion(bf16[3,8,128,64]{2,3,1,0:T(8,128)(2,1)} %get-tuple-element.270, s32[]{:T(128)} %get-tuple-element.269, bf16[8,128,896]{2,1,0:T(8,128)(2,1)S(1)} %get-tuple-element.246, bf16[8,1152,64]{1,2,0:T(8,128)(2,1)} %get-tuple-element.298, s32[]{:T(128)S(6)} %select_n.77), kind=kOutput, calls=%fused_computation.10.clone.1 | convolution fusion | flops 117506048 | bytes 2884100 | tf_op jit(solution)/shard_map/while/body/eval_jaxpr/hqk,hkd->hqd/dot_general | solution.py:133
  95.6 4.0 %multiply_reduce_fusion.2 = (f32[8,128]{1,0:T(8,128)S(1)}, f32[8,128,896]{2,1,0:T(8,128)S(1)}) fusion(f32[8,128]{1,0:T(8,128)S(1)} %fusion.105, f32[8,128]{1,0:T(8,128)S(1)} %get-tuple-element.243, f32[8,128,896]{2,1,0:T(8,128)} %copy-done, pred[896]{0:T(1024)(128)(4,1)S(1)} %broadcast_bitcast_fusion.3, bf16[8,1152,64]{1,2,0:T(8,128)(2,1)} %get-tuple-element.298, ...), kind=kOutput, calls=%fused_computation.1.clone.1 | convolution fusion | flops 122944512 | bytes 8401800 | tf_op jit(solution)/shard_map/while/body/eval_jaxpr/hqd,hkd->hqk/dot_general | solution.py:134
  99.7 2.2 multiply_convert_fusion.3
  102.5 2.7 %bitcast_dynamic-update-slice_fusion.3 = (bf16[3,8,128,384]{3,2,1,0:T(8,128)(2,1)}, bf16[3,8,128,384]{3,2,1,0:T(8,128)(2,1)}) fusion(bf16[3,8,128,384]{3,2,1,0:T(8,128)(2,1)} %get-tuple-element.274, s32[]{:T(128)} %get-tuple-element.269, bf16[8,128,896]{2,1,0:T(8,128)(2,1)S(1)} %get-tuple-element.246, s32[]{:T(128)S(6)} %select_n.80, ...), kind=kLoop, calls=%fused_computation.19.clone.1 | loop fusion | bytes 3146244 | tf_op jit(solution)/shard_map/while/body/jit(dynamic_update_index_in_dim)/dynamic_update_slice | solution.py:153
  107.3 2.6 %fusion.106 = bf16[3,8,128,64]{2,3,1,0:T(8,128)(2,1)} fusion(bf16[3,8,128,64]{2,3,1,0:T(8,128)(2,1)} %get-tuple-element.270, s32[]{:T(128)} %get-tuple-element.269, bf16[8,128,896]{2,1,0:T(8,128)(2,1)S(1)} %get-tuple-element.246, bf16[8,1152,64]{1,2,0:T(8,128)(2,1)} %get-tuple-element.298, s32[]{:T(128)S(6)} %select_n.77), kind=kOutput, calls=%fused_computation.10.clone.1 | convolution fusion | flops 117506048 | bytes 2884100 | tf_op jit(solution)/shard_map/while/body/eval_jaxpr/hqk,hkd->hqd/dot_general | solution.py:133
  117.6 4.0 %multiply_reduce_fusion.2 = (f32[8,128]{1,0:T(8,128)S(1)}, f32[8,128,896]{2,1,0:T(8,128)S(1)}) fusion(f32[8,128]{1,0:T(8,128)S(1)} %fusion.105, f32[8,128]{1,0:T(8,128)S(1)} %get-tuple-element.243, f32[8,128,896]{2,1,0:T(8,128)} %copy-done, pred[896]{0:T(1024)(128)(4,1)S(1)} %broadcast_bitcast_fusion.3, bf16[8,1152,64]{1,2,0:T(8,128)(2,1)} %get-tuple-element.298, ...), kind=kOutput, calls=%fused_computation.1.clone.1 | convolution fusion | flops 122944512 | bytes 8401800 | tf_op jit(solution)/shard_map/while/body/eval_jaxpr/hqd,hkd->hqk/dot_general | solution.py:134
  121.6 2.2 multiply_convert_fusion.3
  124.5 2.6 %bitcast_dynamic-update-slice_fusion.3 = (bf16[3,8,128,384]{3,2,1,0:T(8,128)(2,1)}, bf16[3,8,128,384]{3,2,1,0:T(8,128)(2,1)}) fusion(bf16[3,8,128,384]{3,2,1,0:T(8,128)(2,1)} %get-tuple-element.274, s32[]{:T(128)} %get-tuple-element.269, bf16[8,128,896]{2,1,0:T(8,128)(2,1)S(1)} %get-tuple-element.246, s32[]{:T(128)S(6)} %select_n.80, ...), kind=kLoop, calls=%fused_computation.19.clone.1 | loop fusion | bytes 3146244 | tf_op jit(solution)/shard_map/while/body/jit(dynamic_update_index_in_dim)/dynamic_update_slice | solution.py:153
  129.3 2.6 %fusion.106 = bf16[3,8,128,64]{2,3,1,0:T(8,128)(2,1)} fusion(bf16[3,8,128,64]{2,3,1,0:T(8,128)(2,1)} %get-tuple-element.270, s32[]{:T(128)} %get-tuple-element.269, bf16[8,128,896]{2,1,0:T(8,128)(2,1)S(1)} %get-tuple-element.246, bf16[8,1152,64]{1,2,0:T(8,128)(2,1)} %get-tuple-element.298, s32[]{:T(128)S(6)} %select_n.77), kind=kOutput, calls=%fused_computation.10.clone.1 | convolution fusion | flops 117506048 | bytes 2884100 | tf_op jit(solution)/shard_map/while/body/eval_jaxpr/hqk,hkd->hqd/dot_general | solution.py:133
  133.4 3.4 %collective-permute-start.3 = (f32[3,8,384,1]{2,1,0,3:T(8,128)}, f32[3,8,384,1]{2,1,0,3:T(8,128)}, u32[]{:S(2)}, u32[]{:S(2)}) collective-permute-start(f32[3,8,384,1]{2,1,0,3:T(8,128)} %pad_maximum_fusion.5), channel_id=1, source_target_pairs={{0,4},{4,8},{8,12},{12,16},{16,20},{20,24},{24,28},{1,5},{5,9},{9,... | collective-permute-start | bytes 110600 | tf_op jit(solution)/shard_map/ppermute | solution.py:14
  136.8 2.6 %collective-permute-start.4 = (f32[3,8,384,1]{2,1,0,3:T(8,128)}, f32[3,8,384,1]{2,1,0,3:T(8,128)}, u32[]{:S(2)}, u32[]{:S(2)}) collective-permute-start(f32[3,8,384,1]{2,1,0,3:T(8,128)} %pad_maximum_fusion.5), channel_id=1, source_target_pairs={{4,0},{8,4},{12,8},{16,12},{20,16},{24,20},{28,24},{5,1},{9,5},{13... | collective-permute-start | bytes 110600 | tf_op jit(solution)/shard_map/ppermute | solution.py:14
  139.4 3.1 %slice_bitcast_fusion.7 = (bf16[8,128,384]{2,1,0:T(8,128)(2,1)}, bf16[8,128,384]{2,1,0:T(8,128)(2,1)}, bf16[8,128,384]{2,1,0:T(8,128)(2,1)}) fusion(bf16[3,8,128,384]{3,2,1,0:T(8,128)(2,1)} %get-tuple-element.73), kind=kLoop, calls=%fused_computation.98 | loop fusion | bytes 4718592 | tf_op jit(solution)/shard_map/squeeze | solution.py:160
  149.2 6.5 %all-to-all-start = ((bf16[16,64,512]{2,1,0:T(8,128)(2,1)}), bf16[16,64,512]{2,1,0:T(8,128)(2,1)}, u32[]{:S(2)}, u32[]{:S(2)}) async-start(bf16[16,64,512]{2,1,0:T(8,128)(2,1)} %bitcast.87), calls=%async_computation | async-start | bytes 2097152 | tf_op jit(solution)/shard_map/all_to_all | solution.py:57
  157.3 4.7 %fusion.85 = (bf16[8,768,384]{2,1,0:T(8,128)(2,1)S(1)}, f32[8,768,384]{2,1,0:T(8,128)S(1)}) fusion(f32[8,768]{1,0:T(8,128)S(1)} %get-tuple-element.133, f32[8,768]{1,0:T(8,128)S(1)} %get-tuple-element.134, bf16[8,1152,64]{1,2,0:T(8,128)(2,1)S(1)} %get-tuple-element.308, bf16[8,384,64]{1,2,0:T(8,128)(2,1)S(1)} %get-tuple-element.124, ...), kind=kOutput, calls=%fused_computation.155 | convolution fusion | flops 315359232 | bytes 15679488 | tf_op jit(solution)/shard_map/hqd,hkd->hqk/dot_general | solution.py:186
  162.0 3.2 %multiply_convert_fusion.1 = bf16[8,768,384]{2,1,0:T(8,128)(2,1)S(1)} fusion(f32[8,768,384]{2,1,0:T(8,128)S(1)} %get-tuple-element.151, f32[8,768]{1,0:T(8,128)S(1)} %get-tuple-element.132, bf16[8,768,64]{1,2,0:T(8,128)(2,1)S(1)} %bitcast.187, bf16[8,1152,64]{1,2,0:T(8,128)(2,1)} %bitcast.28), kind=kOutput, calls=%fused_computation.33 | convolution fusion | flops 309067776 | bytes 15360000 | tf_op jit(solution)/shard_map/hqd,hkd->hqk/dot_general | solution.py:191
  169.4 2.6 %convolution_convert_fusion.2 = bf16[1024,1024]{0,1:T(8,128)(2,1)} fusion(bf16[384,512]{0,1:T(8,128)(2,1)S(1)} %bitcast.208, bf16[384,512]{0,1:T(8,128)(2,1)S(1)} %bitcast.206, bf16[1,384,1024]{2,1,0:T(8,128)(2,1)S(1)} %copy-done.8), kind=kOutput, calls=%fused_computation.64 | convolution fusion | flops 807927808 | bytes 3670016 | tf_op jit(solution)/shard_map/tr,tf->rf/dot_general | solution.py:217
  172.1 8.5 %all-to-all-done = bf16[16,64,512]{2,1,0:T(8,128)(2,1)} async-done(((bf16[16,64,512]{2,1,0:T(8,128)(2,1)}), bf16[16,64,512]{2,1,0:T(8,128)(2,1)}, u32[]{:S(2)}, u32[]{:S(2)}) %all-to-all-start) | async-done | bytes 1048608 | tf_op jit(solution)/shard_map/all_to_all | solution.py:57
  180.5 5.0 %all-to-all-start.1 = ((bf16[16,64,1024]{2,1,0:T(8,128)(2,1)}), bf16[16,64,1024]{2,1,0:T(8,128)(2,1)}, u32[]{:S(2)}, u32[]{:S(2)}) async-start(bf16[16,64,1024]{2,1,0:T(8,128)(2,1)} %bitcast.189), calls=%async_computation.1 | async-start | bytes 4194304 | tf_op jit(solution)/shard_map/all_to_all | solution.py:57
  191.2 2.3 fusion.65
  195.0 37.5 %all-to-all-done.1 = bf16[16,64,1024]{2,1,0:T(8,128)(2,1)} async-done(((bf16[16,64,1024]{2,1,0:T(8,128)(2,1)}), bf16[16,64,1024]{2,1,0:T(8,128)(2,1)}, u32[]{:S(2)}, u32[]{:S(2)}) %all-to-all-start.1) | async-done | bytes 2097184 | tf_op jit(solution)/shard_map/all_to_all | solution.py:57
  (159 shorter events, 62.2 us)
Async XLA Ops:
  7.2 2.9 %copy-start.6 = (bf16[1,384,1024]{2,1,0:T(8,128)(2,1)S(1)}, bf16[1,384,1024]{2,1,0:T(8,128)(2,1)}, u32[]{:S(2)}) copy-start(bf16[1,384,1024]{2,1,0:T(8,128)(2,1)} %param.8) | copy-start | bytes 2359300
  7.2 8.8 %copy-start.21 = (bf16[1,384,512]{2,1,0:T(8,128)(2,1)S(1)}, bf16[1,384,512]{2,1,0:T(8,128)(2,1)}, u32[]{:S(2)}) copy-start(bf16[1,384,512]{2,1,0:T(8,128)(2,1)} %param.13) | copy-start | bytes 1179652
  7.2 49.1 %all-gather.2.cloned.1.call-start = ((), (), s32[]{:S(2)}) async-start(), calls=%async_computation.2 | async-start | bytes 4718592 | tf_op jit(solution)/shard_map/all_gather | solution.py:93
  7.2 16.0 %copy-start.29 = (s32[24,7]{0,1:T(8,128)S(1)}, s32[24,7]{0,1:T(8,128)}, u32[]{:S(2)}) copy-start(s32[24,7]{0,1:T(8,128)} %param.12) | copy-start | bytes 2020
  10.1 30.7 %collective-permute-start = (bf16[384,512]{1,0:T(8,128)(2,1)S(1)}, bf16[384,512]{1,0:T(8,128)(2,1)S(1)}, u32[]{:S(2)}, u32[]{:S(2)}) collective-permute-start(bf16[384,512]{1,0:T(8,128)(2,1)S(1)} %dynamic-slice_bitcast_fusion), channel_id=1, source_target_pairs={{0,4},{4,8},{8,12},{12,16},{16,20},{20,24},{24,28},{1,5},{5,9},{9,... | collective-permute-start | bytes 1179656 | tf_op jit(solution)/shard_map/ppermute | solution.py:14
  13.6 27.3 %collective-permute-start.1 = (bf16[384,512]{1,0:T(8,128)(2,1)S(1)}, bf16[384,512]{1,0:T(8,128)(2,1)S(1)}, u32[]{:S(2)}, u32[]{:S(2)}) collective-permute-start(bf16[384,512]{1,0:T(8,128)(2,1)S(1)} %dynamic-slice_bitcast_fusion), channel_id=1, source_target_pairs={{4,0},{8,4},{12,8},{16,12},{20,16},{24,20},{28,24},{5,1},{9,5},{13... | collective-permute-start | bytes 1179656 | tf_op jit(solution)/shard_map/ppermute | solution.py:14
  16.0 32.2 %collective-permute-start.5 = (bf16[384,512]{1,0:T(8,128)(2,1)S(1)}, bf16[384,512]{1,0:T(8,128)(2,1)S(1)}, u32[]{:S(2)}, u32[]{:S(2)}) collective-permute-start(bf16[384,512]{1,0:T(8,128)(2,1)S(1)} %bitcast.203), channel_id=1, source_target_pairs={{0,4},{4,8},{8,12},{12,16},{16,20},{20,24},{24,28},{1,5},{5,9},{9,... | collective-permute-start | bytes 1179656 | tf_op jit(solution)/shard_map/ppermute | solution.py:14
  20.3 27.8 %collective-permute-start.6 = (bf16[384,512]{1,0:T(8,128)(2,1)S(1)}, bf16[384,512]{1,0:T(8,128)(2,1)}, u32[]{:S(2)}, u32[]{:S(2)}) collective-permute-start(bf16[384,512]{1,0:T(8,128)(2,1)S(1)} %bitcast.204), channel_id=1, source_target_pairs={{4,0},{8,4},{12,8},{16,12},{20,16},{24,20},{28,24},{5,1},{9,5},{13... | collective-permute-start | bytes 1179656 | tf_op jit(solution)/shard_map/ppermute | solution.py:14
  40.9 9.4 %collective-permute-start.2 = (bf16[2,384,512]{2,1,0:T(8,128)(2,1)S(1)}, bf16[2,384,512]{2,1,0:T(8,128)(2,1)}, u32[]{:S(2)}, u32[]{:S(2)}) collective-permute-start(bf16[2,384,512]{2,1,0:T(8,128)(2,1)S(1)} %pad_maximum_fusion.1), channel_id=1, source_target_pairs={{0,1},{1,0},{2,3},{3,2},{4,5},{5,4},{6,7},{7,6},{8,9},{9,8},{10,11... | collective-permute-start | bytes 2359304 | tf_op jit(solution)/shard_map/ppermute | solution.py:42
  71.0 1.8 copy-start
  73.7 4.0 %copy-start.1 = (f32[8,128,896]{2,1,0:T(8,128)S(1)}, f32[8,128,896]{2,1,0:T(8,128)}, u32[]{:S(2)}) copy-start(f32[8,128,896]{2,1,0:T(8,128)} %copy-done) | copy-start | bytes 11010052 | tf_op jit(solution)/shard_map/while
  80.6 3.2 %copy-start.2 = (bf16[8,128,896]{2,1,0:T(8,128)(2,1)S(1)}, bf16[8,128,896]{2,1,0:T(8,128)(2,1)}, u32[]{:S(2)}) copy-start(bf16[8,128,896]{2,1,0:T(8,128)(2,1)} %get-tuple-element.247) | copy-start | bytes 5505028 | tf_op jit(solution)/shard_map/while
  92.9 1.8 copy-start
  95.6 4.0 %copy-start.1 = (f32[8,128,896]{2,1,0:T(8,128)S(1)}, f32[8,128,896]{2,1,0:T(8,128)}, u32[]{:S(2)}) copy-start(f32[8,128,896]{2,1,0:T(8,128)} %copy-done) | copy-start | bytes 11010052 | tf_op jit(solution)/shard_map/while
  102.5 3.3 %copy-start.2 = (bf16[8,128,896]{2,1,0:T(8,128)(2,1)S(1)}, bf16[8,128,896]{2,1,0:T(8,128)(2,1)}, u32[]{:S(2)}) copy-start(bf16[8,128,896]{2,1,0:T(8,128)(2,1)} %get-tuple-element.247) | copy-start | bytes 5505028 | tf_op jit(solution)/shard_map/while
  117.6 4.0 %copy-start.1 = (f32[8,128,896]{2,1,0:T(8,128)S(1)}, f32[8,128,896]{2,1,0:T(8,128)}, u32[]{:S(2)}) copy-start(f32[8,128,896]{2,1,0:T(8,128)} %copy-done) | copy-start | bytes 11010052 | tf_op jit(solution)/shard_map/while
  124.5 3.3 %copy-start.2 = (bf16[8,128,896]{2,1,0:T(8,128)(2,1)S(1)}, bf16[8,128,896]{2,1,0:T(8,128)(2,1)}, u32[]{:S(2)}) copy-start(bf16[8,128,896]{2,1,0:T(8,128)(2,1)} %get-tuple-element.247) | copy-start | bytes 5505028 | tf_op jit(solution)/shard_map/while
  131.9 10.7 %copy-start.5 = (bf16[3,8,128,384]{3,2,1,0:T(8,128)(2,1)S(1)}, bf16[3,8,128,384]{3,2,1,0:T(8,128)(2,1)}, u32[]{:S(2)}) copy-start(bf16[3,8,128,384]{3,2,1,0:T(8,128)(2,1)} %get-tuple-element.71) | copy-start | bytes 7077892
  133.4 22.3 %collective-permute-start.3 = (f32[3,8,384,1]{2,1,0,3:T(8,128)}, f32[3,8,384,1]{2,1,0,3:T(8,128)}, u32[]{:S(2)}, u32[]{:S(2)}) collective-permute-start(f32[3,8,384,1]{2,1,0,3:T(8,128)} %pad_maximum_fusion.5), channel_id=1, source_target_pairs={{0,4},{4,8},{8,12},{12,16},{16,20},{20,24},{24,28},{1,5},{5,9},{9,... | collective-permute-start | bytes 110600 | tf_op jit(solution)/shard_map/ppermute | solution.py:14
  136.8 19.7 %collective-permute-start.4 = (f32[3,8,384,1]{2,1,0,3:T(8,128)}, f32[3,8,384,1]{2,1,0,3:T(8,128)}, u32[]{:S(2)}, u32[]{:S(2)}) collective-permute-start(f32[3,8,384,1]{2,1,0,3:T(8,128)} %pad_maximum_fusion.5), channel_id=1, source_target_pairs={{4,0},{8,4},{12,8},{16,12},{20,16},{24,20},{28,24},{5,1},{9,5},{13... | collective-permute-start | bytes 110600 | tf_op jit(solution)/shard_map/ppermute | solution.py:14
  142.6 2.4 copy-start.7
  147.8 14.1 %copy-start.18 = (bf16[8,384,64]{1,2,0:T(8,128)(2,1)}, bf16[8,384,64]{1,2,0:T(8,128)(2,1)S(1)}, u32[]{:S(2)}) copy-start(bf16[8,384,64]{1,2,0:T(8,128)(2,1)S(1)} %get-tuple-element.124) | copy-start | bytes 1179652
  149.2 31.3 %all-to-all-start = ((bf16[16,64,512]{2,1,0:T(8,128)(2,1)}), bf16[16,64,512]{2,1,0:T(8,128)(2,1)}, u32[]{:S(2)}, u32[]{:S(2)}) async-start(bf16[16,64,512]{2,1,0:T(8,128)(2,1)} %bitcast.87), calls=%async_computation | async-start | bytes 2097152 | tf_op jit(solution)/shard_map/all_to_all | solution.py:57
  157.2 4.7 %copy-start.4 = (bf16[768,512]{0,1:T(8,128)(2,1)S(1)}, bf16[768,512]{0,1:T(8,128)(2,1)}, u32[]{:S(2)}) copy-start(bf16[768,512]{0,1:T(8,128)(2,1)} %copy.23) | copy-start | bytes 2359300
  162.0 3.2 %copy-start.12 = (bf16[8,128,384]{2,1,0:T(8,128)(2,1)S(1)}, bf16[8,128,384]{2,1,0:T(8,128)(2,1)}, u32[]{:S(2)}) copy-start(bf16[8,128,384]{2,1,0:T(8,128)(2,1)} %get-tuple-element.115) | copy-start | bytes 2359300
  162.0 3.2 %copy-start.13 = (bf16[8,128,384]{2,1,0:T(8,128)(2,1)S(1)}, bf16[8,128,384]{2,1,0:T(8,128)(2,1)}, u32[]{:S(2)}) copy-start(bf16[8,128,384]{2,1,0:T(8,128)(2,1)} %get-tuple-element.116) | copy-start | bytes 2359300
  162.0 3.2 %copy-start.14 = (bf16[8,128,384]{2,1,0:T(8,128)(2,1)S(1)}, bf16[8,128,384]{2,1,0:T(8,128)(2,1)}, u32[]{:S(2)}) copy-start(bf16[8,128,384]{2,1,0:T(8,128)(2,1)} %get-tuple-element.117) | copy-start | bytes 2359300
  162.0 3.2 %copy-start.22 = (bf16[8,384,64]{1,2,0:T(8,128)(2,1)S(1)}, bf16[8,384,64]{1,2,0:T(8,128)(2,1)}, u32[]{:S(2)}) copy-start(bf16[8,384,64]{1,2,0:T(8,128)(2,1)} %get-tuple-element.320) | copy-start | bytes 1179652
  167.0 2.4 copy-start.8
  169.4 16.1 %copy-start.3 = (bf16[3,1024,512]{2,1,0:T(8,128)(2,1)S(1)}, bf16[3,1024,512]{2,1,0:T(8,128)(2,1)}, u32[]{:S(2)}) copy-start(bf16[3,1024,512]{2,1,0:T(8,128)(2,1)} %all-gather.2.cloned.1.call-done) | copy-start | bytes 9437188
  180.5 51.9 %all-to-all-start.1 = ((bf16[16,64,1024]{2,1,0:T(8,128)(2,1)}), bf16[16,64,1024]{2,1,0:T(8,128)(2,1)}, u32[]{:S(2)}, u32[]{:S(2)}) async-start(bf16[16,64,1024]{2,1,0:T(8,128)(2,1)} %bitcast.189), calls=%async_computation.1 | async-start | bytes 4194304 | tf_op jit(solution)/shard_map/all_to_all | solution.py:57
  188.7 2.5 %collective-permute-start.7 = (bf16[384,1024]{1,0:T(8,128)(2,1)}, bf16[384,1024]{1,0:T(8,128)(2,1)S(1)}, u32[]{:S(2)}, u32[]{:S(2)}) collective-permute-start(bf16[384,1024]{1,0:T(8,128)(2,1)} %add_convert_fusion.1), channel_id=1, source_target_pairs={{0,1},{1,0},{2,3},{3,2},{4,5},{5,4},{6,7},{7,6},{8,9},{9,8},{10,11... | collective-permute-start | bytes 2359304 | tf_op jit(solution)/shard_map/ppermute | solution.py:67
  (15 other events, 23.4 us)
Sparse Core Ops, SparseCore 0:
  10.2 46.0 all-gather.1

commit v11 on v9

--- a/solution.py
+++ b/solution.py
@@ -90,12 +90,12 @@
     left_tokens, right_tokens = neighbour_tokens(tokens, halo)
     left_up = shifted(upstream[length - halo :], "ctx", 1)
     right_up = shifted(upstream[:halo], "ctx", -1)
-    gathered = lax.all_gather(jnp.stack([w_query, w_key, w_value]), "dp", axis=1, tiled=True)
-    query_full, key_full, value_full = gathered[0], gathered[1], gathered[2]
+    projection = lax.all_gather(
+        jnp.concatenate([w_query, w_key, w_value], axis=1), "dp", axis=0, tiled=True
+    )
 
     frame_tokens = jnp.concatenate([left_tokens, tokens, right_tokens], axis=0)
-    all_weights = jnp.concatenate([query_full, key_full, value_full], axis=1)
-    frame_proj = jnp.dot(frame_tokens, all_weights, preferred_element_type=jnp.float32).astype(
+    frame_proj = jnp.dot(frame_tokens, projection, preferred_element_type=jnp.float32).astype(
         jnp.bfloat16
     )
     query_h = head_major(frame_proj[:, :features], heads)
@@ -202,10 +202,11 @@
     value_grad = token_major(value_own).astype(jnp.bfloat16)
 
     contract = (((1,), (1,)), ((), ()))
-    partial_input = (
-        lax.dot_general(query_grad, query_full, contract, preferred_element_type=jnp.float32)
-        + lax.dot_general(key_grad, key_full, contract, preferred_element_type=jnp.float32)
-        + lax.dot_general(value_grad, value_full, contract, preferred_element_type=jnp.float32)
+    partial_input = lax.dot_general(
+        jnp.concatenate([query_grad, key_grad, value_grad], axis=1),
+        projection,
+        contract,
+        preferred_element_type=jnp.float32,
     )
     grad_input = section_sum(partial_input)[None]
 

time: 191 us -> 191 us (level)
  matrix products: 36 us -> 38.9 us
  other arithmetic: 19.3 us -> 16.6 us
    dot_general x4 -> x2, matrix products: 7.79 us -> 12.4 us  [the longest x1 7.83 us: per_device(): jnp.dot(frame_tokens, projection, preferred_element_type=jnp.float32)]
    reduce_sum x2, other arithmetic: 3.38 us -> 0.53 us  [summed_rows(): return jnp.sum(parts.astype(jnp.float32), axis=0)]
    another operation x1 -> x0, other arithmetic: 2.77 us -> none  [per_device(): jnp.stack([w_query, w_key, w_value])]
    concatenate x0 -> x1, other arithmetic: none -> 2.71 us  [per_device(): jnp.concatenate([w_query, w_key, w_value], axis=1)]
    squeeze x1 -> x0, local copies, waits for them, and re-layouts: 2.06 us -> none  [per_device(): query_full, key_full, value_full = (gathered[0], gathered[1], gathered[2])]
where the time goes in v11:
time: 191 us; the launch traced here: 190 us
  waiting for transfers between devices  62.4 us (33%)
  matrix products  38.9 us (20%)
  starting transfers between devices  30.6 us (16%)
  between operations  22.4 us (12%)
  local copies, waits for them, and re-layouts  19.3 us (10%)
  other arithmetic  16.6 us (9%)
    all_to_all x2, waiting for transfers between devices, summed_rows(): parts = lax.all_to_all(term, group, 0, 0, tiled=True)  45.5 us
    ppermute x6, starting transfers between devices, shifted(): lax.ppermute(value, axis, [(source, source + steps) for source in range(l...  19.4 us
    ppermute x6, waiting for transfers between devices, shifted(): lax.ppermute(value, axis, [(source, source + steps) for source in range(l...  14 us
    all_to_all x2, starting transfers between devices, summed_rows(): parts = lax.all_to_all(term, group, 0, 0, tiled=True)  11 us
    dot_general x1, matrix products, per_device(): jnp.dot(frame_tokens, projection, preferred_element_type=jnp.float32)  7.83 us
    dot_general x1, matrix products, per_device(): jnp.einsum('hqd,hkd->hqk', near_query, key_part, preferred_element_type=j...  4.94 us
    dot_general x1, matrix products, per_device(): lax.dot_general(jnp.concatenate([query_grad, key_grad, value_grad], axis=...  4.6 us
    dot_general x3, matrix products, per_device(): jnp.einsum('hqd,hkd->hqk', upstream_block, value_window, preferred_elemen...  4.57 us
  transfers between devices with their start and end apart: 11, of which 7 were waited for; matrix products, arithmetic and copies ran while one was open for 23% of the time, Pallas kernels for 0%

profile of v11, /device:TPU:12, one launch (start us, length us, event | category | flops | bytes accessed | tf_op | source)
XLA Modules:
  0.0 190.1 jit_solution(4631207182505510316)
XLA Ops:
  7.2 2.7 %pad_maximum_fusion = bf16[512,1536]{1,0:T(8,128)(2,1)} fusion(bf16[512,512]{1,0:T(8,128)(2,1)} %param.9, bf16[512,512]{1,0:T(8,128)(2,1)} %param.8, bf16[512,512]{1,0:T(8,128)(2,1)} %param.7), kind=kLoop, calls=%fused_computation.55 | loop fusion | flops 4718592 | bytes 3145728 | tf_op jit(solution)/shard_map/concatenate | solution.py:94
  10.0 2.4 %collective-permute-start.1 = (bf16[384,512]{1,0:T(8,128)(2,1)S(1)}, bf16[384,512]{1,0:T(8,128)(2,1)S(1)}, u32[]{:S(2)}, u32[]{:S(2)}) collective-permute-start(bf16[384,512]{1,0:T(8,128)(2,1)S(1)} %dynamic-slice_bitcast_fusion), channel_id=1, source_target_pairs={{4,0},{8,4},{12,8},{16,12},{20,16},{24,20},{28,24},{5,1},{9,5},{13... | collective-permute-start | bytes 1179656 | tf_op jit(solution)/shard_map/ppermute | solution.py:14
  12.5 4.3 %collective-permute-start = (bf16[384,512]{1,0:T(8,128)(2,1)S(1)}, bf16[384,512]{1,0:T(8,128)(2,1)S(1)}, u32[]{:S(2)}, u32[]{:S(2)}) collective-permute-start(bf16[384,512]{1,0:T(8,128)(2,1)S(1)} %dynamic-slice_bitcast_fusion), channel_id=1, source_target_pairs={{0,4},{4,8},{8,12},{12,16},{16,20},{20,24},{24,28},{1,5},{5,9},{9,... | collective-permute-start | bytes 1179656 | tf_op jit(solution)/shard_map/ppermute | solution.py:14
  16.8 1.9 %collective-permute-start.6 = (bf16[384,512]{1,0:T(8,128)(2,1)S(1)}, bf16[384,512]{1,0:T(8,128)(2,1)S(1)}, u32[]{:S(2)}, u32[]{:S(2)}) collective-permute-start(bf16[384,512]{1,0:T(8,128)(2,1)S(1)} %bitcast.176), channel_id=1, source_target_pairs={{4,0},{8,4},{12,8},{16,12},{20,16},{24,20},{28,24},{5,1},{9,5},{13... | collective-permute-start | bytes 1179656 | tf_op jit(solution)/shard_map/ppermute | solution.py:14
  18.7 4.8 %collective-permute-start.5 = (bf16[384,512]{1,0:T(8,128)(2,1)S(1)}, bf16[384,512]{1,0:T(8,128)(2,1)}, u32[]{:S(2)}, u32[]{:S(2)}) collective-permute-start(bf16[384,512]{1,0:T(8,128)(2,1)S(1)} %bitcast.177), channel_id=1, source_target_pairs={{0,4},{4,8},{8,12},{12,16},{16,20},{20,24},{24,28},{1,5},{5,9},{9,... | collective-permute-start | bytes 1179656 | tf_op jit(solution)/shard_map/ppermute | solution.py:14
  32.3 6.5 %collective-permute-done.1 = bf16[384,512]{1,0:T(8,128)(2,1)S(1)} collective-permute-done((bf16[384,512]{1,0:T(8,128)(2,1)S(1)}, bf16[384,512]{1,0:T(8,128)(2,1)S(1)}, u32[]{:S(2)}, u32[]{:S(2)}) %collective-permute-start.1) | collective-permute-done | bytes 393248 | tf_op jit(solution)/shard_map/ppermute | solution.py:14
  38.8 1.8 collective-permute-done
  43.3 2.7 %collective-permute-done.6 = bf16[384,512]{1,0:T(8,128)(2,1)S(1)} collective-permute-done((bf16[384,512]{1,0:T(8,128)(2,1)S(1)}, bf16[384,512]{1,0:T(8,128)(2,1)S(1)}, u32[]{:S(2)}, u32[]{:S(2)}) %collective-permute-start.6) | collective-permute-done | bytes 393248 | tf_op jit(solution)/shard_map/ppermute | solution.py:14
  46.1 3.0 %collective-permute-done.5 = bf16[384,512]{1,0:T(8,128)(2,1)} collective-permute-done((bf16[384,512]{1,0:T(8,128)(2,1)S(1)}, bf16[384,512]{1,0:T(8,128)(2,1)}, u32[]{:S(2)}, u32[]{:S(2)}) %collective-permute-start.5) | collective-permute-done | bytes 393248 | tf_op jit(solution)/shard_map/ppermute | solution.py:14
  51.3 2.0 %maximum_select_fusion = bf16[2,384,1024]{2,1,0:T(8,128)(2,1)S(1)} fusion(bf16[2,384,512]{2,1,0:T(8,128)(2,1)} %collective-permute-done.2, bf16[1,384,512]{2,1,0:T(8,128)(2,1)S(1)} %bitcast.172, bf16[1,384,512]{2,1,0:T(8,128)(2,1)S(1)} %bitcast.174, pred[]{:T(512)S(6)} %eq.3), kind=kLoop, calls=%fused_computation.54 | loop fusion | flops 10223616 | bytes 3145729 | tf_op jit(solution)/shard_map/jit(_where)/select_n | solution.py:27
  53.4 2.8 %all-gather.2.cloned.1.call-done = bf16[1024,1536]{1,0:T(8,128)(2,1)} async-done(((bf16[512,1536]{1,0:T(8,128)(2,1)}), bf16[1024,1536]{1,0:T(8,128)(2,1)}) %all-gather.2.cloned.1.call-update) | async-done | bytes 3145744 | tf_op jit(solution)/shard_map/all_gather | solution.py:93
  56.2 7.8 %convolution_convert_fusion = bf16[1152,1536]{1,0:T(8,128)(2,1)S(1)} fusion(bf16[1024,1536]{1,0:T(8,128)(2,1)} %all-gather.2.cloned.1.call-done, bf16[384,1024]{1,0:T(8,128)(2,1)S(1)} %get-tuple-element.22, bf16[384,1024]{1,0:T(8,128)(2,1)S(1)} %bitcast.167, bf16[384,1024]{1,0:T(8,128)(2,1)S(1)} %get-tuple-element.21), kind=kOutput, calls=%fused_computation.2 | convolution fusion | flops 3632726016 | bytes 9043968 | tf_op jit(solution)/shard_map/dot_general | solution.py:98
  64.3 1.4 copy.20
  68.9 1.5 fusion.16
  75.0 1.5 fusion.22
  76.6 1.5 fusion.24
  79.9 1.5 fusion.19
  81.4 1.3 fusion.21
  82.8 3.5 %collective-permute-start.3 = (f32[3,8,384,1]{2,1,3,0:T(8,128)S(1)}, f32[3,8,384,1]{2,1,3,0:T(8,128)S(1)}, u32[]{:S(2)}, u32[]{:S(2)}) collective-permute-start(f32[3,8,384,1]{2,1,3,0:T(8,128)S(1)} %pad_maximum_fusion.5), channel_id=1, source_target_pairs={{0,4},{4,8},{8,12},{12,16},{16,20},{20,24},{24,28},{1,5},{5,9},{9,... | collective-permute-start | bytes 110600 | tf_op jit(solution)/shard_map/ppermute | solution.py:14
  91.0 2.5 %collective-permute-start.4 = (f32[3,8,384,1]{2,1,3,0:T(8,128)S(1)}, f32[3,8,384,1]{2,1,3,0:T(8,128)S(1)}, u32[]{:S(2)}, u32[]{:S(2)}) collective-permute-start(f32[3,8,384,1]{2,1,3,0:T(8,128)S(1)} %pad_maximum_fusion.5), channel_id=1, source_target_pairs={{4,0},{8,4},{12,8},{16,12},{20,16},{24,20},{28,24},{5,1},{9,5},{13... | collective-permute-start | bytes 110600 | tf_op jit(solution)/shard_map/ppermute | solution.py:14
  97.4 1.4 copy.28
  98.8 6.1 %all-to-all-start = ((bf16[16,64,512]{2,1,0:T(8,128)(2,1)}), bf16[16,64,512]{2,1,0:T(8,128)(2,1)S(1)}, u32[]{:S(2)}, u32[]{:S(2)}) async-start(bf16[16,64,512]{2,1,0:T(8,128)(2,1)} %bitcast.156), calls=%async_computation | async-start | bytes 2097152 | tf_op jit(solution)/shard_map/all_to_all | solution.py:57
  104.9 4.9 %fusion.112 = (bf16[8,768,384]{2,1,0:T(8,128)(2,1)S(1)}, f32[8,768,384]{2,1,0:T(8,128)S(1)}) fusion(f32[8,768]{1,0:T(8,128)S(1)} %get-tuple-element.27, f32[8,768]{1,0:T(8,128)S(1)} %get-tuple-element.28, bf16[8,1152,64]{1,2,0:T(8,128)(2,1)S(1)} %bitcast.151, bf16[8,384,64]{1,2,0:T(8,128)(2,1)} %get-tuple-element.24, ...), kind=kOutput, calls=%fused_computation.167 | convolution fusion | flops 315359232 | bytes 15679488 | tf_op jit(solution)/shard_map/hqd,hkd->hqk/dot_general | solution.py:181
  109.9 3.2 %multiply_convert_fusion = bf16[8,768,384]{2,1,0:T(8,128)(2,1)S(1)} fusion(f32[8,768,384]{2,1,0:T(8,128)S(1)} %get-tuple-element.54, f32[8,768]{1,0:T(8,128)S(1)} %get-tuple-element.26, bf16[8,768,64]{1,2,0:T(8,128)(2,1)S(1)} %bitcast.157, bf16[8,1152,64]{1,2,0:T(8,128)(2,1)} %bitcast.160), kind=kOutput, calls=%fused_computation | convolution fusion | flops 309067776 | bytes 15360000 | tf_op jit(solution)/shard_map/hqd,hkd->hqk/dot_general | solution.py:186
  113.2 1.6 fusion.43
  115.1 1.6 fusion.40
  117.4 2.6 %convolution_convert_fusion.1 = bf16[1024,1024]{0,1:T(8,128)(2,1)} fusion(bf16[384,512]{0,1:T(8,128)(2,1)S(1)} %bitcast.192, bf16[384,512]{0,1:T(8,128)(2,1)S(1)} %bitcast.194, bf16[1,384,1024]{2,1,0:T(8,128)(2,1)S(1)} %copy-done.11), kind=kOutput, calls=%fused_computation.53 | convolution fusion | flops 807927808 | bytes 3670016 | tf_op jit(solution)/shard_map/tr,tf->rf/dot_general | solution.py:213
  120.0 9.6 %all-to-all-done = bf16[16,64,512]{2,1,0:T(8,128)(2,1)S(1)} async-done(((bf16[16,64,512]{2,1,0:T(8,128)(2,1)}), bf16[16,64,512]{2,1,0:T(8,128)(2,1)S(1)}, u32[]{:S(2)}, u32[]{:S(2)}) %all-to-all-start) | async-done | bytes 1048608 | tf_op jit(solution)/shard_map/all_to_all | solution.py:57
  129.6 5.0 %all-to-all-start.1 = ((bf16[16,64,1024]{2,1,0:T(8,128)(2,1)}), bf16[16,64,1024]{2,1,0:T(8,128)(2,1)S(1)}, u32[]{:S(2)}, u32[]{:S(2)}) async-start(bf16[16,64,1024]{2,1,0:T(8,128)(2,1)} %bitcast.159), calls=%async_computation.1 | async-start | bytes 4194304 | tf_op jit(solution)/shard_map/all_to_all | solution.py:57
  134.6 4.6 %convolution_convert_fusion.3 = bf16[384,1024]{1,0:T(8,128)(2,1)} fusion(bf16[1024,1536]{1,0:T(8,128)(2,1)} %all-gather.2.cloned.1.call-done, bf16[384,512]{0,1:T(8,128)(2,1)} %bitcast.193, bf16[384,512]{0,1:T(8,128)(2,1)} %bitcast.195, bf16[384,512]{0,1:T(8,128)(2,1)S(1)} %bitcast.170), kind=kOutput, calls=%fused_computation.58 | convolution fusion | flops 1211891712 | bytes 5111808 | tf_op jit(solution)/shard_map/dot_general | solution.py:205
  142.7 2.6 %fusion.80 = bf16[1,384,1024]{2,1,0:T(8,128)(2,1)} fusion(bf16[384,1024]{1,0:T(8,128)(2,1)} %collective-permute-done.7, bf16[384,1024]{1,0:T(8,128)(2,1)} %convolution_convert_fusion.3), kind=kLoop, calls=%fused_computation.103 | loop fusion | flops 1572864 | bytes 2359296 | tf_op jit(solution)/shard_map/broadcast_in_dim | solution.py:211
  145.5 36.0 %all-to-all-done.1 = bf16[16,64,1024]{2,1,0:T(8,128)(2,1)S(1)} async-done(((bf16[16,64,1024]{2,1,0:T(8,128)(2,1)}), bf16[16,64,1024]{2,1,0:T(8,128)(2,1)S(1)}, u32[]{:S(2)}, u32[]{:S(2)}) %all-to-all-start.1) | async-done | bytes 2097184 | tf_op jit(solution)/shard_map/all_to_all | solution.py:57
  (126 shorter events, 31.1 us)
Async XLA Ops:
  7.2 2.8 %copy-start.9 = (bf16[1,384,1024]{2,1,0:T(8,128)(2,1)S(1)}, bf16[1,384,1024]{2,1,0:T(8,128)(2,1)}, u32[]{:S(2)}) copy-start(bf16[1,384,1024]{2,1,0:T(8,128)(2,1)} %param.6) | copy-start | bytes 2359300
  7.2 9.6 %copy-start.23 = (bf16[1,384,512]{2,1,0:T(8,128)(2,1)S(1)}, bf16[1,384,512]{2,1,0:T(8,128)(2,1)}, u32[]{:S(2)}) copy-start(bf16[1,384,512]{2,1,0:T(8,128)(2,1)} %param.11) | copy-start | bytes 1179652
  7.2 16.4 %copy-start.26 = (s32[24,7]{0,1:T(8,128)S(1)}, s32[24,7]{0,1:T(8,128)}, u32[]{:S(2)}) copy-start(s32[24,7]{0,1:T(8,128)} %param.10) | copy-start | bytes 2020
  7.2 49.0 %all-gather.2.cloned.1.call-start = ((), (), s32[]{:S(2)}) async-start(), calls=%async_computation.2 | async-start | bytes 4718592 | tf_op jit(solution)/shard_map/all_gather | solution.py:93
  10.0 28.8 %collective-permute-start.1 = (bf16[384,512]{1,0:T(8,128)(2,1)S(1)}, bf16[384,512]{1,0:T(8,128)(2,1)S(1)}, u32[]{:S(2)}, u32[]{:S(2)}) collective-permute-start(bf16[384,512]{1,0:T(8,128)(2,1)S(1)} %dynamic-slice_bitcast_fusion), channel_id=1, source_target_pairs={{4,0},{8,4},{12,8},{16,12},{20,16},{24,20},{28,24},{5,1},{9,5},{13... | collective-permute-start | bytes 1179656 | tf_op jit(solution)/shard_map/ppermute | solution.py:14
  12.5 28.2 %collective-permute-start = (bf16[384,512]{1,0:T(8,128)(2,1)S(1)}, bf16[384,512]{1,0:T(8,128)(2,1)S(1)}, u32[]{:S(2)}, u32[]{:S(2)}) collective-permute-start(bf16[384,512]{1,0:T(8,128)(2,1)S(1)} %dynamic-slice_bitcast_fusion), channel_id=1, source_target_pairs={{0,4},{4,8},{8,12},{12,16},{16,20},{20,24},{24,28},{1,5},{5,9},{9,... | collective-permute-start | bytes 1179656 | tf_op jit(solution)/shard_map/ppermute | solution.py:14
  16.8 29.3 %collective-permute-start.6 = (bf16[384,512]{1,0:T(8,128)(2,1)S(1)}, bf16[384,512]{1,0:T(8,128)(2,1)S(1)}, u32[]{:S(2)}, u32[]{:S(2)}) collective-permute-start(bf16[384,512]{1,0:T(8,128)(2,1)S(1)} %bitcast.176), channel_id=1, source_target_pairs={{4,0},{8,4},{12,8},{16,12},{20,16},{24,20},{28,24},{5,1},{9,5},{13... | collective-permute-start | bytes 1179656 | tf_op jit(solution)/shard_map/ppermute | solution.py:14
  18.7 30.3 %collective-permute-start.5 = (bf16[384,512]{1,0:T(8,128)(2,1)S(1)}, bf16[384,512]{1,0:T(8,128)(2,1)}, u32[]{:S(2)}, u32[]{:S(2)}) collective-permute-start(bf16[384,512]{1,0:T(8,128)(2,1)S(1)} %bitcast.177), channel_id=1, source_target_pairs={{0,4},{4,8},{8,12},{12,16},{16,20},{20,24},{24,28},{1,5},{5,9},{9,... | collective-permute-start | bytes 1179656 | tf_op jit(solution)/shard_map/ppermute | solution.py:14
  40.7 10.6 %collective-permute-start.2 = (bf16[2,384,512]{2,1,0:T(8,128)(2,1)S(1)}, bf16[2,384,512]{2,1,0:T(8,128)(2,1)}, u32[]{:S(2)}, u32[]{:S(2)}) collective-permute-start(bf16[2,384,512]{2,1,0:T(8,128)(2,1)S(1)} %pad_maximum_fusion.1), channel_id=1, source_target_pairs={{0,1},{1,0},{2,3},{3,2},{4,5},{5,4},{6,7},{7,6},{8,9},{9,8},{10,11... | collective-permute-start | bytes 2359304 | tf_op jit(solution)/shard_map/ppermute | solution.py:42
  71.7 22.7 %copy-start = (bf16[8,128,896]{2,1,0:T(8,128)(2,1)}, bf16[8,128,896]{2,1,0:T(8,128)(2,1)S(1)}, u32[]{:S(2)}) copy-start(bf16[8,128,896]{2,1,0:T(8,128)(2,1)S(1)} %get-tuple-element.17) | copy-start | bytes 5505028
  78.1 17.3 %copy-start.2 = (bf16[8,128,896]{2,1,0:T(8,128)(2,1)}, bf16[8,128,896]{2,1,0:T(8,128)(2,1)S(1)}, u32[]{:S(2)}) copy-start(bf16[8,128,896]{2,1,0:T(8,128)(2,1)S(1)} %get-tuple-element.13) | copy-start | bytes 5505028
  82.7 13.7 %copy-start.4 = (bf16[8,128,896]{2,1,0:T(8,128)(2,1)}, bf16[8,128,896]{2,1,0:T(8,128)(2,1)S(1)}, u32[]{:S(2)}) copy-start(bf16[8,128,896]{2,1,0:T(8,128)(2,1)S(1)} %get-tuple-element.15) | copy-start | bytes 5505028
  82.7 4.5 %copy-start.10 = (bf16[1,384,1024]{2,1,0:T(8,128)(2,1)S(1)}, bf16[1,384,1024]{2,1,0:T(8,128)(2,1)}, u32[]{:S(2)}) copy-start(bf16[1,384,1024]{2,1,0:T(8,128)(2,1)} %param.6) | copy-start | bytes 2359300
  82.8 22.0 %collective-permute-start.3 = (f32[3,8,384,1]{2,1,3,0:T(8,128)S(1)}, f32[3,8,384,1]{2,1,3,0:T(8,128)S(1)}, u32[]{:S(2)}, u32[]{:S(2)}) collective-permute-start(f32[3,8,384,1]{2,1,3,0:T(8,128)S(1)} %pad_maximum_fusion.5), channel_id=1, source_target_pairs={{0,4},{4,8},{8,12},{12,16},{16,20},{20,24},{24,28},{1,5},{5,9},{9,... | collective-permute-start | bytes 110600 | tf_op jit(solution)/shard_map/ppermute | solution.py:14
  87.2 3.7 %copy-start.12 = (bf16[8,384,64]{1,2,0:T(8,128)(2,1)}, bf16[8,384,64]{1,2,0:T(8,128)(2,1)S(1)}, u32[]{:S(2)}) copy-start(bf16[8,384,64]{1,2,0:T(8,128)(2,1)S(1)} %pad_maximum_fusion.4) | copy-start | bytes 1179652
  91.0 13.9 %collective-permute-start.4 = (f32[3,8,384,1]{2,1,3,0:T(8,128)S(1)}, f32[3,8,384,1]{2,1,3,0:T(8,128)S(1)}, u32[]{:S(2)}, u32[]{:S(2)}) collective-permute-start(f32[3,8,384,1]{2,1,3,0:T(8,128)S(1)} %pad_maximum_fusion.5), channel_id=1, source_target_pairs={{4,0},{8,4},{12,8},{16,12},{20,16},{24,20},{28,24},{5,1},{9,5},{13... | collective-permute-start | bytes 110600 | tf_op jit(solution)/shard_map/ppermute | solution.py:14
  98.8 30.8 %all-to-all-start = ((bf16[16,64,512]{2,1,0:T(8,128)(2,1)}), bf16[16,64,512]{2,1,0:T(8,128)(2,1)S(1)}, u32[]{:S(2)}, u32[]{:S(2)}) async-start(bf16[16,64,512]{2,1,0:T(8,128)(2,1)} %bitcast.156), calls=%async_computation | async-start | bytes 2097152 | tf_op jit(solution)/shard_map/all_to_all | solution.py:57
  104.9 5.0 %copy-start.6 = (bf16[768,512]{0,1:T(8,128)(2,1)S(1)}, bf16[768,512]{0,1:T(8,128)(2,1)}, u32[]{:S(2)}) copy-start(bf16[768,512]{0,1:T(8,128)(2,1)} %copy.27) | copy-start | bytes 2359300
  109.9 3.2 %copy-start.17 = (bf16[8,128,384]{2,1,0:T(8,128)(2,1)S(1)}, bf16[8,128,384]{2,1,0:T(8,128)(2,1)}, u32[]{:S(2)}) copy-start(bf16[8,128,384]{2,1,0:T(8,128)(2,1)} %slice.214) | copy-start | bytes 2359300
  109.9 3.2 %copy-start.18 = (bf16[8,128,384]{2,1,0:T(8,128)(2,1)S(1)}, bf16[8,128,384]{2,1,0:T(8,128)(2,1)}, u32[]{:S(2)}) copy-start(bf16[8,128,384]{2,1,0:T(8,128)(2,1)} %slice.212) | copy-start | bytes 2359300
  109.9 3.2 %copy-start.19 = (bf16[8,128,384]{2,1,0:T(8,128)(2,1)S(1)}, bf16[8,128,384]{2,1,0:T(8,128)(2,1)}, u32[]{:S(2)}) copy-start(bf16[8,128,384]{2,1,0:T(8,128)(2,1)} %slice.213) | copy-start | bytes 2359300
  109.9 3.2 %copy-start.25 = (bf16[1,384,512]{1,2,0:T(8,128)(2,1)S(1)}, bf16[1,384,512]{1,2,0:T(8,128)(2,1)}, u32[]{:S(2)}) copy-start(bf16[1,384,512]{1,2,0:T(8,128)(2,1)} %copy.21) | copy-start | bytes 1179652
  113.1 1.8 copy-start.21
  113.2 1.9 copy-start.22
  114.8 1.9 copy-start.27
  115.1 2.4 %copy-start.11 = (bf16[1,384,1024]{2,1,0:T(8,128)(2,1)S(1)}, bf16[1,384,1024]{2,1,0:T(8,128)(2,1)}, u32[]{:S(2)}) copy-start(bf16[1,384,1024]{2,1,0:T(8,128)(2,1)} %param.6) | copy-start | bytes 2359300
  117.4 17.1 %copy-start.13 = (bf16[8,384,64]{1,2,0:T(8,128)(2,1)S(1)}, bf16[8,384,64]{1,2,0:T(8,128)(2,1)}, u32[]{:S(2)}) copy-start(bf16[8,384,64]{1,2,0:T(8,128)(2,1)} %copy-done.12) | copy-start | bytes 1179652
  129.6 51.9 %all-to-all-start.1 = ((bf16[16,64,1024]{2,1,0:T(8,128)(2,1)}), bf16[16,64,1024]{2,1,0:T(8,128)(2,1)S(1)}, u32[]{:S(2)}, u32[]{:S(2)}) async-start(bf16[16,64,1024]{2,1,0:T(8,128)(2,1)} %bitcast.159), calls=%async_computation.1 | async-start | bytes 4194304 | tf_op jit(solution)/shard_map/all_to_all | solution.py:57
  134.5 4.6 %copy-start.1 = (bf16[8,128,896]{2,1,0:T(8,128)(2,1)S(1)}, bf16[8,128,896]{2,1,0:T(8,128)(2,1)}, u32[]{:S(2)}) copy-start(bf16[8,128,896]{2,1,0:T(8,128)(2,1)} %copy-done) | copy-start | bytes 5505028
  134.6 4.6 %copy-start.8 = (bf16[1152,512]{0,1:T(8,128)(2,1)S(1)}, bf16[1152,512]{0,1:T(8,128)(2,1)}, u32[]{:S(2)}) copy-start(bf16[1152,512]{0,1:T(8,128)(2,1)} %copy.20) | copy-start | bytes 3538948
  134.6 5.4 %copy-start.3 = (bf16[8,128,896]{2,1,0:T(8,128)(2,1)S(1)}, bf16[8,128,896]{2,1,0:T(8,128)(2,1)}, u32[]{:S(2)}) copy-start(bf16[8,128,896]{2,1,0:T(8,128)(2,1)} %copy-done.2) | copy-start | bytes 5505028
  139.2 3.5 %collective-permute-start.7 = (bf16[384,1024]{1,0:T(8,128)(2,1)}, bf16[384,1024]{1,0:T(8,128)(2,1)}, u32[]{:S(2)}, u32[]{:S(2)}) collective-permute-start(bf16[384,1024]{1,0:T(8,128)(2,1)} %convolution_convert_fusion.3), channel_id=1, source_target_pairs={{0,1},{1,0},{2,3},{3,2},{4,5},{5,4},{6,7},{7,6},{8,9},{9,8},{10,11... | collective-permute-start | bytes 2359304 | tf_op jit(solution)/shard_map/ppermute | solution.py:67
  (8 other events, 12.7 us)
Sparse Core Ops, SparseCore 0:
  10.1 46.0 all-gather.1

commit v12 on v9

--- a/solution.py
+++ b/solution.py
@@ -1,5 +1,6 @@
 import jax
 import jax.numpy as jnp
+import numpy as np
 from jax import lax
 from jax.sharding import PartitionSpec as P
 
@@ -164,14 +165,11 @@
     stats_right = shifted(stats[:, :, :halo], "ctx", -1)
 
     near = list(range(REACH)) + list(range(REACH + blocks, frame_blocks))
-    allowed = []
-    for at in near:
-        row = []
-        for block in range(own_low, own_high + 1):
-            slot = block - at + REACH
-            row.append(frame_mask[at, slot] > 0 if 0 <= slot < span_len else jnp.zeros((), bool))
-        allowed.append(jnp.stack(row))
-    allowed = jnp.repeat(jnp.repeat(jnp.stack(allowed), BLOCK, axis=0), BLOCK, axis=1)[None]
+    slots = np.arange(own_low, own_high + 1)[None, :] - np.array(near)[:, None] + REACH
+    inside = (slots >= 0) & (slots < span_len)
+    picked = frame_mask[np.array(near)[:, None], np.clip(slots, 0, span_len - 1)]
+    allowed = (picked > 0) & inside
+    allowed = jnp.repeat(jnp.repeat(allowed, BLOCK, axis=0), BLOCK, axis=1)[None]
     near_stats = jnp.concatenate([stats_left, stats_right], axis=2)
     top, total, delta = near_stats[0], near_stats[1], near_stats[2]
     near_query = jnp.concatenate([rows(query_h, 0, REACH), rows(query_h, REACH + blocks, REACH)], axis=1)
@@ -188,24 +186,25 @@
     )
     score_grad = (probability * (prob_grad - delta)).astype(jnp.bfloat16)
     all_score_grads = jnp.concatenate(own_score_grads + [score_grad], axis=1)
-    all_weights = jnp.concatenate(own_weights + [weights], axis=1)
+    every_weight = jnp.concatenate(own_weights + [weights], axis=1)
     all_queries = jnp.concatenate([rows(query_h, REACH, blocks), near_query], axis=1)
     all_upstream = jnp.concatenate([own_upstream, near_upstream], axis=1)
     key_own = score_scale * jnp.einsum(
         "hqk,hqd->hkd", all_score_grads, all_queries, preferred_element_type=jnp.float32
     )
     value_own = jnp.einsum(
-        "hqk,hqd->hkd", all_weights, all_upstream, preferred_element_type=jnp.float32
+        "hqk,hqd->hkd", every_weight, all_upstream, preferred_element_type=jnp.float32
     )
 
     key_grad = token_major(key_own).astype(jnp.bfloat16)
     value_grad = token_major(value_own).astype(jnp.bfloat16)
 
     contract = (((1,), (1,)), ((), ()))
-    partial_input = (
-        lax.dot_general(query_grad, query_full, contract, preferred_element_type=jnp.float32)
-        + lax.dot_general(key_grad, key_full, contract, preferred_element_type=jnp.float32)
-        + lax.dot_general(value_grad, value_full, contract, preferred_element_type=jnp.float32)
+    partial_input = lax.dot_general(
+        jnp.concatenate([query_grad, key_grad, value_grad], axis=1),
+        all_weights,
+        contract,
+        preferred_element_type=jnp.float32,
     )
     grad_input = section_sum(partial_input)[None]
 

time: 191 us -> 189 us (0.990)
  waiting for transfers between devices: 61.3 us -> 70.2 us
  between operations: 22.4 us -> 14.8 us
  other arithmetic: 19.3 us -> 16.4 us
    ppermute x6, waiting for transfers between devices: 14 us -> 21.7 us  [shifted(): lax.ppermute(value, axis, [(source, source + steps) for source in range(l...]
    reduce_sum x2, other arithmetic: 3.38 us -> 0.53 us  [summed_rows(): return jnp.sum(parts.astype(jnp.float32), axis=0)]
    dot_general x4 -> x2, matrix products: 5.56 us -> 6.19 us  [the longest x1 4.56 us: per_device(): lax.dot_general(jnp.concatenate([query_grad, key_grad, value_grad], axis=...]
    unnamed x64 -> x74, local copies, waits for them, and re-layouts: 3.68 us -> 3.89 us
where the time goes in v12:
time: 189 us; the launch traced here: 188 us
  waiting for transfers between devices  70.2 us (37%)
  matrix products  34.9 us (18%)
  starting transfers between devices  30.6 us (16%)
  local copies, waits for them, and re-layouts  21.6 us (11%)
  other arithmetic  16.4 us (9%)
  between operations  14.8 us (8%)
    all_to_all x2, waiting for transfers between devices, summed_rows(): parts = lax.all_to_all(term, group, 0, 0, tiled=True)  45.5 us
    ppermute x6, waiting for transfers between devices, shifted(): lax.ppermute(value, axis, [(source, source + steps) for source in range(l...  21.7 us
    ppermute x6, starting transfers between devices, shifted(): lax.ppermute(value, axis, [(source, source + steps) for source in range(l...  19.4 us
    all_to_all x2, starting transfers between devices, summed_rows(): parts = lax.all_to_all(term, group, 0, 0, tiled=True)  11 us
    dot_general x1, matrix products, per_device(): jnp.einsum('hqd,hkd->hqk', near_query, key_part, preferred_element_type=j...  4.94 us
    dot_general x3, matrix products, per_device(): jnp.einsum('hqd,hkd->hqk', upstream_block, value_window, preferred_elemen...  4.57 us
    dot_general x1, matrix products, per_device(): lax.dot_general(jnp.concatenate([query_grad, key_grad, value_grad], axis=...  4.56 us
    convert_element_type x3, other arithmetic, per_device(): score_grad = (probability * (prob_grad - row_delta)).astype(jnp.bfloat16)  4.19 us
  transfers between devices with their start and end apart: 11, of which 7 were waited for; matrix products, arithmetic and copies ran while one was open for 23% of the time, Pallas kernels for 0%

profile of v12, /device:TPU:12, one launch (start us, length us, event | category | flops | bytes accessed | tf_op | source)
XLA Modules:
  0.0 188.5 jit_solution(12275218436685909392)
XLA Ops:
  7.3 2.8 %pad_maximum_fusion.1 = bf16[3,512,512]{2,1,0:T(8,128)(2,1)} fusion(bf16[1,512,512]{2,1,0:T(8,128)(2,1)} %bitcast.159, bf16[1,512,512]{2,1,0:T(8,128)(2,1)} %bitcast.160, bf16[1,512,512]{2,1,0:T(8,128)(2,1)} %bitcast.161), kind=kLoop, calls=%fused_computation.57 | loop fusion | flops 1572864 | bytes 3145728 | tf_op jit(solution)/shard_map/stack | solution.py:94
  10.1 2.4 %collective-permute-start.1 = (bf16[384,512]{1,0:T(8,128)(2,1)S(1)}, bf16[384,512]{1,0:T(8,128)(2,1)S(1)}, u32[]{:S(2)}, u32[]{:S(2)}) collective-permute-start(bf16[384,512]{1,0:T(8,128)(2,1)S(1)} %dynamic-slice_bitcast_fusion), channel_id=1, source_target_pairs={{4,0},{8,4},{12,8},{16,12},{20,16},{24,20},{28,24},{5,1},{9,5},{13... | collective-permute-start | bytes 1179656 | tf_op jit(solution)/shard_map/ppermute | solution.py:15
  12.5 4.3 %collective-permute-start = (bf16[384,512]{1,0:T(8,128)(2,1)S(1)}, bf16[384,512]{1,0:T(8,128)(2,1)S(1)}, u32[]{:S(2)}, u32[]{:S(2)}) collective-permute-start(bf16[384,512]{1,0:T(8,128)(2,1)S(1)} %dynamic-slice_bitcast_fusion), channel_id=1, source_target_pairs={{0,4},{4,8},{8,12},{12,16},{16,20},{20,24},{24,28},{1,5},{5,9},{9,... | collective-permute-start | bytes 1179656 | tf_op jit(solution)/shard_map/ppermute | solution.py:15
  16.9 1.9 %collective-permute-start.6 = (bf16[384,512]{1,0:T(8,128)(2,1)S(1)}, bf16[384,512]{1,0:T(8,128)(2,1)S(1)}, u32[]{:S(2)}, u32[]{:S(2)}) collective-permute-start(bf16[384,512]{1,0:T(8,128)(2,1)S(1)} %bitcast.162), channel_id=1, source_target_pairs={{4,0},{8,4},{12,8},{16,12},{20,16},{24,20},{28,24},{5,1},{9,5},{13... | collective-permute-start | bytes 1179656 | tf_op jit(solution)/shard_map/ppermute | solution.py:15
  18.8 4.8 %collective-permute-start.5 = (bf16[384,512]{1,0:T(8,128)(2,1)S(1)}, bf16[384,512]{1,0:T(8,128)(2,1)}, u32[]{:S(2)}, u32[]{:S(2)}) collective-permute-start(bf16[384,512]{1,0:T(8,128)(2,1)S(1)} %bitcast.163), channel_id=1, source_target_pairs={{0,4},{4,8},{8,12},{12,16},{16,20},{20,24},{24,28},{1,5},{5,9},{9,... | collective-permute-start | bytes 1179656 | tf_op jit(solution)/shard_map/ppermute | solution.py:15
  24.7 14.2 %collective-permute-done.1 = bf16[384,512]{1,0:T(8,128)(2,1)S(1)} collective-permute-done((bf16[384,512]{1,0:T(8,128)(2,1)S(1)}, bf16[384,512]{1,0:T(8,128)(2,1)S(1)}, u32[]{:S(2)}, u32[]{:S(2)}) %collective-permute-start.1) | collective-permute-done | bytes 393248 | tf_op jit(solution)/shard_map/ppermute | solution.py:15
  38.9 1.8 collective-permute-done
  43.4 2.7 %collective-permute-done.6 = bf16[384,512]{1,0:T(8,128)(2,1)S(1)} collective-permute-done((bf16[384,512]{1,0:T(8,128)(2,1)S(1)}, bf16[384,512]{1,0:T(8,128)(2,1)S(1)}, u32[]{:S(2)}, u32[]{:S(2)}) %collective-permute-start.6) | collective-permute-done | bytes 393248 | tf_op jit(solution)/shard_map/ppermute | solution.py:15
  46.2 3.0 %collective-permute-done.5 = bf16[384,512]{1,0:T(8,128)(2,1)} collective-permute-done((bf16[384,512]{1,0:T(8,128)(2,1)S(1)}, bf16[384,512]{1,0:T(8,128)(2,1)}, u32[]{:S(2)}, u32[]{:S(2)}) %collective-permute-start.5) | collective-permute-done | bytes 393248 | tf_op jit(solution)/shard_map/ppermute | solution.py:15
  51.3 1.9 maximum_select_fusion
  53.4 2.9 %all-gather.2.cloned.1.call-done = bf16[3,1024,512]{2,1,0:T(8,128)(2,1)} async-done(((bf16[3,512,512]{2,1,0:T(8,128)(2,1)}), bf16[3,1024,512]{2,1,0:T(8,128)(2,1)}) %all-gather.2.cloned.1.call-update) | async-done | bytes 3145744 | tf_op jit(solution)/shard_map/all_gather | solution.py:94
  56.3 2.1 %slice_bitcast_fusion.2 = (bf16[1024,512]{1,0:T(8,128)(2,1)S(1)}, bf16[1024,512]{1,0:T(8,128)(2,1)S(1)}, bf16[1024,512]{1,0:T(8,128)(2,1)S(1)}) fusion(bf16[3,1024,512]{2,1,0:T(8,128)(2,1)} %all-gather.2.cloned.1.call-done), kind=kLoop, calls=%fused_computation.89 | loop fusion | bytes 6291456 | tf_op jit(solution)/shard_map/squeeze | solution.py:95
  58.3 3.8 %convolution_convert_fusion = bf16[1152,1536]{1,0:T(8,128)(2,1)S(1)} fusion(bf16[384,1024]{1,0:T(8,128)(2,1)S(1)} %get-tuple-element.25, bf16[384,1024]{1,0:T(8,128)(2,1)S(1)} %bitcast.150, bf16[384,1024]{1,0:T(8,128)(2,1)S(1)} %get-tuple-element.24, bf16[1024,512]{1,0:T(8,128)(2,1)S(1)} %get-tuple-element.22, bf16[1024,512]{1,0:T(8,128)(2,1)S(1)} %get-tuple-element.23, ...), kind=kOutput, calls=%fused_computation.3 | convolution fusion | flops 3642163200 | bytes 9043968 | tf_op jit(solution)/shard_map/dot_general | solution.py:99
  62.5 1.6 copy.25
  67.3 1.5 fusion.16
  73.5 1.5 fusion.22
  78.1 1.5 fusion.19
  79.6 1.5 fusion.21
  81.2 3.5 %collective-permute-start.3 = (f32[3,8,384,1]{2,1,3,0:T(8,128)S(1)}, f32[3,8,384,1]{2,1,3,0:T(8,128)S(1)}, u32[]{:S(2)}, u32[]{:S(2)}) collective-permute-start(f32[3,8,384,1]{2,1,3,0:T(8,128)S(1)} %pad_maximum_fusion.8), channel_id=1, source_target_pairs={{0,4},{4,8},{8,12},{12,16},{16,20},{20,24},{24,28},{1,5},{5,9},{9,... | collective-permute-start | bytes 110600 | tf_op jit(solution)/shard_map/ppermute | solution.py:15
  89.4 2.4 %collective-permute-start.4 = (f32[3,8,384,1]{2,1,3,0:T(8,128)S(1)}, f32[3,8,384,1]{2,1,3,0:T(8,128)S(1)}, u32[]{:S(2)}, u32[]{:S(2)}) collective-permute-start(f32[3,8,384,1]{2,1,3,0:T(8,128)S(1)} %pad_maximum_fusion.8), channel_id=1, source_target_pairs={{4,0},{8,4},{12,8},{16,12},{20,16},{24,20},{28,24},{5,1},{9,5},{13... | collective-permute-start | bytes 110600 | tf_op jit(solution)/shard_map/ppermute | solution.py:15
  95.8 1.4 copy.33
  97.2 6.1 %all-to-all-start = ((bf16[16,64,512]{2,1,0:T(8,128)(2,1)}), bf16[16,64,512]{2,1,0:T(8,128)(2,1)S(1)}, u32[]{:S(2)}, u32[]{:S(2)}) async-start(bf16[16,64,512]{2,1,0:T(8,128)(2,1)} %bitcast.139), calls=%async_computation | async-start | bytes 2097152 | tf_op jit(solution)/shard_map/all_to_all | solution.py:58
  103.3 4.9 %fusion.111 = (bf16[8,768,384]{2,1,0:T(8,128)(2,1)S(1)}, f32[8,768,384]{2,1,0:T(8,128)S(1)}) fusion(f32[8,768]{1,0:T(8,128)S(1)} %get-tuple-element.30, f32[8,768]{1,0:T(8,128)S(1)} %get-tuple-element.31, bf16[8,1152,64]{1,2,0:T(8,128)(2,1)S(1)} %bitcast.134, bf16[8,384,64]{1,2,0:T(8,128)(2,1)} %get-tuple-element.27, ...), kind=kOutput, calls=%fused_computation.166 | convolution fusion | flops 315359232 | bytes 15679488 | tf_op jit(solution)/shard_map/hqd,hkd->hqk/dot_general | solution.py:179
  108.3 3.2 %multiply_convert_fusion = bf16[8,768,384]{2,1,0:T(8,128)(2,1)S(1)} fusion(f32[8,768,384]{2,1,0:T(8,128)S(1)} %get-tuple-element.45, f32[8,768]{1,0:T(8,128)S(1)} %get-tuple-element.29, bf16[8,768,64]{1,2,0:T(8,128)(2,1)S(1)} %bitcast.140, bf16[8,1152,64]{1,2,0:T(8,128)(2,1)} %bitcast.143), kind=kOutput, calls=%fused_computation.1 | convolution fusion | flops 309067776 | bytes 15360000 | tf_op jit(solution)/shard_map/hqd,hkd->hqk/dot_general | solution.py:184
  111.6 1.6 fusion.43
  113.5 1.6 fusion.40
  115.8 2.6 %convolution_convert_fusion.1 = bf16[1024,1024]{0,1:T(8,128)(2,1)} fusion(bf16[384,512]{0,1:T(8,128)(2,1)S(1)} %bitcast.178, bf16[384,512]{0,1:T(8,128)(2,1)S(1)} %bitcast.180, bf16[1,384,1024]{2,1,0:T(8,128)(2,1)S(1)} %copy-done.11), kind=kOutput, calls=%fused_computation.55 | convolution fusion | flops 807927808 | bytes 3670016 | tf_op jit(solution)/shard_map/tr,tf->rf/dot_general | solution.py:211
  118.5 9.5 %all-to-all-done = bf16[16,64,512]{2,1,0:T(8,128)(2,1)S(1)} async-done(((bf16[16,64,512]{2,1,0:T(8,128)(2,1)}), bf16[16,64,512]{2,1,0:T(8,128)(2,1)S(1)}, u32[]{:S(2)}, u32[]{:S(2)}) %all-to-all-start) | async-done | bytes 1048608 | tf_op jit(solution)/shard_map/all_to_all | solution.py:58
  128.0 5.0 %all-to-all-start.1 = ((bf16[16,64,1024]{2,1,0:T(8,128)(2,1)}), bf16[16,64,1024]{2,1,0:T(8,128)(2,1)S(1)}, u32[]{:S(2)}, u32[]{:S(2)}) async-start(bf16[16,64,1024]{2,1,0:T(8,128)(2,1)} %bitcast.142), calls=%async_computation.1 | async-start | bytes 4194304 | tf_op jit(solution)/shard_map/all_to_all | solution.py:58
  133.0 4.6 %convolution_convert_fusion.3 = bf16[384,1024]{1,0:T(8,128)(2,1)} fusion(bf16[1024,512]{1,0:T(8,128)(2,1)} %copy-done.15, bf16[1024,512]{1,0:T(8,128)(2,1)} %copy-done.16, bf16[1024,512]{1,0:T(8,128)(2,1)} %copy-done.14, bf16[384,512]{0,1:T(8,128)(2,1)} %bitcast.179, bf16[384,512]{0,1:T(8,128)(2,1)} %bitcast.181, bf16[384,512]{0,1:T(8,128)(2,1)S(1)} %bitcast.153), kind=kOutput, calls=%fused_computation.60 | convolution fusion | flops 1221328896 | bytes 5111808 | tf_op jit(solution)/shard_map/dot_general | solution.py:203
  141.1 2.6 %fusion.80 = bf16[1,384,1024]{2,1,0:T(8,128)(2,1)} fusion(bf16[384,1024]{1,0:T(8,128)(2,1)} %collective-permute-done.7, bf16[384,1024]{1,0:T(8,128)(2,1)} %convolution_convert_fusion.3), kind=kLoop, calls=%fused_computation.108 | loop fusion | flops 1572864 | bytes 2359296 | tf_op jit(solution)/shard_map/broadcast_in_dim | solution.py:209
  143.9 36.0 %all-to-all-done.1 = bf16[16,64,1024]{2,1,0:T(8,128)(2,1)S(1)} async-done(((bf16[16,64,1024]{2,1,0:T(8,128)(2,1)}), bf16[16,64,1024]{2,1,0:T(8,128)(2,1)S(1)}, u32[]{:S(2)}, u32[]{:S(2)}) %all-to-all-start.1) | async-done | bytes 2097184 | tf_op jit(solution)/shard_map/all_to_all | solution.py:58
  (135 shorter events, 32.3 us)
Async XLA Ops:
  7.2 16.6 %copy-start.29 = (s32[18]{0:T(128)S(1)}, s32[18]{0:T(128)}, u32[]{:S(2)}) copy-start(s32[18]{0:T(128)} %constant.80) | copy-start | bytes 220
  7.2 9.7 %copy-start.26 = (bf16[1,384,512]{2,1,0:T(8,128)(2,1)S(1)}, bf16[1,384,512]{2,1,0:T(8,128)(2,1)}, u32[]{:S(2)}) copy-start(bf16[1,384,512]{2,1,0:T(8,128)(2,1)} %param.16) | copy-start | bytes 1179652
  7.2 16.4 %copy-start.30 = (s32[24,7]{0,1:T(8,128)S(1)}, s32[24,7]{0,1:T(8,128)}, u32[]{:S(2)}) copy-start(s32[24,7]{0,1:T(8,128)} %param.15) | copy-start | bytes 2020
  7.2 49.0 %all-gather.2.cloned.1.call-start = ((), (), s32[]{:S(2)}) async-start(), calls=%async_computation.2 | async-start | bytes 4718592 | tf_op jit(solution)/shard_map/all_gather | solution.py:94
  10.0 14.5 %copy-start.33 = (pred[18]{0:T(512)(128)(4,1)S(1)}, pred[18]{0:T(512)(128)(4,1)}, u32[]{:S(2)}) copy-start(pred[18]{0:T(512)(128)(4,1)} %constant.81) | copy-start | bytes 58
  10.1 28.8 %collective-permute-start.1 = (bf16[384,512]{1,0:T(8,128)(2,1)S(1)}, bf16[384,512]{1,0:T(8,128)(2,1)S(1)}, u32[]{:S(2)}, u32[]{:S(2)}) collective-permute-start(bf16[384,512]{1,0:T(8,128)(2,1)S(1)} %dynamic-slice_bitcast_fusion), channel_id=1, source_target_pairs={{4,0},{8,4},{12,8},{16,12},{20,16},{24,20},{28,24},{5,1},{9,5},{13... | collective-permute-start | bytes 1179656 | tf_op jit(solution)/shard_map/ppermute | solution.py:15
  12.5 28.2 %collective-permute-start = (bf16[384,512]{1,0:T(8,128)(2,1)S(1)}, bf16[384,512]{1,0:T(8,128)(2,1)S(1)}, u32[]{:S(2)}, u32[]{:S(2)}) collective-permute-start(bf16[384,512]{1,0:T(8,128)(2,1)S(1)} %dynamic-slice_bitcast_fusion), channel_id=1, source_target_pairs={{0,4},{4,8},{8,12},{12,16},{16,20},{20,24},{24,28},{1,5},{5,9},{9,... | collective-permute-start | bytes 1179656 | tf_op jit(solution)/shard_map/ppermute | solution.py:15
  16.9 29.3 %collective-permute-start.6 = (bf16[384,512]{1,0:T(8,128)(2,1)S(1)}, bf16[384,512]{1,0:T(8,128)(2,1)S(1)}, u32[]{:S(2)}, u32[]{:S(2)}) collective-permute-start(bf16[384,512]{1,0:T(8,128)(2,1)S(1)} %bitcast.162), channel_id=1, source_target_pairs={{4,0},{8,4},{12,8},{16,12},{20,16},{24,20},{28,24},{5,1},{9,5},{13... | collective-permute-start | bytes 1179656 | tf_op jit(solution)/shard_map/ppermute | solution.py:15
  18.8 30.3 %collective-permute-start.5 = (bf16[384,512]{1,0:T(8,128)(2,1)S(1)}, bf16[384,512]{1,0:T(8,128)(2,1)}, u32[]{:S(2)}, u32[]{:S(2)}) collective-permute-start(bf16[384,512]{1,0:T(8,128)(2,1)S(1)} %bitcast.163), channel_id=1, source_target_pairs={{0,4},{4,8},{8,12},{12,16},{16,20},{20,24},{24,28},{1,5},{5,9},{9,... | collective-permute-start | bytes 1179656 | tf_op jit(solution)/shard_map/ppermute | solution.py:15
  40.8 10.6 %collective-permute-start.2 = (bf16[2,384,512]{2,1,0:T(8,128)(2,1)S(1)}, bf16[2,384,512]{2,1,0:T(8,128)(2,1)}, u32[]{:S(2)}, u32[]{:S(2)}) collective-permute-start(bf16[2,384,512]{2,1,0:T(8,128)(2,1)S(1)} %pad_maximum_fusion.4), channel_id=1, source_target_pairs={{0,1},{1,0},{2,3},{3,2},{4,5},{5,4},{6,7},{7,6},{8,9},{9,8},{10,11... | collective-permute-start | bytes 2359304 | tf_op jit(solution)/shard_map/ppermute | solution.py:43
  58.3 3.9 %copy-start.14 = (bf16[1024,512]{1,0:T(8,128)(2,1)}, bf16[1024,512]{1,0:T(8,128)(2,1)S(1)}, u32[]{:S(2)}) copy-start(bf16[1024,512]{1,0:T(8,128)(2,1)S(1)} %get-tuple-element.21) | copy-start | bytes 3145732
  58.3 3.9 %copy-start.15 = (bf16[1024,512]{1,0:T(8,128)(2,1)}, bf16[1024,512]{1,0:T(8,128)(2,1)S(1)}, u32[]{:S(2)}) copy-start(bf16[1024,512]{1,0:T(8,128)(2,1)S(1)} %get-tuple-element.22) | copy-start | bytes 3145732
  58.3 3.9 %copy-start.16 = (bf16[1024,512]{1,0:T(8,128)(2,1)}, bf16[1024,512]{1,0:T(8,128)(2,1)S(1)}, u32[]{:S(2)}) copy-start(bf16[1024,512]{1,0:T(8,128)(2,1)S(1)} %get-tuple-element.23) | copy-start | bytes 3145732
  70.2 22.7 %copy-start = (bf16[8,128,896]{2,1,0:T(8,128)(2,1)}, bf16[8,128,896]{2,1,0:T(8,128)(2,1)S(1)}, u32[]{:S(2)}) copy-start(bf16[8,128,896]{2,1,0:T(8,128)(2,1)S(1)} %get-tuple-element.17) | copy-start | bytes 5505028
  76.3 17.5 %copy-start.2 = (bf16[8,128,896]{2,1,0:T(8,128)(2,1)}, bf16[8,128,896]{2,1,0:T(8,128)(2,1)S(1)}, u32[]{:S(2)}) copy-start(bf16[8,128,896]{2,1,0:T(8,128)(2,1)S(1)} %get-tuple-element.13) | copy-start | bytes 5505028
  81.2 13.7 %copy-start.4 = (bf16[8,128,896]{2,1,0:T(8,128)(2,1)}, bf16[8,128,896]{2,1,0:T(8,128)(2,1)S(1)}, u32[]{:S(2)}) copy-start(bf16[8,128,896]{2,1,0:T(8,128)(2,1)S(1)} %get-tuple-element.15) | copy-start | bytes 5505028
  81.2 4.5 %copy-start.10 = (bf16[1,384,1024]{2,1,0:T(8,128)(2,1)S(1)}, bf16[1,384,1024]{2,1,0:T(8,128)(2,1)}, u32[]{:S(2)}) copy-start(bf16[1,384,1024]{2,1,0:T(8,128)(2,1)} %param.11) | copy-start | bytes 2359300
  81.2 22.0 %collective-permute-start.3 = (f32[3,8,384,1]{2,1,3,0:T(8,128)S(1)}, f32[3,8,384,1]{2,1,3,0:T(8,128)S(1)}, u32[]{:S(2)}, u32[]{:S(2)}) collective-permute-start(f32[3,8,384,1]{2,1,3,0:T(8,128)S(1)} %pad_maximum_fusion.8), channel_id=1, source_target_pairs={{0,4},{4,8},{8,12},{12,16},{16,20},{20,24},{24,28},{1,5},{5,9},{9,... | collective-permute-start | bytes 110600 | tf_op jit(solution)/shard_map/ppermute | solution.py:15
  85.7 3.7 %copy-start.12 = (bf16[8,384,64]{1,2,0:T(8,128)(2,1)}, bf16[8,384,64]{1,2,0:T(8,128)(2,1)S(1)}, u32[]{:S(2)}) copy-start(bf16[8,384,64]{1,2,0:T(8,128)(2,1)S(1)} %pad_maximum_fusion.7) | copy-start | bytes 1179652
  89.4 13.9 %collective-permute-start.4 = (f32[3,8,384,1]{2,1,3,0:T(8,128)S(1)}, f32[3,8,384,1]{2,1,3,0:T(8,128)S(1)}, u32[]{:S(2)}, u32[]{:S(2)}) collective-permute-start(f32[3,8,384,1]{2,1,3,0:T(8,128)S(1)} %pad_maximum_fusion.8), channel_id=1, source_target_pairs={{4,0},{8,4},{12,8},{16,12},{20,16},{24,20},{28,24},{5,1},{9,5},{13... | collective-permute-start | bytes 110600 | tf_op jit(solution)/shard_map/ppermute | solution.py:15
  97.2 30.8 %all-to-all-start = ((bf16[16,64,512]{2,1,0:T(8,128)(2,1)}), bf16[16,64,512]{2,1,0:T(8,128)(2,1)S(1)}, u32[]{:S(2)}, u32[]{:S(2)}) async-start(bf16[16,64,512]{2,1,0:T(8,128)(2,1)} %bitcast.139), calls=%async_computation | async-start | bytes 2097152 | tf_op jit(solution)/shard_map/all_to_all | solution.py:58
  103.3 5.0 %copy-start.6 = (bf16[768,512]{0,1:T(8,128)(2,1)S(1)}, bf16[768,512]{0,1:T(8,128)(2,1)}, u32[]{:S(2)}) copy-start(bf16[768,512]{0,1:T(8,128)(2,1)} %copy.32) | copy-start | bytes 2359300
  108.3 3.2 %copy-start.20 = (bf16[8,128,384]{2,1,0:T(8,128)(2,1)S(1)}, bf16[8,128,384]{2,1,0:T(8,128)(2,1)}, u32[]{:S(2)}) copy-start(bf16[8,128,384]{2,1,0:T(8,128)(2,1)} %slice.183) | copy-start | bytes 2359300
  108.3 3.2 %copy-start.21 = (bf16[8,128,384]{2,1,0:T(8,128)(2,1)S(1)}, bf16[8,128,384]{2,1,0:T(8,128)(2,1)}, u32[]{:S(2)}) copy-start(bf16[8,128,384]{2,1,0:T(8,128)(2,1)} %slice.181) | copy-start | bytes 2359300
  108.3 3.2 %copy-start.22 = (bf16[8,128,384]{2,1,0:T(8,128)(2,1)S(1)}, bf16[8,128,384]{2,1,0:T(8,128)(2,1)}, u32[]{:S(2)}) copy-start(bf16[8,128,384]{2,1,0:T(8,128)(2,1)} %slice.182) | copy-start | bytes 2359300
  108.3 3.2 %copy-start.28 = (bf16[1,384,512]{1,2,0:T(8,128)(2,1)S(1)}, bf16[1,384,512]{1,2,0:T(8,128)(2,1)}, u32[]{:S(2)}) copy-start(bf16[1,384,512]{1,2,0:T(8,128)(2,1)} %copy.26) | copy-start | bytes 1179652
  115.8 17.1 %copy-start.13 = (bf16[8,384,64]{1,2,0:T(8,128)(2,1)S(1)}, bf16[8,384,64]{1,2,0:T(8,128)(2,1)}, u32[]{:S(2)}) copy-start(bf16[8,384,64]{1,2,0:T(8,128)(2,1)} %copy-done.12) | copy-start | bytes 1179652
  128.0 51.9 %all-to-all-start.1 = ((bf16[16,64,1024]{2,1,0:T(8,128)(2,1)}), bf16[16,64,1024]{2,1,0:T(8,128)(2,1)S(1)}, u32[]{:S(2)}, u32[]{:S(2)}) async-start(bf16[16,64,1024]{2,1,0:T(8,128)(2,1)} %bitcast.142), calls=%async_computation.1 | async-start | bytes 4194304 | tf_op jit(solution)/shard_map/all_to_all | solution.py:58
  133.0 4.6 %copy-start.1 = (bf16[8,128,896]{2,1,0:T(8,128)(2,1)S(1)}, bf16[8,128,896]{2,1,0:T(8,128)(2,1)}, u32[]{:S(2)}) copy-start(bf16[8,128,896]{2,1,0:T(8,128)(2,1)} %copy-done) | copy-start | bytes 5505028
  133.0 4.6 %copy-start.8 = (bf16[1152,512]{0,1:T(8,128)(2,1)S(1)}, bf16[1152,512]{0,1:T(8,128)(2,1)}, u32[]{:S(2)}) copy-start(bf16[1152,512]{0,1:T(8,128)(2,1)} %copy.25) | copy-start | bytes 3538948
  133.0 5.4 %copy-start.3 = (bf16[8,128,896]{2,1,0:T(8,128)(2,1)S(1)}, bf16[8,128,896]{2,1,0:T(8,128)(2,1)}, u32[]{:S(2)}) copy-start(bf16[8,128,896]{2,1,0:T(8,128)(2,1)} %copy-done.2) | copy-start | bytes 5505028
  137.6 3.5 %collective-permute-start.7 = (bf16[384,1024]{1,0:T(8,128)(2,1)}, bf16[384,1024]{1,0:T(8,128)(2,1)}, u32[]{:S(2)}, u32[]{:S(2)}) collective-permute-start(bf16[384,1024]{1,0:T(8,128)(2,1)} %convolution_convert_fusion.3), channel_id=1, source_target_pairs={{0,1},{1,0},{2,3},{3,2},{4,5},{5,4},{6,7},{7,6},{8,9},{9,8},{10,11... | collective-permute-start | bytes 2359304 | tf_op jit(solution)/shard_map/ppermute | solution.py:68
  (13 other events, 23.5 us)
Sparse Core Ops, SparseCore 0:
  10.2 46.0 all-gather.1

commit v13 on v12

--- a/solution.py
+++ b/solution.py
@@ -89,8 +89,6 @@
     score_scale = HD ** (-0.5)
 
     left_tokens, right_tokens = neighbour_tokens(tokens, halo)
-    left_up = shifted(upstream[length - halo :], "ctx", 1)
-    right_up = shifted(upstream[:halo], "ctx", -1)
     gathered = lax.all_gather(jnp.stack([w_query, w_key, w_value]), "dp", axis=1, tiled=True)
     query_full, key_full, value_full = gathered[0], gathered[1], gathered[2]
 
@@ -99,6 +97,11 @@
     frame_proj = jnp.dot(frame_tokens, all_weights, preferred_element_type=jnp.float32).astype(
         jnp.bfloat16
     )
+    frame_proj, up_head, up_tail = lax.optimization_barrier(
+        (frame_proj, upstream[:halo], upstream[length - halo :])
+    )
+    left_up = shifted(up_tail, "ctx", 1)
+    right_up = shifted(up_head, "ctx", -1)
     query_h = head_major(frame_proj[:, :features], heads)
     key_h = head_major(frame_proj[:, features : 2 * features], heads)
     value_h = head_major(frame_proj[:, 2 * features :], heads)

time: 189 us -> 201 us (1.063)
  matrix products: 34.9 us -> 40.9 us
  starting transfers between devices: 30.6 us -> 34.2 us
  local copies, waits for them, and re-layouts: 21.6 us -> 23.7 us
    all_gather x1, waiting for transfers between devices: 2.9 us -> 17.1 us  [per_device(): lax.all_gather(jnp.stack([w_query, w_key, w_value]), 'dp', axis=1, tiled=...]
    all_to_all x2, waiting for transfers between devices: 45.5 us -> 37.8 us  [summed_rows(): parts = lax.all_to_all(term, group, 0, 0, tiled=True)]
    ppermute x6, waiting for transfers between devices: 21.7 us -> 14.7 us  [shifted(): lax.ppermute(value, axis, [(source, source + steps) for source in range(l...]
    all_to_all x2, starting transfers between devices: 11 us -> 15.1 us  [summed_rows(): parts = lax.all_to_all(term, group, 0, 0, tiled=True)]
    dot_general x1, matrix products: 4.94 us -> 7.76 us  [per_device(): jnp.einsum('hqd,hkd->hqk', near_query, key_part, preferred_element_type=j...]
    unnamed x74 -> x72, local copies, waits for them, and re-layouts: 3.89 us -> 5.93 us
  transfers between devices with their start and end apart: 11 -> 11, of which waited for: 7 -> 6; matrix products, arithmetic and copies ran while one was open for 23% -> 26% of each run, Pallas kernels for 0% -> 0%
where the time goes in v13:
time: 201 us
  waiting for transfers between devices  69.6 us (35%)
  matrix products  40.9 us (20%)
  starting transfers between devices  34.2 us (17%)
  local copies, waits for them, and re-layouts  23.7 us (12%)
  other arithmetic  17.3 us (9%)
  between operations  14.8 us (7%)
    all_to_all x2, waiting for transfers between devices, summed_rows(): parts = lax.all_to_all(term, group, 0, 0, tiled=True)  37.8 us
    ppermute x6, starting transfers between devices, shifted(): lax.ppermute(value, axis, [(source, source + steps) for source in range(l...  18.9 us
    all_gather x1, waiting for transfers between devices, per_device(): lax.all_gather(jnp.stack([w_query, w_key, w_value]), 'dp', axis=1, tiled=...  17.1 us
    all_to_all x2, starting transfers between devices, summed_rows(): parts = lax.all_to_all(term, group, 0, 0, tiled=True)  15.1 us
    ppermute x6, waiting for transfers between devices, shifted(): lax.ppermute(value, axis, [(source, source + steps) for source in range(l...  14.7 us
    dot_general x1, matrix products, per_device(): jnp.einsum('hqd,hkd->hqk', near_query, key_part, preferred_element_type=j...  7.76 us
    unnamed x72, local copies, waits for them, and re-layouts  5.93 us
    dot_general x1, matrix products, per_device(): jnp.einsum('hqd,hkd->hqk', near_upstream, value_part, preferred_element_t...  4.98 us
  transfers between devices with their start and end apart: 11, of which 6 were waited for; matrix products, arithmetic and copies ran while one was open for 26% of the time, Pallas kernels for 0%

profile of v13, /device:TPU:12, one launch (start us, length us, event | category | flops | bytes accessed | tf_op | source)
XLA Modules:
  0.0 200.6 jit_solution(13625335206948560072)
XLA Ops:
  7.2 2.8 %pad_maximum_fusion.1 = bf16[3,512,512]{2,1,0:T(8,128)(2,1)} fusion(bf16[1,512,512]{2,1,0:T(8,128)(2,1)} %bitcast.158, bf16[1,512,512]{2,1,0:T(8,128)(2,1)} %bitcast.159, bf16[1,512,512]{2,1,0:T(8,128)(2,1)} %bitcast.160), kind=kLoop, calls=%fused_computation.57 | loop fusion | flops 1572864 | bytes 3145728 | tf_op jit(solution)/shard_map/stack | solution.py:92
  10.1 2.4 %collective-permute-start.1 = (bf16[384,512]{1,0:T(8,128)(2,1)S(1)}, bf16[384,512]{1,0:T(8,128)(2,1)S(1)}, u32[]{:S(2)}, u32[]{:S(2)}) collective-permute-start(bf16[384,512]{1,0:T(8,128)(2,1)S(1)} %dynamic-slice_bitcast_fusion), channel_id=1, source_target_pairs={{4,0},{8,4},{12,8},{16,12},{20,16},{24,20},{28,24},{5,1},{9,5},{13... | collective-permute-start | bytes 1179656 | tf_op jit(solution)/shard_map/ppermute | solution.py:15
  12.5 4.3 %collective-permute-start = (bf16[384,512]{1,0:T(8,128)(2,1)S(1)}, bf16[384,512]{1,0:T(8,128)(2,1)S(1)}, u32[]{:S(2)}, u32[]{:S(2)}) collective-permute-start(bf16[384,512]{1,0:T(8,128)(2,1)S(1)} %dynamic-slice_bitcast_fusion), channel_id=1, source_target_pairs={{0,4},{4,8},{8,12},{12,16},{16,20},{20,24},{24,28},{1,5},{5,9},{9,... | collective-permute-start | bytes 1179656 | tf_op jit(solution)/shard_map/ppermute | solution.py:15
  17.7 11.6 %collective-permute-done.1 = bf16[384,512]{1,0:T(8,128)(2,1)S(1)} collective-permute-done((bf16[384,512]{1,0:T(8,128)(2,1)S(1)}, bf16[384,512]{1,0:T(8,128)(2,1)S(1)}, u32[]{:S(2)}, u32[]{:S(2)}) %collective-permute-start.1) | collective-permute-done | bytes 393248 | tf_op jit(solution)/shard_map/ppermute | solution.py:15
  29.3 2.9 %collective-permute-done = bf16[384,512]{1,0:T(8,128)(2,1)S(1)} collective-permute-done((bf16[384,512]{1,0:T(8,128)(2,1)S(1)}, bf16[384,512]{1,0:T(8,128)(2,1)S(1)}, u32[]{:S(2)}, u32[]{:S(2)}) %collective-permute-start) | collective-permute-done | bytes 393248 | tf_op jit(solution)/shard_map/ppermute | solution.py:15
  33.9 1.9 copy.26
  36.2 1.9 maximum_select_fusion
  39.1 17.1 %all-gather.2.cloned.1.call-done = bf16[3,1024,512]{2,1,0:T(8,128)(2,1)} async-done(((bf16[3,512,512]{2,1,0:T(8,128)(2,1)}), bf16[3,1024,512]{2,1,0:T(8,128)(2,1)}) %all-gather.2.cloned.1.call-update) | async-done | bytes 3145744 | tf_op jit(solution)/shard_map/all_gather | solution.py:92
  56.2 2.1 %slice_bitcast_fusion.2 = (bf16[1024,512]{1,0:T(8,128)(2,1)S(1)}, bf16[1024,512]{1,0:T(8,128)(2,1)S(1)}, bf16[1024,512]{1,0:T(8,128)(2,1)S(1)}) fusion(bf16[3,1024,512]{2,1,0:T(8,128)(2,1)} %all-gather.2.cloned.1.call-done), kind=kLoop, calls=%fused_computation.89 | loop fusion | bytes 6291456 | tf_op jit(solution)/shard_map/squeeze | solution.py:93
  58.4 3.8 %convolution_convert_fusion = bf16[1152,1536]{1,0:T(8,128)(2,1)S(1)} fusion(bf16[384,1024]{1,0:T(8,128)(2,1)S(1)} %copy-done.24, bf16[384,1024]{1,0:T(8,128)(2,1)S(1)} %bitcast.149, bf16[384,1024]{1,0:T(8,128)(2,1)S(1)} %get-tuple-element.30, bf16[1024,512]{1,0:T(8,128)(2,1)S(1)} %get-tuple-element.28, bf16[1024,512]{1,0:T(8,128)(2,1)S(1)} %get-tuple-element.29, ...), kind=kOutput, calls=%fused_computation.3 | convolution fusion | flops 3642163200 | bytes 9043968 | tf_op jit(solution)/shard_map/dot_general | solution.py:97
  62.6 1.6 copy.25
  67.3 1.5 fusion.16
  73.5 1.5 fusion.22
  78.1 1.5 fusion.19
  79.6 1.5 fusion.21
  81.2 3.5 %collective-permute-start.3 = (f32[3,8,384,1]{2,1,3,0:T(8,128)S(1)}, f32[3,8,384,1]{2,1,3,0:T(8,128)S(1)}, u32[]{:S(2)}, u32[]{:S(2)}) collective-permute-start(f32[3,8,384,1]{2,1,3,0:T(8,128)S(1)} %pad_maximum_fusion.8), channel_id=1, source_target_pairs={{0,4},{4,8},{8,12},{12,16},{16,20},{20,24},{24,28},{1,5},{5,9},{9,... | collective-permute-start | bytes 110600 | tf_op jit(solution)/shard_map/ppermute | solution.py:15
  89.6 2.4 %collective-permute-start.4 = (f32[3,8,384,1]{2,1,3,0:T(8,128)S(1)}, f32[3,8,384,1]{2,1,3,0:T(8,128)S(1)}, u32[]{:S(2)}, u32[]{:S(2)}) collective-permute-start(f32[3,8,384,1]{2,1,3,0:T(8,128)S(1)} %pad_maximum_fusion.8), channel_id=1, source_target_pairs={{4,0},{8,4},{12,8},{16,12},{20,16},{24,20},{28,24},{5,1},{9,5},{13... | collective-permute-start | bytes 110600 | tf_op jit(solution)/shard_map/ppermute | solution.py:15
  93.0 4.3 %collective-permute-start.5 = (bf16[384,512]{1,0:T(8,128)(2,1)}, bf16[384,512]{1,0:T(8,128)(2,1)}, u32[]{:S(2)}, u32[]{:S(2)}) collective-permute-start(bf16[384,512]{1,0:T(8,128)(2,1)} %bitcast.13), channel_id=1, source_target_pairs={{0,4},{4,8},{8,12},{12,16},{16,20},{20,24},{24,28},{1,5},{5,9},{9,... | collective-permute-start | bytes 1179656 | tf_op jit(solution)/shard_map/ppermute | solution.py:15
  97.3 1.9 collective-permute-start.6
  102.2 1.4 copy.33
  103.5 6.6 %all-to-all-start = ((bf16[16,64,512]{2,1,0:T(8,128)(2,1)}), bf16[16,64,512]{2,1,0:T(8,128)(2,1)S(1)}, u32[]{:S(2)}, u32[]{:S(2)}) async-start(bf16[16,64,512]{2,1,0:T(8,128)(2,1)} %bitcast.61), calls=%async_computation | async-start | bytes 2097152 | tf_op jit(solution)/shard_map/all_to_all | solution.py:58
  110.2 7.8 %fusion.111 = (bf16[8,768,384]{2,1,0:T(8,128)(2,1)}, f32[8,768,384]{2,1,0:T(8,128)}) fusion(f32[8,768]{1,0:T(8,128)S(1)} %get-tuple-element.36, f32[8,768]{1,0:T(8,128)S(1)} %get-tuple-element.37, bf16[8,1152,64]{1,2,0:T(8,128)(2,1)S(1)} %bitcast.134, bf16[8,384,64]{1,2,0:T(8,128)(2,1)} %get-tuple-element.33, bf16[8,384,64]{1,2,0:T(8,128)(2,1)} %get-tuple-element.34, ...), kind=kOutput, calls=%fused_computation.166 | convolution fusion | flops 315359232 | bytes 15679488 | tf_op jit(solution)/shard_map/hqd,hkd->hqk/dot_general | solution.py:182
  119.6 5.0 %multiply_convert_fusion = bf16[8,768,384]{2,1,0:T(8,128)(2,1)S(1)} fusion(f32[8,768,384]{2,1,0:T(8,128)} %get-tuple-element.51, f32[8,768]{1,0:T(8,128)S(1)} %get-tuple-element.35, bf16[8,768,64]{1,2,0:T(8,128)(2,1)S(1)} %bitcast.139, bf16[8,1152,64]{1,2,0:T(8,128)(2,1)} %bitcast.142), kind=kOutput, calls=%fused_computation.1 | convolution fusion | flops 309067776 | bytes 15360000 | tf_op jit(solution)/shard_map/hqd,hkd->hqk/dot_general | solution.py:187
  124.7 3.2 %fusion.43 = bf16[8,384,64]{1,2,0:T(8,128)(2,1)S(1)} fusion(bf16[8,768,384]{2,1,0:T(8,128)(2,1)} %get-tuple-element.50, bf16[8,128,384]{2,1,0:T(8,128)(2,1)S(1)} %copy-done.21, bf16[8,128,384]{2,1,0:T(8,128)(2,1)S(1)} %copy-done.23, bf16[8,128,384]{2,1,0:T(8,128)(2,1)S(1)} %copy-done.22, bf16[8,768,64]{1,2,0:T(8,128)(2,1)S(1)} %bitcast.140, ...), kind=kOutput, calls=%fused_computation.64 | convolution fusion | flops 483852288 | bytes 8650752 | tf_op jit(solution)/shard_map/hqk,hqd->hkd/dot_general | solution.py:198
  128.0 1.6 fusion.40
  129.7 2.6 %convolution_convert_fusion.1 = bf16[1024,1024]{0,1:T(8,128)(2,1)} fusion(bf16[384,512]{0,1:T(8,128)(2,1)S(1)} %bitcast.175, bf16[384,512]{0,1:T(8,128)(2,1)S(1)} %bitcast.177, bf16[1,384,1024]{2,1,0:T(8,128)(2,1)S(1)} %copy-done.12), kind=kOutput, calls=%fused_computation.55 | convolution fusion | flops 807927808 | bytes 3670016 | tf_op jit(solution)/shard_map/tr,tf->rf/dot_general | solution.py:214
  132.3 2.0 %all-to-all-done = bf16[16,64,512]{2,1,0:T(8,128)(2,1)S(1)} async-done(((bf16[16,64,512]{2,1,0:T(8,128)(2,1)}), bf16[16,64,512]{2,1,0:T(8,128)(2,1)S(1)}, u32[]{:S(2)}, u32[]{:S(2)}) %all-to-all-start) | async-done | bytes 1048608 | tf_op jit(solution)/shard_map/all_to_all | solution.py:58
  135.3 8.5 %all-to-all-start.1 = ((bf16[16,64,1024]{2,1,0:T(8,128)(2,1)}), bf16[16,64,1024]{2,1,0:T(8,128)(2,1)S(1)}, u32[]{:S(2)}, u32[]{:S(2)}) async-start(bf16[16,64,1024]{2,1,0:T(8,128)(2,1)} %bitcast.141), calls=%async_computation.1 | async-start | bytes 4194304 | tf_op jit(solution)/shard_map/all_to_all | solution.py:58
  143.9 4.3 %convolution_convert_fusion.3 = bf16[384,1024]{1,0:T(8,128)(2,1)} fusion(bf16[1024,512]{1,0:T(8,128)(2,1)} %copy-done.16, bf16[1024,512]{1,0:T(8,128)(2,1)} %copy-done.17, bf16[1024,512]{1,0:T(8,128)(2,1)} %copy-done.15, bf16[384,512]{0,1:T(8,128)(2,1)S(1)} %bitcast.176, bf16[384,512]{0,1:T(8,128)(2,1)S(1)} %bitcast.178, bf16[384,512]{0,1:T(8,128)(2,1)S(1)} %bitcast.152), kind=kOutput, calls=%fused_computation.60 | convolution fusion | flops 1221328896 | bytes 5111808 | tf_op jit(solution)/shard_map/dot_general | solution.py:206
  151.5 1.9 copy.34
  153.4 2.6 %fusion.80 = bf16[1,384,1024]{2,1,0:T(8,128)(2,1)} fusion(bf16[384,1024]{1,0:T(8,128)(2,1)} %collective-permute-done.7, bf16[384,1024]{1,0:T(8,128)(2,1)} %convolution_convert_fusion.3), kind=kLoop, calls=%fused_computation.108 | loop fusion | flops 1572864 | bytes 2359296 | tf_op jit(solution)/shard_map/broadcast_in_dim | solution.py:212
  156.2 35.8 %all-to-all-done.1 = bf16[16,64,1024]{2,1,0:T(8,128)(2,1)S(1)} async-done(((bf16[16,64,1024]{2,1,0:T(8,128)(2,1)}), bf16[16,64,1024]{2,1,0:T(8,128)(2,1)S(1)}, u32[]{:S(2)}, u32[]{:S(2)}) %all-to-all-start.1) | async-done | bytes 2097184 | tf_op jit(solution)/shard_map/all_to_all | solution.py:58
  (133 shorter events, 31.8 us)
Async XLA Ops:
  7.2 9.8 %copy-start.30 = (s32[18]{0:T(128)S(1)}, s32[18]{0:T(128)}, u32[]{:S(2)}) copy-start(s32[18]{0:T(128)} %constant.80) | copy-start | bytes 220
  7.2 9.7 %copy-start.31 = (s32[24,7]{0,1:T(8,128)S(1)}, s32[24,7]{0,1:T(8,128)}, u32[]{:S(2)}) copy-start(s32[24,7]{0,1:T(8,128)} %param.15) | copy-start | bytes 2020
  7.2 49.0 %all-gather.2.cloned.1.call-start = ((), (), s32[]{:S(2)}) async-start(), calls=%async_computation.2 | async-start | bytes 4718592 | tf_op jit(solution)/shard_map/all_gather | solution.py:92
  10.0 22.4 %copy-start.32 = (pred[18]{0:T(512)(128)(4,1)S(1)}, pred[18]{0:T(512)(128)(4,1)}, u32[]{:S(2)}) copy-start(pred[18]{0:T(512)(128)(4,1)} %constant.81) | copy-start | bytes 58
  10.1 19.2 %collective-permute-start.1 = (bf16[384,512]{1,0:T(8,128)(2,1)S(1)}, bf16[384,512]{1,0:T(8,128)(2,1)S(1)}, u32[]{:S(2)}, u32[]{:S(2)}) collective-permute-start(bf16[384,512]{1,0:T(8,128)(2,1)S(1)} %dynamic-slice_bitcast_fusion), channel_id=1, source_target_pairs={{4,0},{8,4},{12,8},{16,12},{20,16},{24,20},{28,24},{5,1},{9,5},{13... | collective-permute-start | bytes 1179656 | tf_op jit(solution)/shard_map/ppermute | solution.py:15
  12.5 19.7 %collective-permute-start = (bf16[384,512]{1,0:T(8,128)(2,1)S(1)}, bf16[384,512]{1,0:T(8,128)(2,1)S(1)}, u32[]{:S(2)}, u32[]{:S(2)}) collective-permute-start(bf16[384,512]{1,0:T(8,128)(2,1)S(1)} %dynamic-slice_bitcast_fusion), channel_id=1, source_target_pairs={{0,4},{4,8},{8,12},{12,16},{16,20},{20,24},{24,28},{1,5},{5,9},{9,... | collective-permute-start | bytes 1179656 | tf_op jit(solution)/shard_map/ppermute | solution.py:15
  32.2 3.9 %collective-permute-start.2 = (bf16[2,384,512]{2,1,0:T(8,128)(2,1)S(1)}, bf16[2,384,512]{2,1,0:T(8,128)(2,1)}, u32[]{:S(2)}, u32[]{:S(2)}) collective-permute-start(bf16[2,384,512]{2,1,0:T(8,128)(2,1)S(1)} %pad_maximum_fusion.4), channel_id=1, source_target_pairs={{0,1},{1,0},{2,3},{3,2},{4,5},{5,4},{6,7},{7,6},{8,9},{9,8},{10,11... | collective-permute-start | bytes 2359304 | tf_op jit(solution)/shard_map/ppermute | solution.py:43
  58.4 3.9 %copy-start.15 = (bf16[1024,512]{1,0:T(8,128)(2,1)}, bf16[1024,512]{1,0:T(8,128)(2,1)S(1)}, u32[]{:S(2)}) copy-start(bf16[1024,512]{1,0:T(8,128)(2,1)S(1)} %get-tuple-element.27) | copy-start | bytes 3145732
  58.4 3.9 %copy-start.16 = (bf16[1024,512]{1,0:T(8,128)(2,1)}, bf16[1024,512]{1,0:T(8,128)(2,1)S(1)}, u32[]{:S(2)}) copy-start(bf16[1024,512]{1,0:T(8,128)(2,1)S(1)} %get-tuple-element.28) | copy-start | bytes 3145732
  58.4 3.9 %copy-start.17 = (bf16[1024,512]{1,0:T(8,128)(2,1)}, bf16[1024,512]{1,0:T(8,128)(2,1)S(1)}, u32[]{:S(2)}) copy-start(bf16[1024,512]{1,0:T(8,128)(2,1)S(1)} %get-tuple-element.29) | copy-start | bytes 3145732
  70.2 29.0 %copy-start.2 = (bf16[8,128,896]{2,1,0:T(8,128)(2,1)}, bf16[8,128,896]{2,1,0:T(8,128)(2,1)S(1)}, u32[]{:S(2)}) copy-start(bf16[8,128,896]{2,1,0:T(8,128)(2,1)S(1)} %get-tuple-element.23) | copy-start | bytes 5505028
  76.3 23.8 %copy-start.4 = (bf16[8,128,896]{2,1,0:T(8,128)(2,1)}, bf16[8,128,896]{2,1,0:T(8,128)(2,1)S(1)}, u32[]{:S(2)}) copy-start(bf16[8,128,896]{2,1,0:T(8,128)(2,1)S(1)} %get-tuple-element.19) | copy-start | bytes 5505028
  81.2 20.0 %copy-start.6 = (bf16[8,128,896]{2,1,0:T(8,128)(2,1)}, bf16[8,128,896]{2,1,0:T(8,128)(2,1)S(1)}, u32[]{:S(2)}) copy-start(bf16[8,128,896]{2,1,0:T(8,128)(2,1)S(1)} %get-tuple-element.21) | copy-start | bytes 5505028
  81.2 4.5 %copy-start.11 = (bf16[1,384,1024]{2,1,0:T(8,128)(2,1)S(1)}, bf16[1,384,1024]{2,1,0:T(8,128)(2,1)}, u32[]{:S(2)}) copy-start(bf16[1,384,1024]{2,1,0:T(8,128)(2,1)} %param.11) | copy-start | bytes 2359300
  81.2 28.9 %collective-permute-start.3 = (f32[3,8,384,1]{2,1,3,0:T(8,128)S(1)}, f32[3,8,384,1]{2,1,3,0:T(8,128)S(1)}, u32[]{:S(2)}, u32[]{:S(2)}) collective-permute-start(f32[3,8,384,1]{2,1,3,0:T(8,128)S(1)} %pad_maximum_fusion.8), channel_id=1, source_target_pairs={{0,4},{4,8},{8,12},{12,16},{16,20},{20,24},{24,28},{1,5},{5,9},{9,... | collective-permute-start | bytes 110600 | tf_op jit(solution)/shard_map/ppermute | solution.py:15
  85.7 3.9 %copy-start.13 = (bf16[8,384,64]{1,2,0:T(8,128)(2,1)}, bf16[8,384,64]{1,2,0:T(8,128)(2,1)S(1)}, u32[]{:S(2)}) copy-start(bf16[8,384,64]{1,2,0:T(8,128)(2,1)S(1)} %pad_maximum_fusion.7) | copy-start | bytes 1179652
  89.6 20.6 %collective-permute-start.4 = (f32[3,8,384,1]{2,1,3,0:T(8,128)S(1)}, f32[3,8,384,1]{2,1,3,0:T(8,128)S(1)}, u32[]{:S(2)}, u32[]{:S(2)}) collective-permute-start(f32[3,8,384,1]{2,1,3,0:T(8,128)S(1)} %pad_maximum_fusion.8), channel_id=1, source_target_pairs={{4,0},{8,4},{12,8},{16,12},{20,16},{24,20},{28,24},{5,1},{9,5},{13... | collective-permute-start | bytes 110600 | tf_op jit(solution)/shard_map/ppermute | solution.py:15
  93.0 25.1 %collective-permute-start.5 = (bf16[384,512]{1,0:T(8,128)(2,1)}, bf16[384,512]{1,0:T(8,128)(2,1)}, u32[]{:S(2)}, u32[]{:S(2)}) collective-permute-start(bf16[384,512]{1,0:T(8,128)(2,1)} %bitcast.13), channel_id=1, source_target_pairs={{0,4},{4,8},{8,12},{12,16},{16,20},{20,24},{24,28},{1,5},{5,9},{9,... | collective-permute-start | bytes 1179656 | tf_op jit(solution)/shard_map/ppermute | solution.py:15
  97.3 20.9 %collective-permute-start.6 = (bf16[384,512]{1,0:T(8,128)(2,1)}, bf16[384,512]{1,0:T(8,128)(2,1)}, u32[]{:S(2)}, u32[]{:S(2)}) collective-permute-start(bf16[384,512]{1,0:T(8,128)(2,1)} %bitcast.13), channel_id=1, source_target_pairs={{4,0},{8,4},{12,8},{16,12},{20,16},{24,20},{28,24},{5,1},{9,5},{13... | collective-permute-start | bytes 1179656 | tf_op jit(solution)/shard_map/ppermute | solution.py:15
  103.5 30.8 %all-to-all-start = ((bf16[16,64,512]{2,1,0:T(8,128)(2,1)}), bf16[16,64,512]{2,1,0:T(8,128)(2,1)S(1)}, u32[]{:S(2)}, u32[]{:S(2)}) async-start(bf16[16,64,512]{2,1,0:T(8,128)(2,1)} %bitcast.61), calls=%async_computation | async-start | bytes 2097152 | tf_op jit(solution)/shard_map/all_to_all | solution.py:58
  119.6 5.0 %copy-start.21 = (bf16[8,128,384]{2,1,0:T(8,128)(2,1)S(1)}, bf16[8,128,384]{2,1,0:T(8,128)(2,1)}, u32[]{:S(2)}) copy-start(bf16[8,128,384]{2,1,0:T(8,128)(2,1)} %slice.180) | copy-start | bytes 2359300
  119.6 5.0 %copy-start.22 = (bf16[8,128,384]{2,1,0:T(8,128)(2,1)S(1)}, bf16[8,128,384]{2,1,0:T(8,128)(2,1)}, u32[]{:S(2)}) copy-start(bf16[8,128,384]{2,1,0:T(8,128)(2,1)} %slice.178) | copy-start | bytes 2359300
  119.6 5.0 %copy-start.23 = (bf16[8,128,384]{2,1,0:T(8,128)(2,1)S(1)}, bf16[8,128,384]{2,1,0:T(8,128)(2,1)}, u32[]{:S(2)}) copy-start(bf16[8,128,384]{2,1,0:T(8,128)(2,1)} %slice.179) | copy-start | bytes 2359300
  119.6 5.0 %copy-start.29 = (bf16[1,384,512]{1,2,0:T(8,128)(2,1)S(1)}, bf16[1,384,512]{1,2,0:T(8,128)(2,1)}, u32[]{:S(2)}) copy-start(bf16[1,384,512]{1,2,0:T(8,128)(2,1)} %copy.26) | copy-start | bytes 1179652
  124.7 3.3 %copy-start.27 = (bf16[8,384,64]{1,2,0:T(8,128)(2,1)S(1)}, bf16[8,384,64]{1,2,0:T(8,128)(2,1)}, u32[]{:S(2)}) copy-start(bf16[8,384,64]{1,2,0:T(8,128)(2,1)} %get-tuple-element.34) | copy-start | bytes 1179652
  129.7 14.2 %copy-start.14 = (bf16[8,384,64]{1,2,0:T(8,128)(2,1)S(1)}, bf16[8,384,64]{1,2,0:T(8,128)(2,1)}, u32[]{:S(2)}) copy-start(bf16[8,384,64]{1,2,0:T(8,128)(2,1)} %copy-done.13) | copy-start | bytes 1179652
  135.3 56.7 %all-to-all-start.1 = ((bf16[16,64,1024]{2,1,0:T(8,128)(2,1)}), bf16[16,64,1024]{2,1,0:T(8,128)(2,1)S(1)}, u32[]{:S(2)}, u32[]{:S(2)}) async-start(bf16[16,64,1024]{2,1,0:T(8,128)(2,1)} %bitcast.141), calls=%async_computation.1 | async-start | bytes 4194304 | tf_op jit(solution)/shard_map/all_to_all | solution.py:58
  143.8 4.4 %copy-start.3 = (bf16[8,128,896]{2,1,0:T(8,128)(2,1)S(1)}, bf16[8,128,896]{2,1,0:T(8,128)(2,1)}, u32[]{:S(2)}) copy-start(bf16[8,128,896]{2,1,0:T(8,128)(2,1)} %copy-done.2) | copy-start | bytes 5505028
  143.9 4.4 %copy-start.9 = (bf16[1152,512]{0,1:T(8,128)(2,1)S(1)}, bf16[1152,512]{0,1:T(8,128)(2,1)}, u32[]{:S(2)}) copy-start(bf16[1152,512]{0,1:T(8,128)(2,1)} %copy.25) | copy-start | bytes 3538948
  143.9 5.2 %copy-start.5 = (bf16[8,128,896]{2,1,0:T(8,128)(2,1)S(1)}, bf16[8,128,896]{2,1,0:T(8,128)(2,1)}, u32[]{:S(2)}) copy-start(bf16[8,128,896]{2,1,0:T(8,128)(2,1)} %copy-done.4) | copy-start | bytes 5505028
  148.2 5.2 %collective-permute-start.7 = (bf16[384,1024]{1,0:T(8,128)(2,1)}, bf16[384,1024]{1,0:T(8,128)(2,1)}, u32[]{:S(2)}, u32[]{:S(2)}) collective-permute-start(bf16[384,1024]{1,0:T(8,128)(2,1)} %convolution_convert_fusion.3), channel_id=1, source_target_pairs={{0,1},{1,0},{2,3},{3,2},{4,5},{5,4},{6,7},{7,6},{8,9},{9,8},{10,11... | collective-permute-start | bytes 2359304 | tf_op jit(solution)/shard_map/ppermute | solution.py:68
  149.8 6.1 %copy-start.1 = (bf16[16,64,512]{2,1,0:T(8,128)(2,1)S(1)}, bf16[16,64,512]{2,1,0:T(8,128)(2,1)}, u32[]{:S(2)}) copy-start(bf16[16,64,512]{2,1,0:T(8,128)(2,1)} %copy-done) | copy-start | bytes 3145732
  (12 other events, 29.3 us)
Sparse Core Ops, SparseCore 0:
  10.1 46.0 all-gather.1

commit v14 on v12

--- a/solution.py
+++ b/solution.py
@@ -96,9 +96,26 @@
 
     frame_tokens = jnp.concatenate([left_tokens, tokens, right_tokens], axis=0)
     all_weights = jnp.concatenate([query_full, key_full, value_full], axis=1)
-    frame_proj = jnp.dot(frame_tokens, all_weights, preferred_element_type=jnp.float32).astype(
-        jnp.bfloat16
-    )
+    if lax.axis_size("dp") == 2:
+        share = w_query.shape[0]
+        mine = lax.axis_index("dp") * share
+        local_weights = jnp.concatenate([w_query, w_key, w_value], axis=1)
+        remote_weights = lax.dynamic_slice_in_dim(all_weights, share - mine, share, 0)
+        local_part = jnp.dot(
+            lax.dynamic_slice_in_dim(frame_tokens, mine, share, 1),
+            local_weights,
+            preferred_element_type=jnp.float32,
+        )
+        remote_part = jnp.dot(
+            lax.dynamic_slice_in_dim(frame_tokens, share - mine, share, 1),
+            remote_weights,
+            preferred_element_type=jnp.float32,
+        )
+        frame_proj = (local_part + remote_part).astype(jnp.bfloat16)
+    else:
+        frame_proj = jnp.dot(
+            frame_tokens, all_weights, preferred_element_type=jnp.float32
+        ).astype(jnp.bfloat16)
     query_h = head_major(frame_proj[:, :features], heads)
     key_h = head_major(frame_proj[:, features : 2 * features], heads)
     value_h = head_major(frame_proj[:, 2 * features :], heads)

time: 189 us -> 198 us (1.048)
  local copies, waits for them, and re-layouts: 21.6 us -> 28.3 us
  waiting for transfers between devices: 70.2 us -> 66.3 us
  matrix products: 34.9 us -> 38.7 us
  other arithmetic: 16.4 us -> 18.9 us
    unnamed x74 -> x82, local copies, waits for them, and re-layouts: 3.89 us -> 8.57 us
    dot_general x1 -> x2, matrix products: 3.85 us -> 6.89 us  [the longest x1 4.86 us: per_device(): jnp.dot(lax.dynamic_slice_in_dim(frame_tokens, mine, share, 1), local_wei...]
    all_gather x1, waiting for transfers between devices: 2.9 us -> 0.01 us  [per_device(): lax.all_gather(jnp.stack([w_query, w_key, w_value]), 'dp', axis=1, tiled=...]
  transfers between devices with their start and end apart: 11 -> 11, of which waited for: 7 -> 6; matrix products, arithmetic and copies ran while one was open for 23% -> 25% of each run, Pallas kernels for 0% -> 0%
where the time goes in v14:
time: 198 us
  waiting for transfers between devices  66.3 us (33%)
  matrix products  38.7 us (20%)
  starting transfers between devices  30.6 us (15%)
  local copies, waits for them, and re-layouts  28.3 us (14%)
  other arithmetic  18.9 us (10%)
  between operations  14.8 us (7%)
    all_to_all x2, waiting for transfers between devices, summed_rows(): parts = lax.all_to_all(term, group, 0, 0, tiled=True)  43.9 us
    ppermute x6, waiting for transfers between devices, shifted(): lax.ppermute(value, axis, [(source, source + steps) for source in range(l...  22.4 us
    ppermute x6, starting transfers between devices, shifted(): lax.ppermute(value, axis, [(source, source + steps) for source in range(l...  19.3 us
    all_to_all x2, starting transfers between devices, summed_rows(): parts = lax.all_to_all(term, group, 0, 0, tiled=True)  11.2 us
    unnamed x82, local copies, waits for them, and re-layouts  8.57 us
    dot_general x1, matrix products, per_device(): jnp.einsum('hqd,hkd->hqk', near_query, key_part, preferred_element_type=j...  4.94 us
    dot_general x1, matrix products, per_device(): jnp.dot(lax.dynamic_slice_in_dim(frame_tokens, mine, share, 1), local_wei...  4.86 us
    dot_general x3, matrix products, per_device(): jnp.einsum('hqd,hkd->hqk', upstream_block, value_window, preferred_elemen...  4.57 us
  transfers between devices with their start and end apart: 11, of which 6 were waited for; matrix products, arithmetic and copies ran while one was open for 25% of the time, Pallas kernels for 0%

profile of v14, /device:TPU:12, one launch (start us, length us, event | category | flops | bytes accessed | tf_op | source)
XLA Modules:
  0.0 197.7 jit_solution(11234375929174881119)
XLA Ops:
  7.3 2.8 %pad_maximum_fusion.2 = bf16[3,512,512]{2,1,0:T(8,128)(2,1)} fusion(bf16[1,512,512]{2,1,0:T(8,128)(2,1)} %bitcast.159, bf16[1,512,512]{2,1,0:T(8,128)(2,1)} %bitcast.160, bf16[1,512,512]{2,1,0:T(8,128)(2,1)} %bitcast.161), kind=kLoop, calls=%fused_computation.60 | loop fusion | flops 1572864 | bytes 3145728 | tf_op jit(solution)/shard_map/stack | solution.py:94
  10.1 2.4 %collective-permute-start.1 = (bf16[384,512]{1,0:T(8,128)(2,1)S(1)}, bf16[384,512]{1,0:T(8,128)(2,1)S(1)}, u32[]{:S(2)}, u32[]{:S(2)}) collective-permute-start(bf16[384,512]{1,0:T(8,128)(2,1)S(1)} %dynamic-slice_bitcast_fusion), channel_id=1, source_target_pairs={{4,0},{8,4},{12,8},{16,12},{20,16},{24,20},{28,24},{5,1},{9,5},{13... | collective-permute-start | bytes 1179656 | tf_op jit(solution)/shard_map/ppermute | solution.py:15
  12.5 4.3 %collective-permute-start = (bf16[384,512]{1,0:T(8,128)(2,1)S(1)}, bf16[384,512]{1,0:T(8,128)(2,1)S(1)}, u32[]{:S(2)}, u32[]{:S(2)}) collective-permute-start(bf16[384,512]{1,0:T(8,128)(2,1)S(1)} %dynamic-slice_bitcast_fusion), channel_id=1, source_target_pairs={{0,4},{4,8},{8,12},{12,16},{16,20},{20,24},{24,28},{1,5},{5,9},{9,... | collective-permute-start | bytes 1179656 | tf_op jit(solution)/shard_map/ppermute | solution.py:15
  16.9 1.9 collective-permute-start.6
  18.8 4.8 %collective-permute-start.5 = (bf16[384,512]{1,0:T(8,128)(2,1)S(1)}, bf16[384,512]{1,0:T(8,128)(2,1)}, u32[]{:S(2)}, u32[]{:S(2)}) collective-permute-start(bf16[384,512]{1,0:T(8,128)(2,1)S(1)} %bitcast.163), channel_id=1, source_target_pairs={{0,4},{4,8},{8,12},{12,16},{16,20},{20,24},{24,28},{1,5},{5,9},{9,... | collective-permute-start | bytes 1179656 | tf_op jit(solution)/shard_map/ppermute | solution.py:15
  24.7 14.2 %collective-permute-done.1 = bf16[384,512]{1,0:T(8,128)(2,1)S(1)} collective-permute-done((bf16[384,512]{1,0:T(8,128)(2,1)S(1)}, bf16[384,512]{1,0:T(8,128)(2,1)S(1)}, u32[]{:S(2)}, u32[]{:S(2)}) %collective-permute-start.1) | collective-permute-done | bytes 393248 | tf_op jit(solution)/shard_map/ppermute | solution.py:15
  38.9 1.8 collective-permute-done
  42.7 3.4 %collective-permute-done.6 = bf16[384,512]{1,0:T(8,128)(2,1)} collective-permute-done((bf16[384,512]{1,0:T(8,128)(2,1)S(1)}, bf16[384,512]{1,0:T(8,128)(2,1)}, u32[]{:S(2)}, u32[]{:S(2)}) %collective-permute-start.6) | collective-permute-done | bytes 393248 | tf_op jit(solution)/shard_map/ppermute | solution.py:15
  46.2 3.0 %collective-permute-done.5 = bf16[384,512]{1,0:T(8,128)(2,1)} collective-permute-done((bf16[384,512]{1,0:T(8,128)(2,1)S(1)}, bf16[384,512]{1,0:T(8,128)(2,1)}, u32[]{:S(2)}, u32[]{:S(2)}) %collective-permute-start.5) | collective-permute-done | bytes 393248 | tf_op jit(solution)/shard_map/ppermute | solution.py:15
  51.5 1.9 maximum_select_fusion
  54.7 4.9 %fusion.32 = f32[1152,1536]{1,0:T(8,128)} fusion(bf16[512,512]{1,0:T(8,128)(2,1)S(1)} %copy-done.21, bf16[512,512]{1,0:T(8,128)(2,1)S(1)} %copy-done.22, bf16[512,512]{1,0:T(8,128)(2,1)S(1)} %copy-done.23, bf16[1152,1024]{1,0:T(8,128)(2,1)S(1)} %pad_maximum_fusion.1, s32[]{:T(128)S(6)} %select_n.56), kind=kOutput, calls=%fused_computation.54 | convolution fusion | flops 1816657920 | bytes 9830404 | tf_op jit(solution)/shard_map/dot_general | solution.py:104
  59.6 2.2 %slice_bitcast_fusion.2 = (bf16[1024,512]{1,0:T(8,128)(2,1)S(1)}, bf16[1024,512]{1,0:T(8,128)(2,1)S(1)}, bf16[1024,512]{1,0:T(8,128)(2,1)S(1)}) fusion(bf16[3,1024,512]{2,1,0:T(8,128)(2,1)} %all-gather.2.cloned.1.call-done), kind=kLoop, calls=%fused_computation.95 | loop fusion | bytes 6291456 | tf_op jit(solution)/shard_map/squeeze | solution.py:95
  64.7 2.0 %fusion = bf16[1152,1536]{1,0:T(8,128)(2,1)S(1)} fusion(f32[1152,1536]{1,0:T(8,128)S(1)} %copy-done.37, bf16[1024,1536]{1,0:T(8,128)(2,1)S(1)} %pad_maximum_fusion, s32[]{:T(128)S(6)} %select_n.57, bf16[1152,1024]{1,0:T(8,128)(2,1)S(1)} %pad_maximum_fusion.1), kind=kOutput, calls=%fused_computation.4 | convolution fusion | flops 1815478272 | bytes 13370368 | tf_op jit(solution)/shard_map/dot_general | solution.py:109
  70.2 1.7 copy.23
  73.6 1.5 fusion.17
  79.8 1.5 fusion.23
  81.3 1.5 fusion.25
  84.6 1.5 fusion.20
  88.2 2.5 %collective-permute-start.3 = (f32[3,8,384,1]{2,1,3,0:T(8,128)}, f32[3,8,384,1]{2,1,3,0:T(8,128)}, u32[]{:S(2)}, u32[]{:S(2)}) collective-permute-start(f32[3,8,384,1]{2,1,3,0:T(8,128)} %pad_maximum_fusion.7), channel_id=1, source_target_pairs={{0,4},{4,8},{8,12},{12,16},{16,20},{20,24},{24,28},{1,5},{5,9},{9,... | collective-permute-start | bytes 110600 | tf_op jit(solution)/shard_map/ppermute | solution.py:15
  91.7 1.7 fusion.39
  96.4 3.3 %collective-permute-start.4 = (f32[3,8,384,1]{2,1,3,0:T(8,128)}, f32[3,8,384,1]{2,1,3,0:T(8,128)S(1)}, u32[]{:S(2)}, u32[]{:S(2)}) collective-permute-start(f32[3,8,384,1]{2,1,3,0:T(8,128)} %pad_maximum_fusion.7), channel_id=1, source_target_pairs={{4,0},{8,4},{12,8},{16,12},{20,16},{24,20},{28,24},{5,1},{9,5},{13... | collective-permute-start | bytes 110600 | tf_op jit(solution)/shard_map/ppermute | solution.py:15
  105.1 6.2 %all-to-all-start = ((bf16[16,64,512]{2,1,0:T(8,128)(2,1)}), bf16[16,64,512]{2,1,0:T(8,128)(2,1)S(1)}, u32[]{:S(2)}, u32[]{:S(2)}) async-start(bf16[16,64,512]{2,1,0:T(8,128)(2,1)} %bitcast.140), calls=%async_computation | async-start | bytes 2097152 | tf_op jit(solution)/shard_map/all_to_all | solution.py:58
  112.1 4.9 %fusion.118 = (bf16[8,768,384]{2,1,0:T(8,128)(2,1)S(1)}, f32[8,768,384]{2,1,0:T(8,128)S(1)}) fusion(f32[8,768]{1,0:T(8,128)S(1)} %get-tuple-element.30, f32[8,768]{1,0:T(8,128)S(1)} %get-tuple-element.31, bf16[8,1152,64]{1,2,0:T(8,128)(2,1)S(1)} %bitcast.134, bf16[8,384,64]{1,2,0:T(8,128)(2,1)} %get-tuple-element.27, ...), kind=kOutput, calls=%fused_computation.174 | convolution fusion | flops 315359232 | bytes 15679488 | tf_op jit(solution)/shard_map/hqd,hkd->hqk/dot_general | solution.py:196
  117.1 3.2 %multiply_convert_fusion = bf16[8,768,384]{2,1,0:T(8,128)(2,1)S(1)} fusion(f32[8,768,384]{2,1,0:T(8,128)S(1)} %get-tuple-element.45, f32[8,768]{1,0:T(8,128)S(1)} %get-tuple-element.29, bf16[8,768,64]{1,2,0:T(8,128)(2,1)S(1)} %bitcast.141, bf16[8,1152,64]{1,2,0:T(8,128)(2,1)} %bitcast.144), kind=kOutput, calls=%fused_computation.2 | convolution fusion | flops 309067776 | bytes 15360000 | tf_op jit(solution)/shard_map/hqd,hkd->hqk/dot_general | solution.py:201
  120.4 1.6 fusion.46
  122.3 1.6 fusion.43
  124.6 2.7 %convolution_convert_fusion = bf16[1024,1024]{0,1:T(8,128)(2,1)} fusion(bf16[384,512]{0,1:T(8,128)(2,1)S(1)} %bitcast.178, bf16[384,512]{0,1:T(8,128)(2,1)S(1)} %bitcast.180, bf16[1,384,1024]{2,1,0:T(8,128)(2,1)S(1)} %copy-done), kind=kOutput, calls=%fused_computation.52 | convolution fusion | flops 807927808 | bytes 3670016 | tf_op jit(solution)/shard_map/tr,tf->rf/dot_general | solution.py:228
  127.3 8.9 %all-to-all-done = bf16[16,64,512]{2,1,0:T(8,128)(2,1)S(1)} async-done(((bf16[16,64,512]{2,1,0:T(8,128)(2,1)}), bf16[16,64,512]{2,1,0:T(8,128)(2,1)S(1)}, u32[]{:S(2)}, u32[]{:S(2)}) %all-to-all-start) | async-done | bytes 1048608 | tf_op jit(solution)/shard_map/all_to_all | solution.py:58
  137.2 5.0 %all-to-all-start.1 = ((bf16[16,64,1024]{2,1,0:T(8,128)(2,1)}), bf16[16,64,1024]{2,1,0:T(8,128)(2,1)S(1)}, u32[]{:S(2)}, u32[]{:S(2)}) async-start(bf16[16,64,1024]{2,1,0:T(8,128)(2,1)} %bitcast.143), calls=%async_computation.1 | async-start | bytes 4194304 | tf_op jit(solution)/shard_map/all_to_all | solution.py:58
  142.2 4.3 %convolution_convert_fusion.2 = bf16[384,1024]{1,0:T(8,128)(2,1)} fusion(bf16[384,512]{0,1:T(8,128)(2,1)S(1)} %bitcast.179, bf16[384,512]{0,1:T(8,128)(2,1)S(1)} %bitcast.181, bf16[384,512]{0,1:T(8,128)(2,1)S(1)} %bitcast.153, bf16[1024,512]{1,0:T(8,128)(2,1)} %copy-done.4, bf16[1024,512]{1,0:T(8,128)(2,1)} %copy-done.5, bf16[1024,512]{1,0:T(8,128)(2,1)} %copy-done.3), kind=kOutput, calls=%fused_computation.64 | convolution fusion | flops 1221328896 | bytes 5111808 | tf_op jit(solution)/shard_map/dot_general | solution.py:220
  150.1 2.6 %fusion.85 = bf16[1,384,1024]{2,1,0:T(8,128)(2,1)} fusion(bf16[384,1024]{1,0:T(8,128)(2,1)} %collective-permute-done.7, bf16[384,1024]{1,0:T(8,128)(2,1)} %convolution_convert_fusion.2), kind=kLoop, calls=%fused_computation.114 | loop fusion | flops 1572864 | bytes 2359296 | tf_op jit(solution)/shard_map/broadcast_in_dim | solution.py:226
  154.1 35.0 %all-to-all-done.1 = bf16[16,64,1024]{2,1,0:T(8,128)(2,1)S(1)} async-done(((bf16[16,64,1024]{2,1,0:T(8,128)(2,1)}), bf16[16,64,1024]{2,1,0:T(8,128)(2,1)S(1)}, u32[]{:S(2)}, u32[]{:S(2)}) %all-to-all-start.1) | async-done | bytes 2097184 | tf_op jit(solution)/shard_map/all_to_all | solution.py:58
  (146 shorter events, 42.0 us)
Async XLA Ops:
  7.2 16.6 %copy-start.30 = (s32[18]{0:T(128)S(1)}, s32[18]{0:T(128)}, u32[]{:S(2)}) copy-start(s32[18]{0:T(128)} %constant.84) | copy-start | bytes 220
  7.2 2.9 %copy-start = (bf16[1,384,1024]{2,1,0:T(8,128)(2,1)S(1)}, bf16[1,384,1024]{2,1,0:T(8,128)(2,1)}, u32[]{:S(2)}) copy-start(bf16[1,384,1024]{2,1,0:T(8,128)(2,1)} %param.11) | copy-start | bytes 2359300
  7.2 9.7 %copy-start.27 = (bf16[1,384,512]{2,1,0:T(8,128)(2,1)S(1)}, bf16[1,384,512]{2,1,0:T(8,128)(2,1)}, u32[]{:S(2)}) copy-start(bf16[1,384,512]{2,1,0:T(8,128)(2,1)} %param.16) | copy-start | bytes 1179652
  7.2 16.4 %copy-start.31 = (s32[24,7]{0,1:T(8,128)S(1)}, s32[24,7]{0,1:T(8,128)}, u32[]{:S(2)}) copy-start(s32[24,7]{0,1:T(8,128)} %param.15) | copy-start | bytes 2020
  7.2 52.4 %all-gather.2.cloned.1.call-start = ((), (), s32[]{:S(2)}) async-start(), calls=%async_computation.2 | async-start | bytes 4718592 | tf_op jit(solution)/shard_map/all_gather | solution.py:94
  10.0 14.5 %copy-start.36 = (pred[18]{0:T(512)(128)(4,1)S(1)}, pred[18]{0:T(512)(128)(4,1)}, u32[]{:S(2)}) copy-start(pred[18]{0:T(512)(128)(4,1)} %constant.85) | copy-start | bytes 58
  10.1 28.8 %collective-permute-start.1 = (bf16[384,512]{1,0:T(8,128)(2,1)S(1)}, bf16[384,512]{1,0:T(8,128)(2,1)S(1)}, u32[]{:S(2)}, u32[]{:S(2)}) collective-permute-start(bf16[384,512]{1,0:T(8,128)(2,1)S(1)} %dynamic-slice_bitcast_fusion), channel_id=1, source_target_pairs={{4,0},{8,4},{12,8},{16,12},{20,16},{24,20},{28,24},{5,1},{9,5},{13... | collective-permute-start | bytes 1179656 | tf_op jit(solution)/shard_map/ppermute | solution.py:15
  12.5 28.2 %collective-permute-start = (bf16[384,512]{1,0:T(8,128)(2,1)S(1)}, bf16[384,512]{1,0:T(8,128)(2,1)S(1)}, u32[]{:S(2)}, u32[]{:S(2)}) collective-permute-start(bf16[384,512]{1,0:T(8,128)(2,1)S(1)} %dynamic-slice_bitcast_fusion), channel_id=1, source_target_pairs={{0,4},{4,8},{8,12},{12,16},{16,20},{20,24},{24,28},{1,5},{5,9},{9,... | collective-permute-start | bytes 1179656 | tf_op jit(solution)/shard_map/ppermute | solution.py:15
  16.9 29.3 %collective-permute-start.6 = (bf16[384,512]{1,0:T(8,128)(2,1)S(1)}, bf16[384,512]{1,0:T(8,128)(2,1)}, u32[]{:S(2)}, u32[]{:S(2)}) collective-permute-start(bf16[384,512]{1,0:T(8,128)(2,1)S(1)} %bitcast.162), channel_id=1, source_target_pairs={{4,0},{8,4},{12,8},{16,12},{20,16},{24,20},{28,24},{5,1},{9,5},{13... | collective-permute-start | bytes 1179656 | tf_op jit(solution)/shard_map/ppermute | solution.py:15
  18.8 30.3 %collective-permute-start.5 = (bf16[384,512]{1,0:T(8,128)(2,1)S(1)}, bf16[384,512]{1,0:T(8,128)(2,1)}, u32[]{:S(2)}, u32[]{:S(2)}) collective-permute-start(bf16[384,512]{1,0:T(8,128)(2,1)S(1)} %bitcast.163), channel_id=1, source_target_pairs={{0,4},{4,8},{8,12},{12,16},{16,20},{20,24},{24,28},{1,5},{5,9},{9,... | collective-permute-start | bytes 1179656 | tf_op jit(solution)/shard_map/ppermute | solution.py:15
  40.8 10.7 %collective-permute-start.2 = (bf16[2,384,512]{2,1,0:T(8,128)(2,1)S(1)}, bf16[2,384,512]{2,1,0:T(8,128)(2,1)}, u32[]{:S(2)}, u32[]{:S(2)}) collective-permute-start(bf16[2,384,512]{2,1,0:T(8,128)(2,1)S(1)} %pad_maximum_fusion.3), channel_id=1, source_target_pairs={{0,1},{1,0},{2,3},{3,2},{4,5},{5,4},{6,7},{7,6},{8,9},{9,8},{10,11... | collective-permute-start | bytes 2359304 | tf_op jit(solution)/shard_map/ppermute | solution.py:43
  41.2 43.5 %copy-start.28 = (bf16[1,384,512]{1,2,0:T(8,128)(2,1)}, bf16[1,384,512]{1,2,0:T(8,128)(2,1)S(1)}, u32[]{:S(2)}) copy-start(bf16[1,384,512]{1,2,0:T(8,128)(2,1)S(1)} %copy.26) | copy-start | bytes 1179652
  59.6 5.1 %copy-start.37 = (f32[1152,1536]{1,0:T(8,128)S(1)}, f32[1152,1536]{1,0:T(8,128)}, u32[]{:S(2)}) copy-start(f32[1152,1536]{1,0:T(8,128)} %fusion.32) | copy-start | bytes 21233668
  76.5 24.3 %copy-start.6 = (bf16[8,128,896]{2,1,0:T(8,128)(2,1)}, bf16[8,128,896]{2,1,0:T(8,128)(2,1)S(1)}, u32[]{:S(2)}) copy-start(bf16[8,128,896]{2,1,0:T(8,128)(2,1)S(1)} %get-tuple-element.17) | copy-start | bytes 5505028
  82.9 18.8 %copy-start.8 = (bf16[8,128,896]{2,1,0:T(8,128)(2,1)}, bf16[8,128,896]{2,1,0:T(8,128)(2,1)S(1)}, u32[]{:S(2)}) copy-start(bf16[8,128,896]{2,1,0:T(8,128)(2,1)S(1)} %get-tuple-element.13) | copy-start | bytes 5505028
  87.5 15.2 %copy-start.10 = (bf16[8,128,896]{2,1,0:T(8,128)(2,1)}, bf16[8,128,896]{2,1,0:T(8,128)(2,1)S(1)}, u32[]{:S(2)}) copy-start(bf16[8,128,896]{2,1,0:T(8,128)(2,1)S(1)} %get-tuple-element.15) | copy-start | bytes 5505028
  88.2 23.1 %collective-permute-start.3 = (f32[3,8,384,1]{2,1,3,0:T(8,128)}, f32[3,8,384,1]{2,1,3,0:T(8,128)}, u32[]{:S(2)}, u32[]{:S(2)}) collective-permute-start(f32[3,8,384,1]{2,1,3,0:T(8,128)} %pad_maximum_fusion.7), channel_id=1, source_target_pairs={{0,4},{4,8},{8,12},{12,16},{16,20},{20,24},{24,28},{1,5},{5,9},{9,... | collective-permute-start | bytes 110600 | tf_op jit(solution)/shard_map/ppermute | solution.py:15
  95.4 8.3 %copy-start.2 = (bf16[1024,512]{0,1:T(8,128)(2,1)S(1)}, bf16[1024,512]{0,1:T(8,128)(2,1)}, u32[]{:S(2)}) copy-start(bf16[1024,512]{0,1:T(8,128)(2,1)} %fusion.39) | copy-start | bytes 3145732
  96.4 15.7 %collective-permute-start.4 = (f32[3,8,384,1]{2,1,3,0:T(8,128)}, f32[3,8,384,1]{2,1,3,0:T(8,128)S(1)}, u32[]{:S(2)}, u32[]{:S(2)}) collective-permute-start(f32[3,8,384,1]{2,1,3,0:T(8,128)} %pad_maximum_fusion.7), channel_id=1, source_target_pairs={{4,0},{8,4},{12,8},{16,12},{20,16},{24,20},{28,24},{5,1},{9,5},{13... | collective-permute-start | bytes 110600 | tf_op jit(solution)/shard_map/ppermute | solution.py:15
  105.1 31.1 %all-to-all-start = ((bf16[16,64,512]{2,1,0:T(8,128)(2,1)}), bf16[16,64,512]{2,1,0:T(8,128)(2,1)S(1)}, u32[]{:S(2)}, u32[]{:S(2)}) async-start(bf16[16,64,512]{2,1,0:T(8,128)(2,1)} %bitcast.140), calls=%async_computation | async-start | bytes 2097152 | tf_op jit(solution)/shard_map/all_to_all | solution.py:58
  112.1 5.0 %copy-start.12 = (bf16[768,512]{0,1:T(8,128)(2,1)S(1)}, bf16[768,512]{0,1:T(8,128)(2,1)}, u32[]{:S(2)}) copy-start(bf16[768,512]{0,1:T(8,128)(2,1)} %copy.32) | copy-start | bytes 2359300
  117.1 3.2 %copy-start.18 = (bf16[8,128,384]{2,1,0:T(8,128)(2,1)S(1)}, bf16[8,128,384]{2,1,0:T(8,128)(2,1)}, u32[]{:S(2)}) copy-start(bf16[8,128,384]{2,1,0:T(8,128)(2,1)} %slice.183) | copy-start | bytes 2359300
  117.1 3.2 %copy-start.19 = (bf16[8,128,384]{2,1,0:T(8,128)(2,1)S(1)}, bf16[8,128,384]{2,1,0:T(8,128)(2,1)}, u32[]{:S(2)}) copy-start(bf16[8,128,384]{2,1,0:T(8,128)(2,1)} %slice.181) | copy-start | bytes 2359300
  117.1 3.2 %copy-start.20 = (bf16[8,128,384]{2,1,0:T(8,128)(2,1)S(1)}, bf16[8,128,384]{2,1,0:T(8,128)(2,1)}, u32[]{:S(2)}) copy-start(bf16[8,128,384]{2,1,0:T(8,128)(2,1)} %slice.182) | copy-start | bytes 2359300
  117.1 3.2 %copy-start.29 = (bf16[1,384,512]{1,2,0:T(8,128)(2,1)S(1)}, bf16[1,384,512]{1,2,0:T(8,128)(2,1)}, u32[]{:S(2)}) copy-start(bf16[1,384,512]{1,2,0:T(8,128)(2,1)} %copy-done.28) | copy-start | bytes 1179652
  127.3 14.9 %copy-start.33 = (bf16[8,384,64]{1,2,0:T(8,128)(2,1)S(1)}, bf16[8,384,64]{1,2,0:T(8,128)(2,1)}, u32[]{:S(2)}) copy-start(bf16[8,384,64]{1,2,0:T(8,128)(2,1)} %copy-done.32) | copy-start | bytes 1179652
  127.3 14.9 %copy-start.35 = (bf16[8,384,64]{1,2,0:T(8,128)(2,1)S(1)}, bf16[8,384,64]{1,2,0:T(8,128)(2,1)}, u32[]{:S(2)}) copy-start(bf16[8,384,64]{1,2,0:T(8,128)(2,1)} %copy-done.34) | copy-start | bytes 1179652
  137.2 51.9 %all-to-all-start.1 = ((bf16[16,64,1024]{2,1,0:T(8,128)(2,1)}), bf16[16,64,1024]{2,1,0:T(8,128)(2,1)S(1)}, u32[]{:S(2)}, u32[]{:S(2)}) async-start(bf16[16,64,1024]{2,1,0:T(8,128)(2,1)} %bitcast.143), calls=%async_computation.1 | async-start | bytes 4194304 | tf_op jit(solution)/shard_map/all_to_all | solution.py:58
  142.2 4.4 %copy-start.7 = (bf16[8,128,896]{2,1,0:T(8,128)(2,1)S(1)}, bf16[8,128,896]{2,1,0:T(8,128)(2,1)}, u32[]{:S(2)}) copy-start(bf16[8,128,896]{2,1,0:T(8,128)(2,1)} %copy-done.6) | copy-start | bytes 5505028
  142.2 4.4 %copy-start.14 = (bf16[1152,512]{0,1:T(8,128)(2,1)S(1)}, bf16[1152,512]{0,1:T(8,128)(2,1)}, u32[]{:S(2)}) copy-start(bf16[1152,512]{0,1:T(8,128)(2,1)} %copy.25) | copy-start | bytes 3538948
  142.2 5.2 %copy-start.9 = (bf16[8,128,896]{2,1,0:T(8,128)(2,1)S(1)}, bf16[8,128,896]{2,1,0:T(8,128)(2,1)}, u32[]{:S(2)}) copy-start(bf16[8,128,896]{2,1,0:T(8,128)(2,1)} %copy-done.8) | copy-start | bytes 5505028
  146.6 3.5 %collective-permute-start.7 = (bf16[384,1024]{1,0:T(8,128)(2,1)}, bf16[384,1024]{1,0:T(8,128)(2,1)}, u32[]{:S(2)}, u32[]{:S(2)}) collective-permute-start(bf16[384,1024]{1,0:T(8,128)(2,1)} %convolution_convert_fusion.2), channel_id=1, source_target_pairs={{0,1},{1,0},{2,3},{3,2},{4,5},{5,4},{6,7},{7,6},{8,9},{9,8},{10,11... | collective-permute-start | bytes 2359304 | tf_op jit(solution)/shard_map/ppermute | solution.py:68
  (17 other events, 24.9 us)
Sparse Core Ops, SparseCore 0:
  10.2 46.0 all-gather.1

commit v15 on v12

--- a/solution.py
+++ b/solution.py
@@ -91,8 +91,9 @@
     left_tokens, right_tokens = neighbour_tokens(tokens, halo)
     left_up = shifted(upstream[length - halo :], "ctx", 1)
     right_up = shifted(upstream[:halo], "ctx", -1)
-    gathered = lax.all_gather(jnp.stack([w_query, w_key, w_value]), "dp", axis=1, tiled=True)
-    query_full, key_full, value_full = gathered[0], gathered[1], gathered[2]
+    query_full = full_rows(w_query)
+    gathered = lax.all_gather(jnp.stack([w_key, w_value]), "dp", axis=1, tiled=True)
+    key_full, value_full = gathered[0], gathered[1]
 
     frame_tokens = jnp.concatenate([left_tokens, tokens, right_tokens], axis=0)
     all_weights = jnp.concatenate([query_full, key_full, value_full], axis=1)

time: 189 us -> 189 us (level)
  waiting for transfers between devices: 70.2 us -> 65.9 us
    all_gather x1, waiting for transfers between devices: 2.9 us -> 0.02 us  [per_device(): lax.all_gather(jnp.stack([w_key, w_value]), 'dp', axis=1, tiled=True)]
    select_n x1 -> x2, other arithmetic: 1.87 us -> 4.08 us  [ordered_pair(): jnp.where(first, jnp.concatenate([mine, other], axis=dim), jnp.concatenat...]
    unnamed x74 -> x76, local copies, waits for them, and re-layouts: 3.89 us -> 3.9 us
  transfers between devices with their start and end apart: 11 -> 12, of which waited for: 7 -> 6; matrix products, arithmetic and copies ran while one was open for 23% -> 24% of each run, Pallas kernels for 0% -> 0%
where the time goes in v15:
time: 189 us; the launch traced here: 188 us
  waiting for transfers between devices  65.9 us (35%)
  matrix products  34.9 us (18%)
  starting transfers between devices  32.3 us (17%)
  local copies, waits for them, and re-layouts  22.3 us (12%)
  other arithmetic  18.2 us (10%)
  between operations  14.8 us (8%)
    all_to_all x2, waiting for transfers between devices, summed_rows(): parts = lax.all_to_all(term, group, 0, 0, tiled=True)  45.7 us
    ppermute x6, waiting for transfers between devices, shifted(): lax.ppermute(value, axis, [(source, source + steps) for source in range(l...  20.2 us
    ppermute x6, starting transfers between devices, shifted(): lax.ppermute(value, axis, [(source, source + steps) for source in range(l...  19.4 us
    all_to_all x2, starting transfers between devices, summed_rows(): parts = lax.all_to_all(term, group, 0, 0, tiled=True)  11.1 us
    dot_general x1, matrix products, per_device(): jnp.einsum('hqd,hkd->hqk', near_query, key_part, preferred_element_type=j...  4.94 us
    dot_general x3, matrix products, per_device(): jnp.einsum('hqd,hkd->hqk', upstream_block, value_window, preferred_elemen...  4.57 us
    dot_general x1, matrix products, per_device(): lax.dot_general(jnp.concatenate([query_grad, key_grad, value_grad], axis=...  4.56 us
    convert_element_type x3, other arithmetic, per_device(): score_grad = (probability * (prob_grad - row_delta)).astype(jnp.bfloat16)  4.19 us
  transfers between devices with their start and end apart: 12, of which 6 were waited for; matrix products, arithmetic and copies ran while one was open for 24% of the time, Pallas kernels for 0%

profile of v15, /device:TPU:12, one launch (start us, length us, event | category | flops | bytes accessed | tf_op | source)
XLA Modules:
  0.0 188.4 jit_solution(3515792313190223921)
XLA Ops:
  7.3 2.3 %pad_maximum_fusion.3 = bf16[2,512,512]{2,1,0:T(8,128)(2,1)} fusion(bf16[1,512,512]{2,1,0:T(8,128)(2,1)} %bitcast.156, bf16[1,512,512]{2,1,0:T(8,128)(2,1)} %bitcast.157), kind=kLoop, calls=%fused_computation.89 | loop fusion | flops 524288 | bytes 2097152 | tf_op jit(solution)/shard_map/stack | solution.py:95
  10.7 2.4 %collective-permute-start.1 = (bf16[384,512]{1,0:T(8,128)(2,1)S(1)}, bf16[384,512]{1,0:T(8,128)(2,1)S(1)}, u32[]{:S(2)}, u32[]{:S(2)}) collective-permute-start(bf16[384,512]{1,0:T(8,128)(2,1)S(1)} %dynamic-slice_bitcast_fusion), channel_id=1, source_target_pairs={{4,0},{8,4},{12,8},{16,12},{20,16},{24,20},{28,24},{5,1},{9,5},{13... | collective-permute-start | bytes 1179656 | tf_op jit(solution)/shard_map/ppermute | solution.py:15
  13.1 4.3 %collective-permute-start = (bf16[384,512]{1,0:T(8,128)(2,1)S(1)}, bf16[384,512]{1,0:T(8,128)(2,1)S(1)}, u32[]{:S(2)}, u32[]{:S(2)}) collective-permute-start(bf16[384,512]{1,0:T(8,128)(2,1)S(1)} %dynamic-slice_bitcast_fusion), channel_id=1, source_target_pairs={{0,4},{4,8},{8,12},{12,16},{16,20},{20,24},{24,28},{1,5},{5,9},{9,... | collective-permute-start | bytes 1179656 | tf_op jit(solution)/shard_map/ppermute | solution.py:15
  17.4 1.9 %collective-permute-start.7 = (bf16[384,512]{1,0:T(8,128)(2,1)S(1)}, bf16[384,512]{1,0:T(8,128)(2,1)S(1)}, u32[]{:S(2)}, u32[]{:S(2)}) collective-permute-start(bf16[384,512]{1,0:T(8,128)(2,1)S(1)} %bitcast.158), channel_id=1, source_target_pairs={{4,0},{8,4},{12,8},{16,12},{20,16},{24,20},{28,24},{5,1},{9,5},{13... | collective-permute-start | bytes 1179656 | tf_op jit(solution)/shard_map/ppermute | solution.py:15
  19.4 4.8 %collective-permute-start.6 = (bf16[384,512]{1,0:T(8,128)(2,1)S(1)}, bf16[384,512]{1,0:T(8,128)(2,1)}, u32[]{:S(2)}, u32[]{:S(2)}) collective-permute-start(bf16[384,512]{1,0:T(8,128)(2,1)S(1)} %bitcast.159), channel_id=1, source_target_pairs={{0,4},{4,8},{8,12},{12,16},{16,20},{20,24},{24,28},{1,5},{5,9},{9,... | collective-permute-start | bytes 1179656 | tf_op jit(solution)/shard_map/ppermute | solution.py:15
  24.2 1.6 collective-permute-start.3
  29.0 10.5 %collective-permute-done.1 = bf16[384,512]{1,0:T(8,128)(2,1)S(1)} collective-permute-done((bf16[384,512]{1,0:T(8,128)(2,1)S(1)}, bf16[384,512]{1,0:T(8,128)(2,1)S(1)}, u32[]{:S(2)}, u32[]{:S(2)}) %collective-permute-start.1) | collective-permute-done | bytes 393248 | tf_op jit(solution)/shard_map/ppermute | solution.py:15
  39.4 1.8 collective-permute-done
  41.8 4.9 %collective-permute-done.7 = bf16[384,512]{1,0:T(8,128)(2,1)S(1)} collective-permute-done((bf16[384,512]{1,0:T(8,128)(2,1)S(1)}, bf16[384,512]{1,0:T(8,128)(2,1)S(1)}, u32[]{:S(2)}, u32[]{:S(2)}) %collective-permute-start.7) | collective-permute-done | bytes 393248 | tf_op jit(solution)/shard_map/ppermute | solution.py:15
  46.7 3.0 %collective-permute-done.6 = bf16[384,512]{1,0:T(8,128)(2,1)} collective-permute-done((bf16[384,512]{1,0:T(8,128)(2,1)S(1)}, bf16[384,512]{1,0:T(8,128)(2,1)}, u32[]{:S(2)}, u32[]{:S(2)}) %collective-permute-start.6) | collective-permute-done | bytes 393248 | tf_op jit(solution)/shard_map/ppermute | solution.py:15
  51.9 1.8 maximum_select_fusion.1
  53.8 2.2 %maximum_select_fusion = bf16[2,384,1024]{2,1,0:T(8,128)(2,1)S(1)} fusion(bf16[2,384,512]{2,1,0:T(8,128)(2,1)} %collective-permute-done.2, bf16[1,384,512]{2,1,0:T(8,128)(2,1)S(1)} %bitcast.152, bf16[1,384,512]{2,1,0:T(8,128)(2,1)S(1)} %bitcast.154, pred[]{:T(512)S(6)} %eq.6), kind=kLoop, calls=%fused_computation.56 | loop fusion | flops 10223616 | bytes 3145729 | tf_op jit(solution)/shard_map/jit(_where)/select_n | solution.py:28
  56.2 1.7 slice_bitcast_fusion.1
  58.0 3.8 %convolution_convert_fusion = bf16[1152,1536]{1,0:T(8,128)(2,1)S(1)} fusion(bf16[384,1024]{1,0:T(8,128)(2,1)S(1)} %get-tuple-element.24, bf16[384,1024]{1,0:T(8,128)(2,1)S(1)} %bitcast.147, bf16[384,1024]{1,0:T(8,128)(2,1)S(1)} %get-tuple-element.23, bf16[1024,512]{1,0:T(8,128)(2,1)S(1)} %get-tuple-element.22, bf16[1024,512]{1,0:T(8,128)(2,1)S(1)} %get-tuple-element.21, ...), kind=kOutput, calls=%fused_computation.3 | convolution fusion | flops 3642163200 | bytes 9043968 | tf_op jit(solution)/shard_map/dot_general | solution.py:100
  62.1 1.6 copy.25
  66.9 1.5 fusion.16
  73.1 1.5 fusion.22
  77.7 1.5 fusion.19
  79.2 1.5 fusion.21
  80.9 2.6 %collective-permute-start.4 = (f32[3,8,384,1]{2,1,3,0:T(8,128)S(1)}, f32[3,8,384,1]{2,1,3,0:T(8,128)S(1)}, u32[]{:S(2)}, u32[]{:S(2)}) collective-permute-start(f32[3,8,384,1]{2,1,3,0:T(8,128)S(1)} %pad_maximum_fusion.8), channel_id=1, source_target_pairs={{0,4},{4,8},{8,12},{12,16},{16,20},{20,24},{24,28},{1,5},{5,9},{9,... | collective-permute-start | bytes 110600 | tf_op jit(solution)/shard_map/ppermute | solution.py:15
  88.1 3.4 %collective-permute-start.5 = (f32[3,8,384,1]{2,1,3,0:T(8,128)S(1)}, f32[3,8,384,1]{2,1,3,0:T(8,128)S(1)}, u32[]{:S(2)}, u32[]{:S(2)}) collective-permute-start(f32[3,8,384,1]{2,1,3,0:T(8,128)S(1)} %pad_maximum_fusion.8), channel_id=1, source_target_pairs={{4,0},{8,4},{12,8},{16,12},{20,16},{24,20},{28,24},{5,1},{9,5},{13... | collective-permute-start | bytes 110600 | tf_op jit(solution)/shard_map/ppermute | solution.py:15
  96.9 6.2 %all-to-all-start = ((bf16[16,64,512]{2,1,0:T(8,128)(2,1)}), bf16[16,64,512]{2,1,0:T(8,128)(2,1)S(1)}, u32[]{:S(2)}, u32[]{:S(2)}) async-start(bf16[16,64,512]{2,1,0:T(8,128)(2,1)} %bitcast.136), calls=%async_computation | async-start | bytes 2097152 | tf_op jit(solution)/shard_map/all_to_all | solution.py:58
  103.1 4.9 %fusion.111 = (bf16[8,768,384]{2,1,0:T(8,128)(2,1)S(1)}, f32[8,768,384]{2,1,0:T(8,128)S(1)}) fusion(f32[8,768]{1,0:T(8,128)S(1)} %get-tuple-element.29, f32[8,768]{1,0:T(8,128)S(1)} %get-tuple-element.30, bf16[8,1152,64]{1,2,0:T(8,128)(2,1)S(1)} %bitcast.131, bf16[8,384,64]{1,2,0:T(8,128)(2,1)} %get-tuple-element.26, ...), kind=kOutput, calls=%fused_computation.166 | convolution fusion | flops 315359232 | bytes 15679488 | tf_op jit(solution)/shard_map/hqd,hkd->hqk/dot_general | solution.py:180
  108.1 3.2 %multiply_convert_fusion = bf16[8,768,384]{2,1,0:T(8,128)(2,1)S(1)} fusion(f32[8,768,384]{2,1,0:T(8,128)S(1)} %get-tuple-element.44, f32[8,768]{1,0:T(8,128)S(1)} %get-tuple-element.28, bf16[8,768,64]{1,2,0:T(8,128)(2,1)S(1)} %bitcast.137, bf16[8,1152,64]{1,2,0:T(8,128)(2,1)} %bitcast.140), kind=kOutput, calls=%fused_computation.1 | convolution fusion | flops 309067776 | bytes 15360000 | tf_op jit(solution)/shard_map/hqd,hkd->hqk/dot_general | solution.py:185
  111.4 1.6 fusion.43
  113.3 1.6 fusion.40
  115.6 2.6 %convolution_convert_fusion.1 = bf16[1024,1024]{0,1:T(8,128)(2,1)} fusion(bf16[384,512]{0,1:T(8,128)(2,1)S(1)} %bitcast.174, bf16[384,512]{0,1:T(8,128)(2,1)S(1)} %bitcast.176, bf16[1,384,1024]{2,1,0:T(8,128)(2,1)S(1)} %copy-done.11), kind=kOutput, calls=%fused_computation.55 | convolution fusion | flops 807927808 | bytes 3670016 | tf_op jit(solution)/shard_map/tr,tf->rf/dot_general | solution.py:212
  118.2 9.7 %all-to-all-done = bf16[16,64,512]{2,1,0:T(8,128)(2,1)S(1)} async-done(((bf16[16,64,512]{2,1,0:T(8,128)(2,1)}), bf16[16,64,512]{2,1,0:T(8,128)(2,1)S(1)}, u32[]{:S(2)}, u32[]{:S(2)}) %all-to-all-start) | async-done | bytes 1048608 | tf_op jit(solution)/shard_map/all_to_all | solution.py:58
  127.9 5.0 %all-to-all-start.1 = ((bf16[16,64,1024]{2,1,0:T(8,128)(2,1)}), bf16[16,64,1024]{2,1,0:T(8,128)(2,1)S(1)}, u32[]{:S(2)}, u32[]{:S(2)}) async-start(bf16[16,64,1024]{2,1,0:T(8,128)(2,1)} %bitcast.139), calls=%async_computation.1 | async-start | bytes 4194304 | tf_op jit(solution)/shard_map/all_to_all | solution.py:58
  133.0 4.6 %convolution_convert_fusion.3 = bf16[384,1024]{1,0:T(8,128)(2,1)} fusion(bf16[1024,512]{1,0:T(8,128)(2,1)} %copy-done.16, bf16[1024,512]{1,0:T(8,128)(2,1)} %copy-done.15, bf16[1024,512]{1,0:T(8,128)(2,1)} %copy-done.14, bf16[384,512]{0,1:T(8,128)(2,1)} %bitcast.175, bf16[384,512]{0,1:T(8,128)(2,1)} %bitcast.177, bf16[384,512]{0,1:T(8,128)(2,1)S(1)} %bitcast.150), kind=kOutput, calls=%fused_computation.59 | convolution fusion | flops 1221328896 | bytes 5111808 | tf_op jit(solution)/shard_map/dot_general | solution.py:204
  141.0 2.6 %fusion.80 = bf16[1,384,1024]{2,1,0:T(8,128)(2,1)} fusion(bf16[384,1024]{1,0:T(8,128)(2,1)} %collective-permute-done.8, bf16[384,1024]{1,0:T(8,128)(2,1)} %convolution_convert_fusion.3), kind=kLoop, calls=%fused_computation.108 | loop fusion | flops 1572864 | bytes 2359296 | tf_op jit(solution)/shard_map/broadcast_in_dim | solution.py:210
  143.8 36.0 %all-to-all-done.1 = bf16[16,64,1024]{2,1,0:T(8,128)(2,1)S(1)} async-done(((bf16[16,64,1024]{2,1,0:T(8,128)(2,1)}), bf16[16,64,1024]{2,1,0:T(8,128)(2,1)S(1)}, u32[]{:S(2)}, u32[]{:S(2)}) %all-to-all-start.1) | async-done | bytes 2097184 | tf_op jit(solution)/shard_map/all_to_all | solution.py:58
  (140 shorter events, 34.8 us)
Async XLA Ops:
  7.2 19.6 %copy-start.30 = (s32[18]{0:T(128)S(1)}, s32[18]{0:T(128)}, u32[]{:S(2)}) copy-start(s32[18]{0:T(128)} %constant.82) | copy-start | bytes 220
  7.2 10.2 %copy-start.27 = (bf16[1,384,512]{2,1,0:T(8,128)(2,1)S(1)}, bf16[1,384,512]{2,1,0:T(8,128)(2,1)}, u32[]{:S(2)}) copy-start(bf16[1,384,512]{2,1,0:T(8,128)(2,1)} %param.16) | copy-start | bytes 1179652
  7.2 17.0 %copy-start.23 = (bf16[512,512]{1,0:T(8,128)(2,1)S(1)}, bf16[512,512]{1,0:T(8,128)(2,1)}, u32[]{:S(2)}) copy-start(bf16[512,512]{1,0:T(8,128)(2,1)} %param.12) | copy-start | bytes 1572868
  7.2 19.5 %copy-start.31 = (s32[24,7]{0,1:T(8,128)S(1)}, s32[24,7]{0,1:T(8,128)}, u32[]{:S(2)}) copy-start(s32[24,7]{0,1:T(8,128)} %param.15) | copy-start | bytes 2020
  7.2 49.0 %all-gather.2.cloned.1.call-start = ((), (), s32[]{:S(2)}) async-start(), calls=%async_computation.2 | async-start | bytes 3145728 | tf_op jit(solution)/shard_map/all_gather | solution.py:95
  9.6 17.9 %copy-start.34 = (pred[18]{0:T(512)(128)(4,1)S(1)}, pred[18]{0:T(512)(128)(4,1)}, u32[]{:S(2)}) copy-start(pred[18]{0:T(512)(128)(4,1)} %constant.83) | copy-start | bytes 58
  10.7 28.8 %collective-permute-start.1 = (bf16[384,512]{1,0:T(8,128)(2,1)S(1)}, bf16[384,512]{1,0:T(8,128)(2,1)S(1)}, u32[]{:S(2)}, u32[]{:S(2)}) collective-permute-start(bf16[384,512]{1,0:T(8,128)(2,1)S(1)} %dynamic-slice_bitcast_fusion), channel_id=1, source_target_pairs={{4,0},{8,4},{12,8},{16,12},{20,16},{24,20},{28,24},{5,1},{9,5},{13... | collective-permute-start | bytes 1179656 | tf_op jit(solution)/shard_map/ppermute | solution.py:15
  13.1 28.2 %collective-permute-start = (bf16[384,512]{1,0:T(8,128)(2,1)S(1)}, bf16[384,512]{1,0:T(8,128)(2,1)S(1)}, u32[]{:S(2)}, u32[]{:S(2)}) collective-permute-start(bf16[384,512]{1,0:T(8,128)(2,1)S(1)} %dynamic-slice_bitcast_fusion), channel_id=1, source_target_pairs={{0,4},{4,8},{8,12},{12,16},{16,20},{20,24},{24,28},{1,5},{5,9},{9,... | collective-permute-start | bytes 1179656 | tf_op jit(solution)/shard_map/ppermute | solution.py:15
  17.4 29.3 %collective-permute-start.7 = (bf16[384,512]{1,0:T(8,128)(2,1)S(1)}, bf16[384,512]{1,0:T(8,128)(2,1)S(1)}, u32[]{:S(2)}, u32[]{:S(2)}) collective-permute-start(bf16[384,512]{1,0:T(8,128)(2,1)S(1)} %bitcast.158), channel_id=1, source_target_pairs={{4,0},{8,4},{12,8},{16,12},{20,16},{24,20},{28,24},{5,1},{9,5},{13... | collective-permute-start | bytes 1179656 | tf_op jit(solution)/shard_map/ppermute | solution.py:15
  19.4 30.3 %collective-permute-start.6 = (bf16[384,512]{1,0:T(8,128)(2,1)S(1)}, bf16[384,512]{1,0:T(8,128)(2,1)}, u32[]{:S(2)}, u32[]{:S(2)}) collective-permute-start(bf16[384,512]{1,0:T(8,128)(2,1)S(1)} %bitcast.159), channel_id=1, source_target_pairs={{0,4},{4,8},{8,12},{12,16},{16,20},{20,24},{24,28},{1,5},{5,9},{9,... | collective-permute-start | bytes 1179656 | tf_op jit(solution)/shard_map/ppermute | solution.py:15
  24.2 27.7 %collective-permute-start.3 = (bf16[512,512]{1,0:T(8,128)(2,1)S(1)}, bf16[512,512]{1,0:T(8,128)(2,1)}, u32[]{:S(2)}, u32[]{:S(2)}) collective-permute-start(bf16[512,512]{1,0:T(8,128)(2,1)S(1)} %copy-done.23), channel_id=1, source_target_pairs={{0,2},{2,0},{1,3},{3,1},{4,6},{6,4},{5,7},{7,5},{8,10},{10,8},{9,1... | collective-permute-start | bytes 1572872 | tf_op jit(solution)/shard_map/ppermute | solution.py:51
  41.3 12.4 %collective-permute-start.2 = (bf16[2,384,512]{2,1,0:T(8,128)(2,1)S(1)}, bf16[2,384,512]{2,1,0:T(8,128)(2,1)}, u32[]{:S(2)}, u32[]{:S(2)}) collective-permute-start(bf16[2,384,512]{2,1,0:T(8,128)(2,1)S(1)} %pad_maximum_fusion.4), channel_id=1, source_target_pairs={{0,1},{1,0},{2,3},{3,2},{4,5},{5,4},{6,7},{7,6},{8,9},{9,8},{10,11... | collective-permute-start | bytes 2359304 | tf_op jit(solution)/shard_map/ppermute | solution.py:43
  53.8 4.2 %copy-start.14 = (bf16[1024,512]{1,0:T(8,128)(2,1)}, bf16[1024,512]{1,0:T(8,128)(2,1)S(1)}, u32[]{:S(2)}) copy-start(bf16[1024,512]{1,0:T(8,128)(2,1)S(1)} %maximum_select_fusion.1) | copy-start | bytes 3145732
  57.9 3.9 %copy-start.15 = (bf16[1024,512]{1,0:T(8,128)(2,1)}, bf16[1024,512]{1,0:T(8,128)(2,1)S(1)}, u32[]{:S(2)}) copy-start(bf16[1024,512]{1,0:T(8,128)(2,1)S(1)} %get-tuple-element.21) | copy-start | bytes 3145732
  57.9 3.9 %copy-start.16 = (bf16[1024,512]{1,0:T(8,128)(2,1)}, bf16[1024,512]{1,0:T(8,128)(2,1)S(1)}, u32[]{:S(2)}) copy-start(bf16[1024,512]{1,0:T(8,128)(2,1)S(1)} %get-tuple-element.22) | copy-start | bytes 3145732
  69.8 22.8 %copy-start = (bf16[8,128,896]{2,1,0:T(8,128)(2,1)}, bf16[8,128,896]{2,1,0:T(8,128)(2,1)S(1)}, u32[]{:S(2)}) copy-start(bf16[8,128,896]{2,1,0:T(8,128)(2,1)S(1)} %get-tuple-element.17) | copy-start | bytes 5505028
  75.9 17.6 %copy-start.2 = (bf16[8,128,896]{2,1,0:T(8,128)(2,1)}, bf16[8,128,896]{2,1,0:T(8,128)(2,1)S(1)}, u32[]{:S(2)}) copy-start(bf16[8,128,896]{2,1,0:T(8,128)(2,1)S(1)} %get-tuple-element.13) | copy-start | bytes 5505028
  80.8 13.7 %copy-start.4 = (bf16[8,128,896]{2,1,0:T(8,128)(2,1)}, bf16[8,128,896]{2,1,0:T(8,128)(2,1)S(1)}, u32[]{:S(2)}) copy-start(bf16[8,128,896]{2,1,0:T(8,128)(2,1)S(1)} %get-tuple-element.15) | copy-start | bytes 5505028
  80.8 3.6 %copy-start.10 = (bf16[1,384,1024]{2,1,0:T(8,128)(2,1)S(1)}, bf16[1,384,1024]{2,1,0:T(8,128)(2,1)}, u32[]{:S(2)}) copy-start(bf16[1,384,1024]{2,1,0:T(8,128)(2,1)} %param.11) | copy-start | bytes 2359300
  80.9 22.2 %collective-permute-start.4 = (f32[3,8,384,1]{2,1,3,0:T(8,128)S(1)}, f32[3,8,384,1]{2,1,3,0:T(8,128)S(1)}, u32[]{:S(2)}, u32[]{:S(2)}) collective-permute-start(f32[3,8,384,1]{2,1,3,0:T(8,128)S(1)} %pad_maximum_fusion.8), channel_id=1, source_target_pairs={{0,4},{4,8},{8,12},{12,16},{16,20},{20,24},{24,28},{1,5},{5,9},{9,... | collective-permute-start | bytes 110600 | tf_op jit(solution)/shard_map/ppermute | solution.py:15
  84.3 3.7 %copy-start.12 = (bf16[8,384,64]{1,2,0:T(8,128)(2,1)}, bf16[8,384,64]{1,2,0:T(8,128)(2,1)S(1)}, u32[]{:S(2)}) copy-start(bf16[8,384,64]{1,2,0:T(8,128)(2,1)S(1)} %pad_maximum_fusion.7) | copy-start | bytes 1179652
  88.1 15.0 %collective-permute-start.5 = (f32[3,8,384,1]{2,1,3,0:T(8,128)S(1)}, f32[3,8,384,1]{2,1,3,0:T(8,128)S(1)}, u32[]{:S(2)}, u32[]{:S(2)}) collective-permute-start(f32[3,8,384,1]{2,1,3,0:T(8,128)S(1)} %pad_maximum_fusion.8), channel_id=1, source_target_pairs={{4,0},{8,4},{12,8},{16,12},{20,16},{24,20},{28,24},{5,1},{9,5},{13... | collective-permute-start | bytes 110600 | tf_op jit(solution)/shard_map/ppermute | solution.py:15
  96.9 31.1 %all-to-all-start = ((bf16[16,64,512]{2,1,0:T(8,128)(2,1)}), bf16[16,64,512]{2,1,0:T(8,128)(2,1)S(1)}, u32[]{:S(2)}, u32[]{:S(2)}) async-start(bf16[16,64,512]{2,1,0:T(8,128)(2,1)} %bitcast.136), calls=%async_computation | async-start | bytes 2097152 | tf_op jit(solution)/shard_map/all_to_all | solution.py:58
  103.1 5.0 %copy-start.6 = (bf16[768,512]{0,1:T(8,128)(2,1)S(1)}, bf16[768,512]{0,1:T(8,128)(2,1)}, u32[]{:S(2)}) copy-start(bf16[768,512]{0,1:T(8,128)(2,1)} %copy.32) | copy-start | bytes 2359300
  108.1 3.2 %copy-start.20 = (bf16[8,128,384]{2,1,0:T(8,128)(2,1)S(1)}, bf16[8,128,384]{2,1,0:T(8,128)(2,1)}, u32[]{:S(2)}) copy-start(bf16[8,128,384]{2,1,0:T(8,128)(2,1)} %slice.178) | copy-start | bytes 2359300
  108.1 3.2 %copy-start.21 = (bf16[8,128,384]{2,1,0:T(8,128)(2,1)S(1)}, bf16[8,128,384]{2,1,0:T(8,128)(2,1)}, u32[]{:S(2)}) copy-start(bf16[8,128,384]{2,1,0:T(8,128)(2,1)} %slice.176) | copy-start | bytes 2359300
  115.6 17.3 %copy-start.13 = (bf16[8,384,64]{1,2,0:T(8,128)(2,1)S(1)}, bf16[8,384,64]{1,2,0:T(8,128)(2,1)}, u32[]{:S(2)}) copy-start(bf16[8,384,64]{1,2,0:T(8,128)(2,1)} %copy-done.12) | copy-start | bytes 1179652
  127.9 51.9 %all-to-all-start.1 = ((bf16[16,64,1024]{2,1,0:T(8,128)(2,1)}), bf16[16,64,1024]{2,1,0:T(8,128)(2,1)S(1)}, u32[]{:S(2)}, u32[]{:S(2)}) async-start(bf16[16,64,1024]{2,1,0:T(8,128)(2,1)} %bitcast.139), calls=%async_computation.1 | async-start | bytes 4194304 | tf_op jit(solution)/shard_map/all_to_all | solution.py:58
  132.9 4.6 %copy-start.1 = (bf16[8,128,896]{2,1,0:T(8,128)(2,1)S(1)}, bf16[8,128,896]{2,1,0:T(8,128)(2,1)}, u32[]{:S(2)}) copy-start(bf16[8,128,896]{2,1,0:T(8,128)(2,1)} %copy-done) | copy-start | bytes 5505028
  132.9 4.6 %copy-start.8 = (bf16[1152,512]{0,1:T(8,128)(2,1)S(1)}, bf16[1152,512]{0,1:T(8,128)(2,1)}, u32[]{:S(2)}) copy-start(bf16[1152,512]{0,1:T(8,128)(2,1)} %copy.25) | copy-start | bytes 3538948
  132.9 5.4 %copy-start.3 = (bf16[8,128,896]{2,1,0:T(8,128)(2,1)S(1)}, bf16[8,128,896]{2,1,0:T(8,128)(2,1)}, u32[]{:S(2)}) copy-start(bf16[8,128,896]{2,1,0:T(8,128)(2,1)} %copy-done.2) | copy-start | bytes 5505028
  137.5 3.5 %collective-permute-start.8 = (bf16[384,1024]{1,0:T(8,128)(2,1)}, bf16[384,1024]{1,0:T(8,128)(2,1)}, u32[]{:S(2)}, u32[]{:S(2)}) collective-permute-start(bf16[384,1024]{1,0:T(8,128)(2,1)} %convolution_convert_fusion.3), channel_id=1, source_target_pairs={{0,1},{1,0},{2,3},{3,2},{4,5},{5,4},{6,7},{7,6},{8,9},{9,8},{10,11... | collective-permute-start | bytes 2359304 | tf_op jit(solution)/shard_map/ppermute | solution.py:68
  (15 other events, 29.0 us)
Sparse Core Ops, SparseCore 0:
  9.7 45.4 all-gather.1
